TPU v7x, 32 devices: a whole 2x2x4 slice. The times are simulated.
32 devices in a mesh: groups: 2 (over x), frame: 16 (over z, y, core).
Axes of the slice: x: 2, y: 2, z: 4, core: 2. Of those that a mesh axis runs over, the one named last changes fastest.
Arguments:
- latents: bfloat16 [32, 72, 32, 320], P(('groups', 'frame')), parts along dimension 0, may hold values from -30 to 30
- conv1_weight: bfloat16 [3, 3, 320, 320], replicated, may hold values from -0.109375 to 0.109375
- qkv_weight: bfloat16 [320, 960], replicated, may hold values from -0.3125 to 0.3125
- out_weight: bfloat16 [320, 320], replicated, may hold values from -0.3125 to 0.3125
- pos_bias: float32 [5, 4, 4], replicated, may hold values from -4 to 305
- conv2_weight: bfloat16 [3, 3, 320, 320], replicated, may hold values from -0.109375 to 0.109375
Outputs:
- denoised: bfloat16 [32, 72, 32, 320], P(('groups', 'frame')), parts along dimension 0
There are 2 independent parts, one for each index of `groups`. A program takes and returns all parts, laid end to end along the dimension named above; an argument that names none is the same for every part. Nothing has to cross between parts.
All inputs are finite; a program needn't handle non-finite values.
Results may differ from a plain program's by a relative error of at most 0.01.
Values may be sent and summed in bfloat16 or wider, within the bound.
No kernel may reach another device: no remote copies, remote signals or barrier semaphores. Data moves between devices by JAX's collectives and lax.ppermute only.
A program may use at most 128 MiB of HBM per device.

v0:
```python
import jax
import jax.numpy as jnp
from jax import lax
from jax.experimental import pallas as pl
from jax.experimental.pallas import tpu as pltpu
from jax.sharding import Mesh, PartitionSpec as P

HEADS = 5


def shifted(block, axis, distance):
    devices = range(lax.axis_size(axis))
    route = [(i - distance, i) for i in devices if i - distance in devices]
    return lax.ppermute(block, axis, route)


def convolve(field_in, weight):
    left_rim = shifted(field_in[:, :, -1:, :], "quarter", 1)
    right_rim = shifted(field_in[:, :, :1, :], "quarter", -1)
    widened = jnp.concatenate([left_rim, field_in, right_rim], axis=2)
    return lax.conv_general_dilated(
        widened,
        weight,
        (1, 1),
        ((1, 1), (0, 0)),
        dimension_numbers=("NHWC", "HWIO", "NHWC"),
        preferred_element_type=jnp.float32,
    )


def attend_kernel(x_ref, wqkv_ref, bias_ref, wout_ref, o_ref, qkv_s, blend_s):
    frames_all, count, channels = x_ref.shape
    head_dim = channels // HEADS
    scale = head_dim ** (-0.5)
    block = min(frames_all, 4)

    def project(f, carry):
        qkv_s[f] = lax.dot_general(
            wqkv_ref[...], x_ref[f], (((1,), (1,)), ((), ())), preferred_element_type=jnp.float32
        ).astype(jnp.bfloat16)
        return carry

    lax.fori_loop(0, frames_all, project, 0, unroll=frames_all <= 4)

    def head_block(h, first):
        frames = pl.ds(first, block)
        queries = qkv_s[frames, pl.ds(h * head_dim, head_dim), :].astype(jnp.float32)
        scores = []
        for g in range(frames_all):
            key_part = qkv_s[g, pl.ds(channels + h * head_dim, head_dim), :].astype(jnp.float32)
            bias = bias_ref[h, g, frames]
            scores.append(jnp.sum(queries * key_part[None], axis=1) * scale + bias)
        top = scores[0]
        for g in range(1, frames_all):
            top = jnp.maximum(top, scores[g])
        weights = [jnp.exp(s - top) for s in scores]
        total = weights[0]
        for g in range(1, frames_all):
            total = total + weights[g]
        blended = None
        for g in range(frames_all):
            value_part = qkv_s[g, pl.ds(2 * channels + h * head_dim, head_dim), :].astype(jnp.float32)
            prob = (weights[g] / total).astype(jnp.bfloat16).astype(jnp.float32)
            term = prob[:, None, :] * value_part[None]
            blended = term if blended is None else blended + term
        blend_s[frames, pl.ds(h * head_dim, head_dim), :] = blended.astype(jnp.bfloat16)

    def frame_block(i, carry):
        for h in range(HEADS):
            head_block(h, i * block)
        return carry

    lax.fori_loop(0, frames_all // block, frame_block, 0, unroll=frames_all <= 4)

    def out_project(f, carry):
        o_ref[f] = jnp.dot(wout_ref[...], blend_s[f], preferred_element_type=jnp.float32).astype(
            jnp.bfloat16
        )
        return carry

    lax.fori_loop(0, frames_all, out_project, 0, unroll=frames_all <= 4)


def attend(grid, qkv_weight, pos_bias, out_weight):
    frames_all, count, channels = grid.shape
    vmem = pl.BlockSpec(memory_space=pltpu.VMEM)
    return pl.pallas_call(
        attend_kernel,
        out_shape=jax.ShapeDtypeStruct((frames_all, channels, count), jnp.bfloat16),
        in_specs=[vmem] * 4,
        out_specs=vmem,
        scratch_shapes=[
            pltpu.VMEM((frames_all, 3 * channels, count), jnp.bfloat16),
            pltpu.VMEM((frames_all, channels, count), jnp.bfloat16),
        ],
    )(grid, qkv_weight.T, pos_bias.transpose(0, 2, 1)[..., None], out_weight.T)


def body(latents, conv1_weight, qkv_weight, out_weight, pos_bias, conv2_weight):
    frames_dev, row_count, col_count, channels = latents.shape
    frames_all = lax.axis_size("frame")
    pix_piece = row_count * col_count // frames_all
    first = convolve(latents, conv1_weight)
    normed = first * lax.rsqrt(jnp.mean(first * first, axis=-1, keepdims=True) + 1e-06)
    hidden = jax.nn.gelu(normed, approximate=True).astype(jnp.bfloat16)
    pieces = lax.all_to_all(
        hidden.reshape(frames_all, pix_piece, channels), "frame", split_axis=0, concat_axis=0, tiled=True
    )
    attended = attend(pieces, qkv_weight, pos_bias, out_weight)
    returned = lax.all_to_all(attended, "frame", split_axis=0, concat_axis=0, tiled=True)
    returned = returned.transpose(0, 2, 1).reshape(frames_dev, row_count, col_count, channels)
    joined = (hidden.astype(jnp.float32) + returned.astype(jnp.float32)).astype(jnp.bfloat16)
    return convolve(joined, conv2_weight).astype(jnp.bfloat16)


def solution(mesh):
    groups = mesh.shape["groups"]
    frames_all = mesh.shape["frame"] // 4
    split_mesh = Mesh(
        mesh.devices.reshape(groups, 4, frames_all), ("groups", "quarter", "frame")
    )
    tiles = P(("groups", "quarter", "frame"), None, None, None)
    placed = (tiles, P(), P(), P(), P(), P())
    return jax.shard_map(
        body,
        mesh=split_mesh,
        in_specs=placed,
        out_specs=tiles,
        check_vma=False,
    )
```

profile of v0, /device:TPU:0, one launch (start us, length us, event | category | flops | bytes accessed | tf_op | source)
XLA Modules:
  0.0 175.0 jit_solution(11740959580542453253)
XLA Ops:
  0.0 5.6 %copy.46 = bf16[1,72,32,320]{3,0,2,1:T(2,128)(2,1)S(1)} copy(bf16[1,72,32,320]{3,2,1,0:T(8,128)(2,1)} %param.6) | data formatting | bytes 2949120 | tf_op args[0]
  5.6 0.2 fusion.24
  5.9 4.9 %collective-permute-start = (bf16[1,72,1,320]{3,0,2,1:T(2,128)(2,1)S(1)}, bf16[1,72,1,320]{3,0,2,1:T(2,128)(2,1)S(1)}, u32[]{:S(2)}, u32[]{:S(2)}) collective-permute-start(bf16[1,72,1,320]{3,0,2,1:T(2,128)(2,1)S(1)} %get-tuple-element.5), channel_id=1, source_target_pairs={{0,4},{4,8},{8,12},{1,5},{5,9},{9,13},{2,6},{6,10},{10,14},{3,7},{... | collective-permute-start | bytes 138248 | tf_op jit(solution)/shard_map/ppermute | solution.py:14
  10.8 1.5 collective-permute-start.1
  12.3 0.8 collective-permute-done
  13.1 4.3 %collective-permute-done.1 = bf16[1,72,1,320]{3,0,2,1:T(2,128)(2,1)S(1)} collective-permute-done((bf16[1,72,1,320]{3,0,2,1:T(2,128)(2,1)S(1)}, bf16[1,72,1,320]{3,0,2,1:T(2,128)(2,1)S(1)}, u32[]{:S(2)}, u32[]{:S(2)}) %collective-permute-start.1) | collective-permute-done | bytes 46112 | tf_op jit(solution)/shard_map/ppermute | solution.py:14
  17.5 53.7 %multiply_reduce_fusion = (f32[72,32]{1,0:T(8,128)S(1)}, f32[1,72,32,320]{3,0,2,1:T(1,128)S(1)}) fusion(bf16[3,3,320,320]{3,2,1,0:T(8,128)(2,1)S(1)} %copy-done.5, bf16[1,72,1,320]{3,0,2,1:T(2,128)(2,1)S(1)} %collective-permute-done.1, bf16[1,72,32,320]{3,0,2,1:T(2,128)(2,1)S(1)} %copy.46, bf16[1,72,1,320]{3,0,2,1:T(2,128)(2,1)S(1)} %collective-permute-done), kind=kOutput, calls=%fused_computation.16 | convolution fusion | flops 4213583616 | bytes 6368256 | tf_op jit(solution)/shard_map/conv_general_dilated | solution.py:21
  71.2 1.7 copy-done.1
  73.0 2.4 %fusion.9 = bf16[1,72,32,320]{3,2,1,0:T(8,128)(2,1)} fusion(f32[1,72,32,320]{3,0,2,1:T(1,128)S(1)} %get-tuple-element.10, f32[72,32]{1,0:T(8,128)S(1)} %add_rsqrt_fusion), kind=kLoop, calls=%fused_computation.13 | loop fusion | flops 7372800 | bytes 4432896 | tf_op jit(solution)/shard_map/convert_element_type | solution.py:105
  75.3 3.8 %copy.50 = bf16[4,576,320]{1,2,0:T(8,128)(2,1)} copy(bf16[4,576,320]{2,1,0:T(8,128)(2,1)} %bitcast.27) | data formatting | bytes 2949120 | tf_op jit(solution)/shard_map/reshape | solution.py:107
  79.2 4.6 %all-to-all-start = ((bf16[4,576,320]{1,2,0:T(8,128)(2,1)}), bf16[4,576,320]{1,2,0:T(8,128)(2,1)}, u32[]{:S(2)}, u32[]{:S(2)}) async-start(bf16[4,576,320]{1,2,0:T(8,128)(2,1)} %copy.50), calls=%async_computation | async-start | bytes 3276800 | tf_op jit(solution)/shard_map/all_to_all | solution.py:106
  83.8 0.8 copy.55.bias_ref
  84.6 0.9 copy.53
  85.5 1.1 copy.51
  86.6 17.8 %all-to-all-done = bf16[4,576,320]{1,2,0:T(8,128)(2,1)} async-done(((bf16[4,576,320]{1,2,0:T(8,128)(2,1)}), bf16[4,576,320]{1,2,0:T(8,128)(2,1)}, u32[]{:S(2)}, u32[]{:S(2)}) %all-to-all-start) | async-done | bytes 1474592 | tf_op jit(solution)/shard_map/all_to_all | solution.py:106
  104.4 3.6 %copy.54.x_ref = bf16[4,576,320]{2,1,0:T(8,128)(2,1)} copy(bf16[4,576,320]{1,2,0:T(8,128)(2,1)} %all-to-all-done) | data formatting | bytes 2949120 | tf_op jit(solution)/shard_map/all_to_all | solution.py:106
  108.0 8.0 %shard_map.64 = bf16[4,320,576]{2,1,0:T(8,128)(2,1)} custom-call(bf16[4,576,320]{2,1,0:T(8,128)(2,1)} %copy.54.x_ref, bf16[960,320]{1,0:T(8,128)(2,1)} %bitcast.28, f32[5,4,4,1]{3,2,1,0:T(4,128)} %copy.55.bias_ref, bf16[320,320]{1,0:T(8,128)(2,1)} %bitcast.29), custom_call_target="tpu_custom_call" | custom-call | tf_op jit(solution)/shard_map/pallas_call | solution.py:87
  116.0 24.3 %all_to_all.10 = bf16[4,320,576]{2,1,0:T(8,128)(2,1)S(1)} all-to-all(bf16[4,320,576]{2,1,0:T(8,128)(2,1)} %shard_map.64), channel_id=1, replica_groups=mesh['groups'=2,'quarter'=4,'frame'=4] {'frame'}, dimensions={0} | all-to-all | bytes 2949120 | tf_op jit(solution)/shard_map/all_to_all | solution.py:110
  140.3 2.0 %convert_bitcast_fusion = f32[4,576,320]{1,2,0:T(8,128)} fusion(bf16[4,320,576]{2,1,0:T(8,128)(2,1)S(1)} %all_to_all.10), kind=kLoop, calls=%fused_computation.17 | loop fusion | flops 737280 | bytes 4423680 | tf_op jit(solution)/shard_map/convert_element_type | solution.py:112
  142.3 4.8 %copy.56 = f32[4,576,320]{2,1,0:T(8,128)} copy(f32[4,576,320]{1,2,0:T(8,128)} %convert_bitcast_fusion) | data formatting | bytes 5898240 | tf_op jit(solution)/shard_map/convert_element_type | solution.py:112
  147.1 3.9 %add_convert_fusion = bf16[1,72,32,320]{3,2,1,0:T(8,128)(2,1)S(1)} fusion(f32[1,72,32,320]{3,2,1,0:T(8,128)} %bitcast.23, f32[72,32]{1,0:T(8,128)S(1)} %add_rsqrt_fusion, f32[1,72,32,320]{3,0,2,1:T(1,128)} %copy-done.1), kind=kLoop, calls=%fused_computation.15 | loop fusion | flops 9584640 | bytes 7382016 | tf_op jit(solution)/shard_map/convert_element_type | solution.py:112
  151.1 3.5 %collective-permute-start.2 = (bf16[1,72,1,320]{3,2,1,0:T(2,128)(2,1)S(1)}, bf16[1,72,1,320]{3,2,1,0:T(2,128)(2,1)S(1)}, u32[]{:S(2)}, u32[]{:S(2)}) collective-permute-start(bf16[1,72,1,320]{3,2,1,0:T(2,128)(2,1)S(1)} %get-tuple-element.7), channel_id=1, source_target_pairs={{0,4},{4,8},{8,12},{1,5},{5,9},{9,13},{2,6},{6,10},{10,14},{3,7},{... | collective-permute-start | bytes 138248 | tf_op jit(solution)/shard_map/ppermute | solution.py:14
  154.6 1.6 collective-permute-start.3
  156.2 0.7 collective-permute-done.2
  156.9 4.3 %collective-permute-done.3 = bf16[1,72,1,320]{3,2,1,0:T(2,128)(2,1)S(1)} collective-permute-done((bf16[1,72,1,320]{3,2,1,0:T(2,128)(2,1)S(1)}, bf16[1,72,1,320]{3,2,1,0:T(2,128)(2,1)S(1)}, u32[]{:S(2)}, u32[]{:S(2)}) %collective-permute-start.3) | collective-permute-done | bytes 46112 | tf_op jit(solution)/shard_map/ppermute | solution.py:14
  161.3 1.3 pad_maximum_fusion.2
  162.6 0.2 copy.70
  162.9 0.2 pad
  163.1 0.3 copy.59
  163.8 9.3 %select_convert_fusion = bf16[72,8,5,320]{3,1,2,0:T(8,128)(2,1)S(1)} fusion(pred[8,5]{0,1:T(8,128)(4,1)S(1)} %copy-done.6, bf16[3,3,320,320]{3,2,1,0:T(8,128)(2,1)S(1)} %copy-done, bf16[72,1,7,2,320]{4,2,3,0,1:T(8,128)(2,1)S(1)} %slice.22, bf16[72,1,8,5,320]{4,2,3,0,1:T(8,128)(2,1)S(1)} %copy.59), kind=kOutput, calls=%fused_computation.3 | convolution fusion | flops 5268848640 | bytes 6174760 | tf_op jit(solution)/shard_map/conv_general_dilated | solution.py:21
  173.1 0.3 copy.60
  173.6 1.5 copy.61
  (17 shorter events, 0.8 us)
Async XLA Ops:
  0.0 163.6 %copy-start = (bf16[3,3,320,320]{3,2,1,0:T(8,128)(2,1)S(1)}, bf16[3,3,320,320]{3,2,1,0:T(8,128)(2,1)}, u32[]{:S(2)}) copy-start(bf16[3,3,320,320]{3,2,1,0:T(8,128)(2,1)} %param.11) | copy-start | bytes 5529604
  0.0 17.5 %copy-start.5 = (bf16[3,3,320,320]{3,2,1,0:T(8,128)(2,1)S(1)}, bf16[3,3,320,320]{3,2,1,0:T(8,128)(2,1)}, u32[]{:S(2)}) copy-start(bf16[3,3,320,320]{3,2,1,0:T(8,128)(2,1)} %param.7) | copy-start | bytes 5529604
  5.9 7.2 %collective-permute-start = (bf16[1,72,1,320]{3,0,2,1:T(2,128)(2,1)S(1)}, bf16[1,72,1,320]{3,0,2,1:T(2,128)(2,1)S(1)}, u32[]{:S(2)}, u32[]{:S(2)}) collective-permute-start(bf16[1,72,1,320]{3,0,2,1:T(2,128)(2,1)S(1)} %get-tuple-element.5), channel_id=1, source_target_pairs={{0,4},{4,8},{8,12},{1,5},{5,9},{9,13},{2,6},{6,10},{10,14},{3,7},{... | collective-permute-start | bytes 138248 | tf_op jit(solution)/shard_map/ppermute | solution.py:14
  10.8 6.6 %collective-permute-start.1 = (bf16[1,72,1,320]{3,0,2,1:T(2,128)(2,1)S(1)}, bf16[1,72,1,320]{3,0,2,1:T(2,128)(2,1)S(1)}, u32[]{:S(2)}, u32[]{:S(2)}) collective-permute-start(bf16[1,72,1,320]{3,0,2,1:T(2,128)(2,1)S(1)} %get-tuple-element.6), channel_id=1, source_target_pairs={{4,0},{8,4},{12,8},{5,1},{9,5},{13,9},{6,2},{10,6},{14,10},{7,3},{... | collective-permute-start | bytes 138248 | tf_op jit(solution)/shard_map/ppermute | solution.py:14
  71.2 1.8 %copy-start.1 = (f32[1,72,32,320]{3,0,2,1:T(1,128)}, f32[1,72,32,320]{3,0,2,1:T(1,128)S(1)}, u32[]{:S(2)}) copy-start(f32[1,72,32,320]{3,0,2,1:T(1,128)S(1)} %get-tuple-element.10) | copy-start | bytes 8847364
  75.3 8.5 %copy-start.4 = (f32[5,4,4]{0,2,1:T(4,128)S(1)}, f32[5,4,4]{0,2,1:T(4,128)}, u32[]{:S(2)}) copy-start(f32[5,4,4]{0,2,1:T(4,128)} %param.10) | copy-start | bytes 964
  75.3 9.3 %copy-start.3 = (bf16[320,320]{1,0:T(8,128)(2,1)S(1)}, bf16[320,320]{1,0:T(8,128)(2,1)}, u32[]{:S(2)}) copy-start(bf16[320,320]{1,0:T(8,128)(2,1)} %param.9) | copy-start | bytes 614404
  75.3 10.2 %copy-start.2 = (bf16[320,960]{1,0:T(8,128)(2,1)S(1)}, bf16[320,960]{1,0:T(8,128)(2,1)}, u32[]{:S(2)}) copy-start(bf16[320,960]{1,0:T(8,128)(2,1)} %param.8) | copy-start | bytes 1843204
  79.2 25.2 %all-to-all-start = ((bf16[4,576,320]{1,2,0:T(8,128)(2,1)}), bf16[4,576,320]{1,2,0:T(8,128)(2,1)}, u32[]{:S(2)}, u32[]{:S(2)}) async-start(bf16[4,576,320]{1,2,0:T(8,128)(2,1)} %copy.50), calls=%async_computation | async-start | bytes 3276800 | tf_op jit(solution)/shard_map/all_to_all | solution.py:106
  151.1 5.8 %collective-permute-start.2 = (bf16[1,72,1,320]{3,2,1,0:T(2,128)(2,1)S(1)}, bf16[1,72,1,320]{3,2,1,0:T(2,128)(2,1)S(1)}, u32[]{:S(2)}, u32[]{:S(2)}) collective-permute-start(bf16[1,72,1,320]{3,2,1,0:T(2,128)(2,1)S(1)} %get-tuple-element.7), channel_id=1, source_target_pairs={{0,4},{4,8},{8,12},{1,5},{5,9},{9,13},{2,6},{6,10},{10,14},{3,7},{... | collective-permute-start | bytes 138248 | tf_op jit(solution)/shard_map/ppermute | solution.py:14
  154.6 6.6 %collective-permute-start.3 = (bf16[1,72,1,320]{3,2,1,0:T(2,128)(2,1)S(1)}, bf16[1,72,1,320]{3,2,1,0:T(2,128)(2,1)S(1)}, u32[]{:S(2)}, u32[]{:S(2)}) collective-permute-start(bf16[1,72,1,320]{3,2,1,0:T(2,128)(2,1)S(1)} %get-tuple-element.8), channel_id=1, source_target_pairs={{4,0},{8,4},{12,8},{5,1},{9,5},{13,9},{6,2},{10,6},{14,10},{7,3},{... | collective-permute-start | bytes 138248 | tf_op jit(solution)/shard_map/ppermute | solution.py:14
  163.1 0.7 copy-start.6
where the time goes:
time: 176 us; the launch traced here: 175 us
  matrix products  63.1 us (36%)
  waiting for transfers between devices  28 us (16%)
  local copies, waits for them, and re-layouts  25.9 us (15%)
  blocking collectives  24.3 us (14%)
  starting transfers between devices  16 us (9%)
  other arithmetic  9.53 us (5%)
  Pallas kernels  7.97 us (5%)
    conv_general_dilated x2, matrix products, convolve(): lax.conv_general_dilated(widened, weight, (1, 1), ((1, 1), (0, 0)), dimen...  63.1 us
    all_to_all x1, blocking collectives, body(): lax.all_to_all(attended, 'frame', split_axis=0, concat_axis=0, tiled=True)  24.3 us
    all_to_all x1, waiting for transfers between devices, body(): lax.all_to_all(hidden.reshape(frames_all, pix_piece, channels), 'frame',...  17.8 us
    ppermute x4, starting transfers between devices, shifted(): return lax.ppermute(block, axis, route)  11.4 us
    ppermute x4, waiting for transfers between devices, shifted(): return lax.ppermute(block, axis, route)  10.2 us
    unnamed x17, local copies, waits for them, and re-layouts  9.51 us
    pallas_call x1, Pallas kernels, attend(): pl.pallas_call(attend_kernel, out_shape=jax.ShapeDtypeStruct((frames_all,...  7.97 us
    convert_element_type x1, local copies, waits for them, and re-layouts, body(): returned.astype(jnp.float32)  4.83 us
  transfers between devices with their start and end apart: 5, of which 5 were waited for; matrix products, arithmetic and copies ran while one was open for 2% of the time, Pallas kernels for 0%

commit v1 on v0

--- a/solution.py
+++ b/solution.py
@@ -1,3 +1,5 @@
+import functools
+
 import jax
 import jax.numpy as jnp
 from jax import lax
@@ -14,18 +16,77 @@
     return lax.ppermute(block, axis, route)
 
 
-def convolve(field_in, weight):
-    left_rim = shifted(field_in[:, :, -1:, :], "quarter", 1)
-    right_rim = shifted(field_in[:, :, :1, :], "quarter", -1)
-    widened = jnp.concatenate([left_rim, field_in, right_rim], axis=2)
-    return lax.conv_general_dilated(
-        widened,
-        weight,
-        (1, 1),
-        ((1, 1), (0, 0)),
-        dimension_numbers=("NHWC", "HWIO", "NHWC"),
-        preferred_element_type=jnp.float32,
-    )
+def conv_kernel(*refs, parts, finish):
+    sources = refs[:parts]
+    left_ref, right_ref, w_ref, o_ref, side_l, side_c, side_r, shift_s = refs[parts:]
+    row_count, col_count, channels = o_ref.shape
+    band = 8
+    span = band * col_count
+    zeros = jnp.zeros((col_count, channels), jnp.bfloat16)
+    for side in (side_l, side_c, side_r):
+        side[pl.ds(0, col_count)] = zeros
+        side[pl.ds((row_count + 1) * col_count, col_count)] = zeros
+    column = lax.broadcasted_iota(jnp.int32, (band, col_count, channels), 1)
+
+    def build(i, carry):
+        r0 = i * band
+        block = sources[0][pl.ds(r0, band)].astype(jnp.float32)
+        for extra in sources[1:]:
+            block = block + extra[pl.ds(r0, band)].astype(jnp.float32)
+        block = block.astype(jnp.bfloat16)
+        flat = block.astype(jnp.float32).reshape(span, channels)
+        shift_s[pl.ds(8, span)] = flat
+        before = shift_s[pl.ds(7, span)].reshape(band, col_count, channels)
+        after = shift_s[pl.ds(9, span)].reshape(band, col_count, channels)
+        rim_l = left_ref[pl.ds(r0, band)].astype(jnp.float32)[:, None, :]
+        rim_r = right_ref[pl.ds(r0, band)].astype(jnp.float32)[:, None, :]
+        before = jnp.where(column == 0, rim_l, before)
+        after = jnp.where(column == col_count - 1, rim_r, after)
+        at = pl.ds(pl.multiple_of((r0 + 1) * col_count, col_count), span)
+        side_c[at] = block.reshape(span, channels)
+        side_l[at] = before.reshape(span, channels).astype(jnp.bfloat16)
+        side_r[at] = after.reshape(span, channels).astype(jnp.bfloat16)
+        return carry
+
+    lax.fori_loop(0, row_count // band, build, 0)
+
+    def compute(i, carry):
+        r0 = i * band
+        acc = None
+        for a in range(3):
+            at = pl.ds(pl.multiple_of((r0 + a) * col_count, col_count), span)
+            for b, side in enumerate((side_l, side_c, side_r)):
+                term = jnp.dot(side[at], w_ref[a, b], preferred_element_type=jnp.float32)
+                acc = term if acc is None else acc + term
+        o_ref[pl.ds(r0, band)] = finish(acc).reshape(band, col_count, channels)
+        return carry
+
+    lax.fori_loop(0, row_count // band, compute, 0)
+
+
+def norm_gelu(first):
+    normed = first * lax.rsqrt(jnp.mean(first * first, axis=-1, keepdims=True) + 1e-06)
+    return jax.nn.gelu(normed, approximate=True).astype(jnp.bfloat16)
+
+
+def to_bf16(acc):
+    return acc.astype(jnp.bfloat16)
+
+
+def convolve(sources, edge_of, weight, finish):
+    row_count, col_count, channels = sources[0].shape
+    left_rim = shifted(edge_of(-1), "quarter", 1)
+    right_rim = shifted(edge_of(0), "quarter", -1)
+    vmem = pl.BlockSpec(memory_space=pltpu.VMEM)
+    padded = (row_count + 2) * col_count
+    return pl.pallas_call(
+        functools.partial(conv_kernel, parts=len(sources), finish=finish),
+        out_shape=jax.ShapeDtypeStruct((row_count, col_count, channels), jnp.bfloat16),
+        in_specs=[vmem] * (len(sources) + 3),
+        out_specs=vmem,
+        scratch_shapes=[pltpu.VMEM((padded, channels), jnp.bfloat16)] * 3
+        + [pltpu.VMEM((8 * col_count + 16, channels), jnp.float32)],
+    )(*sources, left_rim, right_rim, weight)
 
 
 def attend_kernel(x_ref, wqkv_ref, bias_ref, wout_ref, o_ref, qkv_s, blend_s):
@@ -73,9 +134,9 @@
     lax.fori_loop(0, frames_all // block, frame_block, 0, unroll=frames_all <= 4)
 
     def out_project(f, carry):
-        o_ref[f] = jnp.dot(wout_ref[...], blend_s[f], preferred_element_type=jnp.float32).astype(
-            jnp.bfloat16
-        )
+        o_ref[f] = lax.dot_general(
+            blend_s[f], wout_ref[...], (((0,), (0,)), ((), ())), preferred_element_type=jnp.float32
+        ).astype(jnp.bfloat16)
         return carry
 
     lax.fori_loop(0, frames_all, out_project, 0, unroll=frames_all <= 4)
@@ -86,31 +147,35 @@
     vmem = pl.BlockSpec(memory_space=pltpu.VMEM)
     return pl.pallas_call(
         attend_kernel,
-        out_shape=jax.ShapeDtypeStruct((frames_all, channels, count), jnp.bfloat16),
+        out_shape=jax.ShapeDtypeStruct((frames_all, count, channels), jnp.bfloat16),
         in_specs=[vmem] * 4,
         out_specs=vmem,
         scratch_shapes=[
             pltpu.VMEM((frames_all, 3 * channels, count), jnp.bfloat16),
             pltpu.VMEM((frames_all, channels, count), jnp.bfloat16),
         ],
-    )(grid, qkv_weight.T, pos_bias.transpose(0, 2, 1)[..., None], out_weight.T)
+    )(grid, qkv_weight.T, pos_bias.transpose(0, 2, 1)[..., None], out_weight)
 
 
 def body(latents, conv1_weight, qkv_weight, out_weight, pos_bias, conv2_weight):
     frames_dev, row_count, col_count, channels = latents.shape
     frames_all = lax.axis_size("frame")
     pix_piece = row_count * col_count // frames_all
-    first = convolve(latents, conv1_weight)
-    normed = first * lax.rsqrt(jnp.mean(first * first, axis=-1, keepdims=True) + 1e-06)
-    hidden = jax.nn.gelu(normed, approximate=True).astype(jnp.bfloat16)
+    tile = latents.reshape(row_count, col_count, channels)
+    hidden = convolve([tile], lambda c: tile[:, c, :], conv1_weight, norm_gelu)
     pieces = lax.all_to_all(
         hidden.reshape(frames_all, pix_piece, channels), "frame", split_axis=0, concat_axis=0, tiled=True
     )
     attended = attend(pieces, qkv_weight, pos_bias, out_weight)
     returned = lax.all_to_all(attended, "frame", split_axis=0, concat_axis=0, tiled=True)
-    returned = returned.transpose(0, 2, 1).reshape(frames_dev, row_count, col_count, channels)
-    joined = (hidden.astype(jnp.float32) + returned.astype(jnp.float32)).astype(jnp.bfloat16)
-    return convolve(joined, conv2_weight).astype(jnp.bfloat16)
+    returned = returned.reshape(row_count, col_count, channels)
+
+    def joined_edge(c):
+        summed = hidden[:, c, :].astype(jnp.float32) + returned[:, c, :].astype(jnp.float32)
+        return summed.astype(jnp.bfloat16)
+
+    second = convolve([hidden, returned], joined_edge, conv2_weight, to_bf16)
+    return second.reshape(frames_dev, row_count, col_count, channels)
 
 
 def solution(mesh):

time: 176 us -> 127 us (0.72)
  matrix products: 63.1 us -> 0 us
  Pallas kernels: 7.97 us -> 43.3 us
  blocking collectives: 24.3 us -> 0 us
  waiting for transfers between devices: 28 us -> 44.1 us
  other arithmetic: 9.53 us -> 1.05 us
  local copies, waits for them, and re-layouts: 25.9 us -> 18.6 us
  starting transfers between devices: 16 us -> 19.3 us
    conv_general_dilated x2 -> x0, matrix products: 63.1 us -> none  [convolve(): lax.conv_general_dilated(widened, weight, (1, 1), ((1, 1), (0, 0)), dimen...]
    pallas_call x0 -> x2, Pallas kernels: none -> 34.8 us  [convolve(): pl.pallas_call(functools.partial(conv_kernel, parts=len(sources), finish=...]
    all_to_all x1 -> x0, blocking collectives: 24.3 us -> none  [body(): lax.all_to_all(attended, 'frame', split_axis=0, concat_axis=0, tiled=True)]
    all_to_all x0 -> x1, waiting for transfers between devices: none -> 18.8 us  [body(): lax.all_to_all(attended, 'frame', split_axis=0, concat_axis=0, tiled=True)]
    convert_element_type x3 -> x2, other arithmetic: 8.18 us -> 1.05 us  [joined_edge(): return summed.astype(jnp.bfloat16)]
    convert_element_type x4 -> x0, local copies, waits for them, and re-layouts: 6.74 us -> none  [the longest x1 4.83 us: body(): returned.astype(jnp.float32)]
    unnamed x17 -> x16, local copies, waits for them, and re-layouts: 9.51 us -> 4.5 us
    pallas_call x0 -> x1, local copies, waits for them, and re-layouts: none -> 3.77 us  [attend(): pl.pallas_call(attend_kernel, out_shape=jax.ShapeDtypeStruct((frames_all,...]
  transfers between devices with their start and end apart: 5 -> 6, of which waited for: 5 -> 6; matrix products, arithmetic and copies ran while one was open for 2% -> 3% of each run, Pallas kernels for 0% -> 0%
where the time goes in v1:
time: 127 us; the launch traced here: 126 us
  waiting for transfers between devices  44.1 us (35%)
  Pallas kernels  43.3 us (34%)
  starting transfers between devices  19.3 us (15%)
  local copies, waits for them, and re-layouts  18.6 us (15%)
    pallas_call x2, Pallas kernels, convolve(): pl.pallas_call(functools.partial(conv_kernel, parts=len(sources), finish=...  34.8 us
    all_to_all x1, waiting for transfers between devices, body(): lax.all_to_all(attended, 'frame', split_axis=0, concat_axis=0, tiled=True)  18.8 us
    all_to_all x1, waiting for transfers between devices, body(): lax.all_to_all(hidden.reshape(frames_all, pix_piece, channels), 'frame',...  18.8 us
    ppermute x4, starting transfers between devices, shifted(): return lax.ppermute(block, axis, route)  12.1 us
    pallas_call x1, Pallas kernels, attend(): pl.pallas_call(attend_kernel, out_shape=jax.ShapeDtypeStruct((frames_all,...  8.45 us
    ppermute x4, waiting for transfers between devices, shifted(): return lax.ppermute(block, axis, route)  6.53 us
    unnamed x16, local copies, waits for them, and re-layouts  4.5 us
    reshape x1, local copies, waits for them, and re-layouts, body(): hidden.reshape(frames_all, pix_piece, channels)  3.77 us
  transfers between devices with their start and end apart: 6, of which 6 were waited for; matrix products, arithmetic and copies ran while one was open for 3% of the time, Pallas kernels for 0%

profile of v1, /device:TPU:0, one launch (start us, length us, event | category | flops | bytes accessed | tf_op | source)
XLA Modules:
  0.0 126.4 jit_solution(16982832478343194532)
XLA Ops:
  0.0 2.1 %copy.49 = bf16[1,72,32,320]{3,1,2,0:T(8,128)(2,1)S(1)} copy(bf16[1,72,32,320]{3,2,1,0:T(8,128)(2,1)} %param.6) | data formatting | bytes 2949120 | tf_op args[0]
  2.1 4.9 %collective-permute-start = (bf16[72,320]{1,0:T(8,128)(2,1)S(1)}, bf16[72,320]{1,0:T(8,128)(2,1)S(1)}, u32[]{:S(2)}, u32[]{:S(2)}) collective-permute-start(bf16[72,320]{1,0:T(8,128)(2,1)S(1)} %get-tuple-element.10), channel_id=1, source_target_pairs={{0,4},{4,8},{8,12},{1,5},{5,9},{9,13},{2,6},{6,10},{10,14},{3,7},{... | collective-permute-start | bytes 138248 | tf_op jit(solution)/shard_map/ppermute | solution.py:16
  7.1 1.3 %collective-permute-start.1 = (bf16[72,320]{1,0:T(8,128)(2,1)S(1)}, bf16[72,320]{1,0:T(8,128)(2,1)S(1)}, u32[]{:S(2)}, u32[]{:S(2)}) collective-permute-start(bf16[72,320]{1,0:T(8,128)(2,1)S(1)} %get-tuple-element.9), channel_id=1, source_target_pairs={{4,0},{8,4},{12,8},{5,1},{9,5},{13,9},{6,2},{10,6},{14,10},{7,3},{... | collective-permute-start | bytes 138248 | tf_op jit(solution)/shard_map/ppermute | solution.py:16
  8.4 0.5 collective-permute-done.refs_1_
  8.8 4.3 %collective-permute-done.1.refs_2_ = bf16[72,320]{1,0:T(8,128)(2,1)S(1)} collective-permute-done((bf16[72,320]{1,0:T(8,128)(2,1)S(1)}, bf16[72,320]{1,0:T(8,128)(2,1)S(1)}, u32[]{:S(2)}, u32[]{:S(2)}) %collective-permute-start.1) | collective-permute-done | bytes 46112 | tf_op jit(solution)/shard_map/ppermute | solution.py:16
  13.1 0.0 copy-done.3
  13.1 0.6 copy-done.5
  13.7 17.8 %shard_map.64.refs_0_ = bf16[72,32,320]{2,1,0:T(8,128)(2,1)} custom-call(bf16[72,32,320]{2,1,0:T(8,128)(2,1)} %bitcast.22, bf16[72,320]{1,0:T(8,128)(2,1)} %copy-done.3, bf16[72,320]{1,0:T(8,128)(2,1)} %copy-done.5, bf16[3,3,320,320]{3,2,1,0:T(8,128)(2,1)} %refs_3_.1), custom_call_target="tpu_custom_call" | custom-call | tf_op jit(solution)/shard_map/pallas_call | solution.py:82
  31.5 3.8 %copy.26 = bf16[4,576,320]{1,2,0:T(8,128)(2,1)} copy(bf16[4,576,320]{2,1,0:T(8,128)(2,1)} %bitcast.19) | data formatting | bytes 2949120 | tf_op jit(solution)/shard_map/reshape | solution.py:167
  35.3 3.7 %all-to-all-start = ((bf16[4,576,320]{1,2,0:T(8,128)(2,1)}), bf16[4,576,320]{1,2,0:T(8,128)(2,1)S(1)}, u32[]{:S(2)}, u32[]{:S(2)}) async-start(bf16[4,576,320]{1,2,0:T(8,128)(2,1)} %copy.26), calls=%async_computation | async-start | bytes 3276800 | tf_op jit(solution)/shard_map/all_to_all | solution.py:166
  39.0 0.0 copy-done.1
  39.0 1.2 copy.27
  40.2 0.0 copy-done.6
  40.2 0.8 copy.30.bias_ref
  41.0 18.8 %all-to-all-done = bf16[4,576,320]{1,2,0:T(8,128)(2,1)S(1)} async-done(((bf16[4,576,320]{1,2,0:T(8,128)(2,1)}), bf16[4,576,320]{1,2,0:T(8,128)(2,1)S(1)}, u32[]{:S(2)}, u32[]{:S(2)}) %all-to-all-start) | async-done | bytes 1474592 | tf_op jit(solution)/shard_map/all_to_all | solution.py:166
  59.7 2.3 %copy.29.x_ref = bf16[4,576,320]{2,1,0:T(8,128)(2,1)} copy(bf16[4,576,320]{1,2,0:T(8,128)(2,1)S(1)} %all-to-all-done) | data formatting | bytes 2949120 | tf_op jit(solution)/shard_map/all_to_all | solution.py:166
  62.0 8.5 %shard_map.65 = bf16[4,576,320]{2,1,0:T(8,128)(2,1)} custom-call(bf16[4,576,320]{2,1,0:T(8,128)(2,1)} %copy.29.x_ref, bf16[960,320]{1,0:T(8,128)(2,1)} %bitcast.23, f32[5,4,4,1]{3,2,1,0:T(4,128)} %copy.30.bias_ref, bf16[320,320]{1,0:T(8,128)(2,1)} %wout_ref.1), custom_call_target="tpu_custom_call" | custom-call | tf_op jit(solution)/shard_map/pallas_call | solution.py:148
  70.5 3.8 %copy.31 = bf16[4,576,320]{1,2,0:T(8,128)(2,1)} copy(bf16[4,576,320]{2,1,0:T(8,128)(2,1)} %shard_map.65) | data formatting | bytes 2949120 | tf_op jit(solution)/shard_map/pallas_call | solution.py:148
  74.3 3.6 %all-to-all-start.1 = ((bf16[4,576,320]{1,2,0:T(8,128)(2,1)}), bf16[4,576,320]{1,2,0:T(8,128)(2,1)S(1)}, u32[]{:S(2)}, u32[]{:S(2)}) async-start(bf16[4,576,320]{1,2,0:T(8,128)(2,1)} %copy.31), calls=%async_computation.1 | async-start | bytes 3276800 | tf_op jit(solution)/shard_map/all_to_all | solution.py:170
  77.8 2.0 %fusion.2 = (bf16[72,1,320]{2,1,0:T(2,128)(2,1)}, bf16[72,1,320]{2,1,0:T(2,128)(2,1)S(1)}) fusion(bf16[72,32,320]{2,1,0:T(8,128)(2,1)} %shard_map.64.refs_0_), kind=kLoop, calls=%fused_computation.7 | loop fusion | bytes 184320 | tf_op jit(solution)/shard_map/slice | solution.py:174
  79.8 18.8 %all-to-all-done.1 = bf16[4,576,320]{1,2,0:T(8,128)(2,1)S(1)} async-done(((bf16[4,576,320]{1,2,0:T(8,128)(2,1)}), bf16[4,576,320]{1,2,0:T(8,128)(2,1)S(1)}, u32[]{:S(2)}, u32[]{:S(2)}) %all-to-all-start.1) | async-done | bytes 1474592 | tf_op jit(solution)/shard_map/all_to_all | solution.py:170
  98.6 1.3 %copy.32 = bf16[4,576,320]{2,1,0:T(8,128)(2,1)S(1)} copy(bf16[4,576,320]{1,2,0:T(8,128)(2,1)S(1)} %all-to-all-done.1) | data formatting | bytes 2949120 | tf_op jit(solution)/shard_map/all_to_all | solution.py:170
  99.9 0.0 copy-start
  99.9 0.2 fusion.3
  100.0 1.0 fusion.1
  101.1 1.3 %collective-permute-start.3 = (bf16[72,320]{1,0:T(8,128)(2,1)S(1)}, bf16[72,320]{1,0:T(8,128)(2,1)S(1)}, u32[]{:S(2)}, u32[]{:S(2)}) collective-permute-start(bf16[72,320]{1,0:T(8,128)(2,1)S(1)} %fusion.1), channel_id=1, source_target_pairs={{4,0},{8,4},{12,8},{5,1},{9,5},{13,9},{6,2},{10,6},{14,10},{7,3},{... | collective-permute-start | bytes 138248 | tf_op jit(solution)/shard_map/ppermute | solution.py:16
  102.4 4.5 %collective-permute-start.2 = (bf16[72,320]{1,0:T(8,128)(2,1)S(1)}, bf16[72,320]{1,0:T(8,128)(2,1)S(1)}, u32[]{:S(2)}, u32[]{:S(2)}) collective-permute-start(bf16[72,320]{1,0:T(8,128)(2,1)S(1)} %fusion), channel_id=1, source_target_pairs={{0,4},{4,8},{8,12},{1,5},{5,9},{9,13},{2,6},{6,10},{10,14},{3,7},{... | collective-permute-start | bytes 138248 | tf_op jit(solution)/shard_map/ppermute | solution.py:16
  107.0 0.2 collective-permute-done.3.refs_3_
  107.1 1.6 %collective-permute-done.2.refs_2_ = bf16[72,320]{1,0:T(8,128)(2,1)S(1)} collective-permute-done((bf16[72,320]{1,0:T(8,128)(2,1)S(1)}, bf16[72,320]{1,0:T(8,128)(2,1)S(1)}, u32[]{:S(2)}, u32[]{:S(2)}) %collective-permute-start.2) | collective-permute-done | bytes 46112 | tf_op jit(solution)/shard_map/ppermute | solution.py:16
  108.8 0.0 copy-done
  108.8 0.6 copy-done.4
  109.4 17.0 %shard_map.66 = bf16[72,32,320]{2,1,0:T(8,128)(2,1)} custom-call(bf16[72,32,320]{2,1,0:T(8,128)(2,1)} %shard_map.64.refs_0_, bf16[72,32,320]{2,1,0:T(8,128)(2,1)} %bitcast.21, bf16[72,320]{1,0:T(8,128)(2,1)} %copy-done.4, bf16[72,320]{1,0:T(8,128)(2,1)} %copy-done.2, bf16[3,3,320,320]{3,2,1,0:T(8,128)(2,1)} %refs_4_.1), custom_call_target="tpu_custom_call" | custom-call | tf_op jit(solution)/shard_map/pallas_call | solution.py:82
  (9 shorter events, 0.0 us)
Async XLA Ops:
  2.1 6.7 %collective-permute-start = (bf16[72,320]{1,0:T(8,128)(2,1)S(1)}, bf16[72,320]{1,0:T(8,128)(2,1)S(1)}, u32[]{:S(2)}, u32[]{:S(2)}) collective-permute-start(bf16[72,320]{1,0:T(8,128)(2,1)S(1)} %get-tuple-element.10), channel_id=1, source_target_pairs={{0,4},{4,8},{8,12},{1,5},{5,9},{9,13},{2,6},{6,10},{10,14},{3,7},{... | collective-permute-start | bytes 138248 | tf_op jit(solution)/shard_map/ppermute | solution.py:16
  7.1 6.0 %collective-permute-start.1 = (bf16[72,320]{1,0:T(8,128)(2,1)S(1)}, bf16[72,320]{1,0:T(8,128)(2,1)S(1)}, u32[]{:S(2)}, u32[]{:S(2)}) collective-permute-start(bf16[72,320]{1,0:T(8,128)(2,1)S(1)} %get-tuple-element.9), channel_id=1, source_target_pairs={{4,0},{8,4},{12,8},{5,1},{9,5},{13,9},{6,2},{10,6},{14,10},{7,3},{... | collective-permute-start | bytes 138248 | tf_op jit(solution)/shard_map/ppermute | solution.py:16
  8.8 4.3 %copy-start.3 = (bf16[72,320]{1,0:T(8,128)(2,1)}, bf16[72,320]{1,0:T(8,128)(2,1)S(1)}, u32[]{:S(2)}) copy-start(bf16[72,320]{1,0:T(8,128)(2,1)S(1)} %collective-permute-done.refs_1_) | copy-start | bytes 138244
  13.1 0.6 copy-start.5
  35.3 3.7 %copy-start.1 = (bf16[320,960]{1,0:T(8,128)(2,1)S(1)}, bf16[320,960]{1,0:T(8,128)(2,1)}, u32[]{:S(2)}) copy-start(bf16[320,960]{1,0:T(8,128)(2,1)} %param.8) | copy-start | bytes 1843204
  35.3 4.9 %copy-start.6 = (f32[5,4,4]{0,2,1:T(4,128)S(1)}, f32[5,4,4]{0,2,1:T(4,128)}, u32[]{:S(2)}) copy-start(f32[5,4,4]{0,2,1:T(4,128)} %param.10) | copy-start | bytes 964
  35.3 24.5 %all-to-all-start = ((bf16[4,576,320]{1,2,0:T(8,128)(2,1)}), bf16[4,576,320]{1,2,0:T(8,128)(2,1)S(1)}, u32[]{:S(2)}, u32[]{:S(2)}) async-start(bf16[4,576,320]{1,2,0:T(8,128)(2,1)} %copy.26), calls=%async_computation | async-start | bytes 3276800 | tf_op jit(solution)/shard_map/all_to_all | solution.py:166
  74.3 24.3 %all-to-all-start.1 = ((bf16[4,576,320]{1,2,0:T(8,128)(2,1)}), bf16[4,576,320]{1,2,0:T(8,128)(2,1)S(1)}, u32[]{:S(2)}, u32[]{:S(2)}) async-start(bf16[4,576,320]{1,2,0:T(8,128)(2,1)} %copy.31), calls=%async_computation.1 | async-start | bytes 3276800 | tf_op jit(solution)/shard_map/all_to_all | solution.py:170
  99.9 8.9 %copy-start = (bf16[4,576,320]{2,1,0:T(8,128)(2,1)}, bf16[4,576,320]{2,1,0:T(8,128)(2,1)S(1)}, u32[]{:S(2)}) copy-start(bf16[4,576,320]{2,1,0:T(8,128)(2,1)S(1)} %copy.32) | copy-start | bytes 4423684
  101.1 6.0 %collective-permute-start.3 = (bf16[72,320]{1,0:T(8,128)(2,1)S(1)}, bf16[72,320]{1,0:T(8,128)(2,1)S(1)}, u32[]{:S(2)}, u32[]{:S(2)}) collective-permute-start(bf16[72,320]{1,0:T(8,128)(2,1)S(1)} %fusion.1), channel_id=1, source_target_pairs={{4,0},{8,4},{12,8},{5,1},{9,5},{13,9},{6,2},{10,6},{14,10},{7,3},{... | collective-permute-start | bytes 138248 | tf_op jit(solution)/shard_map/ppermute | solution.py:16
  102.4 6.3 %collective-permute-start.2 = (bf16[72,320]{1,0:T(8,128)(2,1)S(1)}, bf16[72,320]{1,0:T(8,128)(2,1)S(1)}, u32[]{:S(2)}, u32[]{:S(2)}) collective-permute-start(bf16[72,320]{1,0:T(8,128)(2,1)S(1)} %fusion), channel_id=1, source_target_pairs={{0,4},{4,8},{8,12},{1,5},{5,9},{9,13},{2,6},{6,10},{10,14},{3,7},{... | collective-permute-start | bytes 138248 | tf_op jit(solution)/shard_map/ppermute | solution.py:16
  107.1 1.6 %copy-start.2 = (bf16[72,320]{1,0:T(8,128)(2,1)}, bf16[72,320]{1,0:T(8,128)(2,1)S(1)}, u32[]{:S(2)}) copy-start(bf16[72,320]{1,0:T(8,128)(2,1)S(1)} %collective-permute-done.3.refs_3_) | copy-start | bytes 138244
  108.8 0.6 copy-start.4

commit v2 on v1

--- a/solution.py
+++ b/solution.py
@@ -18,14 +18,18 @@
 
 def conv_kernel(*refs, parts, finish):
     sources = refs[:parts]
-    left_ref, right_ref, w_ref, o_ref, side_l, side_c, side_r, shift_s = refs[parts:]
+    left_ref, right_ref, w_ref, o_ref, slab, shift_s = refs[parts:]
     row_count, col_count, channels = o_ref.shape
-    band = 8
+    lanes = slab.shape[1] // 3
+    band = 24
     span = band * col_count
-    zeros = jnp.zeros((col_count, channels), jnp.bfloat16)
-    for side in (side_l, side_c, side_r):
-        side[pl.ds(0, col_count)] = zeros
-        side[pl.ds((row_count + 1) * col_count, col_count)] = zeros
+    padded_rows = slab.shape[0]
+    slab[pl.ds(0, col_count)] = jnp.zeros((col_count, slab.shape[1]), jnp.bfloat16)
+    slab[pl.ds(padded_rows - col_count, col_count)] = jnp.zeros((col_count, slab.shape[1]), jnp.bfloat16)
+    if lanes > channels:
+        pad = jnp.zeros((padded_rows, lanes - channels), jnp.bfloat16)
+        for b in range(3):
+            slab[:, pl.ds(b * lanes + channels, lanes - channels)] = pad
     column = lax.broadcasted_iota(jnp.int32, (band, col_count, channels), 1)
 
     def build(i, carry):
@@ -34,18 +38,17 @@
         for extra in sources[1:]:
             block = block + extra[pl.ds(r0, band)].astype(jnp.float32)
         block = block.astype(jnp.bfloat16)
-        flat = block.astype(jnp.float32).reshape(span, channels)
-        shift_s[pl.ds(8, span)] = flat
+        shift_s[pl.ds(8, span)] = block.astype(jnp.float32).reshape(span, channels)
         before = shift_s[pl.ds(7, span)].reshape(band, col_count, channels)
         after = shift_s[pl.ds(9, span)].reshape(band, col_count, channels)
         rim_l = left_ref[pl.ds(r0, band)].astype(jnp.float32)[:, None, :]
         rim_r = right_ref[pl.ds(r0, band)].astype(jnp.float32)[:, None, :]
         before = jnp.where(column == 0, rim_l, before)
         after = jnp.where(column == col_count - 1, rim_r, after)
-        at = pl.ds(pl.multiple_of((r0 + 1) * col_count, col_count), span)
-        side_c[at] = block.reshape(span, channels)
-        side_l[at] = before.reshape(span, channels).astype(jnp.bfloat16)
-        side_r[at] = after.reshape(span, channels).astype(jnp.bfloat16)
+        rows = pl.ds(pl.multiple_of((r0 + 1) * col_count, col_count), span)
+        slab[rows, pl.ds(0, channels)] = before.reshape(span, channels).astype(jnp.bfloat16)
+        slab[rows, pl.ds(lanes, channels)] = block.reshape(span, channels)
+        slab[rows, pl.ds(2 * lanes, channels)] = after.reshape(span, channels).astype(jnp.bfloat16)
         return carry
 
     lax.fori_loop(0, row_count // band, build, 0)
@@ -54,10 +57,9 @@
         r0 = i * band
         acc = None
         for a in range(3):
-            at = pl.ds(pl.multiple_of((r0 + a) * col_count, col_count), span)
-            for b, side in enumerate((side_l, side_c, side_r)):
-                term = jnp.dot(side[at], w_ref[a, b], preferred_element_type=jnp.float32)
-                acc = term if acc is None else acc + term
+            rows = pl.ds(pl.multiple_of((r0 + a) * col_count, col_count), span)
+            term = jnp.dot(slab[rows, :], w_ref[a], preferred_element_type=jnp.float32)
+            acc = term if acc is None else acc + term
         o_ref[pl.ds(r0, band)] = finish(acc).reshape(band, col_count, channels)
         return carry
 
@@ -79,14 +81,19 @@
     right_rim = shifted(edge_of(0), "quarter", -1)
     vmem = pl.BlockSpec(memory_space=pltpu.VMEM)
     padded = (row_count + 2) * col_count
+    lanes = -(-channels // 128) * 128
+    stacked = jnp.pad(weight, ((0, 0), (0, 0), (0, lanes - channels), (0, 0)))
+    stacked = stacked.reshape(3, 3 * lanes, channels)
     return pl.pallas_call(
         functools.partial(conv_kernel, parts=len(sources), finish=finish),
         out_shape=jax.ShapeDtypeStruct((row_count, col_count, channels), jnp.bfloat16),
         in_specs=[vmem] * (len(sources) + 3),
         out_specs=vmem,
-        scratch_shapes=[pltpu.VMEM((padded, channels), jnp.bfloat16)] * 3
-        + [pltpu.VMEM((8 * col_count + 16, channels), jnp.float32)],
-    )(*sources, left_rim, right_rim, weight)
+        scratch_shapes=[
+            pltpu.VMEM((padded, 3 * lanes), jnp.bfloat16),
+            pltpu.VMEM((24 * col_count + 16, channels), jnp.float32),
+        ],
+    )(*sources, left_rim, right_rim, stacked)
 
 
 def attend_kernel(x_ref, wqkv_ref, bias_ref, wout_ref, o_ref, qkv_s, blend_s):

time: 127 us -> 124 us (0.976)
  waiting for transfers between devices: 44.1 us -> 37.3 us
  local copies, waits for them, and re-layouts: 18.6 us -> 24 us
  Pallas kernels: 43.3 us -> 40.2 us
    ppermute x4, waiting for transfers between devices: 6.53 us -> 0.01 us  [shifted(): return lax.ppermute(block, axis, route)]
    pad x0 -> x2, local copies, waits for them, and re-layouts: none -> 5.21 us  [convolve(): stacked = jnp.pad(weight, ((0, 0), (0, 0), (0, lanes - channels), (0, 0)))]
    pallas_call x2, Pallas kernels: 34.8 us -> 31.7 us  [convolve(): pl.pallas_call(functools.partial(conv_kernel, parts=len(sources), finish=...]
    unnamed x16 -> x18, local copies, waits for them, and re-layouts: 4.5 us -> 4.67 us
  transfers between devices with their start and end apart: 6 -> 6, of which waited for: 6 -> 2; matrix products, arithmetic and copies ran while one was open for 3% -> 7% of each run, Pallas kernels for 0% -> 0%
where the time goes in v2:
time: 124 us; the launch traced here: 123 us
  Pallas kernels  40.2 us (32%)
  waiting for transfers between devices  37.3 us (30%)
  local copies, waits for them, and re-layouts  24 us (19%)
  starting transfers between devices  20.4 us (16%)
    pallas_call x2, Pallas kernels, convolve(): pl.pallas_call(functools.partial(conv_kernel, parts=len(sources), finish=...  31.7 us
    all_to_all x1, waiting for transfers between devices, body(): lax.all_to_all(hidden.reshape(frames_all, pix_piece, channels), 'frame',...  18.7 us
    all_to_all x1, waiting for transfers between devices, body(): lax.all_to_all(attended, 'frame', split_axis=0, concat_axis=0, tiled=True)  18.6 us
    ppermute x4, starting transfers between devices, shifted(): return lax.ppermute(block, axis, route)  13 us
    pallas_call x1, Pallas kernels, attend(): pl.pallas_call(attend_kernel, out_shape=jax.ShapeDtypeStruct((frames_all,...  8.49 us
    pad x2, local copies, waits for them, and re-layouts, convolve(): stacked = jnp.pad(weight, ((0, 0), (0, 0), (0, lanes - channels), (0, 0)))  5.21 us
    unnamed x18, local copies, waits for them, and re-layouts  4.67 us
    reshape x1, local copies, waits for them, and re-layouts, body(): hidden.reshape(frames_all, pix_piece, channels)  3.77 us
  transfers between devices with their start and end apart: 6, of which 2 were waited for; matrix products, arithmetic and copies ran while one was open for 7% of the time, Pallas kernels for 0%

profile of v2, /device:TPU:0, one launch (start us, length us, event | category | flops | bytes accessed | tf_op | source)
XLA Modules:
  0.0 123.2 jit_solution(3634880418113578121)
XLA Ops:
  0.0 2.2 %copy.49 = bf16[1,72,32,320]{3,1,2,0:T(8,128)(2,1)S(1)} copy(bf16[1,72,32,320]{3,2,1,0:T(8,128)(2,1)} %param.6) | data formatting | bytes 2949120 | tf_op args[0]
  2.3 1.3 %collective-permute-start.1 = (bf16[72,320]{1,0:T(8,128)(2,1)S(1)}, bf16[72,320]{1,0:T(8,128)(2,1)S(1)}, u32[]{:S(2)}, u32[]{:S(2)}) collective-permute-start(bf16[72,320]{1,0:T(8,128)(2,1)S(1)} %get-tuple-element.9), channel_id=1, source_target_pairs={{4,0},{8,4},{12,8},{5,1},{9,5},{13,9},{6,2},{10,6},{14,10},{7,3},{... | collective-permute-start | bytes 138248 | tf_op jit(solution)/shard_map/ppermute | solution.py:16
  3.6 5.6 %collective-permute-start = (bf16[72,320]{1,0:T(8,128)(2,1)S(1)}, bf16[72,320]{1,0:T(8,128)(2,1)S(1)}, u32[]{:S(2)}, u32[]{:S(2)}) collective-permute-start(bf16[72,320]{1,0:T(8,128)(2,1)S(1)} %get-tuple-element.10), channel_id=1, source_target_pairs={{0,4},{4,8},{8,12},{1,5},{5,9},{9,13},{2,6},{6,10},{10,14},{3,7},{... | collective-permute-start | bytes 138248 | tf_op jit(solution)/shard_map/ppermute | solution.py:16
  9.1 1.8 %pad.7 = bf16[3,3,384,320]{3,2,1,0:T(8,128)(2,1)} pad(bf16[3,3,320,320]{3,2,1,0:T(8,128)(2,1)S(1)} %copy-done.1, bf16[]{:T(256)} %constant.2.clone.1), padding=0_0x0_0x0_64x0_0 | pad | bytes 4055042 | tf_op jit(solution)/shard_map/jit(_pad)/pad | solution.py:85
  10.9 0.0 collective-permute-done.1.refs_2_
  10.9 0.0 collective-permute-done.refs_1_
  10.9 0.0 copy-start.6
  11.0 0.6 copy-done.5
  11.6 0.0 copy-done.6
  11.6 16.0 %shard_map.64.refs_0_ = bf16[72,32,320]{2,1,0:T(8,128)(2,1)} custom-call(bf16[72,32,320]{2,1,0:T(8,128)(2,1)} %bitcast.26, bf16[72,320]{1,0:T(8,128)(2,1)} %copy-done.6, bf16[72,320]{1,0:T(8,128)(2,1)} %copy-done.5, bf16[3,1152,320]{2,1,0:T(8,128)(2,1)} %bitcast.23), custom_call_target="tpu_custom_call" | custom-call | tf_op jit(solution)/shard_map/pallas_call | solution.py:87
  27.6 3.8 %copy.26 = bf16[4,576,320]{1,2,0:T(8,128)(2,1)} copy(bf16[4,576,320]{2,1,0:T(8,128)(2,1)} %bitcast.21) | data formatting | bytes 2949120 | tf_op jit(solution)/shard_map/reshape | solution.py:174
  31.4 3.7 %all-to-all-start = ((bf16[4,576,320]{1,2,0:T(8,128)(2,1)}), bf16[4,576,320]{1,2,0:T(8,128)(2,1)S(1)}, u32[]{:S(2)}, u32[]{:S(2)}) async-start(bf16[4,576,320]{1,2,0:T(8,128)(2,1)} %copy.26), calls=%async_computation | async-start | bytes 3276800 | tf_op jit(solution)/shard_map/all_to_all | solution.py:173
  35.1 0.8 copy.30.bias_ref
  35.9 1.2 copy.27
  37.1 18.7 %all-to-all-done = bf16[4,576,320]{1,2,0:T(8,128)(2,1)S(1)} async-done(((bf16[4,576,320]{1,2,0:T(8,128)(2,1)}), bf16[4,576,320]{1,2,0:T(8,128)(2,1)S(1)}, u32[]{:S(2)}, u32[]{:S(2)}) %all-to-all-start) | async-done | bytes 1474592 | tf_op jit(solution)/shard_map/all_to_all | solution.py:173
  55.8 2.3 %copy.29.x_ref = bf16[4,576,320]{2,1,0:T(8,128)(2,1)} copy(bf16[4,576,320]{1,2,0:T(8,128)(2,1)S(1)} %all-to-all-done) | data formatting | bytes 2949120 | tf_op jit(solution)/shard_map/all_to_all | solution.py:173
  58.1 8.5 %shard_map.65 = bf16[4,576,320]{2,1,0:T(8,128)(2,1)} custom-call(bf16[4,576,320]{2,1,0:T(8,128)(2,1)} %copy.29.x_ref, bf16[960,320]{1,0:T(8,128)(2,1)} %bitcast.27, f32[5,4,4,1]{3,2,1,0:T(4,128)} %copy.30.bias_ref, bf16[320,320]{1,0:T(8,128)(2,1)} %wout_ref.1), custom_call_target="tpu_custom_call" | custom-call | tf_op jit(solution)/shard_map/pallas_call | solution.py:155
  66.6 3.8 %copy.31 = bf16[4,576,320]{1,2,0:T(8,128)(2,1)} copy(bf16[4,576,320]{2,1,0:T(8,128)(2,1)} %shard_map.65) | data formatting | bytes 2949120 | tf_op jit(solution)/shard_map/pallas_call | solution.py:155
  70.4 3.7 %all-to-all-start.1 = ((bf16[4,576,320]{1,2,0:T(8,128)(2,1)}), bf16[4,576,320]{1,2,0:T(8,128)(2,1)S(1)}, u32[]{:S(2)}, u32[]{:S(2)}) async-start(bf16[4,576,320]{1,2,0:T(8,128)(2,1)} %copy.31), calls=%async_computation.1 | async-start | bytes 3276800 | tf_op jit(solution)/shard_map/all_to_all | solution.py:177
  74.1 2.0 %fusion.2 = (bf16[72,1,320]{2,1,0:T(2,128)(2,1)}, bf16[72,1,320]{2,1,0:T(2,128)(2,1)S(1)}) fusion(bf16[72,32,320]{2,1,0:T(8,128)(2,1)} %shard_map.64.refs_0_), kind=kLoop, calls=%fused_computation.7 | loop fusion | bytes 184320 | tf_op jit(solution)/shard_map/slice | solution.py:181
  76.1 18.6 %all-to-all-done.1 = bf16[4,576,320]{1,2,0:T(8,128)(2,1)S(1)} async-done(((bf16[4,576,320]{1,2,0:T(8,128)(2,1)}), bf16[4,576,320]{1,2,0:T(8,128)(2,1)S(1)}, u32[]{:S(2)}, u32[]{:S(2)}) %all-to-all-start.1) | async-done | bytes 1474592 | tf_op jit(solution)/shard_map/all_to_all | solution.py:177
  94.7 1.3 %copy.32 = bf16[4,576,320]{2,1,0:T(8,128)(2,1)S(1)} copy(bf16[4,576,320]{1,2,0:T(8,128)(2,1)S(1)} %all-to-all-done.1) | data formatting | bytes 2949120 | tf_op jit(solution)/shard_map/all_to_all | solution.py:177
  96.0 0.2 fusion.3
  96.2 1.0 fusion.1
  97.2 1.3 %collective-permute-start.3 = (bf16[72,320]{1,0:T(8,128)(2,1)S(1)}, bf16[72,320]{1,0:T(8,128)(2,1)S(1)}, u32[]{:S(2)}, u32[]{:S(2)}) collective-permute-start(bf16[72,320]{1,0:T(8,128)(2,1)S(1)} %fusion.1), channel_id=1, source_target_pairs={{4,0},{8,4},{12,8},{5,1},{9,5},{13,9},{6,2},{10,6},{14,10},{7,3},{... | collective-permute-start | bytes 138248 | tf_op jit(solution)/shard_map/ppermute | solution.py:16
  98.5 4.8 %collective-permute-start.2 = (bf16[72,320]{1,0:T(8,128)(2,1)S(1)}, bf16[72,320]{1,0:T(8,128)(2,1)S(1)}, u32[]{:S(2)}, u32[]{:S(2)}) collective-permute-start(bf16[72,320]{1,0:T(8,128)(2,1)S(1)} %fusion), channel_id=1, source_target_pairs={{0,4},{4,8},{8,12},{1,5},{5,9},{9,13},{2,6},{6,10},{10,14},{3,7},{... | collective-permute-start | bytes 138248 | tf_op jit(solution)/shard_map/ppermute | solution.py:16
  103.4 3.4 %pad.8 = bf16[3,3,384,320]{3,2,1,0:T(8,128)(2,1)} pad(bf16[3,3,320,320]{3,2,1,0:T(8,128)(2,1)} %param.11, bf16[]{:T(256)} %constant.2.clone.1), padding=0_0x0_0x0_64x0_0 | pad | bytes 4055042 | tf_op jit(solution)/shard_map/jit(_pad)/pad | solution.py:85
  106.8 0.0 collective-permute-done.3.refs_3_
  106.8 0.0 collective-permute-done.2.refs_2_
  106.8 0.6 copy-done.3
  107.4 0.0 copy-done.4
  107.5 15.7 %shard_map.66 = bf16[72,32,320]{2,1,0:T(8,128)(2,1)} custom-call(bf16[72,32,320]{2,1,0:T(8,128)(2,1)} %shard_map.64.refs_0_, bf16[72,32,320]{2,1,0:T(8,128)(2,1)} %bitcast.25, bf16[72,320]{1,0:T(8,128)(2,1)} %copy-done.4, bf16[72,320]{1,0:T(8,128)(2,1)} %copy-done.3, bf16[3,1152,320]{2,1,0:T(8,128)(2,1)} %bitcast.22), custom_call_target="tpu_custom_call" | custom-call | tf_op jit(solution)/shard_map/pallas_call | solution.py:87
  (13 shorter events, 0.1 us)
Async XLA Ops:
  0.0 9.1 %copy-start.1 = (bf16[3,3,320,320]{3,2,1,0:T(8,128)(2,1)S(1)}, bf16[3,3,320,320]{3,2,1,0:T(8,128)(2,1)}, u32[]{:S(2)}) copy-start(bf16[3,3,320,320]{3,2,1,0:T(8,128)(2,1)} %param.7) | copy-start | bytes 5529604
  2.3 8.7 %collective-permute-start.1 = (bf16[72,320]{1,0:T(8,128)(2,1)S(1)}, bf16[72,320]{1,0:T(8,128)(2,1)S(1)}, u32[]{:S(2)}, u32[]{:S(2)}) collective-permute-start(bf16[72,320]{1,0:T(8,128)(2,1)S(1)} %get-tuple-element.9), channel_id=1, source_target_pairs={{4,0},{8,4},{12,8},{5,1},{9,5},{13,9},{6,2},{10,6},{14,10},{7,3},{... | collective-permute-start | bytes 138248 | tf_op jit(solution)/shard_map/ppermute | solution.py:16
  3.6 7.4 %collective-permute-start = (bf16[72,320]{1,0:T(8,128)(2,1)S(1)}, bf16[72,320]{1,0:T(8,128)(2,1)S(1)}, u32[]{:S(2)}, u32[]{:S(2)}) collective-permute-start(bf16[72,320]{1,0:T(8,128)(2,1)S(1)} %get-tuple-element.10), channel_id=1, source_target_pairs={{0,4},{4,8},{8,12},{1,5},{5,9},{9,13},{2,6},{6,10},{10,14},{3,7},{... | collective-permute-start | bytes 138248 | tf_op jit(solution)/shard_map/ppermute | solution.py:16
  10.9 0.6 copy-start.5
  10.9 0.6 copy-start.6
  31.3 3.7 %copy-start.7 = (f32[5,4,4]{0,2,1:T(4,128)S(1)}, f32[5,4,4]{0,2,1:T(4,128)}, u32[]{:S(2)}) copy-start(f32[5,4,4]{0,2,1:T(4,128)} %param.10) | copy-start | bytes 964
  31.3 4.5 %copy-start.2 = (bf16[320,960]{1,0:T(8,128)(2,1)S(1)}, bf16[320,960]{1,0:T(8,128)(2,1)}, u32[]{:S(2)}) copy-start(bf16[320,960]{1,0:T(8,128)(2,1)} %param.8) | copy-start | bytes 1843204
  31.4 24.5 %all-to-all-start = ((bf16[4,576,320]{1,2,0:T(8,128)(2,1)}), bf16[4,576,320]{1,2,0:T(8,128)(2,1)S(1)}, u32[]{:S(2)}, u32[]{:S(2)}) async-start(bf16[4,576,320]{1,2,0:T(8,128)(2,1)} %copy.26), calls=%async_computation | async-start | bytes 3276800 | tf_op jit(solution)/shard_map/all_to_all | solution.py:173
  70.4 24.3 %all-to-all-start.1 = ((bf16[4,576,320]{1,2,0:T(8,128)(2,1)}), bf16[4,576,320]{1,2,0:T(8,128)(2,1)S(1)}, u32[]{:S(2)}, u32[]{:S(2)}) async-start(bf16[4,576,320]{1,2,0:T(8,128)(2,1)} %copy.31), calls=%async_computation.1 | async-start | bytes 3276800 | tf_op jit(solution)/shard_map/all_to_all | solution.py:177
  96.0 10.8 %copy-start = (bf16[4,576,320]{2,1,0:T(8,128)(2,1)}, bf16[4,576,320]{2,1,0:T(8,128)(2,1)S(1)}, u32[]{:S(2)}) copy-start(bf16[4,576,320]{2,1,0:T(8,128)(2,1)S(1)} %copy.32) | copy-start | bytes 4423684
  97.2 9.6 %collective-permute-start.3 = (bf16[72,320]{1,0:T(8,128)(2,1)S(1)}, bf16[72,320]{1,0:T(8,128)(2,1)S(1)}, u32[]{:S(2)}, u32[]{:S(2)}) collective-permute-start(bf16[72,320]{1,0:T(8,128)(2,1)S(1)} %fusion.1), channel_id=1, source_target_pairs={{4,0},{8,4},{12,8},{5,1},{9,5},{13,9},{6,2},{10,6},{14,10},{7,3},{... | collective-permute-start | bytes 138248 | tf_op jit(solution)/shard_map/ppermute | solution.py:16
  98.5 8.3 %collective-permute-start.2 = (bf16[72,320]{1,0:T(8,128)(2,1)S(1)}, bf16[72,320]{1,0:T(8,128)(2,1)S(1)}, u32[]{:S(2)}, u32[]{:S(2)}) collective-permute-start(bf16[72,320]{1,0:T(8,128)(2,1)S(1)} %fusion), channel_id=1, source_target_pairs={{0,4},{4,8},{8,12},{1,5},{5,9},{9,13},{2,6},{6,10},{10,14},{3,7},{... | collective-permute-start | bytes 138248 | tf_op jit(solution)/shard_map/ppermute | solution.py:16
  106.8 0.6 copy-start.3
  106.8 0.6 copy-start.4

commit v3 on v2

--- a/solution.py
+++ b/solution.py
@@ -81,9 +81,8 @@
     right_rim = shifted(edge_of(0), "quarter", -1)
     vmem = pl.BlockSpec(memory_space=pltpu.VMEM)
     padded = (row_count + 2) * col_count
-    lanes = -(-channels // 128) * 128
-    stacked = jnp.pad(weight, ((0, 0), (0, 0), (0, lanes - channels), (0, 0)))
-    stacked = stacked.reshape(3, 3 * lanes, channels)
+    lanes = channels
+    stacked = weight.reshape(3, 3 * lanes, channels)
     return pl.pallas_call(
         functools.partial(conv_kernel, parts=len(sources), finish=finish),
         out_shape=jax.ShapeDtypeStruct((row_count, col_count, channels), jnp.bfloat16),
@@ -171,10 +170,12 @@
     tile = latents.reshape(row_count, col_count, channels)
     hidden = convolve([tile], lambda c: tile[:, c, :], conv1_weight, norm_gelu)
     pieces = lax.all_to_all(
-        hidden.reshape(frames_all, pix_piece, channels), "frame", split_axis=0, concat_axis=0, tiled=True
-    )
-    attended = attend(pieces, qkv_weight, pos_bias, out_weight)
-    returned = lax.all_to_all(attended, "frame", split_axis=0, concat_axis=0, tiled=True)
+        hidden.reshape(frames_all, pix_piece * channels), "frame", split_axis=0, concat_axis=0, tiled=True
+    )
+    attended = attend(pieces.reshape(frames_all, pix_piece, channels), qkv_weight, pos_bias, out_weight)
+    returned = lax.all_to_all(
+        attended.reshape(frames_all, pix_piece * channels), "frame", split_axis=0, concat_axis=0, tiled=True
+    )
     returned = returned.reshape(row_count, col_count, channels)
 
     def joined_edge(c):

time: 124 us -> 179 us (1.44)
  other arithmetic: 1.05 us -> 41.5 us
  local copies, waits for them, and re-layouts: 24 us -> 38.8 us
  Pallas kernels: 40.2 us -> 35.3 us
  waiting for transfers between devices: 37.3 us -> 41.2 us
    all_to_all x0 -> x4, other arithmetic: none -> 41.5 us  [the longest x2 20.9 us: body(): lax.all_to_all(attended.reshape(frames_all, pix_piece * channels), 'frame...]
    unnamed x18 -> x22, local copies, waits for them, and re-layouts: 4.67 us -> 24.1 us
    ppermute x4, waiting for transfers between devices: 0.01 us -> 6.53 us  [shifted(): return lax.ppermute(block, axis, route)]
    pad x2 -> x0, local copies, waits for them, and re-layouts: 5.21 us -> none  [convolve(): stacked = jnp.pad(weight, ((0, 0), (0, 0), (0, lanes - channels), (0, 0)))]
    pallas_call x2, Pallas kernels: 31.7 us -> 26.9 us  [convolve(): pl.pallas_call(functools.partial(conv_kernel, parts=len(sources), finish=...]
    all_to_all x2 -> x3, local copies, waits for them, and re-layouts: 3.57 us -> 8.02 us  [the longest x2 4.27 us: body(): lax.all_to_all(hidden.reshape(frames_all, pix_piece * channels), 'frame',...]
    pallas_call x1 -> x0, local copies, waits for them, and re-layouts: 3.77 us -> none  [attend(): pl.pallas_call(attend_kernel, out_shape=jax.ShapeDtypeStruct((frames_all,...]
    all_to_all x2, waiting for transfers between devices: 37.3 us -> 34.7 us  [the longest x1 17.8 us: body(): lax.all_to_all(attended.reshape(frames_all, pix_piece * channels), 'frame...]
  transfers between devices with their start and end apart: 6 -> 6, of which waited for: 2 -> 6; matrix products, arithmetic and copies ran while one was open for 7% -> 2% of each run, Pallas kernels for 0% -> 0%
where the time goes in v3:
time: 179 us; the launch traced here: 178 us
  other arithmetic  41.5 us (23%)
  waiting for transfers between devices  41.2 us (23%)
  local copies, waits for them, and re-layouts  38.8 us (22%)
  Pallas kernels  35.3 us (20%)
  starting transfers between devices  21 us (12%)
    pallas_call x2, Pallas kernels, convolve(): pl.pallas_call(functools.partial(conv_kernel, parts=len(sources), finish=...  26.9 us
    unnamed x22, local copies, waits for them, and re-layouts  24.1 us
    all_to_all x2, other arithmetic, body(): lax.all_to_all(attended.reshape(frames_all, pix_piece * channels), 'frame...  20.9 us
    all_to_all x2, other arithmetic, body(): lax.all_to_all(hidden.reshape(frames_all, pix_piece * channels), 'frame',...  20.6 us
    all_to_all x1, waiting for transfers between devices, body(): lax.all_to_all(attended.reshape(frames_all, pix_piece * channels), 'frame...  17.8 us
    all_to_all x1, waiting for transfers between devices, body(): lax.all_to_all(hidden.reshape(frames_all, pix_piece * channels), 'frame',...  16.9 us
    ppermute x4, starting transfers between devices, shifted(): return lax.ppermute(block, axis, route)  12.1 us
    pallas_call x1, Pallas kernels, attend(): pl.pallas_call(attend_kernel, out_shape=jax.ShapeDtypeStruct((frames_all,...  8.43 us
  transfers between devices with their start and end apart: 6, of which 6 were waited for; matrix products, arithmetic and copies ran while one was open for 2% of the time, Pallas kernels for 0%

profile of v3, /device:TPU:0, one launch (start us, length us, event | category | flops | bytes accessed | tf_op | source)
XLA Modules:
  0.0 178.0 jit_solution(7729578527425820549)
XLA Ops:
  0.0 2.1 %copy.47 = bf16[1,72,32,320]{3,1,2,0:T(8,128)(2,1)S(1)} copy(bf16[1,72,32,320]{3,2,1,0:T(8,128)(2,1)} %param.6) | data formatting | bytes 2949120 | tf_op args[0]
  2.1 4.9 %collective-permute-start = (bf16[72,320]{1,0:T(8,128)(2,1)S(1)}, bf16[72,320]{1,0:T(8,128)(2,1)S(1)}, u32[]{:S(2)}, u32[]{:S(2)}) collective-permute-start(bf16[72,320]{1,0:T(8,128)(2,1)S(1)} %get-tuple-element.10), channel_id=1, source_target_pairs={{0,4},{4,8},{8,12},{1,5},{5,9},{9,13},{2,6},{6,10},{10,14},{3,7},{... | collective-permute-start | bytes 138248 | tf_op jit(solution)/shard_map/ppermute | solution.py:16
  7.1 1.3 collective-permute-start.1
  8.8 4.3 %collective-permute-done.1.refs_2_ = bf16[72,320]{1,0:T(8,128)(2,1)S(1)} collective-permute-done((bf16[72,320]{1,0:T(8,128)(2,1)S(1)}, bf16[72,320]{1,0:T(8,128)(2,1)S(1)}, u32[]{:S(2)}, u32[]{:S(2)}) %collective-permute-start.1) | collective-permute-done | bytes 46112 | tf_op jit(solution)/shard_map/ppermute | solution.py:16
  13.7 13.6 %shard_map.64.refs_0_ = bf16[72,32,320]{2,1,0:T(8,128)(2,1)} custom-call(bf16[72,32,320]{2,1,0:T(8,128)(2,1)} %bitcast.19, bf16[72,320]{1,0:T(8,128)(2,1)} %copy-done.3, bf16[72,320]{1,0:T(8,128)(2,1)} %copy-done.5, bf16[3,960,320]{2,1,0:T(8,128)(2,1)} %bitcast.21), custom_call_target="tpu_custom_call" | custom-call | tf_op jit(solution)/shard_map/pallas_call | solution.py:86
  27.3 3.7 %all_to_all.16 = bf16[4,1,184320]{2,1,0:T(2,128)(2,1)S(1)} reshape(bf16[72,32,320]{2,1,0:T(8,128)(2,1)} %shard_map.64.refs_0_) | data formatting | bytes 2949120 | tf_op jit(solution)/shard_map/all_to_all | solution.py:172
  31.6 10.6 %reduce.2 = bf16[4,184320]{1,0:T(4,128)(2,1)} reduce(bf16[4,1,184320]{2,1,0:T(2,128)(2,1)S(1)} %all_to_all.16, bf16[]{:T(256)} %broadcast.2), dimensions={1}, to_apply=%all_to_all.16.reduce_sub_computation | reduce | bytes 2949122 | tf_op jit(solution)/shard_map/all_to_all | solution.py:172
  42.2 4.0 %reshape.48 = bf16[4,2,92160]{2,1,0:T(2,128)(2,1)} reshape(bf16[4,184320]{1,0:T(4,128)(2,1)} %reduce.2) | data formatting | bytes 2949120
  46.2 4.6 %all-to-all-start = ((bf16[4,2,92160]{2,1,0:T(2,128)(2,1)}), bf16[4,2,92160]{2,1,0:T(2,128)(2,1)}, u32[]{:S(2)}, u32[]{:S(2)}) async-start(bf16[4,2,92160]{2,1,0:T(2,128)(2,1)} %reshape.48), calls=%async_computation | async-start | bytes 2949120 | tf_op jit(solution)/shard_map/all_to_all | solution.py:172
  50.9 1.2 copy.27
  52.0 0.8 copy.29.bias_ref
  52.8 16.9 %all-to-all-done = bf16[4,2,92160]{2,1,0:T(2,128)(2,1)} async-done(((bf16[4,2,92160]{2,1,0:T(2,128)(2,1)}), bf16[4,2,92160]{2,1,0:T(2,128)(2,1)}, u32[]{:S(2)}, u32[]{:S(2)}) %all-to-all-start) | async-done | bytes 1474592 | tf_op jit(solution)/shard_map/all_to_all | solution.py:172
  69.8 3.0 %reshape.49 = bf16[4,1,184320]{2,1,0:T(2,128)(2,1)S(1)} reshape(bf16[4,2,92160]{2,1,0:T(2,128)(2,1)} %all-to-all-done) | data formatting | bytes 2949120
  72.7 10.0 %reduce = bf16[4,184320]{1,0:T(4,128)(2,1)} reduce(bf16[4,1,184320]{2,1,0:T(2,128)(2,1)S(1)} %reshape.49, bf16[]{:T(256)} %constant.1), dimensions={1}, to_apply=%all_to_all.13.reduce_sub_computation | reduce | bytes 2949122 | tf_op jit(solution)/shard_map/all_to_all | solution.py:172
  82.7 2.8 %reshape.44 = bf16[737280]{0:T(1024)(128)(2,1)S(1)} reshape(bf16[4,184320]{1,0:T(4,128)(2,1)} %reduce) | data formatting | bytes 2949120
  85.6 2.7 %reshape.38.x_ref = bf16[4,576,320]{2,1,0:T(8,128)(2,1)} reshape(bf16[737280]{0:T(1024)(128)(2,1)S(1)} %reshape.44) | data formatting | bytes 2949120 | tf_op jit(solution)/shard_map/reshape | solution.py:175
  88.3 8.4 %shard_map.65 = bf16[4,576,320]{2,1,0:T(8,128)(2,1)} custom-call(bf16[4,576,320]{2,1,0:T(8,128)(2,1)} %reshape.38.x_ref, bf16[960,320]{1,0:T(8,128)(2,1)} %bitcast.20, f32[5,4,4,1]{3,2,1,0:T(4,128)} %copy.29.bias_ref, bf16[320,320]{1,0:T(8,128)(2,1)} %wout_ref.1), custom_call_target="tpu_custom_call" | custom-call | tf_op jit(solution)/shard_map/pallas_call | solution.py:154
  96.7 3.7 %all_to_all.17 = bf16[4,1,184320]{2,1,0:T(2,128)(2,1)S(1)} reshape(bf16[4,576,320]{2,1,0:T(8,128)(2,1)} %shard_map.65) | data formatting | bytes 2949120 | tf_op jit(solution)/shard_map/all_to_all | solution.py:176
  100.5 10.8 %reduce.3 = bf16[4,184320]{1,0:T(4,128)(2,1)} reduce(bf16[4,1,184320]{2,1,0:T(2,128)(2,1)S(1)} %all_to_all.17, bf16[]{:T(256)} %broadcast.2), dimensions={1}, to_apply=%all_to_all.17.reduce_sub_computation | reduce | bytes 2949122 | tf_op jit(solution)/shard_map/all_to_all | solution.py:176
  111.3 4.0 %reshape.50 = bf16[4,2,92160]{2,1,0:T(2,128)(2,1)} reshape(bf16[4,184320]{1,0:T(4,128)(2,1)} %reduce.3) | data formatting | bytes 2949120
  115.3 4.3 %all-to-all-start.1 = ((bf16[4,2,92160]{2,1,0:T(2,128)(2,1)}), bf16[4,2,92160]{2,1,0:T(2,128)(2,1)}, u32[]{:S(2)}, u32[]{:S(2)}) async-start(bf16[4,2,92160]{2,1,0:T(2,128)(2,1)} %reshape.50), calls=%async_computation.1 | async-start | bytes 2949120 | tf_op jit(solution)/shard_map/all_to_all | solution.py:176
  119.6 1.3 fusion.2
  121.0 17.8 %all-to-all-done.1 = bf16[4,2,92160]{2,1,0:T(2,128)(2,1)} async-done(((bf16[4,2,92160]{2,1,0:T(2,128)(2,1)}), bf16[4,2,92160]{2,1,0:T(2,128)(2,1)}, u32[]{:S(2)}, u32[]{:S(2)}) %all-to-all-start.1) | async-done | bytes 1474592 | tf_op jit(solution)/shard_map/all_to_all | solution.py:176
  138.7 3.0 %reshape.51 = bf16[4,1,184320]{2,1,0:T(2,128)(2,1)S(1)} reshape(bf16[4,2,92160]{2,1,0:T(2,128)(2,1)} %all-to-all-done.1) | data formatting | bytes 2949120
  141.7 10.0 %reduce.1 = bf16[4,184320]{1,0:T(4,128)(2,1)} reduce(bf16[4,1,184320]{2,1,0:T(2,128)(2,1)S(1)} %reshape.51, bf16[]{:T(256)} %constant.1), dimensions={1}, to_apply=%all_to_all.15.reduce_sub_computation | reduce | bytes 2949122 | tf_op jit(solution)/shard_map/all_to_all | solution.py:176
  151.7 2.8 %reshape.46 = bf16[737280]{0:T(1024)(128)(2,1)S(1)} reshape(bf16[4,184320]{1,0:T(4,128)(2,1)} %reduce.1) | data formatting | bytes 2949120
  154.6 1.6 reshape.39.refs_1_
  156.4 1.3 collective-permute-start.3
  157.7 4.5 %collective-permute-start.2 = (bf16[72,320]{1,0:T(8,128)(2,1)S(1)}, bf16[72,320]{1,0:T(8,128)(2,1)S(1)}, u32[]{:S(2)}, u32[]{:S(2)}) collective-permute-start(bf16[72,320]{1,0:T(8,128)(2,1)S(1)} %fusion), channel_id=1, source_target_pairs={{0,4},{4,8},{8,12},{1,5},{5,9},{9,13},{2,6},{6,10},{10,14},{3,7},{... | collective-permute-start | bytes 138248 | tf_op jit(solution)/shard_map/ppermute | solution.py:16
  162.5 1.6 collective-permute-done.2.refs_2_
  164.1 0.6 copy-done.4
  164.7 13.3 %shard_map.66 = bf16[72,32,320]{2,1,0:T(8,128)(2,1)} custom-call(bf16[72,32,320]{2,1,0:T(8,128)(2,1)} %shard_map.64.refs_0_, bf16[72,32,320]{2,1,0:T(8,128)(2,1)} %copy-done, bf16[72,320]{1,0:T(8,128)(2,1)} %copy-done.4, bf16[72,320]{1,0:T(8,128)(2,1)} %copy-done.2, bf16[3,960,320]{2,1,0:T(8,128)(2,1)} %bitcast.22), custom_call_target="tpu_custom_call" | custom-call | tf_op jit(solution)/shard_map/pallas_call | solution.py:86
  (20 shorter events, 2.0 us)
Async XLA Ops:
  2.1 6.7 %collective-permute-start = (bf16[72,320]{1,0:T(8,128)(2,1)S(1)}, bf16[72,320]{1,0:T(8,128)(2,1)S(1)}, u32[]{:S(2)}, u32[]{:S(2)}) collective-permute-start(bf16[72,320]{1,0:T(8,128)(2,1)S(1)} %get-tuple-element.10), channel_id=1, source_target_pairs={{0,4},{4,8},{8,12},{1,5},{5,9},{9,13},{2,6},{6,10},{10,14},{3,7},{... | collective-permute-start | bytes 138248 | tf_op jit(solution)/shard_map/ppermute | solution.py:16
  7.1 6.0 %collective-permute-start.1 = (bf16[72,320]{1,0:T(8,128)(2,1)S(1)}, bf16[72,320]{1,0:T(8,128)(2,1)S(1)}, u32[]{:S(2)}, u32[]{:S(2)}) collective-permute-start(bf16[72,320]{1,0:T(8,128)(2,1)S(1)} %get-tuple-element.9), channel_id=1, source_target_pairs={{4,0},{8,4},{12,8},{5,1},{9,5},{13,9},{6,2},{10,6},{14,10},{7,3},{... | collective-permute-start | bytes 138248 | tf_op jit(solution)/shard_map/ppermute | solution.py:16
  8.8 4.3 %copy-start.3 = (bf16[72,320]{1,0:T(8,128)(2,1)}, bf16[72,320]{1,0:T(8,128)(2,1)S(1)}, u32[]{:S(2)}) copy-start(bf16[72,320]{1,0:T(8,128)(2,1)S(1)} %collective-permute-done.refs_1_) | copy-start | bytes 138244
  13.1 0.6 copy-start.5
  46.2 4.7 %copy-start.1 = (bf16[320,960]{1,0:T(8,128)(2,1)S(1)}, bf16[320,960]{1,0:T(8,128)(2,1)}, u32[]{:S(2)}) copy-start(bf16[320,960]{1,0:T(8,128)(2,1)} %param.8) | copy-start | bytes 1843204
  46.2 5.8 %copy-start.6 = (f32[5,4,4]{0,2,1:T(4,128)S(1)}, f32[5,4,4]{0,2,1:T(4,128)}, u32[]{:S(2)}) copy-start(f32[5,4,4]{0,2,1:T(4,128)} %param.10) | copy-start | bytes 964
  46.2 23.6 %all-to-all-start = ((bf16[4,2,92160]{2,1,0:T(2,128)(2,1)}), bf16[4,2,92160]{2,1,0:T(2,128)(2,1)}, u32[]{:S(2)}, u32[]{:S(2)}) async-start(bf16[4,2,92160]{2,1,0:T(2,128)(2,1)} %reshape.48), calls=%async_computation | async-start | bytes 2949120 | tf_op jit(solution)/shard_map/all_to_all | solution.py:172
  115.3 23.4 %all-to-all-start.1 = ((bf16[4,2,92160]{2,1,0:T(2,128)(2,1)}), bf16[4,2,92160]{2,1,0:T(2,128)(2,1)}, u32[]{:S(2)}, u32[]{:S(2)}) async-start(bf16[4,2,92160]{2,1,0:T(2,128)(2,1)} %reshape.50), calls=%async_computation.1 | async-start | bytes 2949120 | tf_op jit(solution)/shard_map/all_to_all | solution.py:176
  156.2 7.9 %copy-start = (bf16[72,32,320]{2,1,0:T(8,128)(2,1)}, bf16[72,32,320]{2,1,0:T(8,128)(2,1)S(1)}, u32[]{:S(2)}) copy-start(bf16[72,32,320]{2,1,0:T(8,128)(2,1)S(1)} %reshape.39.refs_1_) | copy-start | bytes 4423684
  156.4 6.0 %collective-permute-start.3 = (bf16[72,320]{1,0:T(8,128)(2,1)S(1)}, bf16[72,320]{1,0:T(8,128)(2,1)S(1)}, u32[]{:S(2)}, u32[]{:S(2)}) collective-permute-start(bf16[72,320]{1,0:T(8,128)(2,1)S(1)} %fusion.1), channel_id=1, source_target_pairs={{4,0},{8,4},{12,8},{5,1},{9,5},{13,9},{6,2},{10,6},{14,10},{7,3},{... | collective-permute-start | bytes 138248 | tf_op jit(solution)/shard_map/ppermute | solution.py:16
  157.7 6.3 %collective-permute-start.2 = (bf16[72,320]{1,0:T(8,128)(2,1)S(1)}, bf16[72,320]{1,0:T(8,128)(2,1)S(1)}, u32[]{:S(2)}, u32[]{:S(2)}) collective-permute-start(bf16[72,320]{1,0:T(8,128)(2,1)S(1)} %fusion), channel_id=1, source_target_pairs={{0,4},{4,8},{8,12},{1,5},{5,9},{9,13},{2,6},{6,10},{10,14},{3,7},{... | collective-permute-start | bytes 138248 | tf_op jit(solution)/shard_map/ppermute | solution.py:16
  162.5 1.6 copy-start.2
  164.1 0.6 copy-start.4

commit v4 on v3

--- a/solution.py
+++ b/solution.py
@@ -169,13 +169,13 @@
     pix_piece = row_count * col_count // frames_all
     tile = latents.reshape(row_count, col_count, channels)
     hidden = convolve([tile], lambda c: tile[:, c, :], conv1_weight, norm_gelu)
-    pieces = lax.all_to_all(
-        hidden.reshape(frames_all, pix_piece * channels), "frame", split_axis=0, concat_axis=0, tiled=True
-    )
+    if row_count % frames_all == 0:
+        piece_shape = (frames_all, row_count // frames_all, col_count, channels)
+    else:
+        piece_shape = (frames_all, pix_piece, channels)
+    pieces = lax.all_to_all(hidden.reshape(piece_shape), "frame", split_axis=0, concat_axis=0, tiled=True)
     attended = attend(pieces.reshape(frames_all, pix_piece, channels), qkv_weight, pos_bias, out_weight)
-    returned = lax.all_to_all(
-        attended.reshape(frames_all, pix_piece * channels), "frame", split_axis=0, concat_axis=0, tiled=True
-    )
+    returned = lax.all_to_all(attended.reshape(piece_shape), "frame", split_axis=0, concat_axis=0, tiled=True)
     returned = returned.reshape(row_count, col_count, channels)
 
     def joined_edge(c):

time: 179 us -> 109 us (0.61)
  other arithmetic: 41.5 us -> 0.03 us
  local copies, waits for them, and re-layouts: 38.8 us -> 8.04 us
  waiting for transfers between devices: 41.2 us -> 44.6 us
    all_to_all x4 -> x0, other arithmetic: 41.5 us -> none  [the longest x2 20.9 us: body(): lax.all_to_all(attended.reshape(frames_all, pix_piece * channels), 'frame...]
    unnamed x22 -> x18, local copies, waits for them, and re-layouts: 24.1 us -> 5.7 us
    all_to_all x3 -> x0, local copies, waits for them, and re-layouts: 8.02 us -> none  [the longest x2 4.27 us: body(): lax.all_to_all(hidden.reshape(frames_all, pix_piece * channels), 'frame',...]
    all_to_all x2, waiting for transfers between devices: 34.7 us -> 41 us  [the longest x1 20.8 us: body(): lax.all_to_all(attended.reshape(piece_shape), 'frame', split_axis=0, conc...]
    reshape x2 -> x0, local copies, waits for them, and re-layouts: 4.3 us -> none  [the longest x1 2.69 us: body(): pieces.reshape(frames_all, pix_piece, channels)]
    ppermute x4, waiting for transfers between devices: 6.53 us -> 3.57 us  [shifted(): return lax.ppermute(block, axis, route)]
  transfers between devices with their start and end apart: 6 -> 6, of which waited for: 6 -> 6; matrix products, arithmetic and copies ran while one was open for 2% -> 3% of each run, Pallas kernels for 0% -> 0%
where the time goes in v4:
time: 109 us; the launch traced here: 108 us
  waiting for transfers between devices  44.6 us (41%)
  Pallas kernels  35.4 us (32%)
  starting transfers between devices  20.3 us (19%)
  local copies, waits for them, and re-layouts  8.04 us (7%)
    pallas_call x2, Pallas kernels, convolve(): pl.pallas_call(functools.partial(conv_kernel, parts=len(sources), finish=...  26.9 us
    all_to_all x1, waiting for transfers between devices, body(): lax.all_to_all(attended.reshape(piece_shape), 'frame', split_axis=0, conc...  20.8 us
    all_to_all x1, waiting for transfers between devices, body(): lax.all_to_all(hidden.reshape(piece_shape), 'frame', split_axis=0, concat...  20.2 us
    ppermute x4, starting transfers between devices, shifted(): return lax.ppermute(block, axis, route)  13 us
    pallas_call x1, Pallas kernels, attend(): pl.pallas_call(attend_kernel, out_shape=jax.ShapeDtypeStruct((frames_all,...  8.46 us
    unnamed x18, local copies, waits for them, and re-layouts  5.7 us
    all_to_all x1, starting transfers between devices, body(): lax.all_to_all(hidden.reshape(piece_shape), 'frame', split_axis=0, concat...  3.71 us
    all_to_all x1, starting transfers between devices, body(): lax.all_to_all(attended.reshape(piece_shape), 'frame', split_axis=0, conc...  3.58 us
  transfers between devices with their start and end apart: 6, of which 6 were waited for; matrix products, arithmetic and copies ran while one was open for 3% of the time, Pallas kernels for 0%

profile of v4, /device:TPU:0, one launch (start us, length us, event | category | flops | bytes accessed | tf_op | source)
XLA Modules:
  0.0 108.4 jit_solution(14264180969197587499)
XLA Ops:
  0.0 2.1 %copy.37 = bf16[1,72,32,320]{3,1,2,0:T(8,128)(2,1)S(1)} copy(bf16[1,72,32,320]{3,2,1,0:T(8,128)(2,1)} %param.6) | data formatting | bytes 2949120 | tf_op args[0]
  2.1 1.3 %collective-permute-start.1 = (bf16[72,320]{1,0:T(8,128)(2,1)S(1)}, bf16[72,320]{1,0:T(8,128)(2,1)S(1)}, u32[]{:S(2)}, u32[]{:S(2)}) collective-permute-start(bf16[72,320]{1,0:T(8,128)(2,1)S(1)} %get-tuple-element.9), channel_id=1, source_target_pairs={{4,0},{8,4},{12,8},{5,1},{9,5},{13,9},{6,2},{10,6},{14,10},{7,3},{... | collective-permute-start | bytes 138248 | tf_op jit(solution)/shard_map/ppermute | solution.py:16
  3.4 5.6 %collective-permute-start = (bf16[72,320]{1,0:T(8,128)(2,1)S(1)}, bf16[72,320]{1,0:T(8,128)(2,1)S(1)}, u32[]{:S(2)}, u32[]{:S(2)}) collective-permute-start(bf16[72,320]{1,0:T(8,128)(2,1)S(1)} %get-tuple-element.10), channel_id=1, source_target_pairs={{0,4},{4,8},{8,12},{1,5},{5,9},{9,13},{2,6},{6,10},{10,14},{3,7},{... | collective-permute-start | bytes 138248 | tf_op jit(solution)/shard_map/ppermute | solution.py:16
  9.0 0.2 collective-permute-done.1.refs_2_
  9.2 0.0 copy-start.4
  9.2 1.6 %collective-permute-done.refs_1_ = bf16[72,320]{1,0:T(8,128)(2,1)S(1)} collective-permute-done((bf16[72,320]{1,0:T(8,128)(2,1)S(1)}, bf16[72,320]{1,0:T(8,128)(2,1)S(1)}, u32[]{:S(2)}, u32[]{:S(2)}) %collective-permute-start) | collective-permute-done | bytes 46112 | tf_op jit(solution)/shard_map/ppermute | solution.py:16
  10.8 0.0 copy-start.6
  10.8 0.0 copy-done.4
  10.8 0.6 copy-done.6
  11.4 13.6 %shard_map.64.refs_0_ = bf16[72,32,320]{2,1,0:T(8,128)(2,1)} custom-call(bf16[72,32,320]{2,1,0:T(8,128)(2,1)} %bitcast.26, bf16[72,320]{1,0:T(8,128)(2,1)} %copy-done.6, bf16[72,320]{1,0:T(8,128)(2,1)} %copy-done.4, bf16[3,960,320]{2,1,0:T(8,128)(2,1)} %bitcast.30), custom_call_target="tpu_custom_call" | custom-call | tf_op jit(solution)/shard_map/pallas_call | solution.py:86
  25.0 0.0 copy-start.7
  25.0 0.0 copy-start.2
  25.0 3.7 %all-to-all-start = ((bf16[4,18,32,320]{3,2,1,0:T(8,128)(2,1)}), bf16[4,18,32,320]{3,2,1,0:T(8,128)(2,1)S(1)}, u32[]{:S(2)}, u32[]{:S(2)}) async-start(bf16[4,18,32,320]{3,2,1,0:T(8,128)(2,1)} %bitcast.23), calls=%async_computation | async-start | bytes 3538944 | tf_op jit(solution)/shard_map/all_to_all | solution.py:176
  28.7 0.0 copy-done.7
  28.7 0.8 copy.20.bias_ref
  29.6 0.0 copy-done.2
  29.6 1.2 %copy.18 = bf16[320,960]{0,1:T(8,128)(2,1)} copy(bf16[320,960]{1,0:T(8,128)(2,1)S(1)} %copy-done.2) | data formatting | bytes 1228800 | tf_op args[2]
  30.7 20.2 %all-to-all-done = bf16[4,18,32,320]{3,2,1,0:T(8,128)(2,1)S(1)} async-done(((bf16[4,18,32,320]{3,2,1,0:T(8,128)(2,1)}), bf16[4,18,32,320]{3,2,1,0:T(8,128)(2,1)S(1)}, u32[]{:S(2)}, u32[]{:S(2)}) %all-to-all-start) | async-done | bytes 1474592 | tf_op jit(solution)/shard_map/all_to_all | solution.py:176
  50.9 1.2 %copy-done.1 = bf16[4,18,32,320]{3,2,1,0:T(8,128)(2,1)} copy-done((bf16[4,18,32,320]{3,2,1,0:T(8,128)(2,1)}, bf16[4,18,32,320]{3,2,1,0:T(8,128)(2,1)S(1)}, u32[]{:S(2)}) %copy-start.1) | copy-done | bytes 1474584
  52.1 8.5 %shard_map.65 = bf16[4,576,320]{2,1,0:T(8,128)(2,1)} custom-call(bf16[4,576,320]{2,1,0:T(8,128)(2,1)} %bitcast.27, bf16[960,320]{1,0:T(8,128)(2,1)} %bitcast.29, f32[5,4,4,1]{3,2,1,0:T(4,128)} %copy.20.bias_ref, bf16[320,320]{1,0:T(8,128)(2,1)} %wout_ref.1), custom_call_target="tpu_custom_call" | custom-call | tf_op jit(solution)/shard_map/pallas_call | solution.py:154
  60.5 3.6 %all-to-all-start.1 = ((bf16[4,18,32,320]{3,2,1,0:T(8,128)(2,1)}), bf16[4,18,32,320]{3,2,1,0:T(8,128)(2,1)S(1)}, u32[]{:S(2)}, u32[]{:S(2)}) async-start(bf16[4,18,32,320]{3,2,1,0:T(8,128)(2,1)} %bitcast.28), calls=%async_computation.1 | async-start | bytes 3538944 | tf_op jit(solution)/shard_map/all_to_all | solution.py:178
  64.1 1.3 %fusion.2 = (bf16[72,1,320]{2,1,0:T(2,128)(2,1)S(1)}, bf16[72,1,320]{2,1,0:T(2,128)(2,1)S(1)}) fusion(bf16[72,32,320]{2,1,0:T(8,128)(2,1)} %shard_map.64.refs_0_), kind=kLoop, calls=%fused_computation.7 | loop fusion | bytes 184320 | tf_op jit(solution)/shard_map/slice | solution.py:182
  65.5 20.8 %all-to-all-done.1 = bf16[4,18,32,320]{3,2,1,0:T(8,128)(2,1)S(1)} async-done(((bf16[4,18,32,320]{3,2,1,0:T(8,128)(2,1)}), bf16[4,18,32,320]{3,2,1,0:T(8,128)(2,1)S(1)}, u32[]{:S(2)}, u32[]{:S(2)}) %all-to-all-start.1) | async-done | bytes 1474592 | tf_op jit(solution)/shard_map/all_to_all | solution.py:178
  86.3 0.2 fusion.3
  86.5 1.3 %collective-permute-start.3 = (bf16[72,320]{1,0:T(8,128)(2,1)S(1)}, bf16[72,320]{1,0:T(8,128)(2,1)S(1)}, u32[]{:S(2)}, u32[]{:S(2)}) collective-permute-start(bf16[72,320]{1,0:T(8,128)(2,1)S(1)} %fusion.1), channel_id=1, source_target_pairs={{4,0},{8,4},{12,8},{5,1},{9,5},{13,9},{6,2},{10,6},{14,10},{7,3},{... | collective-permute-start | bytes 138248 | tf_op jit(solution)/shard_map/ppermute | solution.py:16
  87.8 4.9 %collective-permute-start.2 = (bf16[72,320]{1,0:T(8,128)(2,1)S(1)}, bf16[72,320]{1,0:T(8,128)(2,1)S(1)}, u32[]{:S(2)}, u32[]{:S(2)}) collective-permute-start(bf16[72,320]{1,0:T(8,128)(2,1)S(1)} %fusion), channel_id=1, source_target_pairs={{0,4},{4,8},{8,12},{1,5},{5,9},{9,13},{2,6},{6,10},{10,14},{3,7},{... | collective-permute-start | bytes 138248 | tf_op jit(solution)/shard_map/ppermute | solution.py:16
  92.7 0.2 collective-permute-done.3.refs_3_
  92.9 1.6 %collective-permute-done.2.refs_2_ = bf16[72,320]{1,0:T(8,128)(2,1)S(1)} collective-permute-done((bf16[72,320]{1,0:T(8,128)(2,1)S(1)}, bf16[72,320]{1,0:T(8,128)(2,1)S(1)}, u32[]{:S(2)}, u32[]{:S(2)}) %collective-permute-start.2) | collective-permute-done | bytes 46112 | tf_op jit(solution)/shard_map/ppermute | solution.py:16
  94.5 0.0 copy-done
  94.5 0.0 copy-done.3
  94.5 0.6 copy-done.5
  95.1 13.3 %shard_map.66 = bf16[72,32,320]{2,1,0:T(8,128)(2,1)} custom-call(bf16[72,32,320]{2,1,0:T(8,128)(2,1)} %shard_map.64.refs_0_, bf16[72,32,320]{2,1,0:T(8,128)(2,1)} %bitcast.25, bf16[72,320]{1,0:T(8,128)(2,1)} %copy-done.5, bf16[72,320]{1,0:T(8,128)(2,1)} %copy-done.3, bf16[3,960,320]{2,1,0:T(8,128)(2,1)} %bitcast.31), custom_call_target="tpu_custom_call" | custom-call | tf_op jit(solution)/shard_map/pallas_call | solution.py:86
  (7 shorter events, 0.1 us)
Async XLA Ops:
  2.1 7.1 %collective-permute-start.1 = (bf16[72,320]{1,0:T(8,128)(2,1)S(1)}, bf16[72,320]{1,0:T(8,128)(2,1)S(1)}, u32[]{:S(2)}, u32[]{:S(2)}) collective-permute-start(bf16[72,320]{1,0:T(8,128)(2,1)S(1)} %get-tuple-element.9), channel_id=1, source_target_pairs={{4,0},{8,4},{12,8},{5,1},{9,5},{13,9},{6,2},{10,6},{14,10},{7,3},{... | collective-permute-start | bytes 138248 | tf_op jit(solution)/shard_map/ppermute | solution.py:16
  3.4 7.4 %collective-permute-start = (bf16[72,320]{1,0:T(8,128)(2,1)S(1)}, bf16[72,320]{1,0:T(8,128)(2,1)S(1)}, u32[]{:S(2)}, u32[]{:S(2)}) collective-permute-start(bf16[72,320]{1,0:T(8,128)(2,1)S(1)} %get-tuple-element.10), channel_id=1, source_target_pairs={{0,4},{4,8},{8,12},{1,5},{5,9},{9,13},{2,6},{6,10},{10,14},{3,7},{... | collective-permute-start | bytes 138248 | tf_op jit(solution)/shard_map/ppermute | solution.py:16
  9.2 1.6 %copy-start.4 = (bf16[72,320]{1,0:T(8,128)(2,1)}, bf16[72,320]{1,0:T(8,128)(2,1)S(1)}, u32[]{:S(2)}) copy-start(bf16[72,320]{1,0:T(8,128)(2,1)S(1)} %collective-permute-done.1.refs_2_) | copy-start | bytes 138244
  10.8 0.6 copy-start.6
  25.0 3.7 %copy-start.7 = (f32[5,4,4]{0,2,1:T(4,128)S(1)}, f32[5,4,4]{0,2,1:T(4,128)}, u32[]{:S(2)}) copy-start(f32[5,4,4]{0,2,1:T(4,128)} %param.10) | copy-start | bytes 964
  25.0 4.6 %copy-start.2 = (bf16[320,960]{1,0:T(8,128)(2,1)S(1)}, bf16[320,960]{1,0:T(8,128)(2,1)}, u32[]{:S(2)}) copy-start(bf16[320,960]{1,0:T(8,128)(2,1)} %param.8) | copy-start | bytes 1843204
  25.0 25.9 %all-to-all-start = ((bf16[4,18,32,320]{3,2,1,0:T(8,128)(2,1)}), bf16[4,18,32,320]{3,2,1,0:T(8,128)(2,1)S(1)}, u32[]{:S(2)}, u32[]{:S(2)}) async-start(bf16[4,18,32,320]{3,2,1,0:T(8,128)(2,1)} %bitcast.23), calls=%async_computation | async-start | bytes 3538944 | tf_op jit(solution)/shard_map/all_to_all | solution.py:176
  50.9 1.2 %copy-start.1 = (bf16[4,18,32,320]{3,2,1,0:T(8,128)(2,1)}, bf16[4,18,32,320]{3,2,1,0:T(8,128)(2,1)S(1)}, u32[]{:S(2)}) copy-start(bf16[4,18,32,320]{3,2,1,0:T(8,128)(2,1)S(1)} %all-to-all-done) | copy-start | bytes 4423684
  60.5 25.7 %all-to-all-start.1 = ((bf16[4,18,32,320]{3,2,1,0:T(8,128)(2,1)}), bf16[4,18,32,320]{3,2,1,0:T(8,128)(2,1)S(1)}, u32[]{:S(2)}, u32[]{:S(2)}) async-start(bf16[4,18,32,320]{3,2,1,0:T(8,128)(2,1)} %bitcast.28), calls=%async_computation.1 | async-start | bytes 3538944 | tf_op jit(solution)/shard_map/all_to_all | solution.py:178
  86.3 8.2 %copy-start = (bf16[4,18,32,320]{3,2,1,0:T(8,128)(2,1)}, bf16[4,18,32,320]{3,2,1,0:T(8,128)(2,1)S(1)}, u32[]{:S(2)}) copy-start(bf16[4,18,32,320]{3,2,1,0:T(8,128)(2,1)S(1)} %all-to-all-done.1) | copy-start | bytes 4423684
  86.5 6.4 %collective-permute-start.3 = (bf16[72,320]{1,0:T(8,128)(2,1)S(1)}, bf16[72,320]{1,0:T(8,128)(2,1)S(1)}, u32[]{:S(2)}, u32[]{:S(2)}) collective-permute-start(bf16[72,320]{1,0:T(8,128)(2,1)S(1)} %fusion.1), channel_id=1, source_target_pairs={{4,0},{8,4},{12,8},{5,1},{9,5},{13,9},{6,2},{10,6},{14,10},{7,3},{... | collective-permute-start | bytes 138248 | tf_op jit(solution)/shard_map/ppermute | solution.py:16
  87.8 6.7 %collective-permute-start.2 = (bf16[72,320]{1,0:T(8,128)(2,1)S(1)}, bf16[72,320]{1,0:T(8,128)(2,1)S(1)}, u32[]{:S(2)}, u32[]{:S(2)}) collective-permute-start(bf16[72,320]{1,0:T(8,128)(2,1)S(1)} %fusion), channel_id=1, source_target_pairs={{0,4},{4,8},{8,12},{1,5},{5,9},{9,13},{2,6},{6,10},{10,14},{3,7},{... | collective-permute-start | bytes 138248 | tf_op jit(solution)/shard_map/ppermute | solution.py:16
  92.9 1.6 %copy-start.3 = (bf16[72,320]{1,0:T(8,128)(2,1)}, bf16[72,320]{1,0:T(8,128)(2,1)S(1)}, u32[]{:S(2)}) copy-start(bf16[72,320]{1,0:T(8,128)(2,1)S(1)} %collective-permute-done.3.refs_3_) | copy-start | bytes 138244
  94.5 0.6 copy-start.5

commit v5 on v4

--- a/solution.py
+++ b/solution.py
@@ -18,7 +18,7 @@
 
 def conv_kernel(*refs, parts, finish):
     sources = refs[:parts]
-    left_ref, right_ref, w_ref, o_ref, slab, shift_s = refs[parts:]
+    w_ref, o_ref, edge_ref, slab, shift_s = refs[parts:]
     row_count, col_count, channels = o_ref.shape
     lanes = slab.shape[1] // 3
     band = 24
@@ -26,10 +26,6 @@
     padded_rows = slab.shape[0]
     slab[pl.ds(0, col_count)] = jnp.zeros((col_count, slab.shape[1]), jnp.bfloat16)
     slab[pl.ds(padded_rows - col_count, col_count)] = jnp.zeros((col_count, slab.shape[1]), jnp.bfloat16)
-    if lanes > channels:
-        pad = jnp.zeros((padded_rows, lanes - channels), jnp.bfloat16)
-        for b in range(3):
-            slab[:, pl.ds(b * lanes + channels, lanes - channels)] = pad
     column = lax.broadcasted_iota(jnp.int32, (band, col_count, channels), 1)
 
     def build(i, carry):
@@ -41,10 +37,8 @@
         shift_s[pl.ds(8, span)] = block.astype(jnp.float32).reshape(span, channels)
         before = shift_s[pl.ds(7, span)].reshape(band, col_count, channels)
         after = shift_s[pl.ds(9, span)].reshape(band, col_count, channels)
-        rim_l = left_ref[pl.ds(r0, band)].astype(jnp.float32)[:, None, :]
-        rim_r = right_ref[pl.ds(r0, band)].astype(jnp.float32)[:, None, :]
-        before = jnp.where(column == 0, rim_l, before)
-        after = jnp.where(column == col_count - 1, rim_r, after)
+        before = jnp.where(column == 0, 0.0, before)
+        after = jnp.where(column == col_count - 1, 0.0, after)
         rows = pl.ds(pl.multiple_of((r0 + 1) * col_count, col_count), span)
         slab[rows, pl.ds(0, channels)] = before.reshape(span, channels).astype(jnp.bfloat16)
         slab[rows, pl.ds(lanes, channels)] = block.reshape(span, channels)
@@ -60,10 +54,32 @@
             rows = pl.ds(pl.multiple_of((r0 + a) * col_count, col_count), span)
             term = jnp.dot(slab[rows, :], w_ref[a], preferred_element_type=jnp.float32)
             acc = term if acc is None else acc + term
+        grid = acc.reshape(band, col_count, channels)
         o_ref[pl.ds(r0, band)] = finish(acc).reshape(band, col_count, channels)
+        edge_ref[0, pl.ds(r0, band)] = grid[:, 0, :]
+        edge_ref[1, pl.ds(r0, band)] = grid[:, col_count - 1, :]
         return carry
 
     lax.fori_loop(0, row_count // band, compute, 0)
+
+
+def edge_kernel(x_ref, o_ref):
+    block = x_ref[...]
+    last = block.shape[1] - 1
+    o_ref[0] = jnp.where(pl.program_id(0) == 0, block[:, 0, :], block[:, last, :])
+
+
+def tile_edges(tile):
+    row_count, col_count, channels = tile.shape
+    width = 16
+    blocks = col_count // width
+    return pl.pallas_call(
+        edge_kernel,
+        out_shape=jax.ShapeDtypeStruct((2, row_count, channels), tile.dtype),
+        grid=(2,),
+        in_specs=[pl.BlockSpec((row_count, width, channels), lambda i: (0, i * (blocks - 1), 0))],
+        out_specs=pl.BlockSpec((1, row_count, channels), lambda i: (i, 0, 0)),
+    )(tile)
 
 
 def norm_gelu(first):
@@ -75,24 +91,36 @@
     return acc.astype(jnp.bfloat16)
 
 
-def convolve(sources, edge_of, weight, finish):
+def rim_term(rim, taps):
+    padded = jnp.pad(rim, ((1, 1), (0, 0)))
+    row_count = rim.shape[0]
+    stacked = jnp.concatenate([padded[a : a + row_count] for a in range(3)], axis=1)
+    return jnp.dot(stacked, taps.reshape(-1, taps.shape[-1]), preferred_element_type=jnp.float32)
+
+
+def convolve(sources, edges, weight, finish):
     row_count, col_count, channels = sources[0].shape
-    left_rim = shifted(edge_of(-1), "quarter", 1)
-    right_rim = shifted(edge_of(0), "quarter", -1)
+    left_rim = shifted(edges[1], "quarter", 1)
+    right_rim = shifted(edges[0], "quarter", -1)
     vmem = pl.BlockSpec(memory_space=pltpu.VMEM)
     padded = (row_count + 2) * col_count
-    lanes = channels
-    stacked = weight.reshape(3, 3 * lanes, channels)
-    return pl.pallas_call(
+    main, raw = pl.pallas_call(
         functools.partial(conv_kernel, parts=len(sources), finish=finish),
-        out_shape=jax.ShapeDtypeStruct((row_count, col_count, channels), jnp.bfloat16),
-        in_specs=[vmem] * (len(sources) + 3),
-        out_specs=vmem,
+        out_shape=(
+            jax.ShapeDtypeStruct((row_count, col_count, channels), jnp.bfloat16),
+            jax.ShapeDtypeStruct((2, row_count, channels), jnp.float32),
+        ),
+        in_specs=[vmem] * (len(sources) + 1),
+        out_specs=(vmem, vmem),
         scratch_shapes=[
-            pltpu.VMEM((padded, 3 * lanes), jnp.bfloat16),
+            pltpu.VMEM((padded, 3 * channels), jnp.bfloat16),
             pltpu.VMEM((24 * col_count + 16, channels), jnp.float32),
         ],
-    )(*sources, left_rim, right_rim, stacked)
+    )(*sources, weight.reshape(3, 3 * channels, channels))
+    first_col = finish(raw[0] + rim_term(left_rim, weight[:, 0]))
+    last_col = finish(raw[1] + rim_term(right_rim, weight[:, 2]))
+    main = main.at[:, 0, :].set(first_col)
+    return main.at[:, col_count - 1, :].set(last_col)
 
 
 def attend_kernel(x_ref, wqkv_ref, bias_ref, wout_ref, o_ref, qkv_s, blend_s):
@@ -168,7 +196,7 @@
     frames_all = lax.axis_size("frame")
     pix_piece = row_count * col_count // frames_all
     tile = latents.reshape(row_count, col_count, channels)
-    hidden = convolve([tile], lambda c: tile[:, c, :], conv1_weight, norm_gelu)
+    hidden = convolve([tile], tile_edges(tile), conv1_weight, norm_gelu)
     if row_count % frames_all == 0:
         piece_shape = (frames_all, row_count // frames_all, col_count, channels)
     else:
@@ -178,11 +206,10 @@
     returned = lax.all_to_all(attended.reshape(piece_shape), "frame", split_axis=0, concat_axis=0, tiled=True)
     returned = returned.reshape(row_count, col_count, channels)
 
-    def joined_edge(c):
-        summed = hidden[:, c, :].astype(jnp.float32) + returned[:, c, :].astype(jnp.float32)
-        return summed.astype(jnp.bfloat16)
-
-    second = convolve([hidden, returned], joined_edge, conv2_weight, to_bf16)
+    joined_edges = (
+        tile_edges(hidden).astype(jnp.float32) + tile_edges(returned).astype(jnp.float32)
+    ).astype(jnp.bfloat16)
+    second = convolve([hidden, returned], joined_edges, conv2_weight, to_bf16)
     return second.reshape(frames_dev, row_count, col_count, channels)
 
 

time: 109 us -> 132 us (1.21)
  local copies, waits for them, and re-layouts: 8.04 us -> 22.7 us
  Pallas kernels: 35.4 us -> 41.9 us
  matrix products: 0 us -> 4.09 us
  waiting for transfers between devices: 44.6 us -> 40.6 us
    scatter x0 -> x4, local copies, waits for them, and re-layouts: none -> 14 us  [the longest x2 7.01 us: convolve(): main = main.at[:, 0, :].set(first_col)]
    pallas_call x0 -> x3, Pallas kernels: none -> 6.65 us  [tile_edges(): pl.pallas_call(edge_kernel, out_shape=jax.ShapeDtypeStruct((2, row_count,...]
    dot_general x0 -> x4, matrix products: none -> 4.09 us  [rim_term(): jnp.dot(stacked, taps.reshape(-1, taps.shape[-1]), preferred_element_type...]
    ppermute x4, waiting for transfers between devices: 3.57 us -> 0.47 us  [shifted(): return lax.ppermute(block, axis, route)]
    unnamed x18 -> x13, local copies, waits for them, and re-layouts: 5.7 us -> 3.61 us
    slice x2 -> x6, local copies, waits for them, and re-layouts: 1.5 us -> 3.11 us  [the longest x2 2.99 us: convolve(): last_col = finish(raw[1] + rim_term(right_rim, weight[:, 2]))]
  transfers between devices with their start and end apart: 6 -> 6, of which waited for: 6 -> 3; matrix products, arithmetic and copies ran while one was open for 3% -> 6% of each run, Pallas kernels for 0% -> 22%
where the time goes in v5:
time: 132 us; the launch traced here: 131 us
  Pallas kernels  41.9 us (32%)
  waiting for transfers between devices  40.6 us (31%)
  local copies, waits for them, and re-layouts  22.7 us (17%)
  starting transfers between devices  20.1 us (15%)
  matrix products  4.09 us (3%)
    pallas_call x2, Pallas kernels, convolve(): pl.pallas_call(functools.partial(conv_kernel, parts=len(sources), finish=...  26.8 us
    all_to_all x1, waiting for transfers between devices, body(): lax.all_to_all(hidden.reshape(piece_shape), 'frame', split_axis=0, concat...  20.2 us
    all_to_all x1, waiting for transfers between devices, body(): lax.all_to_all(attended.reshape(piece_shape), 'frame', split_axis=0, conc...  19.9 us
    ppermute x4, starting transfers between devices, shifted(): return lax.ppermute(block, axis, route)  12.9 us
    pallas_call x1, Pallas kernels, attend(): pl.pallas_call(attend_kernel, out_shape=jax.ShapeDtypeStruct((frames_all,...  8.48 us
    scatter x2, local copies, waits for them, and re-layouts, convolve(): main = main.at[:, 0, :].set(first_col)  7.01 us
    scatter x2, local copies, waits for them, and re-layouts, convolve(): return main.at[:, col_count - 1, :].set(last_col)  6.98 us
    pallas_call x3, Pallas kernels, tile_edges(): pl.pallas_call(edge_kernel, out_shape=jax.ShapeDtypeStruct((2, row_count,...  6.65 us
  transfers between devices with their start and end apart: 6, of which 3 were waited for; matrix products, arithmetic and copies ran while one was open for 6% of the time, Pallas kernels for 22%

profile of v5, /device:TPU:0, one launch (start us, length us, event | category | flops | bytes accessed | tf_op | source)
XLA Modules:
  0.0 130.9 jit_solution(54604863278128450)
XLA Ops:
  0.0 2.2 %shard_map.65 = bf16[2,72,320]{2,1,0:T(8,128)(2,1)} custom-call(bf16[72,32,320]{2,1,0:T(8,128)(2,1)} %bitcast.48), custom_call_target="tpu_custom_call" | custom-call | tf_op jit(solution)/shard_map/pallas_call | solution.py:76
  2.2 0.9 slice_bitcast_fusion.2
  3.1 4.9 %collective-permute-start = (bf16[72,320]{1,0:T(8,128)(2,1)S(1)}, bf16[72,320]{1,0:T(8,128)(2,1)S(1)}, u32[]{:S(2)}, u32[]{:S(2)}) collective-permute-start(bf16[72,320]{1,0:T(8,128)(2,1)S(1)} %get-tuple-element.68), channel_id=1, source_target_pairs={{0,4},{4,8},{8,12},{1,5},{5,9},{9,13},{2,6},{6,10},{10,14},{3,7},{... | collective-permute-start | bytes 138248 | tf_op jit(solution)/shard_map/ppermute | solution.py:16
  8.0 1.3 collective-permute-start.1
  9.3 1.5 %fusion.47 = (bf16[3,1,320,320]{3,2,1,0:T(8,128)(2,1)S(1)}, bf16[3,1,320,320]{3,2,1,0:T(8,128)(2,1)S(1)}) fusion(bf16[3,3,320,320]{3,2,1,0:T(8,128)(2,1)} %param.15), kind=kLoop, calls=%fused_computation.70 | loop fusion | bytes 2457600 | tf_op jit(solution)/shard_map/slice | solution.py:121
  10.8 13.5 %shard_map.64 = (bf16[72,32,320]{2,1,0:T(8,128)(2,1)}, f32[2,72,320]{2,1,0:T(8,128)}) custom-call(bf16[72,32,320]{2,1,0:T(8,128)(2,1)} %bitcast.49, bf16[3,960,320]{2,1,0:T(8,128)(2,1)} %bitcast.51), custom_call_target="tpu_custom_call" | custom-call | tf_op jit(solution)/shard_map/pallas_call | solution.py:107
  24.4 1.3 %multiply_reduce_fusion.1 = (f32[72]{0:T(128)S(1)}, f32[72,320]{1,0:T(8,128)S(1)}) fusion(bf16[960,320]{1,0:T(8,128)(2,1)S(1)} %bitcast.56, bf16[72,320]{1,0:T(8,128)(2,1)S(1)} %get-tuple-element.76, bf16[72,320]{1,0:T(8,128)(2,1)S(1)} %collective-permute-done, bf16[72,320]{1,0:T(8,128)(2,1)S(1)} %get-tuple-element.75, f32[2,72,320]{2,1,0:T(8,128)} %get-tuple-element.58), kind=kOutput, calls=%fused_computation.48 | convolution fusion | flops 44720568 | bytes 937248 | tf_op jit(solution)/shard_map/dot_general | solution.py:98
  25.7 0.1 fusion.41
  26.0 0.4 multiply_reduce_fusion
  26.6 3.5 %scatter.14 = bf16[72,32,320]{2,1,0:T(8,128)(2,1)} dynamic-update-slice(bf16[72,32,320]{2,1,0:T(8,128)(2,1)} %get-tuple-element.57, bf16[72,1,320]{2,1,0:T(2,128)(2,1)S(1)} %copy.19, s32[]{:T(128)} %constant.114.clone.1, s32[]{:T(128)} %constant.114.clone.1, s32[]{:T(128)} %constant.114.clone.1) | dynamic-update-slice | bytes 92164 | tf_op jit(solution)/shard_map/scatter | solution.py:122
  30.1 3.5 %scatter.15.refs_0_.x_ref = bf16[72,32,320]{2,1,0:T(8,128)(2,1)} dynamic-update-slice(bf16[72,32,320]{2,1,0:T(8,128)(2,1)} %scatter.14, bf16[72,1,320]{2,1,0:T(2,128)(2,1)S(1)} %copy.20, s32[]{:T(128)} %constant.114.clone.1, s32[]{:T(128)} %constant.115.clone.1, s32[]{:T(128)} %constant.114.clone.1) | dynamic-update-slice | bytes 92164 | tf_op jit(solution)/shard_map/scatter | solution.py:123
  33.6 3.7 %all-to-all-start = ((bf16[4,18,32,320]{3,2,1,0:T(8,128)(2,1)}), bf16[4,18,32,320]{3,2,1,0:T(8,128)(2,1)S(1)}, u32[]{:S(2)}, u32[]{:S(2)}) async-start(bf16[4,18,32,320]{3,2,1,0:T(8,128)(2,1)} %bitcast.10), calls=%async_computation | async-start | bytes 3538944 | tf_op jit(solution)/shard_map/all_to_all | solution.py:204
  37.4 1.1 copy.21
  38.5 0.8 copy.23.bias_ref
  39.3 20.2 %all-to-all-done = bf16[4,18,32,320]{3,2,1,0:T(8,128)(2,1)S(1)} async-done(((bf16[4,18,32,320]{3,2,1,0:T(8,128)(2,1)}), bf16[4,18,32,320]{3,2,1,0:T(8,128)(2,1)S(1)}, u32[]{:S(2)}, u32[]{:S(2)}) %all-to-all-start) | async-done | bytes 1474592 | tf_op jit(solution)/shard_map/all_to_all | solution.py:204
  59.5 1.2 copy-done.1
  60.7 8.5 %shard_map.66 = bf16[4,576,320]{2,1,0:T(8,128)(2,1)} custom-call(bf16[4,576,320]{2,1,0:T(8,128)(2,1)} %bitcast.46, bf16[960,320]{1,0:T(8,128)(2,1)} %bitcast.52, f32[5,4,4,1]{3,2,1,0:T(4,128)} %copy.23.bias_ref, bf16[320,320]{1,0:T(8,128)(2,1)} %wout_ref.1), custom_call_target="tpu_custom_call" | custom-call | tf_op jit(solution)/shard_map/pallas_call | solution.py:182
  69.2 3.6 %all-to-all-start.1 = ((bf16[4,18,32,320]{3,2,1,0:T(8,128)(2,1)}), bf16[4,18,32,320]{3,2,1,0:T(8,128)(2,1)S(1)}, u32[]{:S(2)}, u32[]{:S(2)}) async-start(bf16[4,18,32,320]{3,2,1,0:T(8,128)(2,1)} %bitcast.47), calls=%async_computation.1 | async-start | bytes 3538944 | tf_op jit(solution)/shard_map/all_to_all | solution.py:206
  72.8 2.2 %shard_map.68 = bf16[2,72,320]{2,1,0:T(8,128)(2,1)} custom-call(bf16[72,32,320]{2,1,0:T(8,128)(2,1)} %scatter.15.refs_0_.x_ref), custom_call_target="tpu_custom_call" | custom-call | tf_op jit(solution)/shard_map/pallas_call | solution.py:76
  75.0 19.9 %all-to-all-done.1 = bf16[4,18,32,320]{3,2,1,0:T(8,128)(2,1)S(1)} async-done(((bf16[4,18,32,320]{3,2,1,0:T(8,128)(2,1)}), bf16[4,18,32,320]{3,2,1,0:T(8,128)(2,1)S(1)}, u32[]{:S(2)}, u32[]{:S(2)}) %all-to-all-start.1) | async-done | bytes 1474592 | tf_op jit(solution)/shard_map/all_to_all | solution.py:206
  94.9 1.2 copy-done
  96.2 2.2 %shard_map.69 = bf16[2,72,320]{2,1,0:T(8,128)(2,1)} custom-call(bf16[72,32,320]{2,1,0:T(8,128)(2,1)} %bitcast.44), custom_call_target="tpu_custom_call" | custom-call | tf_op jit(solution)/shard_map/pallas_call | solution.py:76
  98.4 0.9 add_convert_fusion
  99.4 1.5 %collective-permute-start.3 = (bf16[72,320]{1,0:T(8,128)(2,1)S(1)}, bf16[72,320]{1,0:T(8,128)(2,1)S(1)}, u32[]{:S(2)}, u32[]{:S(2)}) collective-permute-start(bf16[72,320]{1,0:T(8,128)(2,1)S(1)} %get-tuple-element.65), channel_id=1, source_target_pairs={{4,0},{8,4},{12,8},{5,1},{9,5},{13,9},{6,2},{10,6},{14,10},{7,3},{... | collective-permute-start | bytes 138248 | tf_op jit(solution)/shard_map/ppermute | solution.py:16
  100.8 1.5 %fusion.46 = (bf16[3,1,320,320]{3,2,1,0:T(8,128)(2,1)S(1)}, bf16[3,1,320,320]{3,2,1,0:T(8,128)(2,1)S(1)}) fusion(bf16[3,3,320,320]{3,2,1,0:T(8,128)(2,1)} %param.19), kind=kLoop, calls=%fused_computation.69 | loop fusion | bytes 2457600 | tf_op jit(solution)/shard_map/slice | solution.py:121
  102.3 13.3 %shard_map.67 = (bf16[72,32,320]{2,1,0:T(8,128)(2,1)}, f32[2,72,320]{2,1,0:T(8,128)}) custom-call(bf16[72,32,320]{2,1,0:T(8,128)(2,1)} %scatter.15.refs_0_.x_ref, bf16[72,32,320]{2,1,0:T(8,128)(2,1)} %bitcast.45, bf16[3,960,320]{2,1,0:T(8,128)(2,1)} %bitcast.50), custom_call_target="tpu_custom_call" | custom-call | tf_op jit(solution)/shard_map/pallas_call | solution.py:107
  115.6 5.2 %collective-permute-start.2 = (bf16[72,320]{1,0:T(8,128)(2,1)S(1)}, bf16[72,320]{1,0:T(8,128)(2,1)S(1)}, u32[]{:S(2)}, u32[]{:S(2)}) collective-permute-start(bf16[72,320]{1,0:T(8,128)(2,1)S(1)} %get-tuple-element.66), channel_id=1, source_target_pairs={{0,4},{4,8},{8,12},{1,5},{5,9},{9,13},{2,6},{6,10},{10,14},{3,7},{... | collective-permute-start | bytes 138248 | tf_op jit(solution)/shard_map/ppermute | solution.py:16
  120.8 1.2 fusion.2
  122.1 0.5 collective-permute-done.2
  122.6 1.2 fusion.3
  123.9 3.5 %scatter.16 = bf16[1,72,32,320]{3,2,1,0:T(8,128)(2,1)} dynamic-update-slice(bf16[1,72,32,320]{3,2,1,0:T(8,128)(2,1)} %bitcast.58, bf16[1,72,1,320]{3,2,1,0:T(2,128)(2,1)S(1)} %copy.24, s32[]{:T(128)} %constant.114.clone.1, s32[]{:T(128)} %constant.114.clone.1, s32[]{:T(128)} %constant.114.clone.1, s32[]{:T(128)} %constant.114.clone.1) | dynamic-update-slice | bytes 92164 | tf_op jit(solution)/shard_map/scatter | solution.py:122
  127.4 3.5 %scatter.19 = bf16[1,72,32,320]{3,2,1,0:T(8,128)(2,1)} dynamic-update-slice(bf16[1,72,32,320]{3,2,1,0:T(8,128)(2,1)} %scatter.16, bf16[1,72,1,320]{3,2,1,0:T(2,128)(2,1)S(1)} %copy.25, s32[]{:T(128)} %constant.114.clone.1, s32[]{:T(128)} %constant.114.clone.1, s32[]{:T(128)} %constant.115.clone.1, s32[]{:T(128)} %constant.114.clone.1) | dynamic-update-slice | bytes 92164 | tf_op jit(solution)/shard_map/scatter | solution.py:123
  (25 shorter events, 0.6 us)
Async XLA Ops:
  3.1 21.3 %collective-permute-start = (bf16[72,320]{1,0:T(8,128)(2,1)S(1)}, bf16[72,320]{1,0:T(8,128)(2,1)S(1)}, u32[]{:S(2)}, u32[]{:S(2)}) collective-permute-start(bf16[72,320]{1,0:T(8,128)(2,1)S(1)} %get-tuple-element.68), channel_id=1, source_target_pairs={{0,4},{4,8},{8,12},{1,5},{5,9},{9,13},{2,6},{6,10},{10,14},{3,7},{... | collective-permute-start | bytes 138248 | tf_op jit(solution)/shard_map/ppermute | solution.py:16
  8.0 17.9 %collective-permute-start.1 = (bf16[72,320]{1,0:T(8,128)(2,1)S(1)}, bf16[72,320]{1,0:T(8,128)(2,1)S(1)}, u32[]{:S(2)}, u32[]{:S(2)}) collective-permute-start(bf16[72,320]{1,0:T(8,128)(2,1)S(1)} %get-tuple-element.67), channel_id=1, source_target_pairs={{4,0},{8,4},{12,8},{5,1},{9,5},{13,9},{6,2},{10,6},{14,10},{7,3},{... | collective-permute-start | bytes 138248 | tf_op jit(solution)/shard_map/ppermute | solution.py:16
  24.3 1.7 %copy-start.4 = (f32[2,72,320]{2,1,0:T(8,128)S(1)}, f32[2,72,320]{2,1,0:T(8,128)}, u32[]{:S(2)}) copy-start(f32[2,72,320]{2,1,0:T(8,128)} %get-tuple-element.58) | copy-start | bytes 552964
  33.6 3.7 %copy-start.2 = (bf16[320,960]{1,0:T(8,128)(2,1)S(1)}, bf16[320,960]{1,0:T(8,128)(2,1)}, u32[]{:S(2)}) copy-start(bf16[320,960]{1,0:T(8,128)(2,1)} %param.16) | copy-start | bytes 1843204
  33.6 4.9 %copy-start.5 = (f32[5,4,4]{0,2,1:T(4,128)S(1)}, f32[5,4,4]{0,2,1:T(4,128)}, u32[]{:S(2)}) copy-start(f32[5,4,4]{0,2,1:T(4,128)} %param.18) | copy-start | bytes 964
  33.6 25.9 %all-to-all-start = ((bf16[4,18,32,320]{3,2,1,0:T(8,128)(2,1)}), bf16[4,18,32,320]{3,2,1,0:T(8,128)(2,1)S(1)}, u32[]{:S(2)}, u32[]{:S(2)}) async-start(bf16[4,18,32,320]{3,2,1,0:T(8,128)(2,1)} %bitcast.10), calls=%async_computation | async-start | bytes 3538944 | tf_op jit(solution)/shard_map/all_to_all | solution.py:204
  59.5 1.2 copy-start.1
  69.2 25.7 %all-to-all-start.1 = ((bf16[4,18,32,320]{3,2,1,0:T(8,128)(2,1)}), bf16[4,18,32,320]{3,2,1,0:T(8,128)(2,1)S(1)}, u32[]{:S(2)}, u32[]{:S(2)}) async-start(bf16[4,18,32,320]{3,2,1,0:T(8,128)(2,1)} %bitcast.47), calls=%async_computation.1 | async-start | bytes 3538944 | tf_op jit(solution)/shard_map/all_to_all | solution.py:206
  75.0 23.4 %copy-start.3 = (bf16[2,72,320]{2,1,0:T(8,128)(2,1)S(1)}, bf16[2,72,320]{2,1,0:T(8,128)(2,1)}, u32[]{:S(2)}) copy-start(bf16[2,72,320]{2,1,0:T(8,128)(2,1)} %shard_map.68) | copy-start | bytes 276484
  94.9 1.2 copy-start
  99.4 21.4 %collective-permute-start.3 = (bf16[72,320]{1,0:T(8,128)(2,1)S(1)}, bf16[72,320]{1,0:T(8,128)(2,1)S(1)}, u32[]{:S(2)}, u32[]{:S(2)}) collective-permute-start(bf16[72,320]{1,0:T(8,128)(2,1)S(1)} %get-tuple-element.65), channel_id=1, source_target_pairs={{4,0},{8,4},{12,8},{5,1},{9,5},{13,9},{6,2},{10,6},{14,10},{7,3},{... | collective-permute-start | bytes 138248 | tf_op jit(solution)/shard_map/ppermute | solution.py:16
  115.6 7.0 %collective-permute-start.2 = (bf16[72,320]{1,0:T(8,128)(2,1)S(1)}, bf16[72,320]{1,0:T(8,128)(2,1)S(1)}, u32[]{:S(2)}, u32[]{:S(2)}) collective-permute-start(bf16[72,320]{1,0:T(8,128)(2,1)S(1)} %get-tuple-element.66), channel_id=1, source_target_pairs={{0,4},{4,8},{8,12},{1,5},{5,9},{9,13},{2,6},{6,10},{10,14},{3,7},{... | collective-permute-start | bytes 138248 | tf_op jit(solution)/shard_map/ppermute | solution.py:16

commit v6 on v4

--- a/solution.py
+++ b/solution.py
@@ -16,27 +16,34 @@
     return lax.ppermute(block, axis, route)
 
 
-def conv_kernel(*refs, parts, finish):
-    sources = refs[:parts]
-    left_ref, right_ref, w_ref, o_ref, slab, shift_s = refs[parts:]
-    row_count, col_count, channels = o_ref.shape
+def conv_kernel(*refs, layout, lo, hi, finish):
+    count = sum(len(segments) for segments in layout)
+    flat = refs[:count]
+    left_ref, right_ref, w_ref, o_ref, slab, shift_s = refs[count:]
+    row_count = left_ref.shape[0]
+    _, col_count, channels = o_ref.shape
     lanes = slab.shape[1] // 3
-    band = 24
+    band = 12
     span = band * col_count
     padded_rows = slab.shape[0]
     slab[pl.ds(0, col_count)] = jnp.zeros((col_count, slab.shape[1]), jnp.bfloat16)
     slab[pl.ds(padded_rows - col_count, col_count)] = jnp.zeros((col_count, slab.shape[1]), jnp.bfloat16)
-    if lanes > channels:
-        pad = jnp.zeros((padded_rows, lanes - channels), jnp.bfloat16)
-        for b in range(3):
-            slab[:, pl.ds(b * lanes + channels, lanes - channels)] = pad
     column = lax.broadcasted_iota(jnp.int32, (band, col_count, channels), 1)
-
-    def build(i, carry):
-        r0 = i * band
-        block = sources[0][pl.ds(r0, band)].astype(jnp.float32)
-        for extra in sources[1:]:
-            block = block + extra[pl.ds(r0, band)].astype(jnp.float32)
+    addends = []
+    at = 0
+    for segments in layout:
+        addends.append(list(zip(flat[at : at + len(segments)], segments)))
+        at += len(segments)
+
+    def rows_of(ref_list, r0):
+        for ref, (first, last) in ref_list:
+            if first <= r0 < last:
+                return ref[pl.ds(r0 - first, band)]
+
+    for r0 in range(max(lo - band, 0), min(hi + band, row_count), band):
+        block = rows_of(addends[0], r0).astype(jnp.float32)
+        for extra in addends[1:]:
+            block = block + rows_of(extra, r0).astype(jnp.float32)
         block = block.astype(jnp.bfloat16)
         shift_s[pl.ds(8, span)] = block.astype(jnp.float32).reshape(span, channels)
         before = shift_s[pl.ds(7, span)].reshape(band, col_count, channels)
@@ -45,25 +52,18 @@
         rim_r = right_ref[pl.ds(r0, band)].astype(jnp.float32)[:, None, :]
         before = jnp.where(column == 0, rim_l, before)
         after = jnp.where(column == col_count - 1, rim_r, after)
-        rows = pl.ds(pl.multiple_of((r0 + 1) * col_count, col_count), span)
+        rows = pl.ds((r0 + 1) * col_count, span)
         slab[rows, pl.ds(0, channels)] = before.reshape(span, channels).astype(jnp.bfloat16)
         slab[rows, pl.ds(lanes, channels)] = block.reshape(span, channels)
         slab[rows, pl.ds(2 * lanes, channels)] = after.reshape(span, channels).astype(jnp.bfloat16)
-        return carry
-
-    lax.fori_loop(0, row_count // band, build, 0)
-
-    def compute(i, carry):
-        r0 = i * band
+
+    for r0 in range(lo, hi, band):
         acc = None
         for a in range(3):
-            rows = pl.ds(pl.multiple_of((r0 + a) * col_count, col_count), span)
+            rows = pl.ds((r0 + a) * col_count, span)
             term = jnp.dot(slab[rows, :], w_ref[a], preferred_element_type=jnp.float32)
             acc = term if acc is None else acc + term
-        o_ref[pl.ds(r0, band)] = finish(acc).reshape(band, col_count, channels)
-        return carry
-
-    lax.fori_loop(0, row_count // band, compute, 0)
+        o_ref[pl.ds(r0 - lo, band)] = finish(acc).reshape(band, col_count, channels)
 
 
 def norm_gelu(first):
@@ -75,24 +75,35 @@
     return acc.astype(jnp.bfloat16)
 
 
-def convolve(sources, edge_of, weight, finish):
-    row_count, col_count, channels = sources[0].shape
-    left_rim = shifted(edge_of(-1), "quarter", 1)
-    right_rim = shifted(edge_of(0), "quarter", -1)
+def halo(edge_of):
+    return shifted(edge_of(-1), "quarter", 1), shifted(edge_of(0), "quarter", -1)
+
+
+def convolve(groups, rims, weight, finish, lo, hi):
+    row_count, channels = rims[0].shape
+    col_count = groups[0][0].shape[1]
+    layout = []
+    for segments in groups:
+        spans = []
+        first = 0
+        for piece in segments:
+            spans.append((first, first + piece.shape[0]))
+            first += piece.shape[0]
+        layout.append(tuple(spans))
+    flat = [piece for segments in groups for piece in segments]
     vmem = pl.BlockSpec(memory_space=pltpu.VMEM)
     padded = (row_count + 2) * col_count
-    lanes = channels
-    stacked = weight.reshape(3, 3 * lanes, channels)
+    stacked = weight.reshape(3, 3 * channels, channels)
     return pl.pallas_call(
-        functools.partial(conv_kernel, parts=len(sources), finish=finish),
-        out_shape=jax.ShapeDtypeStruct((row_count, col_count, channels), jnp.bfloat16),
-        in_specs=[vmem] * (len(sources) + 3),
+        functools.partial(conv_kernel, layout=tuple(layout), lo=lo, hi=hi, finish=finish),
+        out_shape=jax.ShapeDtypeStruct((hi - lo, col_count, channels), jnp.bfloat16),
+        in_specs=[vmem] * (len(flat) + 3),
         out_specs=vmem,
         scratch_shapes=[
-            pltpu.VMEM((padded, 3 * lanes), jnp.bfloat16),
-            pltpu.VMEM((24 * col_count + 16, channels), jnp.float32),
+            pltpu.VMEM((padded, 3 * channels), jnp.bfloat16),
+            pltpu.VMEM((12 * col_count + 16, channels), jnp.float32),
         ],
-    )(*sources, left_rim, right_rim, stacked)
+    )(*flat, *rims, stacked)
 
 
 def attend_kernel(x_ref, wqkv_ref, bias_ref, wout_ref, o_ref, qkv_s, blend_s):
@@ -166,23 +177,29 @@
 def body(latents, conv1_weight, qkv_weight, out_weight, pos_bias, conv2_weight):
     frames_dev, row_count, col_count, channels = latents.shape
     frames_all = lax.axis_size("frame")
-    pix_piece = row_count * col_count // frames_all
     tile = latents.reshape(row_count, col_count, channels)
-    hidden = convolve([tile], lambda c: tile[:, c, :], conv1_weight, norm_gelu)
-    if row_count % frames_all == 0:
-        piece_shape = (frames_all, row_count // frames_all, col_count, channels)
+    rims = halo(lambda c: tile[:, c, :])
+    half = row_count // 2
+    hidden = []
+    returned = []
+    for lo in (0, half):
+        hidden.append(convolve([[tile]], rims, conv1_weight, norm_gelu, lo, lo + half))
+    pix_piece = half * col_count // frames_all
+    if half % frames_all == 0:
+        piece_shape = (frames_all, half // frames_all, col_count, channels)
     else:
         piece_shape = (frames_all, pix_piece, channels)
-    pieces = lax.all_to_all(hidden.reshape(piece_shape), "frame", split_axis=0, concat_axis=0, tiled=True)
-    attended = attend(pieces.reshape(frames_all, pix_piece, channels), qkv_weight, pos_bias, out_weight)
-    returned = lax.all_to_all(attended.reshape(piece_shape), "frame", split_axis=0, concat_axis=0, tiled=True)
-    returned = returned.reshape(row_count, col_count, channels)
+    for part in hidden:
+        pieces = lax.all_to_all(part.reshape(piece_shape), "frame", split_axis=0, concat_axis=0, tiled=True)
+        attended = attend(pieces.reshape(frames_all, pix_piece, channels), qkv_weight, pos_bias, out_weight)
+        back = lax.all_to_all(attended.reshape(piece_shape), "frame", split_axis=0, concat_axis=0, tiled=True)
+        returned.append(back.reshape(half, col_count, channels))
 
     def joined_edge(c):
-        summed = hidden[:, c, :].astype(jnp.float32) + returned[:, c, :].astype(jnp.float32)
-        return summed.astype(jnp.bfloat16)
-
-    second = convolve([hidden, returned], joined_edge, conv2_weight, to_bf16)
+        summed = [h[:, c, :].astype(jnp.float32) + r[:, c, :].astype(jnp.float32) for h, r in zip(hidden, returned)]
+        return jnp.concatenate(summed, axis=0).astype(jnp.bfloat16)
+
+    second = convolve([hidden, returned], halo(joined_edge), conv2_weight, to_bf16, 0, row_count)
     return second.reshape(frames_dev, row_count, col_count, channels)
 
 

time: 109 us -> 107 us (0.982)
  waiting for transfers between devices: 44.6 us -> 32.9 us
  starting transfers between devices: 20.3 us -> 26.3 us
  Pallas kernels: 35.4 us -> 39.5 us
    all_to_all x1 -> x2, waiting for transfers between devices: 20.2 us -> 9.53 us  [body(): lax.all_to_all(part.reshape(piece_shape), 'frame', split_axis=0, concat_a...]
    all_to_all x1 -> x2, waiting for transfers between devices: 20.8 us -> 16.9 us  [body(): lax.all_to_all(attended.reshape(piece_shape), 'frame', split_axis=0, conc...]
    all_to_all x1 -> x2, starting transfers between devices: 3.58 us -> 7.18 us  [body(): lax.all_to_all(attended.reshape(piece_shape), 'frame', split_axis=0, conc...]
    pallas_call x1 -> x2, Pallas kernels: 8.46 us -> 11.8 us  [attend(): pl.pallas_call(attend_kernel, out_shape=jax.ShapeDtypeStruct((frames_all,...]
    all_to_all x1 -> x2, starting transfers between devices: 3.71 us -> 7 us  [body(): lax.all_to_all(part.reshape(piece_shape), 'frame', split_axis=0, concat_a...]
    ppermute x4, waiting for transfers between devices: 3.57 us -> 6.53 us  [shifted(): return lax.ppermute(block, axis, route)]
    unnamed x18 -> x22, local copies, waits for them, and re-layouts: 5.7 us -> 4.5 us
    slice x2 -> x4, local copies, waits for them, and re-layouts: 1.5 us -> 2.45 us  [the longest x2 2.27 us: joined_edge(): h[:, c, :].astype(jnp.float32) + r[:, c, :].astype(jnp.float32)]
  transfers between devices with their start and end apart: 6 -> 8, of which waited for: 6 -> 8; matrix products, arithmetic and copies ran while one was open for 3% -> 4% of each run, Pallas kernels for 0% -> 18%
where the time goes in v6:
time: 107 us
  Pallas kernels  39.5 us (37%)
  waiting for transfers between devices  32.9 us (31%)
  starting transfers between devices  26.3 us (25%)
  local copies, waits for them, and re-layouts  7.79 us (7%)
    pallas_call x3, Pallas kernels, convolve(): pl.pallas_call(functools.partial(conv_kernel, layout=tuple(layout), lo=lo...  27.6 us
    all_to_all x2, waiting for transfers between devices, body(): lax.all_to_all(attended.reshape(piece_shape), 'frame', split_axis=0, conc...  16.9 us
    ppermute x4, starting transfers between devices, shifted(): return lax.ppermute(block, axis, route)  12.1 us
    pallas_call x2, Pallas kernels, attend(): pl.pallas_call(attend_kernel, out_shape=jax.ShapeDtypeStruct((frames_all,...  11.8 us
    all_to_all x2, waiting for transfers between devices, body(): lax.all_to_all(part.reshape(piece_shape), 'frame', split_axis=0, concat_a...  9.53 us
    all_to_all x2, starting transfers between devices, body(): lax.all_to_all(attended.reshape(piece_shape), 'frame', split_axis=0, conc...  7.18 us
    all_to_all x2, starting transfers between devices, body(): lax.all_to_all(part.reshape(piece_shape), 'frame', split_axis=0, concat_a...  7 us
    ppermute x4, waiting for transfers between devices, shifted(): return lax.ppermute(block, axis, route)  6.53 us
  transfers between devices with their start and end apart: 8, of which 8 were waited for; matrix products, arithmetic and copies ran while one was open for 4% of the time, Pallas kernels for 18%

profile of v6, /device:TPU:0, one launch (start us, length us, event | category | flops | bytes accessed | tf_op | source)
XLA Modules:
  0.0 106.7 jit_solution(1884388003459728544)
XLA Ops:
  0.0 2.1 %copy.57 = bf16[1,72,32,320]{3,1,2,0:T(8,128)(2,1)S(1)} copy(bf16[1,72,32,320]{3,2,1,0:T(8,128)(2,1)} %param.6) | data formatting | bytes 2949120 | tf_op args[0]
  2.1 4.9 %collective-permute-start = (bf16[72,320]{1,0:T(8,128)(2,1)S(1)}, bf16[72,320]{1,0:T(8,128)(2,1)S(1)}, u32[]{:S(2)}, u32[]{:S(2)}) collective-permute-start(bf16[72,320]{1,0:T(8,128)(2,1)S(1)} %get-tuple-element.6), channel_id=1, source_target_pairs={{0,4},{4,8},{8,12},{1,5},{5,9},{9,13},{2,6},{6,10},{10,14},{3,7},{... | collective-permute-start | bytes 138248 | tf_op jit(solution)/shard_map/ppermute | solution.py:16
  7.1 1.3 %collective-permute-start.1 = (bf16[72,320]{1,0:T(8,128)(2,1)S(1)}, bf16[72,320]{1,0:T(8,128)(2,1)S(1)}, u32[]{:S(2)}, u32[]{:S(2)}) collective-permute-start(bf16[72,320]{1,0:T(8,128)(2,1)S(1)} %get-tuple-element.5), channel_id=1, source_target_pairs={{4,0},{8,4},{12,8},{5,1},{9,5},{13,9},{6,2},{10,6},{14,10},{7,3},{... | collective-permute-start | bytes 138248 | tf_op jit(solution)/shard_map/ppermute | solution.py:16
  8.4 0.5 collective-permute-done.refs_1_
  8.8 4.3 %collective-permute-done.1.refs_2_ = bf16[72,320]{1,0:T(8,128)(2,1)S(1)} collective-permute-done((bf16[72,320]{1,0:T(8,128)(2,1)S(1)}, bf16[72,320]{1,0:T(8,128)(2,1)S(1)}, u32[]{:S(2)}, u32[]{:S(2)}) %collective-permute-start.1) | collective-permute-done | bytes 46112 | tf_op jit(solution)/shard_map/ppermute | solution.py:16
  13.1 0.0 copy-done.5
  13.1 0.6 copy-done.6
  13.7 7.8 %shard_map.65.refs_1_ = bf16[36,32,320]{2,1,0:T(8,128)(2,1)} custom-call(bf16[72,32,320]{2,1,0:T(8,128)(2,1)} %bitcast.31, bf16[72,320]{1,0:T(8,128)(2,1)} %copy-done.5, bf16[72,320]{1,0:T(8,128)(2,1)} %copy-done.6, bf16[3,960,320]{2,1,0:T(8,128)(2,1)} %bitcast.33), custom_call_target="tpu_custom_call" | custom-call | tf_op jit(solution)/shard_map/pallas_call | solution.py:97
  21.5 3.5 %all-to-all-start.2 = ((bf16[4,9,32,320]{3,2,1,0:T(8,128)(2,1)}), bf16[4,9,32,320]{3,2,1,0:T(8,128)(2,1)S(1)}, u32[]{:S(2)}, u32[]{:S(2)}) async-start(bf16[4,9,32,320]{3,2,1,0:T(8,128)(2,1)} %bitcast.35), calls=%async_computation.2 | async-start | bytes 1769472 | tf_op jit(solution)/shard_map/all_to_all | solution.py:193
  25.1 7.9 %shard_map.64.refs_0_ = bf16[36,32,320]{2,1,0:T(8,128)(2,1)} custom-call(bf16[72,32,320]{2,1,0:T(8,128)(2,1)} %bitcast.32, bf16[72,320]{1,0:T(8,128)(2,1)} %copy-done.5, bf16[72,320]{1,0:T(8,128)(2,1)} %copy-done.6, bf16[3,960,320]{2,1,0:T(8,128)(2,1)} %bitcast.34), custom_call_target="tpu_custom_call" | custom-call | tf_op jit(solution)/shard_map/pallas_call | solution.py:97
  33.0 4.8 %all-to-all-done.2 = bf16[4,9,32,320]{3,2,1,0:T(8,128)(2,1)S(1)} async-done(((bf16[4,9,32,320]{3,2,1,0:T(8,128)(2,1)}), bf16[4,9,32,320]{3,2,1,0:T(8,128)(2,1)S(1)}, u32[]{:S(2)}, u32[]{:S(2)}) %all-to-all-start.2) | async-done | bytes 737312 | tf_op jit(solution)/shard_map/all_to_all | solution.py:193
  37.7 3.5 %all-to-all-start = ((bf16[4,9,32,320]{3,2,1,0:T(8,128)(2,1)}), bf16[4,9,32,320]{3,2,1,0:T(8,128)(2,1)S(1)}, u32[]{:S(2)}, u32[]{:S(2)}) async-start(bf16[4,9,32,320]{3,2,1,0:T(8,128)(2,1)} %bitcast.36), calls=%async_computation | async-start | bytes 1769472 | tf_op jit(solution)/shard_map/all_to_all | solution.py:193
  41.2 0.0 copy-done.4
  41.2 1.2 %copy.25 = bf16[320,960]{0,1:T(8,128)(2,1)} copy(bf16[320,960]{1,0:T(8,128)(2,1)S(1)} %copy-done.4) | data formatting | bytes 1228800 | tf_op args[2]
  42.4 0.8 copy.27.bias_ref
  43.2 5.9 %shard_map.67 = bf16[4,288,320]{2,1,0:T(8,128)(2,1)} custom-call(bf16[4,288,320]{2,1,0:T(8,128)(2,1)} %bitcast.44, bf16[960,320]{1,0:T(8,128)(2,1)} %bitcast.37, f32[5,4,4,1]{3,2,1,0:T(4,128)} %copy.27.bias_ref, bf16[320,320]{1,0:T(8,128)(2,1)} %wout_ref.3), custom_call_target="tpu_custom_call" | custom-call | tf_op jit(solution)/shard_map/pallas_call | solution.py:165
  49.2 4.8 %all-to-all-done = bf16[4,9,32,320]{3,2,1,0:T(8,128)(2,1)S(1)} async-done(((bf16[4,9,32,320]{3,2,1,0:T(8,128)(2,1)}), bf16[4,9,32,320]{3,2,1,0:T(8,128)(2,1)S(1)}, u32[]{:S(2)}, u32[]{:S(2)}) %all-to-all-start) | async-done | bytes 737312 | tf_op jit(solution)/shard_map/all_to_all | solution.py:193
  53.9 3.7 %all-to-all-start.3 = ((bf16[4,9,32,320]{3,2,1,0:T(8,128)(2,1)}), bf16[4,9,32,320]{3,2,1,0:T(8,128)(2,1)S(1)}, u32[]{:S(2)}, u32[]{:S(2)}) async-start(bf16[4,9,32,320]{3,2,1,0:T(8,128)(2,1)} %bitcast.46), calls=%async_computation.3 | async-start | bytes 1769472 | tf_op jit(solution)/shard_map/all_to_all | solution.py:195
  57.6 5.9 %shard_map.66 = bf16[4,288,320]{2,1,0:T(8,128)(2,1)} custom-call(bf16[4,288,320]{2,1,0:T(8,128)(2,1)} %bitcast.45, bf16[960,320]{1,0:T(8,128)(2,1)} %bitcast.38, f32[5,4,4,1]{3,2,1,0:T(4,128)} %copy.27.bias_ref, bf16[320,320]{1,0:T(8,128)(2,1)} %wout_ref.3), custom_call_target="tpu_custom_call" | custom-call | tf_op jit(solution)/shard_map/pallas_call | solution.py:165
  63.5 6.6 %all-to-all-done.3 = bf16[4,9,32,320]{3,2,1,0:T(8,128)(2,1)S(1)} async-done(((bf16[4,9,32,320]{3,2,1,0:T(8,128)(2,1)}), bf16[4,9,32,320]{3,2,1,0:T(8,128)(2,1)S(1)}, u32[]{:S(2)}, u32[]{:S(2)}) %all-to-all-start.3) | async-done | bytes 737312 | tf_op jit(solution)/shard_map/all_to_all | solution.py:195
  70.1 3.5 %all-to-all-start.1 = ((bf16[4,9,32,320]{3,2,1,0:T(8,128)(2,1)}), bf16[4,9,32,320]{3,2,1,0:T(8,128)(2,1)S(1)}, u32[]{:S(2)}, u32[]{:S(2)}) async-start(bf16[4,9,32,320]{3,2,1,0:T(8,128)(2,1)} %bitcast.43), calls=%async_computation.1 | async-start | bytes 1769472 | tf_op jit(solution)/shard_map/all_to_all | solution.py:195
  73.6 1.1 %fusion.6 = (bf16[36,1,320]{2,1,0:T(2,128)(2,1)S(1)}, bf16[36,1,320]{2,1,0:T(2,128)(2,1)S(1)}) fusion(bf16[36,32,320]{2,1,0:T(8,128)(2,1)} %shard_map.65.refs_1_), kind=kLoop, calls=%fused_computation.15 | loop fusion | bytes 92160 | tf_op jit(solution)/shard_map/slice | solution.py:199
  74.7 1.1 %fusion.4 = (bf16[36,1,320]{2,1,0:T(2,128)(2,1)S(1)}, bf16[36,1,320]{2,1,0:T(2,128)(2,1)S(1)}) fusion(bf16[36,32,320]{2,1,0:T(8,128)(2,1)} %shard_map.64.refs_0_), kind=kLoop, calls=%fused_computation.13 | loop fusion | bytes 92160 | tf_op jit(solution)/shard_map/slice | solution.py:199
  75.9 0.1 fusion.7
  76.0 10.3 %all-to-all-done.1 = bf16[4,9,32,320]{3,2,1,0:T(8,128)(2,1)S(1)} async-done(((bf16[4,9,32,320]{3,2,1,0:T(8,128)(2,1)}), bf16[4,9,32,320]{3,2,1,0:T(8,128)(2,1)S(1)}, u32[]{:S(2)}, u32[]{:S(2)}) %all-to-all-start.1) | async-done | bytes 737312 | tf_op jit(solution)/shard_map/all_to_all | solution.py:195
  86.3 0.1 fusion.5
  86.4 1.3 %collective-permute-start.3 = (bf16[72,320]{1,0:T(8,128)(2,1)S(1)}, bf16[72,320]{1,0:T(8,128)(2,1)S(1)}, u32[]{:S(2)}, u32[]{:S(2)}) collective-permute-start(bf16[72,320]{1,0:T(8,128)(2,1)S(1)} %pad_maximum_fusion.1), channel_id=1, source_target_pairs={{4,0},{8,4},{12,8},{5,1},{9,5},{13,9},{6,2},{10,6},{14,10},{7,3},{... | collective-permute-start | bytes 138248 | tf_op jit(solution)/shard_map/ppermute | solution.py:16
  87.8 4.5 %collective-permute-start.2 = (bf16[72,320]{1,0:T(8,128)(2,1)S(1)}, bf16[72,320]{1,0:T(8,128)(2,1)S(1)}, u32[]{:S(2)}, u32[]{:S(2)}) collective-permute-start(bf16[72,320]{1,0:T(8,128)(2,1)S(1)} %pad_maximum_fusion), channel_id=1, source_target_pairs={{0,4},{4,8},{8,12},{1,5},{5,9},{9,13},{2,6},{6,10},{10,14},{3,7},{... | collective-permute-start | bytes 138248 | tf_op jit(solution)/shard_map/ppermute | solution.py:16
  92.3 0.1 collective-permute-done.3.refs_5_
  92.5 1.6 %collective-permute-done.2.refs_4_ = bf16[72,320]{1,0:T(8,128)(2,1)S(1)} collective-permute-done((bf16[72,320]{1,0:T(8,128)(2,1)S(1)}, bf16[72,320]{1,0:T(8,128)(2,1)S(1)}, u32[]{:S(2)}, u32[]{:S(2)}) %collective-permute-start.2) | collective-permute-done | bytes 46112 | tf_op jit(solution)/shard_map/ppermute | solution.py:16
  94.1 0.6 copy-done.8
  94.7 11.9 %shard_map.68 = bf16[72,32,320]{2,1,0:T(8,128)(2,1)} custom-call(bf16[36,32,320]{2,1,0:T(8,128)(2,1)} %shard_map.64.refs_0_, bf16[36,32,320]{2,1,0:T(8,128)(2,1)} %shard_map.65.refs_1_, bf16[36,32,320]{2,1,0:T(8,128)(2,1)} %bitcast.42, bf16[36,32,320]{2,1,0:T(8,128)(2,1)} %bitcast.40, bf16[72,320]{1,0:T(8,128)(2,1)} %copy-done.8, bf16[72,320]{1,0:T(8,128)(2,1)} %copy-done.7, ...), custom_call_target="tpu_custom_call" | custom-call | tf_op jit(solution)/shard_map/pallas_call | solution.py:97
  (21 shorter events, 0.1 us)
Async XLA Ops:
  2.1 6.7 %collective-permute-start = (bf16[72,320]{1,0:T(8,128)(2,1)S(1)}, bf16[72,320]{1,0:T(8,128)(2,1)S(1)}, u32[]{:S(2)}, u32[]{:S(2)}) collective-permute-start(bf16[72,320]{1,0:T(8,128)(2,1)S(1)} %get-tuple-element.6), channel_id=1, source_target_pairs={{0,4},{4,8},{8,12},{1,5},{5,9},{9,13},{2,6},{6,10},{10,14},{3,7},{... | collective-permute-start | bytes 138248 | tf_op jit(solution)/shard_map/ppermute | solution.py:16
  7.1 6.0 %collective-permute-start.1 = (bf16[72,320]{1,0:T(8,128)(2,1)S(1)}, bf16[72,320]{1,0:T(8,128)(2,1)S(1)}, u32[]{:S(2)}, u32[]{:S(2)}) collective-permute-start(bf16[72,320]{1,0:T(8,128)(2,1)S(1)} %get-tuple-element.5), channel_id=1, source_target_pairs={{4,0},{8,4},{12,8},{5,1},{9,5},{13,9},{6,2},{10,6},{14,10},{7,3},{... | collective-permute-start | bytes 138248 | tf_op jit(solution)/shard_map/ppermute | solution.py:16
  8.8 4.3 %copy-start.5 = (bf16[72,320]{1,0:T(8,128)(2,1)}, bf16[72,320]{1,0:T(8,128)(2,1)S(1)}, u32[]{:S(2)}) copy-start(bf16[72,320]{1,0:T(8,128)(2,1)S(1)} %collective-permute-done.refs_1_) | copy-start | bytes 138244
  13.1 0.6 copy-start.6
  21.5 16.2 %all-to-all-start.2 = ((bf16[4,9,32,320]{3,2,1,0:T(8,128)(2,1)}), bf16[4,9,32,320]{3,2,1,0:T(8,128)(2,1)S(1)}, u32[]{:S(2)}, u32[]{:S(2)}) async-start(bf16[4,9,32,320]{3,2,1,0:T(8,128)(2,1)} %bitcast.35), calls=%async_computation.2 | async-start | bytes 1769472 | tf_op jit(solution)/shard_map/all_to_all | solution.py:193
  32.9 8.3 %copy-start.4 = (bf16[320,960]{1,0:T(8,128)(2,1)S(1)}, bf16[320,960]{1,0:T(8,128)(2,1)}, u32[]{:S(2)}) copy-start(bf16[320,960]{1,0:T(8,128)(2,1)} %param.8) | copy-start | bytes 1843204
  32.9 9.5 %copy-start.9 = (f32[5,4,4]{0,2,1:T(4,128)S(1)}, f32[5,4,4]{0,2,1:T(4,128)}, u32[]{:S(2)}) copy-start(f32[5,4,4]{0,2,1:T(4,128)} %param.10) | copy-start | bytes 964
  37.7 5.5 %copy-start.2 = (bf16[4,9,32,320]{3,2,1,0:T(8,128)(2,1)}, bf16[4,9,32,320]{3,2,1,0:T(8,128)(2,1)S(1)}, u32[]{:S(2)}) copy-start(bf16[4,9,32,320]{3,2,1,0:T(8,128)(2,1)S(1)} %all-to-all-done.2) | copy-start | bytes 2211844
  37.7 16.2 %all-to-all-start = ((bf16[4,9,32,320]{3,2,1,0:T(8,128)(2,1)}), bf16[4,9,32,320]{3,2,1,0:T(8,128)(2,1)S(1)}, u32[]{:S(2)}, u32[]{:S(2)}) async-start(bf16[4,9,32,320]{3,2,1,0:T(8,128)(2,1)} %bitcast.36), calls=%async_computation | async-start | bytes 1769472 | tf_op jit(solution)/shard_map/all_to_all | solution.py:193
  53.9 3.7 %copy-start.3 = (bf16[4,9,32,320]{3,2,1,0:T(8,128)(2,1)}, bf16[4,9,32,320]{3,2,1,0:T(8,128)(2,1)S(1)}, u32[]{:S(2)}) copy-start(bf16[4,9,32,320]{3,2,1,0:T(8,128)(2,1)S(1)} %all-to-all-done) | copy-start | bytes 2211844
  53.9 16.2 %all-to-all-start.3 = ((bf16[4,9,32,320]{3,2,1,0:T(8,128)(2,1)}), bf16[4,9,32,320]{3,2,1,0:T(8,128)(2,1)S(1)}, u32[]{:S(2)}, u32[]{:S(2)}) async-start(bf16[4,9,32,320]{3,2,1,0:T(8,128)(2,1)} %bitcast.46), calls=%async_computation.3 | async-start | bytes 1769472 | tf_op jit(solution)/shard_map/all_to_all | solution.py:195
  70.1 24.0 %copy-start = (bf16[4,9,32,320]{3,2,1,0:T(8,128)(2,1)}, bf16[4,9,32,320]{3,2,1,0:T(8,128)(2,1)S(1)}, u32[]{:S(2)}) copy-start(bf16[4,9,32,320]{3,2,1,0:T(8,128)(2,1)S(1)} %all-to-all-done.3) | copy-start | bytes 2211844
  70.1 16.2 %all-to-all-start.1 = ((bf16[4,9,32,320]{3,2,1,0:T(8,128)(2,1)}), bf16[4,9,32,320]{3,2,1,0:T(8,128)(2,1)S(1)}, u32[]{:S(2)}, u32[]{:S(2)}) async-start(bf16[4,9,32,320]{3,2,1,0:T(8,128)(2,1)} %bitcast.43), calls=%async_computation.1 | async-start | bytes 1769472 | tf_op jit(solution)/shard_map/all_to_all | solution.py:195
  86.3 7.9 %copy-start.1 = (bf16[4,9,32,320]{3,2,1,0:T(8,128)(2,1)}, bf16[4,9,32,320]{3,2,1,0:T(8,128)(2,1)S(1)}, u32[]{:S(2)}) copy-start(bf16[4,9,32,320]{3,2,1,0:T(8,128)(2,1)S(1)} %all-to-all-done.1) | copy-start | bytes 2211844
  86.4 6.0 %collective-permute-start.3 = (bf16[72,320]{1,0:T(8,128)(2,1)S(1)}, bf16[72,320]{1,0:T(8,128)(2,1)S(1)}, u32[]{:S(2)}, u32[]{:S(2)}) collective-permute-start(bf16[72,320]{1,0:T(8,128)(2,1)S(1)} %pad_maximum_fusion.1), channel_id=1, source_target_pairs={{4,0},{8,4},{12,8},{5,1},{9,5},{13,9},{6,2},{10,6},{14,10},{7,3},{... | collective-permute-start | bytes 138248 | tf_op jit(solution)/shard_map/ppermute | solution.py:16
  87.8 6.3 %collective-permute-start.2 = (bf16[72,320]{1,0:T(8,128)(2,1)S(1)}, bf16[72,320]{1,0:T(8,128)(2,1)S(1)}, u32[]{:S(2)}, u32[]{:S(2)}) collective-permute-start(bf16[72,320]{1,0:T(8,128)(2,1)S(1)} %pad_maximum_fusion), channel_id=1, source_target_pairs={{0,4},{4,8},{8,12},{1,5},{5,9},{9,13},{2,6},{6,10},{10,14},{3,7},{... | collective-permute-start | bytes 138248 | tf_op jit(solution)/shard_map/ppermute | solution.py:16
  92.5 1.7 %copy-start.7 = (bf16[72,320]{1,0:T(8,128)(2,1)}, bf16[72,320]{1,0:T(8,128)(2,1)S(1)}, u32[]{:S(2)}) copy-start(bf16[72,320]{1,0:T(8,128)(2,1)S(1)} %collective-permute-done.3.refs_5_) | copy-start | bytes 138244
  94.1 0.6 copy-start.8

commit v7 on v6

--- a/solution.py
+++ b/solution.py
@@ -76,7 +76,19 @@
 
 
 def halo(edge_of):
-    return shifted(edge_of(-1), "quarter", 1), shifted(edge_of(0), "quarter", -1)
+    quarter = lax.axis_index("quarter")
+    quarters = lax.axis_size("quarter")
+    first = edge_of(0)[None]
+    last = edge_of(-1)[None]
+    slot = lax.broadcasted_iota(jnp.int32, (quarters, 1, 1), 0)
+    zero = jnp.zeros_like(first)
+    send = jnp.where(slot == quarter + 1, last, jnp.where(slot == quarter - 1, first, zero))
+    got = lax.all_to_all(send, "quarter", split_axis=0, concat_axis=0, tiled=True)
+    left = lax.dynamic_index_in_dim(got, jnp.maximum(quarter - 1, 0), keepdims=False)
+    right = lax.dynamic_index_in_dim(got, jnp.minimum(quarter + 1, quarters - 1), keepdims=False)
+    left = jnp.where(quarter > 0, left, jnp.zeros_like(left))
+    right = jnp.where(quarter < quarters - 1, right, jnp.zeros_like(right))
+    return left, right
 
 
 def convolve(groups, rims, weight, finish, lo, hi):

time: 107 us -> 115 us (1.075)
  blocking collectives: 0 us -> 10.4 us
  starting transfers between devices: 26.3 us -> 20.5 us
  other arithmetic: 0.08 us -> 5.03 us
  local copies, waits for them, and re-layouts: 7.79 us -> 3.37 us
  waiting for transfers between devices: 32.9 us -> 35.6 us
    ppermute x4 -> x0, starting transfers between devices: 12.1 us -> none  [shifted(): return lax.ppermute(block, axis, route)]
    all_to_all x0 -> x1, blocking collectives: none -> 10.4 us  [halo(): lax.all_to_all(send, 'quarter', split_axis=0, concat_axis=0, tiled=True)]
    all_to_all x0 -> x1, waiting for transfers between devices: none -> 8.04 us  [halo(): lax.all_to_all(send, 'quarter', split_axis=0, concat_axis=0, tiled=True)]
    ppermute x4 -> x0, waiting for transfers between devices: 6.53 us -> none  [shifted(): return lax.ppermute(block, axis, route)]
    all_to_all x0 -> x1, starting transfers between devices: none -> 6.32 us  [halo(): lax.all_to_all(send, 'quarter', split_axis=0, concat_axis=0, tiled=True)]
    unnamed x22 -> x18, local copies, waits for them, and re-layouts: 4.5 us -> 1.22 us
    another operation x0 -> x2, other arithmetic: none -> 2.76 us
    select_n x0 -> x4, other arithmetic: none -> 2.22 us  [the longest x2 1.32 us: halo(): right = jnp.where(quarter < quarters - 1, right, jnp.zeros_like(right))]
  transfers between devices with their start and end apart: 8 -> 5, of which waited for: 8 -> 5; matrix products, arithmetic and copies ran while one was open for 4% -> 3% of each run, Pallas kernels for 18% -> 17%
where the time goes in v7:
time: 115 us
  Pallas kernels  39.5 us (34%)
  waiting for transfers between devices  35.6 us (31%)
  starting transfers between devices  20.5 us (18%)
  blocking collectives  10.4 us (9%)
  other arithmetic  5.03 us (4%)
  local copies, waits for them, and re-layouts  3.37 us (3%)
    pallas_call x3, Pallas kernels, convolve(): pl.pallas_call(functools.partial(conv_kernel, layout=tuple(layout), lo=lo...  27.7 us
    all_to_all x2, waiting for transfers between devices, body(): lax.all_to_all(attended.reshape(piece_shape), 'frame', split_axis=0, conc...  18 us
    pallas_call x2, Pallas kernels, attend(): pl.pallas_call(attend_kernel, out_shape=jax.ShapeDtypeStruct((frames_all,...  11.8 us
    all_to_all x1, blocking collectives, halo(): lax.all_to_all(send, 'quarter', split_axis=0, concat_axis=0, tiled=True)  10.4 us
    all_to_all x2, waiting for transfers between devices, body(): lax.all_to_all(part.reshape(piece_shape), 'frame', split_axis=0, concat_a...  9.55 us
    all_to_all x1, waiting for transfers between devices, halo(): lax.all_to_all(send, 'quarter', split_axis=0, concat_axis=0, tiled=True)  8.04 us
    all_to_all x2, starting transfers between devices, body(): lax.all_to_all(attended.reshape(piece_shape), 'frame', split_axis=0, conc...  7.18 us
    all_to_all x2, starting transfers between devices, body(): lax.all_to_all(part.reshape(piece_shape), 'frame', split_axis=0, concat_a...  7 us
  transfers between devices with their start and end apart: 5, of which 5 were waited for; matrix products, arithmetic and copies ran while one was open for 3% of the time, Pallas kernels for 17%

profile of v7, /device:TPU:0, one launch (start us, length us, event | category | flops | bytes accessed | tf_op | source)
XLA Modules:
  0.0 114.5 jit_solution(2587954805147654509)
XLA Ops:
  0.0 1.3 %fusion.8 = (bf16[72,1,320]{2,1,0:T(2,128)(2,1)S(1)}, bf16[72,1,320]{2,1,0:T(2,128)(2,1)S(1)}) fusion(bf16[72,32,320]{2,1,0:T(8,128)(2,1)} %bitcast.44), kind=kLoop, calls=%fused_computation.32 | loop fusion | bytes 184320 | tf_op jit(solution)/shard_map/slice | solution.py:193
  1.4 0.8 select_select_fusion.1
  2.2 6.3 %all-to-all-start = ((bf16[4,72,320]{2,1,0:T(8,128)(2,1)}), bf16[4,72,320]{2,1,0:T(8,128)(2,1)S(1)}, u32[]{:S(2)}, u32[]{:S(2)}) async-start(bf16[4,72,320]{2,1,0:T(8,128)(2,1)} %select_select_fusion.1), calls=%async_computation | async-start | bytes 442368 | tf_op jit(solution)/shard_map/all_to_all | solution.py:86
  8.5 8.0 %all-to-all-done = bf16[4,72,320]{2,1,0:T(8,128)(2,1)S(1)} async-done(((bf16[4,72,320]{2,1,0:T(8,128)(2,1)}), bf16[4,72,320]{2,1,0:T(8,128)(2,1)S(1)}, u32[]{:S(2)}, u32[]{:S(2)}) %all-to-all-start) | async-done | bytes 184352 | tf_op jit(solution)/shard_map/all_to_all | solution.py:86
  16.5 0.7 select_bitcast_fusion.2
  17.2 7.8 %shard_map.65.refs_1_ = bf16[36,32,320]{2,1,0:T(8,128)(2,1)} custom-call(bf16[72,32,320]{2,1,0:T(8,128)(2,1)} %bitcast.45, bf16[72,320]{1,0:T(8,128)(2,1)} %get-tuple-element.14.refs_1_, bf16[72,320]{1,0:T(8,128)(2,1)} %get-tuple-element.13.refs_2_, bf16[3,960,320]{2,1,0:T(8,128)(2,1)} %bitcast.40), custom_call_target="tpu_custom_call" | custom-call | tf_op jit(solution)/shard_map/pallas_call | solution.py:109
  25.0 3.5 %all-to-all-start.3 = ((bf16[4,9,32,320]{3,2,1,0:T(8,128)(2,1)}), bf16[4,9,32,320]{3,2,1,0:T(8,128)(2,1)S(1)}, u32[]{:S(2)}, u32[]{:S(2)}) async-start(bf16[4,9,32,320]{3,2,1,0:T(8,128)(2,1)} %bitcast.42), calls=%async_computation.3 | async-start | bytes 1769472 | tf_op jit(solution)/shard_map/all_to_all | solution.py:205
  28.5 7.9 %shard_map.64.refs_0_ = bf16[36,32,320]{2,1,0:T(8,128)(2,1)} custom-call(bf16[72,32,320]{2,1,0:T(8,128)(2,1)} %bitcast.46, bf16[72,320]{1,0:T(8,128)(2,1)} %get-tuple-element.14.refs_1_, bf16[72,320]{1,0:T(8,128)(2,1)} %get-tuple-element.13.refs_2_, bf16[3,960,320]{2,1,0:T(8,128)(2,1)} %bitcast.41), custom_call_target="tpu_custom_call" | custom-call | tf_op jit(solution)/shard_map/pallas_call | solution.py:109
  36.4 0.0 copy-start.5
  36.4 4.8 %all-to-all-done.3 = bf16[4,9,32,320]{3,2,1,0:T(8,128)(2,1)S(1)} async-done(((bf16[4,9,32,320]{3,2,1,0:T(8,128)(2,1)}), bf16[4,9,32,320]{3,2,1,0:T(8,128)(2,1)S(1)}, u32[]{:S(2)}, u32[]{:S(2)}) %all-to-all-start.3) | async-done | bytes 737312 | tf_op jit(solution)/shard_map/all_to_all | solution.py:205
  41.2 3.5 %all-to-all-start.1 = ((bf16[4,9,32,320]{3,2,1,0:T(8,128)(2,1)}), bf16[4,9,32,320]{3,2,1,0:T(8,128)(2,1)S(1)}, u32[]{:S(2)}, u32[]{:S(2)}) async-start(bf16[4,9,32,320]{3,2,1,0:T(8,128)(2,1)} %bitcast.43), calls=%async_computation.1 | async-start | bytes 1769472 | tf_op jit(solution)/shard_map/all_to_all | solution.py:205
  44.7 0.0 copy-done.5
  44.7 0.8 copy.29.bias_ref
  45.5 0.0 copy-done.4
  45.5 1.1 %copy.27 = bf16[320,960]{0,1:T(8,128)(2,1)} copy(bf16[320,960]{1,0:T(8,128)(2,1)S(1)} %copy-done.4) | data formatting | bytes 1228800 | tf_op args[2]
  46.7 0.0 copy-done.2
  46.7 5.9 %shard_map.67 = bf16[4,288,320]{2,1,0:T(8,128)(2,1)} custom-call(bf16[4,288,320]{2,1,0:T(8,128)(2,1)} %bitcast.54, bf16[960,320]{1,0:T(8,128)(2,1)} %bitcast.47, f32[5,4,4,1]{3,2,1,0:T(4,128)} %copy.29.bias_ref, bf16[320,320]{1,0:T(8,128)(2,1)} %wout_ref.3), custom_call_target="tpu_custom_call" | custom-call | tf_op jit(solution)/shard_map/pallas_call | solution.py:177
  52.6 4.8 %all-to-all-done.1 = bf16[4,9,32,320]{3,2,1,0:T(8,128)(2,1)S(1)} async-done(((bf16[4,9,32,320]{3,2,1,0:T(8,128)(2,1)}), bf16[4,9,32,320]{3,2,1,0:T(8,128)(2,1)S(1)}, u32[]{:S(2)}, u32[]{:S(2)}) %all-to-all-start.1) | async-done | bytes 737312 | tf_op jit(solution)/shard_map/all_to_all | solution.py:205
  57.4 3.7 %all-to-all-start.4 = ((bf16[4,9,32,320]{3,2,1,0:T(8,128)(2,1)}), bf16[4,9,32,320]{3,2,1,0:T(8,128)(2,1)S(1)}, u32[]{:S(2)}, u32[]{:S(2)}) async-start(bf16[4,9,32,320]{3,2,1,0:T(8,128)(2,1)} %bitcast.56), calls=%async_computation.4 | async-start | bytes 1769472 | tf_op jit(solution)/shard_map/all_to_all | solution.py:207
  61.1 0.0 copy-done.3
  61.1 5.9 %shard_map.66 = bf16[4,288,320]{2,1,0:T(8,128)(2,1)} custom-call(bf16[4,288,320]{2,1,0:T(8,128)(2,1)} %bitcast.55, bf16[960,320]{1,0:T(8,128)(2,1)} %bitcast.48, f32[5,4,4,1]{3,2,1,0:T(4,128)} %copy.29.bias_ref, bf16[320,320]{1,0:T(8,128)(2,1)} %wout_ref.3), custom_call_target="tpu_custom_call" | custom-call | tf_op jit(solution)/shard_map/pallas_call | solution.py:177
  67.0 6.6 %all-to-all-done.4 = bf16[4,9,32,320]{3,2,1,0:T(8,128)(2,1)S(1)} async-done(((bf16[4,9,32,320]{3,2,1,0:T(8,128)(2,1)}), bf16[4,9,32,320]{3,2,1,0:T(8,128)(2,1)S(1)}, u32[]{:S(2)}, u32[]{:S(2)}) %all-to-all-start.4) | async-done | bytes 737312 | tf_op jit(solution)/shard_map/all_to_all | solution.py:207
  73.6 3.5 %all-to-all-start.2 = ((bf16[4,9,32,320]{3,2,1,0:T(8,128)(2,1)}), bf16[4,9,32,320]{3,2,1,0:T(8,128)(2,1)S(1)}, u32[]{:S(2)}, u32[]{:S(2)}) async-start(bf16[4,9,32,320]{3,2,1,0:T(8,128)(2,1)} %bitcast.53), calls=%async_computation.2 | async-start | bytes 1769472 | tf_op jit(solution)/shard_map/all_to_all | solution.py:207
  77.1 1.2 %fusion.5 = (bf16[36,1,320]{2,1,0:T(2,128)(2,1)S(1)}, bf16[36,1,320]{2,1,0:T(2,128)(2,1)S(1)}) fusion(bf16[36,32,320]{2,1,0:T(8,128)(2,1)S(1)} %bitcast.49, bf16[36,32,320]{2,1,0:T(8,128)(2,1)} %shard_map.65.refs_1_), kind=kLoop, calls=%fused_computation.12 | loop fusion | flops 92160 | bytes 138240 | tf_op jit(solution)/shard_map/convert.6
  78.3 11.4 %all-to-all-done.2 = bf16[4,9,32,320]{3,2,1,0:T(8,128)(2,1)S(1)} async-done(((bf16[4,9,32,320]{3,2,1,0:T(8,128)(2,1)}), bf16[4,9,32,320]{3,2,1,0:T(8,128)(2,1)S(1)}, u32[]{:S(2)}, u32[]{:S(2)}) %all-to-all-start.2) | async-done | bytes 737312 | tf_op jit(solution)/shard_map/all_to_all | solution.py:207
  89.8 1.5 %fusion.7 = (bf16[36,1,320]{2,1,0:T(2,128)(2,1)S(1)}, bf16[36,1,320]{2,1,0:T(2,128)(2,1)S(1)}) fusion(bf16[36,32,320]{2,1,0:T(8,128)(2,1)S(1)} %bitcast.51, bf16[36,32,320]{2,1,0:T(8,128)(2,1)} %shard_map.64.refs_0_), kind=kLoop, calls=%fused_computation.16 | loop fusion | flops 92160 | bytes 138240 | tf_op jit(solution)/shard_map/convert.7
  91.4 0.1 select_select_fusion
  91.5 10.4 %all_to_all.30 = bf16[4,72,320]{2,1,0:T(8,128)(2,1)S(1)} all-to-all(bf16[4,72,320]{2,1,0:T(8,128)(2,1)S(1)} %select_select_fusion), channel_id=1, replica_groups=mesh['groups'=2,'quarter'=4,'frame'=4] {'quarter'}, dimensions={0} | all-to-all | bytes 368640 | tf_op jit(solution)/shard_map/all_to_all | solution.py:86
  101.9 0.0 copy-done
  101.9 0.7 select_bitcast_fusion
  102.6 0.0 copy-done.1
  102.6 11.9 %shard_map.68 = bf16[72,32,320]{2,1,0:T(8,128)(2,1)} custom-call(bf16[36,32,320]{2,1,0:T(8,128)(2,1)} %shard_map.64.refs_0_, bf16[36,32,320]{2,1,0:T(8,128)(2,1)} %shard_map.65.refs_1_, bf16[36,32,320]{2,1,0:T(8,128)(2,1)} %bitcast.52, bf16[36,32,320]{2,1,0:T(8,128)(2,1)} %bitcast.50, bf16[72,320]{1,0:T(8,128)(2,1)} %get-tuple-element.12.refs_4_, ...), custom_call_target="tpu_custom_call" | custom-call | tf_op jit(solution)/shard_map/pallas_call | solution.py:109
  (13 shorter events, 0.1 us)
Async XLA Ops:
  2.2 14.4 %all-to-all-start = ((bf16[4,72,320]{2,1,0:T(8,128)(2,1)}), bf16[4,72,320]{2,1,0:T(8,128)(2,1)S(1)}, u32[]{:S(2)}, u32[]{:S(2)}) async-start(bf16[4,72,320]{2,1,0:T(8,128)(2,1)} %select_select_fusion.1), calls=%async_computation | async-start | bytes 442368 | tf_op jit(solution)/shard_map/all_to_all | solution.py:86
  25.0 16.2 %all-to-all-start.3 = ((bf16[4,9,32,320]{3,2,1,0:T(8,128)(2,1)}), bf16[4,9,32,320]{3,2,1,0:T(8,128)(2,1)S(1)}, u32[]{:S(2)}, u32[]{:S(2)}) async-start(bf16[4,9,32,320]{3,2,1,0:T(8,128)(2,1)} %bitcast.42), calls=%async_computation.3 | async-start | bytes 1769472 | tf_op jit(solution)/shard_map/all_to_all | solution.py:205
  36.4 8.3 %copy-start.5 = (f32[5,4,4]{0,2,1:T(4,128)S(1)}, f32[5,4,4]{0,2,1:T(4,128)}, u32[]{:S(2)}) copy-start(f32[5,4,4]{0,2,1:T(4,128)} %param.10) | copy-start | bytes 964
  36.4 9.1 %copy-start.4 = (bf16[320,960]{1,0:T(8,128)(2,1)S(1)}, bf16[320,960]{1,0:T(8,128)(2,1)}, u32[]{:S(2)}) copy-start(bf16[320,960]{1,0:T(8,128)(2,1)} %param.8) | copy-start | bytes 1843204
  41.2 5.5 %copy-start.2 = (bf16[4,9,32,320]{3,2,1,0:T(8,128)(2,1)}, bf16[4,9,32,320]{3,2,1,0:T(8,128)(2,1)S(1)}, u32[]{:S(2)}) copy-start(bf16[4,9,32,320]{3,2,1,0:T(8,128)(2,1)S(1)} %all-to-all-done.3) | copy-start | bytes 2211844
  41.2 16.2 %all-to-all-start.1 = ((bf16[4,9,32,320]{3,2,1,0:T(8,128)(2,1)}), bf16[4,9,32,320]{3,2,1,0:T(8,128)(2,1)S(1)}, u32[]{:S(2)}, u32[]{:S(2)}) async-start(bf16[4,9,32,320]{3,2,1,0:T(8,128)(2,1)} %bitcast.43), calls=%async_computation.1 | async-start | bytes 1769472 | tf_op jit(solution)/shard_map/all_to_all | solution.py:205
  57.4 3.7 %copy-start.3 = (bf16[4,9,32,320]{3,2,1,0:T(8,128)(2,1)}, bf16[4,9,32,320]{3,2,1,0:T(8,128)(2,1)S(1)}, u32[]{:S(2)}) copy-start(bf16[4,9,32,320]{3,2,1,0:T(8,128)(2,1)S(1)} %all-to-all-done.1) | copy-start | bytes 2211844
  57.4 16.2 %all-to-all-start.4 = ((bf16[4,9,32,320]{3,2,1,0:T(8,128)(2,1)}), bf16[4,9,32,320]{3,2,1,0:T(8,128)(2,1)S(1)}, u32[]{:S(2)}, u32[]{:S(2)}) async-start(bf16[4,9,32,320]{3,2,1,0:T(8,128)(2,1)} %bitcast.56), calls=%async_computation.4 | async-start | bytes 1769472 | tf_op jit(solution)/shard_map/all_to_all | solution.py:207
  73.6 28.4 %copy-start = (bf16[4,9,32,320]{3,2,1,0:T(8,128)(2,1)}, bf16[4,9,32,320]{3,2,1,0:T(8,128)(2,1)S(1)}, u32[]{:S(2)}) copy-start(bf16[4,9,32,320]{3,2,1,0:T(8,128)(2,1)S(1)} %all-to-all-done.4) | copy-start | bytes 2211844
  73.6 16.2 %all-to-all-start.2 = ((bf16[4,9,32,320]{3,2,1,0:T(8,128)(2,1)}), bf16[4,9,32,320]{3,2,1,0:T(8,128)(2,1)S(1)}, u32[]{:S(2)}, u32[]{:S(2)}) async-start(bf16[4,9,32,320]{3,2,1,0:T(8,128)(2,1)} %bitcast.53), calls=%async_computation.2 | async-start | bytes 1769472 | tf_op jit(solution)/shard_map/all_to_all | solution.py:207
  89.7 12.9 %copy-start.1 = (bf16[4,9,32,320]{3,2,1,0:T(8,128)(2,1)}, bf16[4,9,32,320]{3,2,1,0:T(8,128)(2,1)S(1)}, u32[]{:S(2)}) copy-start(bf16[4,9,32,320]{3,2,1,0:T(8,128)(2,1)S(1)} %all-to-all-done.2) | copy-start | bytes 2211844

commit v8 on v6

--- a/solution.py
+++ b/solution.py
@@ -11,9 +11,12 @@
 
 
 def shifted(block, axis, distance):
-    devices = range(lax.axis_size(axis))
-    route = [(i - distance, i) for i in devices if i - distance in devices]
-    return lax.ppermute(block, axis, route)
+    size = lax.axis_size(axis)
+    route = [((i - distance) % size, i) for i in range(size)]
+    moved = lax.ppermute(block, axis, route)
+    source = lax.axis_index(axis) - distance
+    inside = (source >= 0) & (source < size)
+    return jnp.where(inside, moved, jnp.zeros_like(moved))
 
 
 def conv_kernel(*refs, layout, lo, hi, finish):

time: 107 us -> 106 us (level)
  starting transfers between devices: 26.3 us -> 21.4 us
  waiting for transfers between devices: 32.9 us -> 35.7 us
  other arithmetic: 0.08 us -> 2.58 us
  local copies, waits for them, and re-layouts: 7.79 us -> 6.54 us
    ppermute x4, starting transfers between devices: 12.1 us -> 7.24 us  [shifted(): moved = lax.ppermute(block, axis, route)]
    ppermute x4, waiting for transfers between devices: 6.53 us -> 9.3 us  [shifted(): moved = lax.ppermute(block, axis, route)]
    select_n x0 -> x4, other arithmetic: none -> 2.51 us  [shifted(): return jnp.where(inside, moved, jnp.zeros_like(moved))]
    unnamed x22 -> x14, local copies, waits for them, and re-layouts: 4.5 us -> 3.26 us
  transfers between devices with their start and end apart: 8 -> 8, of which waited for: 8 -> 8; matrix products, arithmetic and copies ran while one was open for 4% -> 5% of each run, Pallas kernels for 18% -> 19%
where the time goes in v8:
time: 106 us
  Pallas kernels  39.5 us (37%)
  waiting for transfers between devices  35.7 us (34%)
  starting transfers between devices  21.4 us (20%)
  local copies, waits for them, and re-layouts  6.54 us (6%)
  other arithmetic  2.58 us (2%)
    pallas_call x3, Pallas kernels, convolve(): pl.pallas_call(functools.partial(conv_kernel, layout=tuple(layout), lo=lo...  27.7 us
    all_to_all x2, waiting for transfers between devices, body(): lax.all_to_all(attended.reshape(piece_shape), 'frame', split_axis=0, conc...  16.9 us
    pallas_call x2, Pallas kernels, attend(): pl.pallas_call(attend_kernel, out_shape=jax.ShapeDtypeStruct((frames_all,...  11.8 us
    all_to_all x2, waiting for transfers between devices, body(): lax.all_to_all(part.reshape(piece_shape), 'frame', split_axis=0, concat_a...  9.55 us
    ppermute x4, waiting for transfers between devices, shifted(): moved = lax.ppermute(block, axis, route)  9.3 us
    ppermute x4, starting transfers between devices, shifted(): moved = lax.ppermute(block, axis, route)  7.24 us
    all_to_all x2, starting transfers between devices, body(): lax.all_to_all(attended.reshape(piece_shape), 'frame', split_axis=0, conc...  7.18 us
    all_to_all x2, starting transfers between devices, body(): lax.all_to_all(part.reshape(piece_shape), 'frame', split_axis=0, concat_a...  7 us
  transfers between devices with their start and end apart: 8, of which 8 were waited for; matrix products, arithmetic and copies ran while one was open for 5% of the time, Pallas kernels for 19%

profile of v8, /device:TPU:0, one launch (start us, length us, event | category | flops | bytes accessed | tf_op | source)
XLA Modules:
  0.0 105.9 jit_solution(12832566262594237149)
XLA Ops:
  0.0 2.1 %copy.57 = bf16[1,72,32,320]{3,1,2,0:T(8,128)(2,1)S(1)} copy(bf16[1,72,32,320]{3,2,1,0:T(8,128)(2,1)} %param.6) | data formatting | bytes 2949120 | tf_op args[0]
  2.1 5.1 %collective-permute-start.1 = (bf16[72,320]{1,0:T(8,128)(2,1)S(1)}, bf16[72,320]{1,0:T(8,128)(2,1)S(1)}, u32[]{:S(2)}, u32[]{:S(2)}) collective-permute-start(bf16[72,320]{1,0:T(8,128)(2,1)S(1)} %get-tuple-element.5), channel_id=1, source_target_pairs={{4,0},{8,4},{12,8},{0,12},{5,1},{9,5},{13,9},{1,13},{6,2},{10,6},{... | collective-permute-start | bytes 138248 | tf_op jit(solution)/shard_map/ppermute | solution.py:16
  7.2 0.0 collective-permute-start
  7.2 1.8 %collective-permute-done.1 = bf16[72,320]{1,0:T(8,128)(2,1)S(1)} collective-permute-done((bf16[72,320]{1,0:T(8,128)(2,1)S(1)}, bf16[72,320]{1,0:T(8,128)(2,1)S(1)}, u32[]{:S(2)}, u32[]{:S(2)}) %collective-permute-start.1) | collective-permute-done | bytes 46112 | tf_op jit(solution)/shard_map/ppermute | solution.py:16
  9.0 0.6 broadcast_select_fusion.1.refs_2_
  9.7 3.5 %collective-permute-done = bf16[72,320]{1,0:T(8,128)(2,1)S(1)} collective-permute-done((bf16[72,320]{1,0:T(8,128)(2,1)S(1)}, bf16[72,320]{1,0:T(8,128)(2,1)S(1)}, u32[]{:S(2)}, u32[]{:S(2)}) %collective-permute-start) | collective-permute-done | bytes 46112 | tf_op jit(solution)/shard_map/ppermute | solution.py:16
  13.2 0.6 broadcast_select_fusion.3.refs_1_
  13.8 7.8 %shard_map.65.refs_1_ = bf16[36,32,320]{2,1,0:T(8,128)(2,1)} custom-call(bf16[72,32,320]{2,1,0:T(8,128)(2,1)} %bitcast.31, bf16[72,320]{1,0:T(8,128)(2,1)} %broadcast_select_fusion.3.refs_1_, bf16[72,320]{1,0:T(8,128)(2,1)} %broadcast_select_fusion.1.refs_2_, bf16[3,960,320]{2,1,0:T(8,128)(2,1)} %bitcast.33), custom_call_target="tpu_custom_call" | custom-call | tf_op jit(solution)/shard_map/pallas_call | solution.py:100
  21.6 3.5 %all-to-all-start.2 = ((bf16[4,9,32,320]{3,2,1,0:T(8,128)(2,1)}), bf16[4,9,32,320]{3,2,1,0:T(8,128)(2,1)S(1)}, u32[]{:S(2)}, u32[]{:S(2)}) async-start(bf16[4,9,32,320]{3,2,1,0:T(8,128)(2,1)} %bitcast.35), calls=%async_computation.2 | async-start | bytes 1769472 | tf_op jit(solution)/shard_map/all_to_all | solution.py:196
  25.1 7.9 %shard_map.64.refs_0_ = bf16[36,32,320]{2,1,0:T(8,128)(2,1)} custom-call(bf16[72,32,320]{2,1,0:T(8,128)(2,1)} %bitcast.32, bf16[72,320]{1,0:T(8,128)(2,1)} %broadcast_select_fusion.3.refs_1_, bf16[72,320]{1,0:T(8,128)(2,1)} %broadcast_select_fusion.1.refs_2_, bf16[3,960,320]{2,1,0:T(8,128)(2,1)} %bitcast.34), custom_call_target="tpu_custom_call" | custom-call | tf_op jit(solution)/shard_map/pallas_call | solution.py:100
  33.0 4.8 %all-to-all-done.2 = bf16[4,9,32,320]{3,2,1,0:T(8,128)(2,1)S(1)} async-done(((bf16[4,9,32,320]{3,2,1,0:T(8,128)(2,1)}), bf16[4,9,32,320]{3,2,1,0:T(8,128)(2,1)S(1)}, u32[]{:S(2)}, u32[]{:S(2)}) %all-to-all-start.2) | async-done | bytes 737312 | tf_op jit(solution)/shard_map/all_to_all | solution.py:196
  37.8 3.5 %all-to-all-start = ((bf16[4,9,32,320]{3,2,1,0:T(8,128)(2,1)}), bf16[4,9,32,320]{3,2,1,0:T(8,128)(2,1)S(1)}, u32[]{:S(2)}, u32[]{:S(2)}) async-start(bf16[4,9,32,320]{3,2,1,0:T(8,128)(2,1)} %bitcast.36), calls=%async_computation | async-start | bytes 1769472 | tf_op jit(solution)/shard_map/all_to_all | solution.py:196
  41.3 1.1 %copy.25 = bf16[320,960]{0,1:T(8,128)(2,1)} copy(bf16[320,960]{1,0:T(8,128)(2,1)S(1)} %copy-done.4) | data formatting | bytes 1228800 | tf_op args[2]
  42.5 0.8 copy.27.bias_ref
  43.3 5.9 %shard_map.67 = bf16[4,288,320]{2,1,0:T(8,128)(2,1)} custom-call(bf16[4,288,320]{2,1,0:T(8,128)(2,1)} %bitcast.44, bf16[960,320]{1,0:T(8,128)(2,1)} %bitcast.37, f32[5,4,4,1]{3,2,1,0:T(4,128)} %copy.27.bias_ref, bf16[320,320]{1,0:T(8,128)(2,1)} %wout_ref.3), custom_call_target="tpu_custom_call" | custom-call | tf_op jit(solution)/shard_map/pallas_call | solution.py:168
  49.2 4.8 %all-to-all-done = bf16[4,9,32,320]{3,2,1,0:T(8,128)(2,1)S(1)} async-done(((bf16[4,9,32,320]{3,2,1,0:T(8,128)(2,1)}), bf16[4,9,32,320]{3,2,1,0:T(8,128)(2,1)S(1)}, u32[]{:S(2)}, u32[]{:S(2)}) %all-to-all-start) | async-done | bytes 737312 | tf_op jit(solution)/shard_map/all_to_all | solution.py:196
  54.0 3.7 %all-to-all-start.3 = ((bf16[4,9,32,320]{3,2,1,0:T(8,128)(2,1)}), bf16[4,9,32,320]{3,2,1,0:T(8,128)(2,1)S(1)}, u32[]{:S(2)}, u32[]{:S(2)}) async-start(bf16[4,9,32,320]{3,2,1,0:T(8,128)(2,1)} %bitcast.46), calls=%async_computation.3 | async-start | bytes 1769472 | tf_op jit(solution)/shard_map/all_to_all | solution.py:198
  57.7 5.9 %shard_map.66 = bf16[4,288,320]{2,1,0:T(8,128)(2,1)} custom-call(bf16[4,288,320]{2,1,0:T(8,128)(2,1)} %bitcast.45, bf16[960,320]{1,0:T(8,128)(2,1)} %bitcast.38, f32[5,4,4,1]{3,2,1,0:T(4,128)} %copy.27.bias_ref, bf16[320,320]{1,0:T(8,128)(2,1)} %wout_ref.3), custom_call_target="tpu_custom_call" | custom-call | tf_op jit(solution)/shard_map/pallas_call | solution.py:168
  63.6 6.6 %all-to-all-done.3 = bf16[4,9,32,320]{3,2,1,0:T(8,128)(2,1)S(1)} async-done(((bf16[4,9,32,320]{3,2,1,0:T(8,128)(2,1)}), bf16[4,9,32,320]{3,2,1,0:T(8,128)(2,1)S(1)}, u32[]{:S(2)}, u32[]{:S(2)}) %all-to-all-start.3) | async-done | bytes 737312 | tf_op jit(solution)/shard_map/all_to_all | solution.py:198
  70.2 3.5 %all-to-all-start.1 = ((bf16[4,9,32,320]{3,2,1,0:T(8,128)(2,1)}), bf16[4,9,32,320]{3,2,1,0:T(8,128)(2,1)S(1)}, u32[]{:S(2)}, u32[]{:S(2)}) async-start(bf16[4,9,32,320]{3,2,1,0:T(8,128)(2,1)} %bitcast.43), calls=%async_computation.1 | async-start | bytes 1769472 | tf_op jit(solution)/shard_map/all_to_all | solution.py:198
  73.7 1.1 %fusion.6 = (bf16[36,1,320]{2,1,0:T(2,128)(2,1)S(1)}, bf16[36,1,320]{2,1,0:T(2,128)(2,1)S(1)}) fusion(bf16[36,32,320]{2,1,0:T(8,128)(2,1)} %shard_map.65.refs_1_), kind=kLoop, calls=%fused_computation.19 | loop fusion | bytes 92160 | tf_op jit(solution)/shard_map/slice | solution.py:202
  74.8 1.1 %fusion.4 = (bf16[36,1,320]{2,1,0:T(2,128)(2,1)S(1)}, bf16[36,1,320]{2,1,0:T(2,128)(2,1)S(1)}) fusion(bf16[36,32,320]{2,1,0:T(8,128)(2,1)} %shard_map.64.refs_0_), kind=kLoop, calls=%fused_computation.17 | loop fusion | bytes 92160 | tf_op jit(solution)/shard_map/slice | solution.py:202
  76.0 0.1 fusion.7
  76.1 10.3 %all-to-all-done.1 = bf16[4,9,32,320]{3,2,1,0:T(8,128)(2,1)S(1)} async-done(((bf16[4,9,32,320]{3,2,1,0:T(8,128)(2,1)}), bf16[4,9,32,320]{3,2,1,0:T(8,128)(2,1)S(1)}, u32[]{:S(2)}, u32[]{:S(2)}) %all-to-all-start.1) | async-done | bytes 737312 | tf_op jit(solution)/shard_map/all_to_all | solution.py:198
  86.4 0.1 fusion.5
  86.5 0.7 collective-permute-start.3
  87.3 1.4 %collective-permute-start.2 = (bf16[72,320]{1,0:T(8,128)(2,1)S(1)}, bf16[72,320]{1,0:T(8,128)(2,1)S(1)}, u32[]{:S(2)}, u32[]{:S(2)}) collective-permute-start(bf16[72,320]{1,0:T(8,128)(2,1)S(1)} %pad_maximum_fusion), channel_id=1, source_target_pairs={{12,0},{0,4},{4,8},{8,12},{13,1},{1,5},{5,9},{9,13},{14,2},{2,6},{... | collective-permute-start | bytes 138248 | tf_op jit(solution)/shard_map/ppermute | solution.py:16
  88.7 2.0 %collective-permute-done.3 = bf16[72,320]{1,0:T(8,128)(2,1)S(1)} collective-permute-done((bf16[72,320]{1,0:T(8,128)(2,1)S(1)}, bf16[72,320]{1,0:T(8,128)(2,1)S(1)}, u32[]{:S(2)}, u32[]{:S(2)}) %collective-permute-start.3) | collective-permute-done | bytes 46112 | tf_op jit(solution)/shard_map/ppermute | solution.py:16
  90.7 0.6 broadcast_select_fusion.refs_5_
  91.3 1.9 %collective-permute-done.2 = bf16[72,320]{1,0:T(8,128)(2,1)S(1)} collective-permute-done((bf16[72,320]{1,0:T(8,128)(2,1)S(1)}, bf16[72,320]{1,0:T(8,128)(2,1)S(1)}, u32[]{:S(2)}, u32[]{:S(2)}) %collective-permute-start.2) | collective-permute-done | bytes 46112 | tf_op jit(solution)/shard_map/ppermute | solution.py:16
  93.3 0.6 broadcast_select_fusion.2.refs_4_
  93.9 11.9 %shard_map.68 = bf16[72,32,320]{2,1,0:T(8,128)(2,1)} custom-call(bf16[36,32,320]{2,1,0:T(8,128)(2,1)} %shard_map.64.refs_0_, bf16[36,32,320]{2,1,0:T(8,128)(2,1)} %shard_map.65.refs_1_, bf16[36,32,320]{2,1,0:T(8,128)(2,1)} %bitcast.42, bf16[36,32,320]{2,1,0:T(8,128)(2,1)} %bitcast.40, bf16[72,320]{1,0:T(8,128)(2,1)} %broadcast_select_fusion.2.refs_4_, ...), custom_call_target="tpu_custom_call" | custom-call | tf_op jit(solution)/shard_map/pallas_call | solution.py:100
  (17 shorter events, 0.1 us)
Async XLA Ops:
  2.1 6.9 %collective-permute-start.1 = (bf16[72,320]{1,0:T(8,128)(2,1)S(1)}, bf16[72,320]{1,0:T(8,128)(2,1)S(1)}, u32[]{:S(2)}, u32[]{:S(2)}) collective-permute-start(bf16[72,320]{1,0:T(8,128)(2,1)S(1)} %get-tuple-element.5), channel_id=1, source_target_pairs={{4,0},{8,4},{12,8},{0,12},{5,1},{9,5},{13,9},{1,13},{6,2},{10,6},{... | collective-permute-start | bytes 138248 | tf_op jit(solution)/shard_map/ppermute | solution.py:16
  7.2 6.0 %collective-permute-start = (bf16[72,320]{1,0:T(8,128)(2,1)S(1)}, bf16[72,320]{1,0:T(8,128)(2,1)S(1)}, u32[]{:S(2)}, u32[]{:S(2)}) collective-permute-start(bf16[72,320]{1,0:T(8,128)(2,1)S(1)} %get-tuple-element.6), channel_id=1, source_target_pairs={{12,0},{0,4},{4,8},{8,12},{13,1},{1,5},{5,9},{9,13},{14,2},{2,6},{... | collective-permute-start | bytes 138248 | tf_op jit(solution)/shard_map/ppermute | solution.py:16
  21.6 16.2 %all-to-all-start.2 = ((bf16[4,9,32,320]{3,2,1,0:T(8,128)(2,1)}), bf16[4,9,32,320]{3,2,1,0:T(8,128)(2,1)S(1)}, u32[]{:S(2)}, u32[]{:S(2)}) async-start(bf16[4,9,32,320]{3,2,1,0:T(8,128)(2,1)} %bitcast.35), calls=%async_computation.2 | async-start | bytes 1769472 | tf_op jit(solution)/shard_map/all_to_all | solution.py:196
  33.0 8.3 %copy-start.4 = (bf16[320,960]{1,0:T(8,128)(2,1)S(1)}, bf16[320,960]{1,0:T(8,128)(2,1)}, u32[]{:S(2)}) copy-start(bf16[320,960]{1,0:T(8,128)(2,1)} %param.8) | copy-start | bytes 1843204
  33.0 9.4 %copy-start.5 = (f32[5,4,4]{0,2,1:T(4,128)S(1)}, f32[5,4,4]{0,2,1:T(4,128)}, u32[]{:S(2)}) copy-start(f32[5,4,4]{0,2,1:T(4,128)} %param.10) | copy-start | bytes 964
  37.8 5.5 %copy-start.2 = (bf16[4,9,32,320]{3,2,1,0:T(8,128)(2,1)}, bf16[4,9,32,320]{3,2,1,0:T(8,128)(2,1)S(1)}, u32[]{:S(2)}) copy-start(bf16[4,9,32,320]{3,2,1,0:T(8,128)(2,1)S(1)} %all-to-all-done.2) | copy-start | bytes 2211844
  37.8 16.2 %all-to-all-start = ((bf16[4,9,32,320]{3,2,1,0:T(8,128)(2,1)}), bf16[4,9,32,320]{3,2,1,0:T(8,128)(2,1)S(1)}, u32[]{:S(2)}, u32[]{:S(2)}) async-start(bf16[4,9,32,320]{3,2,1,0:T(8,128)(2,1)} %bitcast.36), calls=%async_computation | async-start | bytes 1769472 | tf_op jit(solution)/shard_map/all_to_all | solution.py:196
  54.0 3.7 %copy-start.3 = (bf16[4,9,32,320]{3,2,1,0:T(8,128)(2,1)}, bf16[4,9,32,320]{3,2,1,0:T(8,128)(2,1)S(1)}, u32[]{:S(2)}) copy-start(bf16[4,9,32,320]{3,2,1,0:T(8,128)(2,1)S(1)} %all-to-all-done) | copy-start | bytes 2211844
  54.0 16.2 %all-to-all-start.3 = ((bf16[4,9,32,320]{3,2,1,0:T(8,128)(2,1)}), bf16[4,9,32,320]{3,2,1,0:T(8,128)(2,1)S(1)}, u32[]{:S(2)}, u32[]{:S(2)}) async-start(bf16[4,9,32,320]{3,2,1,0:T(8,128)(2,1)} %bitcast.46), calls=%async_computation.3 | async-start | bytes 1769472 | tf_op jit(solution)/shard_map/all_to_all | solution.py:198
  70.2 21.2 %copy-start = (bf16[4,9,32,320]{3,2,1,0:T(8,128)(2,1)}, bf16[4,9,32,320]{3,2,1,0:T(8,128)(2,1)S(1)}, u32[]{:S(2)}) copy-start(bf16[4,9,32,320]{3,2,1,0:T(8,128)(2,1)S(1)} %all-to-all-done.3) | copy-start | bytes 2211844
  70.2 16.2 %all-to-all-start.1 = ((bf16[4,9,32,320]{3,2,1,0:T(8,128)(2,1)}), bf16[4,9,32,320]{3,2,1,0:T(8,128)(2,1)S(1)}, u32[]{:S(2)}, u32[]{:S(2)}) async-start(bf16[4,9,32,320]{3,2,1,0:T(8,128)(2,1)} %bitcast.43), calls=%async_computation.1 | async-start | bytes 1769472 | tf_op jit(solution)/shard_map/all_to_all | solution.py:198
  86.4 7.6 %copy-start.1 = (bf16[4,9,32,320]{3,2,1,0:T(8,128)(2,1)}, bf16[4,9,32,320]{3,2,1,0:T(8,128)(2,1)S(1)}, u32[]{:S(2)}) copy-start(bf16[4,9,32,320]{3,2,1,0:T(8,128)(2,1)S(1)} %all-to-all-done.1) | copy-start | bytes 2211844
  86.5 4.2 %collective-permute-start.3 = (bf16[72,320]{1,0:T(8,128)(2,1)S(1)}, bf16[72,320]{1,0:T(8,128)(2,1)S(1)}, u32[]{:S(2)}, u32[]{:S(2)}) collective-permute-start(bf16[72,320]{1,0:T(8,128)(2,1)S(1)} %pad_maximum_fusion.1), channel_id=1, source_target_pairs={{4,0},{8,4},{12,8},{0,12},{5,1},{9,5},{13,9},{1,13},{6,2},{10,6},{... | collective-permute-start | bytes 138248 | tf_op jit(solution)/shard_map/ppermute | solution.py:16
  87.3 6.0 %collective-permute-start.2 = (bf16[72,320]{1,0:T(8,128)(2,1)S(1)}, bf16[72,320]{1,0:T(8,128)(2,1)S(1)}, u32[]{:S(2)}, u32[]{:S(2)}) collective-permute-start(bf16[72,320]{1,0:T(8,128)(2,1)S(1)} %pad_maximum_fusion), channel_id=1, source_target_pairs={{12,0},{0,4},{4,8},{8,12},{13,1},{1,5},{5,9},{9,13},{14,2},{2,6},{... | collective-permute-start | bytes 138248 | tf_op jit(solution)/shard_map/ppermute | solution.py:16

commit v9 on v8

--- a/solution.py
+++ b/solution.py
@@ -19,54 +19,58 @@
     return jnp.where(inside, moved, jnp.zeros_like(moved))
 
 
-def conv_kernel(*refs, layout, lo, hi, finish):
-    count = sum(len(segments) for segments in layout)
-    flat = refs[:count]
-    left_ref, right_ref, w_ref, o_ref, slab, shift_s = refs[count:]
-    row_count = left_ref.shape[0]
+def conv_kernel(*refs, segments, parts, lo, band, first_build, lag, finish):
+    count = len(segments) * parts
+    blocks = refs[:count]
+    left_ref, right_ref, w_hbm, o_ref, slab, shift_s, w_vmem, sem = refs[count:]
     _, col_count, channels = o_ref.shape
     lanes = slab.shape[1] // 3
-    band = 12
     span = band * col_count
     padded_rows = slab.shape[0]
-    slab[pl.ds(0, col_count)] = jnp.zeros((col_count, slab.shape[1]), jnp.bfloat16)
-    slab[pl.ds(padded_rows - col_count, col_count)] = jnp.zeros((col_count, slab.shape[1]), jnp.bfloat16)
+    step = pl.program_id(0)
+    weight_copy = pltpu.make_async_copy(w_hbm, w_vmem, sem.at[0])
+
+    @pl.when(step == 0)
+    def _():
+        weight_copy.start()
+        slab[pl.ds(0, col_count)] = jnp.zeros((col_count, slab.shape[1]), jnp.bfloat16)
+        slab[pl.ds(padded_rows - col_count, col_count)] = jnp.zeros((col_count, slab.shape[1]), jnp.bfloat16)
+
+    r0 = first_build + step * band
     column = lax.broadcasted_iota(jnp.int32, (band, col_count, channels), 1)
-    addends = []
-    at = 0
-    for segments in layout:
-        addends.append(list(zip(flat[at : at + len(segments)], segments)))
-        at += len(segments)
-
-    def rows_of(ref_list, r0):
-        for ref, (first, last) in ref_list:
-            if first <= r0 < last:
-                return ref[pl.ds(r0 - first, band)]
-
-    for r0 in range(max(lo - band, 0), min(hi + band, row_count), band):
-        block = rows_of(addends[0], r0).astype(jnp.float32)
-        for extra in addends[1:]:
-            block = block + rows_of(extra, r0).astype(jnp.float32)
-        block = block.astype(jnp.bfloat16)
-        shift_s[pl.ds(8, span)] = block.astype(jnp.float32).reshape(span, channels)
-        before = shift_s[pl.ds(7, span)].reshape(band, col_count, channels)
-        after = shift_s[pl.ds(9, span)].reshape(band, col_count, channels)
-        rim_l = left_ref[pl.ds(r0, band)].astype(jnp.float32)[:, None, :]
-        rim_r = right_ref[pl.ds(r0, band)].astype(jnp.float32)[:, None, :]
-        before = jnp.where(column == 0, rim_l, before)
-        after = jnp.where(column == col_count - 1, rim_r, after)
-        rows = pl.ds((r0 + 1) * col_count, span)
-        slab[rows, pl.ds(0, channels)] = before.reshape(span, channels).astype(jnp.bfloat16)
-        slab[rows, pl.ds(lanes, channels)] = block.reshape(span, channels)
-        slab[rows, pl.ds(2 * lanes, channels)] = after.reshape(span, channels).astype(jnp.bfloat16)
-
-    for r0 in range(lo, hi, band):
+    for t, (first, last) in enumerate(segments):
+
+        @pl.when((r0 >= first) & (r0 < last))
+        def _():
+            block = blocks[t][...].astype(jnp.float32)
+            for k in range(1, parts):
+                block = block + blocks[k * len(segments) + t][...].astype(jnp.float32)
+            block = block.astype(jnp.bfloat16)
+            shift_s[pl.ds(8, span)] = block.astype(jnp.float32).reshape(span, channels)
+            before = shift_s[pl.ds(7, span)].reshape(band, col_count, channels)
+            after = shift_s[pl.ds(9, span)].reshape(band, col_count, channels)
+            rim_l = left_ref[0].astype(jnp.float32)[:, None, :]
+            rim_r = right_ref[0].astype(jnp.float32)[:, None, :]
+            before = jnp.where(column == 0, rim_l, before)
+            after = jnp.where(column == col_count - 1, rim_r, after)
+            rows = pl.ds(pl.multiple_of((r0 + 1) * col_count, col_count), span)
+            slab[rows, pl.ds(0, channels)] = before.reshape(span, channels).astype(jnp.bfloat16)
+            slab[rows, pl.ds(lanes, channels)] = block.reshape(span, channels)
+            slab[rows, pl.ds(2 * lanes, channels)] = after.reshape(span, channels).astype(jnp.bfloat16)
+
+    @pl.when(step == lag)
+    def _():
+        weight_copy.wait()
+
+    @pl.when(step >= lag)
+    def _():
+        out0 = lo + (step - lag) * band
         acc = None
         for a in range(3):
-            rows = pl.ds((r0 + a) * col_count, span)
-            term = jnp.dot(slab[rows, :], w_ref[a], preferred_element_type=jnp.float32)
+            rows = pl.ds(pl.multiple_of((out0 + a) * col_count, col_count), span)
+            term = jnp.dot(slab[rows, :], w_vmem[a], preferred_element_type=jnp.float32)
             acc = term if acc is None else acc + term
-        o_ref[pl.ds(r0 - lo, band)] = finish(acc).reshape(band, col_count, channels)
+        o_ref[...] = finish(acc).reshape(band, col_count, channels)
 
 
 def norm_gelu(first):
@@ -82,31 +86,57 @@
     return shifted(edge_of(-1), "quarter", 1), shifted(edge_of(0), "quarter", -1)
 
 
-def convolve(groups, rims, weight, finish, lo, hi):
+def convolve(groups, rims, weight, finish, lo, hi, band):
     row_count, channels = rims[0].shape
     col_count = groups[0][0].shape[1]
-    layout = []
-    for segments in groups:
-        spans = []
-        first = 0
-        for piece in segments:
-            spans.append((first, first + piece.shape[0]))
-            first += piece.shape[0]
-        layout.append(tuple(spans))
-    flat = [piece for segments in groups for piece in segments]
-    vmem = pl.BlockSpec(memory_space=pltpu.VMEM)
+    segments = []
+    first = 0
+    for piece in groups[0]:
+        segments.append((first, first + piece.shape[0]))
+        first += piece.shape[0]
+    first_build = max(lo - band, 0)
+    builds = len(range(first_build, min(hi + band, row_count), band))
+    lag = (lo + band - first_build) // band
+    steps = (hi - lo) // band + lag
+
+    def source_map(first, last):
+        offset = (first_build - first) // band
+        top = (last - first) // band - 1
+        return lambda s: (jnp.clip(s + offset, 0, top), 0, 0)
+
+    flat = [piece for segs in groups for piece in segs]
+    source_specs = [
+        pl.BlockSpec((band, col_count, channels), source_map(*segments[t % len(segments)]))
+        for t in range(len(flat))
+    ]
+    bands = row_count // band
+    rim_spec = pl.BlockSpec((1, band, channels), lambda s: (jnp.clip(s + first_build // band, 0, bands - 1), 0, 0))
     padded = (row_count + 2) * col_count
     stacked = weight.reshape(3, 3 * channels, channels)
+    kernel = functools.partial(
+        conv_kernel,
+        segments=tuple(segments),
+        parts=len(groups),
+        lo=lo,
+        band=band,
+        first_build=first_build,
+        lag=lag,
+        finish=finish,
+    )
+    del builds
     return pl.pallas_call(
-        functools.partial(conv_kernel, layout=tuple(layout), lo=lo, hi=hi, finish=finish),
+        kernel,
         out_shape=jax.ShapeDtypeStruct((hi - lo, col_count, channels), jnp.bfloat16),
-        in_specs=[vmem] * (len(flat) + 3),
-        out_specs=vmem,
+        grid=(steps,),
+        in_specs=source_specs + [rim_spec, rim_spec, pl.BlockSpec(memory_space=pl.ANY)],
+        out_specs=pl.BlockSpec((band, col_count, channels), lambda s: (jnp.maximum(s - lag, 0), 0, 0)),
         scratch_shapes=[
             pltpu.VMEM((padded, 3 * channels), jnp.bfloat16),
-            pltpu.VMEM((12 * col_count + 16, channels), jnp.float32),
+            pltpu.VMEM((band * col_count + 16, channels), jnp.float32),
+            pltpu.VMEM((3, 3 * channels, channels), weight.dtype),
+            pltpu.SemaphoreType.DMA((1,)),
         ],
-    )(*flat, *rims, stacked)
+    )(*flat, *(rim.reshape(bands, band, channels) for rim in rims), stacked)
 
 
 def attend_kernel(x_ref, wqkv_ref, bias_ref, wout_ref, o_ref, qkv_s, blend_s):
@@ -186,7 +216,7 @@
     hidden = []
     returned = []
     for lo in (0, half):
-        hidden.append(convolve([[tile]], rims, conv1_weight, norm_gelu, lo, lo + half))
+        hidden.append(convolve([[tile]], rims, conv1_weight, norm_gelu, lo, lo + half, 12))
     pix_piece = half * col_count // frames_all
     if half % frames_all == 0:
         piece_shape = (frames_all, half // frames_all, col_count, channels)
@@ -202,7 +232,7 @@
         summed = [h[:, c, :].astype(jnp.float32) + r[:, c, :].astype(jnp.float32) for h, r in zip(hidden, returned)]
         return jnp.concatenate(summed, axis=0).astype(jnp.bfloat16)
 
-    second = convolve([hidden, returned], halo(joined_edge), conv2_weight, to_bf16, 0, row_count)
+    second = convolve([hidden, returned], halo(joined_edge), conv2_weight, to_bf16, 0, row_count, 12)
     return second.reshape(frames_dev, row_count, col_count, channels)
 
 

time: 106 us -> 107 us (level)
  waiting for transfers between devices: 35.7 us -> 31.6 us
  Pallas kernels: 39.5 us -> 42.6 us
  starting transfers between devices: 21.4 us -> 23.1 us
    ppermute x4, waiting for transfers between devices: 9.3 us -> 4.7 us  [shifted(): moved = lax.ppermute(block, axis, route)]
    pallas_call x3, Pallas kernels: 27.7 us -> 30.8 us  [convolve(): pl.pallas_call(kernel, out_shape=jax.ShapeDtypeStruct((hi - lo, col_count...]
    another operation x0 -> x2, other arithmetic: none -> 2.76 us
    reshape x0 -> x4, local copies, waits for them, and re-layouts: none -> 2.6 us  [convolve(): rim.reshape(bands, band, channels)]
    select_n x4, other arithmetic: 2.51 us -> 0.04 us  [shifted(): return jnp.where(inside, moved, jnp.zeros_like(moved))]
    unnamed x14 -> x17, local copies, waits for them, and re-layouts: 3.26 us -> 1.22 us
    ppermute x4, starting transfers between devices: 7.24 us -> 9.1 us  [shifted(): moved = lax.ppermute(block, axis, route)]
    all_to_all x2, waiting for transfers between devices: 16.9 us -> 18.2 us  [body(): lax.all_to_all(attended.reshape(piece_shape), 'frame', split_axis=0, conc...]
  transfers between devices with their start and end apart: 8 -> 8, of which waited for: 8 -> 6; matrix products, arithmetic and copies ran while one was open for 5% -> 4% of each run, Pallas kernels for 19% -> 19%
where the time goes in v9:
time: 107 us; the launch traced here: 106 us
  Pallas kernels  42.6 us (40%)
  waiting for transfers between devices  31.6 us (30%)
  starting transfers between devices  23.1 us (22%)
  local copies, waits for them, and re-layouts  5.97 us (6%)
  other arithmetic  2.84 us (3%)
    pallas_call x3, Pallas kernels, convolve(): pl.pallas_call(kernel, out_shape=jax.ShapeDtypeStruct((hi - lo, col_count...  30.8 us
    all_to_all x2, waiting for transfers between devices, body(): lax.all_to_all(attended.reshape(piece_shape), 'frame', split_axis=0, conc...  18.2 us
    pallas_call x2, Pallas kernels, attend(): pl.pallas_call(attend_kernel, out_shape=jax.ShapeDtypeStruct((frames_all,...  11.8 us
    ppermute x4, starting transfers between devices, shifted(): moved = lax.ppermute(block, axis, route)  9.1 us
    all_to_all x2, waiting for transfers between devices, body(): lax.all_to_all(part.reshape(piece_shape), 'frame', split_axis=0, concat_a...  8.72 us
    all_to_all x2, starting transfers between devices, body(): lax.all_to_all(part.reshape(piece_shape), 'frame', split_axis=0, concat_a...  7.02 us
    all_to_all x2, starting transfers between devices, body(): lax.all_to_all(attended.reshape(piece_shape), 'frame', split_axis=0, conc...  7 us
    ppermute x4, waiting for transfers between devices, shifted(): moved = lax.ppermute(block, axis, route)  4.7 us
  transfers between devices with their start and end apart: 8, of which 6 were waited for; matrix products, arithmetic and copies ran while one was open for 4% of the time, Pallas kernels for 19%

profile of v9, /device:TPU:0, one launch (start us, length us, event | category | flops | bytes accessed | tf_op | source)
XLA Modules:
  0.0 106.3 jit_solution(3925896865724846248)
XLA Ops:
  0.0 1.3 %fusion.8 = (bf16[72,1,320]{2,1,0:T(2,128)(2,1)S(1)}, bf16[72,1,320]{2,1,0:T(2,128)(2,1)S(1)}) fusion(bf16[72,32,320]{2,1,0:T(8,128)(2,1)} %bitcast.34), kind=kLoop, calls=%fused_computation.28 | loop fusion | bytes 184320 | tf_op jit(solution)/shard_map/slice | solution.py:214
  1.3 3.1 %collective-permute-start = (bf16[72,320]{1,0:T(8,128)(2,1)S(1)}, bf16[72,320]{1,0:T(8,128)(2,1)S(1)}, u32[]{:S(2)}, u32[]{:S(2)}) collective-permute-start(bf16[72,320]{1,0:T(8,128)(2,1)S(1)} %bitcast.49), channel_id=1, source_target_pairs={{12,0},{0,4},{4,8},{8,12},{13,1},{1,5},{5,9},{9,13},{14,2},{2,6},{... | collective-permute-start | bytes 138248 | tf_op jit(solution)/shard_map/ppermute | solution.py:16
  4.4 2.1 %collective-permute-start.1 = (bf16[72,320]{1,0:T(8,128)(2,1)S(1)}, bf16[72,320]{1,0:T(8,128)(2,1)S(1)}, u32[]{:S(2)}, u32[]{:S(2)}) collective-permute-start(bf16[72,320]{1,0:T(8,128)(2,1)S(1)} %bitcast.48), channel_id=1, source_target_pairs={{4,0},{8,4},{12,8},{0,12},{5,1},{9,5},{13,9},{1,13},{6,2},{10,6},{... | collective-permute-start | bytes 138248 | tf_op jit(solution)/shard_map/ppermute | solution.py:16
  6.5 2.1 %collective-permute-done = bf16[72,320]{1,0:T(8,128)(2,1)S(1)} collective-permute-done((bf16[72,320]{1,0:T(8,128)(2,1)S(1)}, bf16[72,320]{1,0:T(8,128)(2,1)S(1)}, u32[]{:S(2)}, u32[]{:S(2)}) %collective-permute-start) | collective-permute-done | bytes 46112 | tf_op jit(solution)/shard_map/ppermute | solution.py:16
  8.7 0.7 reshape.68.refs_1_
  9.3 0.0 collective-permute-done.1
  9.3 0.7 reshape.69.refs_2_
  10.0 8.7 %shard_map.65.refs_1_ = bf16[36,32,320]{2,1,0:T(8,128)(2,1)} custom-call(bf16[72,32,320]{2,1,0:T(8,128)(2,1)} %bitcast.35, bf16[6,12,320]{2,1,0:T(8,128)(2,1)} %reshape.68.refs_1_, bf16[6,12,320]{2,1,0:T(8,128)(2,1)} %reshape.69.refs_2_, bf16[3,960,320]{2,1,0:T(8,128)(2,1)} %bitcast.30), custom_call_target="tpu_custom_call" | custom-call | tf_op jit(solution)/shard_map/pallas_call | solution.py:127
  18.7 3.5 %all-to-all-start.2 = ((bf16[4,9,32,320]{3,2,1,0:T(8,128)(2,1)}), bf16[4,9,32,320]{3,2,1,0:T(8,128)(2,1)S(1)}, u32[]{:S(2)}, u32[]{:S(2)}) async-start(bf16[4,9,32,320]{3,2,1,0:T(8,128)(2,1)} %bitcast.32), calls=%async_computation.2 | async-start | bytes 1769472 | tf_op jit(solution)/shard_map/all_to_all | solution.py:226
  22.2 8.7 %shard_map.64.refs_0_ = bf16[36,32,320]{2,1,0:T(8,128)(2,1)} custom-call(bf16[72,32,320]{2,1,0:T(8,128)(2,1)} %bitcast.36, bf16[6,12,320]{2,1,0:T(8,128)(2,1)} %reshape.68.refs_1_, bf16[6,12,320]{2,1,0:T(8,128)(2,1)} %reshape.69.refs_2_, bf16[3,960,320]{2,1,0:T(8,128)(2,1)} %bitcast.31), custom_call_target="tpu_custom_call" | custom-call | tf_op jit(solution)/shard_map/pallas_call | solution.py:127
  30.9 0.0 copy-start.5
  30.9 0.0 copy-start.4
  30.9 3.9 %all-to-all-done.2 = bf16[4,9,32,320]{3,2,1,0:T(8,128)(2,1)S(1)} async-done(((bf16[4,9,32,320]{3,2,1,0:T(8,128)(2,1)}), bf16[4,9,32,320]{3,2,1,0:T(8,128)(2,1)S(1)}, u32[]{:S(2)}, u32[]{:S(2)}) %all-to-all-start.2) | async-done | bytes 737312 | tf_op jit(solution)/shard_map/all_to_all | solution.py:226
  34.9 3.5 %all-to-all-start = ((bf16[4,9,32,320]{3,2,1,0:T(8,128)(2,1)}), bf16[4,9,32,320]{3,2,1,0:T(8,128)(2,1)S(1)}, u32[]{:S(2)}, u32[]{:S(2)}) async-start(bf16[4,9,32,320]{3,2,1,0:T(8,128)(2,1)} %bitcast.33), calls=%async_computation | async-start | bytes 1769472 | tf_op jit(solution)/shard_map/all_to_all | solution.py:226
  38.4 0.8 copy.60.bias_ref
  39.2 1.1 %copy.58 = bf16[320,960]{0,1:T(8,128)(2,1)} copy(bf16[320,960]{1,0:T(8,128)(2,1)S(1)} %copy-done.4) | data formatting | bytes 1228800 | tf_op args[2]
  40.4 5.9 %shard_map.67 = bf16[4,288,320]{2,1,0:T(8,128)(2,1)} custom-call(bf16[4,288,320]{2,1,0:T(8,128)(2,1)} %bitcast.43, bf16[960,320]{1,0:T(8,128)(2,1)} %bitcast.37, f32[5,4,4,1]{3,2,1,0:T(4,128)} %copy.60.bias_ref, bf16[320,320]{1,0:T(8,128)(2,1)} %wout_ref.3), custom_call_target="tpu_custom_call" | custom-call | tf_op jit(solution)/shard_map/pallas_call | solution.py:198
  46.3 4.8 %all-to-all-done = bf16[4,9,32,320]{3,2,1,0:T(8,128)(2,1)S(1)} async-done(((bf16[4,9,32,320]{3,2,1,0:T(8,128)(2,1)}), bf16[4,9,32,320]{3,2,1,0:T(8,128)(2,1)S(1)}, u32[]{:S(2)}, u32[]{:S(2)}) %all-to-all-start) | async-done | bytes 737312 | tf_op jit(solution)/shard_map/all_to_all | solution.py:226
  51.1 3.5 %all-to-all-start.3 = ((bf16[4,9,32,320]{3,2,1,0:T(8,128)(2,1)}), bf16[4,9,32,320]{3,2,1,0:T(8,128)(2,1)S(1)}, u32[]{:S(2)}, u32[]{:S(2)}) async-start(bf16[4,9,32,320]{3,2,1,0:T(8,128)(2,1)} %bitcast.46), calls=%async_computation.3 | async-start | bytes 1769472 | tf_op jit(solution)/shard_map/all_to_all | solution.py:228
  54.6 5.9 %shard_map.66 = bf16[4,288,320]{2,1,0:T(8,128)(2,1)} custom-call(bf16[4,288,320]{2,1,0:T(8,128)(2,1)} %bitcast.44, bf16[960,320]{1,0:T(8,128)(2,1)} %bitcast.38, f32[5,4,4,1]{3,2,1,0:T(4,128)} %copy.60.bias_ref, bf16[320,320]{1,0:T(8,128)(2,1)} %wout_ref.3), custom_call_target="tpu_custom_call" | custom-call | tf_op jit(solution)/shard_map/pallas_call | solution.py:198
  60.5 6.7 %all-to-all-done.3 = bf16[4,9,32,320]{3,2,1,0:T(8,128)(2,1)S(1)} async-done(((bf16[4,9,32,320]{3,2,1,0:T(8,128)(2,1)}), bf16[4,9,32,320]{3,2,1,0:T(8,128)(2,1)S(1)}, u32[]{:S(2)}, u32[]{:S(2)}) %all-to-all-start.3) | async-done | bytes 737312 | tf_op jit(solution)/shard_map/all_to_all | solution.py:228
  67.3 3.5 %all-to-all-start.1 = ((bf16[4,9,32,320]{3,2,1,0:T(8,128)(2,1)}), bf16[4,9,32,320]{3,2,1,0:T(8,128)(2,1)S(1)}, u32[]{:S(2)}, u32[]{:S(2)}) async-start(bf16[4,9,32,320]{3,2,1,0:T(8,128)(2,1)} %bitcast.45), calls=%async_computation.1 | async-start | bytes 1769472 | tf_op jit(solution)/shard_map/all_to_all | solution.py:228
  70.8 1.2 %fusion.1 = (bf16[36,1,320]{2,1,0:T(2,128)(2,1)S(1)}, bf16[36,1,320]{2,1,0:T(2,128)(2,1)S(1)}) fusion(bf16[36,32,320]{2,1,0:T(8,128)(2,1)S(1)} %bitcast.39, bf16[36,32,320]{2,1,0:T(8,128)(2,1)} %shard_map.65.refs_1_), kind=kLoop, calls=%fused_computation.2 | loop fusion | flops 92160 | bytes 138240 | tf_op jit(solution)/shard_map/convert.2
  72.0 11.4 %all-to-all-done.1 = bf16[4,9,32,320]{3,2,1,0:T(8,128)(2,1)S(1)} async-done(((bf16[4,9,32,320]{3,2,1,0:T(8,128)(2,1)}), bf16[4,9,32,320]{3,2,1,0:T(8,128)(2,1)S(1)}, u32[]{:S(2)}, u32[]{:S(2)}) %all-to-all-start.1) | async-done | bytes 737312 | tf_op jit(solution)/shard_map/all_to_all | solution.py:228
  83.4 1.5 %fusion.3 = (bf16[36,1,320]{2,1,0:T(2,128)(2,1)S(1)}, bf16[36,1,320]{2,1,0:T(2,128)(2,1)S(1)}) fusion(bf16[36,32,320]{2,1,0:T(8,128)(2,1)S(1)} %bitcast.41, bf16[36,32,320]{2,1,0:T(8,128)(2,1)} %shard_map.64.refs_0_), kind=kLoop, calls=%fused_computation.6 | loop fusion | flops 92160 | bytes 138240 | tf_op jit(solution)/shard_map/convert.3
  85.0 1.0 collective-permute-start.2
  86.0 3.0 %collective-permute-start.3 = (bf16[72,320]{1,0:T(8,128)(2,1)S(1)}, bf16[72,320]{1,0:T(8,128)(2,1)S(1)}, u32[]{:S(2)}, u32[]{:S(2)}) collective-permute-start(bf16[72,320]{1,0:T(8,128)(2,1)S(1)} %pad_maximum_fusion.1), channel_id=1, source_target_pairs={{4,0},{8,4},{12,8},{0,12},{5,1},{9,5},{13,9},{1,13},{6,2},{10,6},{... | collective-permute-start | bytes 138248 | tf_op jit(solution)/shard_map/ppermute | solution.py:16
  89.0 2.6 %collective-permute-done.2 = bf16[72,320]{1,0:T(8,128)(2,1)S(1)} collective-permute-done((bf16[72,320]{1,0:T(8,128)(2,1)S(1)}, bf16[72,320]{1,0:T(8,128)(2,1)S(1)}, u32[]{:S(2)}, u32[]{:S(2)}) %collective-permute-start.2) | collective-permute-done | bytes 46112 | tf_op jit(solution)/shard_map/ppermute | solution.py:16
  91.6 0.6 reshape.79.refs_4_
  92.2 0.0 collective-permute-done.3
  92.3 0.7 reshape.80.refs_5_
  92.9 13.4 %shard_map.68 = bf16[72,32,320]{2,1,0:T(8,128)(2,1)} custom-call(bf16[36,32,320]{2,1,0:T(8,128)(2,1)} %shard_map.64.refs_0_, bf16[36,32,320]{2,1,0:T(8,128)(2,1)} %shard_map.65.refs_1_, bf16[36,32,320]{2,1,0:T(8,128)(2,1)} %bitcast.42, bf16[36,32,320]{2,1,0:T(8,128)(2,1)} %bitcast.40, bf16[6,12,320]{2,1,0:T(8,128)(2,1)} %reshape.79.refs_4_, ...), custom_call_target="tpu_custom_call" | custom-call | tf_op jit(solution)/shard_map/pallas_call | solution.py:127
  (20 shorter events, 0.1 us)
Async XLA Ops:
  1.3 7.3 %collective-permute-start = (bf16[72,320]{1,0:T(8,128)(2,1)S(1)}, bf16[72,320]{1,0:T(8,128)(2,1)S(1)}, u32[]{:S(2)}, u32[]{:S(2)}) collective-permute-start(bf16[72,320]{1,0:T(8,128)(2,1)S(1)} %bitcast.49), channel_id=1, source_target_pairs={{12,0},{0,4},{4,8},{8,12},{13,1},{1,5},{5,9},{9,13},{14,2},{2,6},{... | collective-permute-start | bytes 138248 | tf_op jit(solution)/shard_map/ppermute | solution.py:16
  4.4 4.9 %collective-permute-start.1 = (bf16[72,320]{1,0:T(8,128)(2,1)S(1)}, bf16[72,320]{1,0:T(8,128)(2,1)S(1)}, u32[]{:S(2)}, u32[]{:S(2)}) collective-permute-start(bf16[72,320]{1,0:T(8,128)(2,1)S(1)} %bitcast.48), channel_id=1, source_target_pairs={{4,0},{8,4},{12,8},{0,12},{5,1},{9,5},{13,9},{1,13},{6,2},{10,6},{... | collective-permute-start | bytes 138248 | tf_op jit(solution)/shard_map/ppermute | solution.py:16
  18.7 16.2 %all-to-all-start.2 = ((bf16[4,9,32,320]{3,2,1,0:T(8,128)(2,1)}), bf16[4,9,32,320]{3,2,1,0:T(8,128)(2,1)S(1)}, u32[]{:S(2)}, u32[]{:S(2)}) async-start(bf16[4,9,32,320]{3,2,1,0:T(8,128)(2,1)} %bitcast.32), calls=%async_computation.2 | async-start | bytes 1769472 | tf_op jit(solution)/shard_map/all_to_all | solution.py:226
  30.9 7.5 %copy-start.5 = (f32[5,4,4]{0,2,1:T(4,128)S(1)}, f32[5,4,4]{0,2,1:T(4,128)}, u32[]{:S(2)}) copy-start(f32[5,4,4]{0,2,1:T(4,128)} %param.10) | copy-start | bytes 964
  30.9 8.3 %copy-start.4 = (bf16[320,960]{1,0:T(8,128)(2,1)S(1)}, bf16[320,960]{1,0:T(8,128)(2,1)}, u32[]{:S(2)}) copy-start(bf16[320,960]{1,0:T(8,128)(2,1)} %param.8) | copy-start | bytes 1843204
  34.9 5.5 %copy-start.2 = (bf16[4,9,32,320]{3,2,1,0:T(8,128)(2,1)}, bf16[4,9,32,320]{3,2,1,0:T(8,128)(2,1)S(1)}, u32[]{:S(2)}) copy-start(bf16[4,9,32,320]{3,2,1,0:T(8,128)(2,1)S(1)} %all-to-all-done.2) | copy-start | bytes 2211844
  34.9 16.2 %all-to-all-start = ((bf16[4,9,32,320]{3,2,1,0:T(8,128)(2,1)}), bf16[4,9,32,320]{3,2,1,0:T(8,128)(2,1)S(1)}, u32[]{:S(2)}, u32[]{:S(2)}) async-start(bf16[4,9,32,320]{3,2,1,0:T(8,128)(2,1)} %bitcast.33), calls=%async_computation | async-start | bytes 1769472 | tf_op jit(solution)/shard_map/all_to_all | solution.py:226
  51.1 3.5 %copy-start.3 = (bf16[4,9,32,320]{3,2,1,0:T(8,128)(2,1)}, bf16[4,9,32,320]{3,2,1,0:T(8,128)(2,1)S(1)}, u32[]{:S(2)}) copy-start(bf16[4,9,32,320]{3,2,1,0:T(8,128)(2,1)S(1)} %all-to-all-done) | copy-start | bytes 2211844
  51.1 16.2 %all-to-all-start.3 = ((bf16[4,9,32,320]{3,2,1,0:T(8,128)(2,1)}), bf16[4,9,32,320]{3,2,1,0:T(8,128)(2,1)S(1)}, u32[]{:S(2)}, u32[]{:S(2)}) async-start(bf16[4,9,32,320]{3,2,1,0:T(8,128)(2,1)} %bitcast.46), calls=%async_computation.3 | async-start | bytes 1769472 | tf_op jit(solution)/shard_map/all_to_all | solution.py:228
  67.3 25.7 %copy-start = (bf16[4,9,32,320]{3,2,1,0:T(8,128)(2,1)}, bf16[4,9,32,320]{3,2,1,0:T(8,128)(2,1)S(1)}, u32[]{:S(2)}) copy-start(bf16[4,9,32,320]{3,2,1,0:T(8,128)(2,1)S(1)} %all-to-all-done.3) | copy-start | bytes 2211844
  67.3 16.2 %all-to-all-start.1 = ((bf16[4,9,32,320]{3,2,1,0:T(8,128)(2,1)}), bf16[4,9,32,320]{3,2,1,0:T(8,128)(2,1)S(1)}, u32[]{:S(2)}, u32[]{:S(2)}) async-start(bf16[4,9,32,320]{3,2,1,0:T(8,128)(2,1)} %bitcast.45), calls=%async_computation.1 | async-start | bytes 1769472 | tf_op jit(solution)/shard_map/all_to_all | solution.py:228
  83.4 9.5 %copy-start.1 = (bf16[4,9,32,320]{3,2,1,0:T(8,128)(2,1)}, bf16[4,9,32,320]{3,2,1,0:T(8,128)(2,1)S(1)}, u32[]{:S(2)}) copy-start(bf16[4,9,32,320]{3,2,1,0:T(8,128)(2,1)S(1)} %all-to-all-done.1) | copy-start | bytes 2211844
  85.0 6.6 %collective-permute-start.2 = (bf16[72,320]{1,0:T(8,128)(2,1)S(1)}, bf16[72,320]{1,0:T(8,128)(2,1)S(1)}, u32[]{:S(2)}, u32[]{:S(2)}) collective-permute-start(bf16[72,320]{1,0:T(8,128)(2,1)S(1)} %pad_maximum_fusion), channel_id=1, source_target_pairs={{12,0},{0,4},{4,8},{8,12},{13,1},{1,5},{5,9},{9,13},{14,2},{2,6},{... | collective-permute-start | bytes 138248 | tf_op jit(solution)/shard_map/ppermute | solution.py:16
  86.0 6.2 %collective-permute-start.3 = (bf16[72,320]{1,0:T(8,128)(2,1)S(1)}, bf16[72,320]{1,0:T(8,128)(2,1)S(1)}, u32[]{:S(2)}, u32[]{:S(2)}) collective-permute-start(bf16[72,320]{1,0:T(8,128)(2,1)S(1)} %pad_maximum_fusion.1), channel_id=1, source_target_pairs={{4,0},{8,4},{12,8},{0,12},{5,1},{9,5},{13,9},{1,13},{6,2},{10,6},{... | collective-permute-start | bytes 138248 | tf_op jit(solution)/shard_map/ppermute | solution.py:16

commit v10 on v8

--- a/solution.py
+++ b/solution.py
@@ -19,14 +19,13 @@
     return jnp.where(inside, moved, jnp.zeros_like(moved))
 
 
-def conv_kernel(*refs, layout, lo, hi, finish):
+def conv_kernel(*refs, layout, lo, hi, band, finish):
     count = sum(len(segments) for segments in layout)
     flat = refs[:count]
     left_ref, right_ref, w_ref, o_ref, slab, shift_s = refs[count:]
     row_count = left_ref.shape[0]
     _, col_count, channels = o_ref.shape
     lanes = slab.shape[1] // 3
-    band = 12
     span = band * col_count
     padded_rows = slab.shape[0]
     slab[pl.ds(0, col_count)] = jnp.zeros((col_count, slab.shape[1]), jnp.bfloat16)
@@ -82,7 +81,7 @@
     return shifted(edge_of(-1), "quarter", 1), shifted(edge_of(0), "quarter", -1)
 
 
-def convolve(groups, rims, weight, finish, lo, hi):
+def convolve(groups, rims, weight, finish, lo, hi, band):
     row_count, channels = rims[0].shape
     col_count = groups[0][0].shape[1]
     layout = []
@@ -98,13 +97,13 @@
     padded = (row_count + 2) * col_count
     stacked = weight.reshape(3, 3 * channels, channels)
     return pl.pallas_call(
-        functools.partial(conv_kernel, layout=tuple(layout), lo=lo, hi=hi, finish=finish),
+        functools.partial(conv_kernel, layout=tuple(layout), lo=lo, hi=hi, band=band, finish=finish),
         out_shape=jax.ShapeDtypeStruct((hi - lo, col_count, channels), jnp.bfloat16),
         in_specs=[vmem] * (len(flat) + 3),
         out_specs=vmem,
         scratch_shapes=[
             pltpu.VMEM((padded, 3 * channels), jnp.bfloat16),
-            pltpu.VMEM((12 * col_count + 16, channels), jnp.float32),
+            pltpu.VMEM((band * col_count + 16, channels), jnp.float32),
         ],
     )(*flat, *rims, stacked)
 
@@ -181,12 +180,13 @@
     frames_dev, row_count, col_count, channels = latents.shape
     frames_all = lax.axis_size("frame")
     tile = latents.reshape(row_count, col_count, channels)
-    rims = halo(lambda c: tile[:, c, :])
+    flat_tile = tile.reshape(row_count * col_count, channels)
+    rims = halo(lambda c: flat_tile[c % col_count :: col_count])
     half = row_count // 2
     hidden = []
     returned = []
     for lo in (0, half):
-        hidden.append(convolve([[tile]], rims, conv1_weight, norm_gelu, lo, lo + half))
+        hidden.append(convolve([[tile]], rims, conv1_weight, norm_gelu, lo, lo + half, 12))
     pix_piece = half * col_count // frames_all
     if half % frames_all == 0:
         piece_shape = (frames_all, half // frames_all, col_count, channels)
@@ -202,7 +202,7 @@
         summed = [h[:, c, :].astype(jnp.float32) + r[:, c, :].astype(jnp.float32) for h, r in zip(hidden, returned)]
         return jnp.concatenate(summed, axis=0).astype(jnp.bfloat16)
 
-    second = convolve([hidden, returned], halo(joined_edge), conv2_weight, to_bf16, 0, row_count)
+    second = convolve([hidden, returned], halo(joined_edge), conv2_weight, to_bf16, 0, row_count, 12)
     return second.reshape(frames_dev, row_count, col_count, channels)
 
 

time: 106 us -> 107 us (level)
  local copies, waits for them, and re-layouts: 6.54 us -> 7.85 us
    slice x0 -> x2, local copies, waits for them, and re-layouts: none -> 3.42 us  [body(): rims = halo(lambda c: flat_tile[c % col_count::col_count])]
    unnamed x14 -> x13, local copies, waits for them, and re-layouts: 3.26 us -> 1.17 us
  transfers between devices with their start and end apart: 8 -> 8, of which waited for: 8 -> 7; matrix products, arithmetic and copies ran while one was open for 5% -> 7% of each run, Pallas kernels for 19% -> 19%
where the time goes in v10:
time: 107 us
  Pallas kernels  39.5 us (37%)
  waiting for transfers between devices  35 us (33%)
  starting transfers between devices  21.5 us (20%)
  local copies, waits for them, and re-layouts  7.85 us (7%)
  other arithmetic  2.58 us (2%)
    pallas_call x3, Pallas kernels, convolve(): pl.pallas_call(functools.partial(conv_kernel, layout=tuple(layout), lo=lo...  27.7 us
    all_to_all x2, waiting for transfers between devices, body(): lax.all_to_all(attended.reshape(piece_shape), 'frame', split_axis=0, conc...  16.9 us
    pallas_call x2, Pallas kernels, attend(): pl.pallas_call(attend_kernel, out_shape=jax.ShapeDtypeStruct((frames_all,...  11.8 us
    all_to_all x2, waiting for transfers between devices, body(): lax.all_to_all(part.reshape(piece_shape), 'frame', split_axis=0, concat_a...  9.48 us
    ppermute x4, waiting for transfers between devices, shifted(): moved = lax.ppermute(block, axis, route)  8.63 us
    ppermute x4, starting transfers between devices, shifted(): moved = lax.ppermute(block, axis, route)  7.27 us
    all_to_all x2, starting transfers between devices, body(): lax.all_to_all(attended.reshape(piece_shape), 'frame', split_axis=0, conc...  7.18 us
    all_to_all x2, starting transfers between devices, body(): lax.all_to_all(part.reshape(piece_shape), 'frame', split_axis=0, concat_a...  7 us
  transfers between devices with their start and end apart: 8, of which 7 were waited for; matrix products, arithmetic and copies ran while one was open for 7% of the time, Pallas kernels for 19%

profile of v10, /device:TPU:0, one launch (start us, length us, event | category | flops | bytes accessed | tf_op | source)
XLA Modules:
  0.0 106.5 jit_solution(7474774369247218604)
XLA Ops:
  0.0 1.7 %slice.31 = bf16[72,320]{1,0:T(8,128)(2,1)S(1)} slice(bf16[2304,320]{1,0:T(8,128)(2,1)} %bitcast.29), slice={[0:2304:32], [0:320:1]} | slice | bytes 92160 | tf_op jit(solution)/shard_map/slice | solution.py:184
  1.7 5.1 %collective-permute-start.1 = (bf16[72,320]{1,0:T(8,128)(2,1)S(1)}, bf16[72,320]{1,0:T(8,128)(2,1)S(1)}, u32[]{:S(2)}, u32[]{:S(2)}) collective-permute-start(bf16[72,320]{1,0:T(8,128)(2,1)S(1)} %slice.31), channel_id=1, source_target_pairs={{4,0},{8,4},{12,8},{0,12},{5,1},{9,5},{13,9},{1,13},{6,2},{10,6},{... | collective-permute-start | bytes 138248 | tf_op jit(solution)/shard_map/ppermute | solution.py:16
  6.8 1.7 %slice.30 = bf16[72,320]{1,0:T(8,128)(2,1)S(1)} slice(bf16[2304,320]{1,0:T(8,128)(2,1)} %bitcast.30), slice={[31:2304:32], [0:320:1]} | slice | bytes 92160 | tf_op jit(solution)/shard_map/slice | solution.py:184
  8.5 0.1 collective-permute-start
  8.6 0.6 broadcast_select_fusion.1.refs_2_
  9.2 5.3 %collective-permute-done = bf16[72,320]{1,0:T(8,128)(2,1)S(1)} collective-permute-done((bf16[72,320]{1,0:T(8,128)(2,1)S(1)}, bf16[72,320]{1,0:T(8,128)(2,1)S(1)}, u32[]{:S(2)}, u32[]{:S(2)}) %collective-permute-start) | collective-permute-done | bytes 46112 | tf_op jit(solution)/shard_map/ppermute | solution.py:16
  14.5 0.6 broadcast_select_fusion.3.refs_1_
  15.2 7.8 %shard_map.65.refs_1_ = bf16[36,32,320]{2,1,0:T(8,128)(2,1)} custom-call(bf16[72,32,320]{2,1,0:T(8,128)(2,1)} %bitcast.31, bf16[72,320]{1,0:T(8,128)(2,1)} %broadcast_select_fusion.3.refs_1_, bf16[72,320]{1,0:T(8,128)(2,1)} %broadcast_select_fusion.1.refs_2_, bf16[3,960,320]{2,1,0:T(8,128)(2,1)} %bitcast.25), custom_call_target="tpu_custom_call" | custom-call | tf_op jit(solution)/shard_map/pallas_call | solution.py:99
  23.0 3.5 %all-to-all-start.2 = ((bf16[4,9,32,320]{3,2,1,0:T(8,128)(2,1)}), bf16[4,9,32,320]{3,2,1,0:T(8,128)(2,1)S(1)}, u32[]{:S(2)}, u32[]{:S(2)}) async-start(bf16[4,9,32,320]{3,2,1,0:T(8,128)(2,1)} %bitcast.27), calls=%async_computation.2 | async-start | bytes 1769472 | tf_op jit(solution)/shard_map/all_to_all | solution.py:196
  26.5 8.0 %shard_map.64.refs_0_ = bf16[36,32,320]{2,1,0:T(8,128)(2,1)} custom-call(bf16[72,32,320]{2,1,0:T(8,128)(2,1)} %bitcast.32, bf16[72,320]{1,0:T(8,128)(2,1)} %broadcast_select_fusion.3.refs_1_, bf16[72,320]{1,0:T(8,128)(2,1)} %broadcast_select_fusion.1.refs_2_, bf16[3,960,320]{2,1,0:T(8,128)(2,1)} %bitcast.26), custom_call_target="tpu_custom_call" | custom-call | tf_op jit(solution)/shard_map/pallas_call | solution.py:99
  34.4 4.7 %all-to-all-done.2 = bf16[4,9,32,320]{3,2,1,0:T(8,128)(2,1)S(1)} async-done(((bf16[4,9,32,320]{3,2,1,0:T(8,128)(2,1)}), bf16[4,9,32,320]{3,2,1,0:T(8,128)(2,1)S(1)}, u32[]{:S(2)}, u32[]{:S(2)}) %all-to-all-start.2) | async-done | bytes 737312 | tf_op jit(solution)/shard_map/all_to_all | solution.py:196
  39.2 3.5 %all-to-all-start = ((bf16[4,9,32,320]{3,2,1,0:T(8,128)(2,1)}), bf16[4,9,32,320]{3,2,1,0:T(8,128)(2,1)S(1)}, u32[]{:S(2)}, u32[]{:S(2)}) async-start(bf16[4,9,32,320]{3,2,1,0:T(8,128)(2,1)} %bitcast.28), calls=%async_computation | async-start | bytes 1769472 | tf_op jit(solution)/shard_map/all_to_all | solution.py:196
  42.7 1.1 %copy.19 = bf16[320,960]{0,1:T(8,128)(2,1)} copy(bf16[320,960]{1,0:T(8,128)(2,1)S(1)} %copy-done.4) | data formatting | bytes 1228800 | tf_op args[2]
  43.8 0.8 copy.21.bias_ref
  44.6 5.9 %shard_map.67 = bf16[4,288,320]{2,1,0:T(8,128)(2,1)} custom-call(bf16[4,288,320]{2,1,0:T(8,128)(2,1)} %bitcast.40, bf16[960,320]{1,0:T(8,128)(2,1)} %bitcast.33, f32[5,4,4,1]{3,2,1,0:T(4,128)} %copy.21.bias_ref, bf16[320,320]{1,0:T(8,128)(2,1)} %wout_ref.3), custom_call_target="tpu_custom_call" | custom-call | tf_op jit(solution)/shard_map/pallas_call | solution.py:167
  50.6 4.8 %all-to-all-done = bf16[4,9,32,320]{3,2,1,0:T(8,128)(2,1)S(1)} async-done(((bf16[4,9,32,320]{3,2,1,0:T(8,128)(2,1)}), bf16[4,9,32,320]{3,2,1,0:T(8,128)(2,1)S(1)}, u32[]{:S(2)}, u32[]{:S(2)}) %all-to-all-start) | async-done | bytes 737312 | tf_op jit(solution)/shard_map/all_to_all | solution.py:196
  55.3 3.7 %all-to-all-start.3 = ((bf16[4,9,32,320]{3,2,1,0:T(8,128)(2,1)}), bf16[4,9,32,320]{3,2,1,0:T(8,128)(2,1)S(1)}, u32[]{:S(2)}, u32[]{:S(2)}) async-start(bf16[4,9,32,320]{3,2,1,0:T(8,128)(2,1)} %bitcast.42), calls=%async_computation.3 | async-start | bytes 1769472 | tf_op jit(solution)/shard_map/all_to_all | solution.py:198
  59.0 5.9 %shard_map.66 = bf16[4,288,320]{2,1,0:T(8,128)(2,1)} custom-call(bf16[4,288,320]{2,1,0:T(8,128)(2,1)} %bitcast.41, bf16[960,320]{1,0:T(8,128)(2,1)} %bitcast.34, f32[5,4,4,1]{3,2,1,0:T(4,128)} %copy.21.bias_ref, bf16[320,320]{1,0:T(8,128)(2,1)} %wout_ref.3), custom_call_target="tpu_custom_call" | custom-call | tf_op jit(solution)/shard_map/pallas_call | solution.py:167
  64.9 6.6 %all-to-all-done.3 = bf16[4,9,32,320]{3,2,1,0:T(8,128)(2,1)S(1)} async-done(((bf16[4,9,32,320]{3,2,1,0:T(8,128)(2,1)}), bf16[4,9,32,320]{3,2,1,0:T(8,128)(2,1)S(1)}, u32[]{:S(2)}, u32[]{:S(2)}) %all-to-all-start.3) | async-done | bytes 737312 | tf_op jit(solution)/shard_map/all_to_all | solution.py:198
  71.5 3.5 %all-to-all-start.1 = ((bf16[4,9,32,320]{3,2,1,0:T(8,128)(2,1)}), bf16[4,9,32,320]{3,2,1,0:T(8,128)(2,1)S(1)}, u32[]{:S(2)}, u32[]{:S(2)}) async-start(bf16[4,9,32,320]{3,2,1,0:T(8,128)(2,1)} %bitcast.39), calls=%async_computation.1 | async-start | bytes 1769472 | tf_op jit(solution)/shard_map/all_to_all | solution.py:198
  75.0 1.1 %fusion.6 = (bf16[36,1,320]{2,1,0:T(2,128)(2,1)S(1)}, bf16[36,1,320]{2,1,0:T(2,128)(2,1)S(1)}) fusion(bf16[36,32,320]{2,1,0:T(8,128)(2,1)} %shard_map.65.refs_1_), kind=kLoop, calls=%fused_computation.16 | loop fusion | bytes 92160 | tf_op jit(solution)/shard_map/slice | solution.py:202
  76.2 1.1 %fusion.4 = (bf16[36,1,320]{2,1,0:T(2,128)(2,1)S(1)}, bf16[36,1,320]{2,1,0:T(2,128)(2,1)S(1)}) fusion(bf16[36,32,320]{2,1,0:T(8,128)(2,1)} %shard_map.64.refs_0_), kind=kLoop, calls=%fused_computation.14 | loop fusion | bytes 92160 | tf_op jit(solution)/shard_map/slice | solution.py:202
  77.3 0.1 fusion.7
  77.4 10.3 %all-to-all-done.1 = bf16[4,9,32,320]{3,2,1,0:T(8,128)(2,1)S(1)} async-done(((bf16[4,9,32,320]{3,2,1,0:T(8,128)(2,1)}), bf16[4,9,32,320]{3,2,1,0:T(8,128)(2,1)S(1)}, u32[]{:S(2)}, u32[]{:S(2)}) %all-to-all-start.1) | async-done | bytes 737312 | tf_op jit(solution)/shard_map/all_to_all | solution.py:198
  87.7 0.1 fusion.5
  87.9 0.1 collective-permute-start.3
  88.0 2.1 %collective-permute-start.2 = (bf16[72,320]{1,0:T(8,128)(2,1)S(1)}, bf16[72,320]{1,0:T(8,128)(2,1)S(1)}, u32[]{:S(2)}, u32[]{:S(2)}) collective-permute-start(bf16[72,320]{1,0:T(8,128)(2,1)S(1)} %pad_maximum_fusion), channel_id=1, source_target_pairs={{12,0},{0,4},{4,8},{8,12},{13,1},{1,5},{5,9},{9,13},{14,2},{2,6},{... | collective-permute-start | bytes 138248 | tf_op jit(solution)/shard_map/ppermute | solution.py:16
  90.0 2.0 %collective-permute-done.3 = bf16[72,320]{1,0:T(8,128)(2,1)S(1)} collective-permute-done((bf16[72,320]{1,0:T(8,128)(2,1)S(1)}, bf16[72,320]{1,0:T(8,128)(2,1)S(1)}, u32[]{:S(2)}, u32[]{:S(2)}) %collective-permute-start.3) | collective-permute-done | bytes 46112 | tf_op jit(solution)/shard_map/ppermute | solution.py:16
  92.1 0.6 broadcast_select_fusion.refs_5_
  92.7 1.3 %collective-permute-done.2 = bf16[72,320]{1,0:T(8,128)(2,1)S(1)} collective-permute-done((bf16[72,320]{1,0:T(8,128)(2,1)S(1)}, bf16[72,320]{1,0:T(8,128)(2,1)S(1)}, u32[]{:S(2)}, u32[]{:S(2)}) %collective-permute-start.2) | collective-permute-done | bytes 46112 | tf_op jit(solution)/shard_map/ppermute | solution.py:16
  94.0 0.6 broadcast_select_fusion.2.refs_4_
  94.6 11.9 %shard_map.68 = bf16[72,32,320]{2,1,0:T(8,128)(2,1)} custom-call(bf16[36,32,320]{2,1,0:T(8,128)(2,1)} %shard_map.64.refs_0_, bf16[36,32,320]{2,1,0:T(8,128)(2,1)} %shard_map.65.refs_1_, bf16[36,32,320]{2,1,0:T(8,128)(2,1)} %bitcast.38, bf16[36,32,320]{2,1,0:T(8,128)(2,1)} %bitcast.36, bf16[72,320]{1,0:T(8,128)(2,1)} %broadcast_select_fusion.2.refs_4_, ...), custom_call_target="tpu_custom_call" | custom-call | tf_op jit(solution)/shard_map/pallas_call | solution.py:99
  (17 shorter events, 0.1 us)
Async XLA Ops:
  1.7 6.9 %collective-permute-start.1 = (bf16[72,320]{1,0:T(8,128)(2,1)S(1)}, bf16[72,320]{1,0:T(8,128)(2,1)S(1)}, u32[]{:S(2)}, u32[]{:S(2)}) collective-permute-start(bf16[72,320]{1,0:T(8,128)(2,1)S(1)} %slice.31), channel_id=1, source_target_pairs={{4,0},{8,4},{12,8},{0,12},{5,1},{9,5},{13,9},{1,13},{6,2},{10,6},{... | collective-permute-start | bytes 138248 | tf_op jit(solution)/shard_map/ppermute | solution.py:16
  8.5 6.0 %collective-permute-start = (bf16[72,320]{1,0:T(8,128)(2,1)S(1)}, bf16[72,320]{1,0:T(8,128)(2,1)S(1)}, u32[]{:S(2)}, u32[]{:S(2)}) collective-permute-start(bf16[72,320]{1,0:T(8,128)(2,1)S(1)} %slice.30), channel_id=1, source_target_pairs={{12,0},{0,4},{4,8},{8,12},{13,1},{1,5},{5,9},{9,13},{14,2},{2,6},{... | collective-permute-start | bytes 138248 | tf_op jit(solution)/shard_map/ppermute | solution.py:16
  23.0 16.2 %all-to-all-start.2 = ((bf16[4,9,32,320]{3,2,1,0:T(8,128)(2,1)}), bf16[4,9,32,320]{3,2,1,0:T(8,128)(2,1)S(1)}, u32[]{:S(2)}, u32[]{:S(2)}) async-start(bf16[4,9,32,320]{3,2,1,0:T(8,128)(2,1)} %bitcast.27), calls=%async_computation.2 | async-start | bytes 1769472 | tf_op jit(solution)/shard_map/all_to_all | solution.py:196
  26.5 16.2 %copy-start.4 = (bf16[320,960]{1,0:T(8,128)(2,1)S(1)}, bf16[320,960]{1,0:T(8,128)(2,1)}, u32[]{:S(2)}) copy-start(bf16[320,960]{1,0:T(8,128)(2,1)} %param.8) | copy-start | bytes 1843204
  34.4 9.4 %copy-start.5 = (f32[5,4,4]{0,2,1:T(4,128)S(1)}, f32[5,4,4]{0,2,1:T(4,128)}, u32[]{:S(2)}) copy-start(f32[5,4,4]{0,2,1:T(4,128)} %param.10) | copy-start | bytes 964
  39.1 5.5 %copy-start.2 = (bf16[4,9,32,320]{3,2,1,0:T(8,128)(2,1)}, bf16[4,9,32,320]{3,2,1,0:T(8,128)(2,1)S(1)}, u32[]{:S(2)}) copy-start(bf16[4,9,32,320]{3,2,1,0:T(8,128)(2,1)S(1)} %all-to-all-done.2) | copy-start | bytes 2211844
  39.2 16.2 %all-to-all-start = ((bf16[4,9,32,320]{3,2,1,0:T(8,128)(2,1)}), bf16[4,9,32,320]{3,2,1,0:T(8,128)(2,1)S(1)}, u32[]{:S(2)}, u32[]{:S(2)}) async-start(bf16[4,9,32,320]{3,2,1,0:T(8,128)(2,1)} %bitcast.28), calls=%async_computation | async-start | bytes 1769472 | tf_op jit(solution)/shard_map/all_to_all | solution.py:196
  55.3 3.7 %copy-start.3 = (bf16[4,9,32,320]{3,2,1,0:T(8,128)(2,1)}, bf16[4,9,32,320]{3,2,1,0:T(8,128)(2,1)S(1)}, u32[]{:S(2)}) copy-start(bf16[4,9,32,320]{3,2,1,0:T(8,128)(2,1)S(1)} %all-to-all-done) | copy-start | bytes 2211844
  55.3 16.2 %all-to-all-start.3 = ((bf16[4,9,32,320]{3,2,1,0:T(8,128)(2,1)}), bf16[4,9,32,320]{3,2,1,0:T(8,128)(2,1)S(1)}, u32[]{:S(2)}, u32[]{:S(2)}) async-start(bf16[4,9,32,320]{3,2,1,0:T(8,128)(2,1)} %bitcast.42), calls=%async_computation.3 | async-start | bytes 1769472 | tf_op jit(solution)/shard_map/all_to_all | solution.py:198
  71.5 23.1 %copy-start = (bf16[4,9,32,320]{3,2,1,0:T(8,128)(2,1)}, bf16[4,9,32,320]{3,2,1,0:T(8,128)(2,1)S(1)}, u32[]{:S(2)}) copy-start(bf16[4,9,32,320]{3,2,1,0:T(8,128)(2,1)S(1)} %all-to-all-done.3) | copy-start | bytes 2211844
  71.5 16.2 %all-to-all-start.1 = ((bf16[4,9,32,320]{3,2,1,0:T(8,128)(2,1)}), bf16[4,9,32,320]{3,2,1,0:T(8,128)(2,1)S(1)}, u32[]{:S(2)}, u32[]{:S(2)}) async-start(bf16[4,9,32,320]{3,2,1,0:T(8,128)(2,1)} %bitcast.39), calls=%async_computation.1 | async-start | bytes 1769472 | tf_op jit(solution)/shard_map/all_to_all | solution.py:198
  87.7 6.9 %copy-start.1 = (bf16[4,9,32,320]{3,2,1,0:T(8,128)(2,1)}, bf16[4,9,32,320]{3,2,1,0:T(8,128)(2,1)S(1)}, u32[]{:S(2)}) copy-start(bf16[4,9,32,320]{3,2,1,0:T(8,128)(2,1)S(1)} %all-to-all-done.1) | copy-start | bytes 2211844
  87.9 4.2 %collective-permute-start.3 = (bf16[72,320]{1,0:T(8,128)(2,1)S(1)}, bf16[72,320]{1,0:T(8,128)(2,1)S(1)}, u32[]{:S(2)}, u32[]{:S(2)}) collective-permute-start(bf16[72,320]{1,0:T(8,128)(2,1)S(1)} %pad_maximum_fusion.1), channel_id=1, source_target_pairs={{4,0},{8,4},{12,8},{0,12},{5,1},{9,5},{13,9},{1,13},{6,2},{10,6},{... | collective-permute-start | bytes 138248 | tf_op jit(solution)/shard_map/ppermute | solution.py:16
  88.0 6.0 %collective-permute-start.2 = (bf16[72,320]{1,0:T(8,128)(2,1)S(1)}, bf16[72,320]{1,0:T(8,128)(2,1)S(1)}, u32[]{:S(2)}, u32[]{:S(2)}) collective-permute-start(bf16[72,320]{1,0:T(8,128)(2,1)S(1)} %pad_maximum_fusion), channel_id=1, source_target_pairs={{12,0},{0,4},{4,8},{8,12},{13,1},{1,5},{5,9},{9,13},{14,2},{2,6},{... | collective-permute-start | bytes 138248 | tf_op jit(solution)/shard_map/ppermute | solution.py:16

commit v11 on v8

--- a/solution.py
+++ b/solution.py
@@ -177,6 +177,31 @@
     )(grid, qkv_weight.T, pos_bias.transpose(0, 2, 1)[..., None], out_weight)
 
 
+def rotated_attention(part, qkv_weight, pos_bias, out_weight):
+    frames_all = lax.axis_size("frame")
+    me = lax.axis_index("frame")
+    rows, col_count, channels = part.shape
+    band = rows // frames_all
+    got = []
+    for s in range(frames_all):
+        piece = lax.dynamic_slice_in_dim(part, ((me + s) % frames_all) * band, band, axis=0)
+        if s:
+            piece = lax.ppermute(piece, "frame", [(i, (i + s) % frames_all) for i in range(frames_all)])
+        got.append(piece)
+    grid = jnp.stack(got).reshape(frames_all, band * col_count, channels)
+    source = (me - jnp.arange(frames_all)) % frames_all
+    bias = jnp.take(jnp.take(pos_bias, source, axis=1), source, axis=2)
+    attended = attend(grid, qkv_weight, bias, out_weight).reshape(frames_all, band, col_count, channels)
+    back = []
+    for s in range(frames_all):
+        piece = attended[s]
+        if s:
+            piece = lax.ppermute(piece, "frame", [(i, (i - s) % frames_all) for i in range(frames_all)])
+        back.append(piece)
+    order = (jnp.arange(frames_all) - me) % frames_all
+    return jnp.take(jnp.stack(back), order, axis=0).reshape(rows, col_count, channels)
+
+
 def body(latents, conv1_weight, qkv_weight, out_weight, pos_bias, conv2_weight):
     frames_dev, row_count, col_count, channels = latents.shape
     frames_all = lax.axis_size("frame")
@@ -192,7 +217,11 @@
         piece_shape = (frames_all, half // frames_all, col_count, channels)
     else:
         piece_shape = (frames_all, pix_piece, channels)
+    rotate = frames_all <= 4 and half % frames_all == 0
     for part in hidden:
+        if rotate:
+            returned.append(rotated_attention(part, qkv_weight, pos_bias, out_weight))
+            continue
         pieces = lax.all_to_all(part.reshape(piece_shape), "frame", split_axis=0, concat_axis=0, tiled=True)
         attended = attend(pieces.reshape(frames_all, pix_piece, channels), qkv_weight, pos_bias, out_weight)
         back = lax.all_to_all(attended.reshape(piece_shape), "frame", split_axis=0, concat_axis=0, tiled=True)

time: 106 us -> 100 us (0.943)
  waiting for transfers between devices: 35.7 us -> 23.3 us
  local copies, waits for them, and re-layouts: 6.54 us -> 13.1 us
  starting transfers between devices: 21.4 us -> 17 us
  other arithmetic: 2.58 us -> 6.66 us
    all_to_all x4 -> x0, waiting for transfers between devices: 26.4 us -> none  [the longest x2 16.9 us: body(): lax.all_to_all(attended.reshape(piece_shape), 'frame', split_axis=0, conc...]
    ppermute x0 -> x12, waiting for transfers between devices: none -> 16.2 us  [the longest x6 9.09 us: rotated_attention(): lax.ppermute(piece, 'frame', [(i, (i - s) % frames_all) for i in range(fr...]
    all_to_all x4 -> x0, starting transfers between devices: 14.2 us -> none  [the longest x2 7.18 us: body(): lax.all_to_all(attended.reshape(piece_shape), 'frame', split_axis=0, conc...]
    ppermute x0 -> x12, starting transfers between devices: none -> 9.59 us  [the longest x6 6.02 us: rotated_attention(): lax.ppermute(piece, 'frame', [(i, (i - s) % frames_all) for i in range(fr...]
    another operation x0 -> x4, other arithmetic: none -> 3.6 us  [the longest x2 2.24 us: rotated_attention(): grid = jnp.stack(got).reshape(frames_all, band * col_count, channels)]
    slice x0 -> x2, local copies, waits for them, and re-layouts: none -> 3.48 us  [rotated_attention(): piece = attended[s]]
    gather x0 -> x4, local copies, waits for them, and re-layouts: none -> 2.63 us  [the longest x2 1.48 us: rotated_attention(): jnp.take(jnp.stack(back), order, axis=0).reshape(rows, col_count, channels)]
    ppermute x4, waiting for transfers between devices: 9.3 us -> 7.12 us  [shifted(): moved = lax.ppermute(block, axis, route)]
  transfers between devices with their start and end apart: 8 -> 16, of which waited for: 8 -> 8; matrix products, arithmetic and copies ran while one was open for 5% -> 14% of each run, Pallas kernels for 19% -> 12%
where the time goes in v11:
time: 100 us
  Pallas kernels  39.6 us (40%)
  waiting for transfers between devices  23.3 us (23%)
  starting transfers between devices  17 us (17%)
  local copies, waits for them, and re-layouts  13.1 us (13%)
  other arithmetic  6.66 us (7%)
    pallas_call x3, Pallas kernels, convolve(): pl.pallas_call(functools.partial(conv_kernel, layout=tuple(layout), lo=lo...  27.7 us
    pallas_call x2, Pallas kernels, attend(): pl.pallas_call(attend_kernel, out_shape=jax.ShapeDtypeStruct((frames_all,...  11.9 us
    ppermute x6, waiting for transfers between devices, rotated_attention(): lax.ppermute(piece, 'frame', [(i, (i - s) % frames_all) for i in range(fr...  9.09 us
    ppermute x4, starting transfers between devices, shifted(): moved = lax.ppermute(block, axis, route)  7.46 us
    ppermute x4, waiting for transfers between devices, shifted(): moved = lax.ppermute(block, axis, route)  7.12 us
    ppermute x6, waiting for transfers between devices, rotated_attention(): lax.ppermute(piece, 'frame', [(i, (i + s) % frames_all) for i in range(fr...  7.06 us
    ppermute x6, starting transfers between devices, rotated_attention(): lax.ppermute(piece, 'frame', [(i, (i - s) % frames_all) for i in range(fr...  6.02 us
    unnamed x22, local copies, waits for them, and re-layouts  3.66 us
  transfers between devices with their start and end apart: 16, of which 8 were waited for; matrix products, arithmetic and copies ran while one was open for 14% of the time, Pallas kernels for 12%

profile of v11, /device:TPU:0, one launch (start us, length us, event | category | flops | bytes accessed | tf_op | source)
XLA Modules:
  0.0 100.0 jit_solution(7212780592132730462)
XLA Ops:
  0.0 2.2 %copy.67 = bf16[1,72,32,320]{3,1,2,0:T(8,128)(2,1)S(1)} copy(bf16[1,72,32,320]{3,2,1,0:T(8,128)(2,1)} %param.12) | data formatting | bytes 2949120 | tf_op args[0]
  2.2 5.1 %collective-permute-start.1 = (bf16[72,320]{1,0:T(8,128)(2,1)S(1)}, bf16[72,320]{1,0:T(8,128)(2,1)S(1)}, u32[]{:S(2)}, u32[]{:S(2)}) collective-permute-start(bf16[72,320]{1,0:T(8,128)(2,1)S(1)} %get-tuple-element.6), channel_id=1, source_target_pairs={{4,0},{8,4},{12,8},{0,12},{5,1},{9,5},{13,9},{1,13},{6,2},{10,6},{... | collective-permute-start | bytes 138248 | tf_op jit(solution)/shard_map/ppermute | solution.py:16
  8.7 0.8 copy.39.bias_ref
  9.6 1.2 %copy.37 = bf16[320,960]{0,1:T(8,128)(2,1)} copy(bf16[320,960]{1,0:T(8,128)(2,1)S(1)} %copy-done.5) | data formatting | bytes 1228800 | tf_op args[2]
  11.3 1.9 %collective-permute-done = bf16[72,320]{1,0:T(8,128)(2,1)S(1)} collective-permute-done((bf16[72,320]{1,0:T(8,128)(2,1)S(1)}, bf16[72,320]{1,0:T(8,128)(2,1)S(1)}, u32[]{:S(2)}, u32[]{:S(2)}) %collective-permute-start) | collective-permute-done | bytes 46112 | tf_op jit(solution)/shard_map/ppermute | solution.py:16
  13.9 7.9 %shard_map.64.refs_0_ = bf16[36,32,320]{2,1,0:T(8,128)(2,1)} custom-call(bf16[72,32,320]{2,1,0:T(8,128)(2,1)} %bitcast.52, bf16[72,320]{1,0:T(8,128)(2,1)} %broadcast_select_fusion.5.refs_1_, bf16[72,320]{1,0:T(8,128)(2,1)} %broadcast_select_fusion.3.refs_2_, bf16[3,960,320]{2,1,0:T(8,128)(2,1)} %bitcast.54), custom_call_target="tpu_custom_call" | custom-call | tf_op jit(solution)/shard_map/pallas_call | solution.py:100
  21.8 7.9 %shard_map.65.refs_1_ = bf16[36,32,320]{2,1,0:T(8,128)(2,1)} custom-call(bf16[72,32,320]{2,1,0:T(8,128)(2,1)} %bitcast.53, bf16[72,320]{1,0:T(8,128)(2,1)} %broadcast_select_fusion.5.refs_1_, bf16[72,320]{1,0:T(8,128)(2,1)} %broadcast_select_fusion.3.refs_2_, bf16[3,960,320]{2,1,0:T(8,128)(2,1)} %bitcast.55), custom_call_target="tpu_custom_call" | custom-call | tf_op jit(solution)/shard_map/pallas_call | solution.py:100
  29.8 1.6 %collective-permute-start.3 = (bf16[9,32,320]{2,1,0:T(8,128)(2,1)S(1)}, bf16[9,32,320]{2,1,0:T(8,128)(2,1)S(1)}, u32[]{:S(2)}, u32[]{:S(2)}) collective-permute-start(bf16[9,32,320]{2,1,0:T(8,128)(2,1)S(1)} %get-tuple-element.32), channel_id=1, source_target_pairs={{0,2},{1,3},{2,0},{3,1},{4,6},{5,7},{6,4},{7,5},{8,10},{9,11},{10,... | collective-permute-start | bytes 552968 | tf_op jit(solution)/shard_map/ppermute | solution.py:189
  31.4 1.4 %collective-permute-start.4 = (bf16[9,32,320]{2,1,0:T(8,128)(2,1)S(1)}, bf16[9,32,320]{2,1,0:T(8,128)(2,1)S(1)}, u32[]{:S(2)}, u32[]{:S(2)}) collective-permute-start(bf16[9,32,320]{2,1,0:T(8,128)(2,1)S(1)} %get-tuple-element.31), channel_id=1, source_target_pairs={{0,3},{1,0},{2,1},{3,2},{4,7},{5,4},{6,5},{7,6},{8,11},{9,8},{10,9... | collective-permute-start | bytes 552968 | tf_op jit(solution)/shard_map/ppermute | solution.py:189
  32.8 0.8 constant_dynamic-slice_fusion.3
  34.1 0.7 fusion.6
  34.9 2.1 %collective-permute-done.2 = bf16[9,32,320]{2,1,0:T(8,128)(2,1)S(1)} collective-permute-done((bf16[9,32,320]{2,1,0:T(8,128)(2,1)S(1)}, bf16[9,32,320]{2,1,0:T(8,128)(2,1)S(1)}, u32[]{:S(2)}, u32[]{:S(2)}) %collective-permute-start.2) | collective-permute-done | bytes 184352 | tf_op jit(solution)/shard_map/ppermute | solution.py:189
  36.9 1.2 %collective-permute-done.3 = bf16[9,32,320]{2,1,0:T(8,128)(2,1)S(1)} collective-permute-done((bf16[9,32,320]{2,1,0:T(8,128)(2,1)S(1)}, bf16[9,32,320]{2,1,0:T(8,128)(2,1)S(1)}, u32[]{:S(2)}, u32[]{:S(2)}) %collective-permute-start.3) | collective-permute-done | bytes 184352 | tf_op jit(solution)/shard_map/ppermute | solution.py:189
  38.1 3.8 %collective-permute-done.4 = bf16[9,32,320]{2,1,0:T(8,128)(2,1)S(1)} collective-permute-done((bf16[9,32,320]{2,1,0:T(8,128)(2,1)S(1)}, bf16[9,32,320]{2,1,0:T(8,128)(2,1)S(1)}, u32[]{:S(2)}, u32[]{:S(2)}) %collective-permute-start.4) | collective-permute-done | bytes 184352 | tf_op jit(solution)/shard_map/ppermute | solution.py:189
  41.9 1.1 %pad_maximum_fusion.x_ref = bf16[4,288,320]{2,1,0:T(8,128)(2,1)} fusion(bf16[1,288,320]{2,1,0:T(8,128)(2,1)S(1)} %bitcast.81, bf16[1,288,320]{2,1,0:T(8,128)(2,1)S(1)} %bitcast.80, bf16[1,288,320]{2,1,0:T(8,128)(2,1)S(1)} %bitcast.77, bf16[1,288,320]{2,1,0:T(8,128)(2,1)S(1)} %bitcast.67), kind=kLoop, calls=%fused_computation.5 | loop fusion | flops 1105920 | bytes 1474560 | tf_op jit(solution)/shard_map/stack | solution.py:191
  43.0 5.9 %shard_map.66 = bf16[4,288,320]{2,1,0:T(8,128)(2,1)} custom-call(bf16[4,288,320]{2,1,0:T(8,128)(2,1)} %pad_maximum_fusion.x_ref, bf16[960,320]{1,0:T(8,128)(2,1)} %bitcast.56, f32[5,4,4,1]{3,2,1,0:T(4,128)} %copy.39.bias_ref, bf16[320,320]{1,0:T(8,128)(2,1)} %wout_ref.3), custom_call_target="tpu_custom_call" | custom-call | tf_op jit(solution)/shard_map/pallas_call | solution.py:168
  49.0 1.4 %fusion.11 = (bf16[1,288,320]{2,1,0:T(8,128)(2,1)S(1)}, bf16[1,288,320]{2,1,0:T(8,128)(2,1)S(1)}, bf16[1,288,320]{2,1,0:T(8,128)(2,1)S(1)}, bf16[1,288,320]{2,1,0:T(8,128)(2,1)S(1)}) fusion(bf16[4,288,320]{2,1,0:T(8,128)(2,1)} %shard_map.66), kind=kLoop, calls=%fused_computation.56 | loop fusion | bytes 1474560 | tf_op jit(solution)/shard_map/slice | solution.py:197
  50.3 2.3 %collective-permute-start.5 = (bf16[9,32,320]{2,1,0:T(8,128)(2,1)S(1)}, bf16[9,32,320]{2,1,0:T(8,128)(2,1)S(1)}, u32[]{:S(2)}, u32[]{:S(2)}) collective-permute-start(bf16[9,32,320]{2,1,0:T(8,128)(2,1)S(1)} %bitcast.75), channel_id=1, source_target_pairs={{0,3},{1,0},{2,1},{3,2},{4,7},{5,4},{6,5},{7,6},{8,11},{9,8},{10,9... | collective-permute-start | bytes 552968 | tf_op jit(solution)/shard_map/ppermute | solution.py:199
  53.1 1.1 %pad_maximum_fusion.2.x_ref = bf16[4,288,320]{2,1,0:T(8,128)(2,1)} fusion(bf16[1,288,320]{2,1,0:T(8,128)(2,1)S(1)} %bitcast.76, bf16[1,288,320]{2,1,0:T(8,128)(2,1)S(1)} %bitcast.73, bf16[1,288,320]{2,1,0:T(8,128)(2,1)S(1)} %bitcast.70, bf16[1,288,320]{2,1,0:T(8,128)(2,1)S(1)} %bitcast.66), kind=kLoop, calls=%fused_computation.7 | loop fusion | flops 1105920 | bytes 1474560 | tf_op jit(solution)/shard_map/stack | solution.py:191
  54.2 5.9 %shard_map.67 = bf16[4,288,320]{2,1,0:T(8,128)(2,1)} custom-call(bf16[4,288,320]{2,1,0:T(8,128)(2,1)} %pad_maximum_fusion.2.x_ref, bf16[960,320]{1,0:T(8,128)(2,1)} %bitcast.57, f32[5,4,4,1]{3,2,1,0:T(4,128)} %copy.39.bias_ref, bf16[320,320]{1,0:T(8,128)(2,1)} %wout_ref.3), custom_call_target="tpu_custom_call" | custom-call | tf_op jit(solution)/shard_map/pallas_call | solution.py:168
  60.2 2.1 %fusion.10 = (bf16[1,288,320]{2,1,0:T(8,128)(2,1)S(1)}, bf16[1,288,320]{2,1,0:T(8,128)(2,1)S(1)}, bf16[1,288,320]{2,1,0:T(8,128)(2,1)}, bf16[1,288,320]{2,1,0:T(8,128)(2,1)}) fusion(bf16[4,288,320]{2,1,0:T(8,128)(2,1)} %shard_map.67), kind=kLoop, calls=%fused_computation.55 | loop fusion | bytes 1474560 | tf_op jit(solution)/shard_map/slice | solution.py:197
  62.3 1.7 %collective-permute-start.11 = (bf16[9,32,320]{2,1,0:T(8,128)(2,1)}, bf16[9,32,320]{2,1,0:T(8,128)(2,1)S(1)}, u32[]{:S(2)}, u32[]{:S(2)}) collective-permute-start(bf16[9,32,320]{2,1,0:T(8,128)(2,1)} %bitcast.27), channel_id=1, source_target_pairs={{0,3},{1,0},{2,1},{3,2},{4,7},{5,4},{6,5},{7,6},{8,11},{9,8},{10,9... | collective-permute-start | bytes 552968 | tf_op jit(solution)/shard_map/ppermute | solution.py:199
  64.0 1.5 %collective-permute-start.12 = (bf16[9,32,320]{2,1,0:T(8,128)(2,1)}, bf16[9,32,320]{2,1,0:T(8,128)(2,1)}, u32[]{:S(2)}, u32[]{:S(2)}) collective-permute-start(bf16[9,32,320]{2,1,0:T(8,128)(2,1)} %bitcast.29), channel_id=1, source_target_pairs={{0,2},{1,3},{2,0},{3,1},{4,6},{5,7},{6,4},{7,5},{8,10},{9,11},{10,... | collective-permute-start | bytes 552968 | tf_op jit(solution)/shard_map/ppermute | solution.py:199
  66.5 0.7 gather_fusion.2
  67.3 2.8 %collective-permute-done.11 = bf16[9,32,320]{2,1,0:T(8,128)(2,1)S(1)} collective-permute-done((bf16[9,32,320]{2,1,0:T(8,128)(2,1)}, bf16[9,32,320]{2,1,0:T(8,128)(2,1)S(1)}, u32[]{:S(2)}, u32[]{:S(2)}) %collective-permute-start.11) | collective-permute-done | bytes 184352 | tf_op jit(solution)/shard_map/ppermute | solution.py:199
  70.1 6.2 %collective-permute-done.12 = bf16[9,32,320]{2,1,0:T(8,128)(2,1)} collective-permute-done((bf16[9,32,320]{2,1,0:T(8,128)(2,1)}, bf16[9,32,320]{2,1,0:T(8,128)(2,1)}, u32[]{:S(2)}, u32[]{:S(2)}) %collective-permute-start.12) | collective-permute-done | bytes 184352 | tf_op jit(solution)/shard_map/ppermute | solution.py:199
  76.3 1.1 %pad_maximum_fusion.3 = bf16[4,9,32,320]{3,2,1,0:T(8,128)(2,1)S(1)} fusion(bf16[1,9,32,320]{3,2,1,0:T(8,128)(2,1)S(1)} %bitcast.82, bf16[1,9,32,320]{3,2,1,0:T(8,128)(2,1)} %bitcast.30, bf16[1,9,32,320]{3,2,1,0:T(8,128)(2,1)S(1)} %bitcast.79, bf16[1,9,32,320]{3,2,1,0:T(8,128)(2,1)S(1)} %bitcast.65), kind=kLoop, calls=%fused_computation.8 | loop fusion | flops 1105920 | bytes 1474560 | tf_op jit(solution)/shard_map/stack | solution.py:202
  77.5 0.7 gather_fusion.3
  79.1 2.0 %collective-permute-start.15 = (bf16[72,320]{1,0:T(8,128)(2,1)S(1)}, bf16[72,320]{1,0:T(8,128)(2,1)S(1)}, u32[]{:S(2)}, u32[]{:S(2)}) collective-permute-start(bf16[72,320]{1,0:T(8,128)(2,1)S(1)} %pad_maximum_fusion.5), channel_id=1, source_target_pairs={{4,0},{8,4},{12,8},{0,12},{5,1},{9,5},{13,9},{1,13},{6,2},{10,6},{... | collective-permute-start | bytes 138248 | tf_op jit(solution)/shard_map/ppermute | solution.py:16
  81.5 2.4 %collective-permute-done.15 = bf16[72,320]{1,0:T(8,128)(2,1)S(1)} collective-permute-done((bf16[72,320]{1,0:T(8,128)(2,1)S(1)}, bf16[72,320]{1,0:T(8,128)(2,1)S(1)}, u32[]{:S(2)}, u32[]{:S(2)}) %collective-permute-start.15) | collective-permute-done | bytes 46112 | tf_op jit(solution)/shard_map/ppermute | solution.py:16
  84.6 2.8 %collective-permute-done.14 = bf16[72,320]{1,0:T(8,128)(2,1)S(1)} collective-permute-done((bf16[72,320]{1,0:T(8,128)(2,1)S(1)}, bf16[72,320]{1,0:T(8,128)(2,1)S(1)}, u32[]{:S(2)}, u32[]{:S(2)}) %collective-permute-start.14) | collective-permute-done | bytes 46112 | tf_op jit(solution)/shard_map/ppermute | solution.py:16
  88.0 11.9 %shard_map.68 = bf16[72,32,320]{2,1,0:T(8,128)(2,1)} custom-call(bf16[36,32,320]{2,1,0:T(8,128)(2,1)} %shard_map.64.refs_0_, bf16[36,32,320]{2,1,0:T(8,128)(2,1)} %shard_map.65.refs_1_, bf16[36,32,320]{2,1,0:T(8,128)(2,1)} %bitcast.61, bf16[36,32,320]{2,1,0:T(8,128)(2,1)} %bitcast.59, bf16[72,320]{1,0:T(8,128)(2,1)} %broadcast_select_fusion.4.refs_4_, ...), custom_call_target="tpu_custom_call" | custom-call | tf_op jit(solution)/shard_map/pallas_call | solution.py:100
  (64 shorter events, 7.3 us)
Async XLA Ops:
  0.0 7.4 %copy-start = (f32[5,4,4]{0,2,1:T(4,128)S(1)}, f32[5,4,4]{0,2,1:T(4,128)}, u32[]{:S(2)}) copy-start(f32[5,4,4]{0,2,1:T(4,128)} %param.16) | copy-start | bytes 964
  0.0 9.6 %copy-start.5 = (bf16[320,960]{1,0:T(8,128)(2,1)S(1)}, bf16[320,960]{1,0:T(8,128)(2,1)}, u32[]{:S(2)}) copy-start(bf16[320,960]{1,0:T(8,128)(2,1)} %param.14) | copy-start | bytes 1843204
  2.2 8.5 %collective-permute-start.1 = (bf16[72,320]{1,0:T(8,128)(2,1)S(1)}, bf16[72,320]{1,0:T(8,128)(2,1)S(1)}, u32[]{:S(2)}, u32[]{:S(2)}) collective-permute-start(bf16[72,320]{1,0:T(8,128)(2,1)S(1)} %get-tuple-element.6), channel_id=1, source_target_pairs={{4,0},{8,4},{12,8},{0,12},{5,1},{9,5},{13,9},{1,13},{6,2},{10,6},{... | collective-permute-start | bytes 138248 | tf_op jit(solution)/shard_map/ppermute | solution.py:16
  7.3 6.0 %collective-permute-start = (bf16[72,320]{1,0:T(8,128)(2,1)S(1)}, bf16[72,320]{1,0:T(8,128)(2,1)S(1)}, u32[]{:S(2)}, u32[]{:S(2)}) collective-permute-start(bf16[72,320]{1,0:T(8,128)(2,1)S(1)} %get-tuple-element.8), channel_id=1, source_target_pairs={{12,0},{0,4},{4,8},{8,12},{13,1},{1,5},{5,9},{9,13},{14,2},{2,6},{... | collective-permute-start | bytes 138248 | tf_op jit(solution)/shard_map/ppermute | solution.py:16
  21.8 7.9 %copy-start.1 = (bf16[36,32,320]{2,1,0:T(8,128)(2,1)S(1)}, bf16[36,32,320]{2,1,0:T(8,128)(2,1)}, u32[]{:S(2)}) copy-start(bf16[36,32,320]{2,1,0:T(8,128)(2,1)} %shard_map.64.refs_0_) | copy-start | bytes 2211844
  29.6 3.2 %copy-start.2 = (bf16[36,32,320]{2,1,0:T(8,128)(2,1)S(1)}, bf16[36,32,320]{2,1,0:T(8,128)(2,1)}, u32[]{:S(2)}) copy-start(bf16[36,32,320]{2,1,0:T(8,128)(2,1)} %shard_map.65.refs_1_) | copy-start | bytes 2211844
  29.8 7.2 %collective-permute-start.2 = (bf16[9,32,320]{2,1,0:T(8,128)(2,1)S(1)}, bf16[9,32,320]{2,1,0:T(8,128)(2,1)S(1)}, u32[]{:S(2)}, u32[]{:S(2)}) collective-permute-start(bf16[9,32,320]{2,1,0:T(8,128)(2,1)S(1)} %get-tuple-element.33), channel_id=1, source_target_pairs={{0,1},{1,2},{2,3},{3,0},{4,5},{5,6},{6,7},{7,4},{8,9},{9,10},{10,1... | collective-permute-start | bytes 552968 | tf_op jit(solution)/shard_map/ppermute | solution.py:189
  29.8 8.3 %collective-permute-start.3 = (bf16[9,32,320]{2,1,0:T(8,128)(2,1)S(1)}, bf16[9,32,320]{2,1,0:T(8,128)(2,1)S(1)}, u32[]{:S(2)}, u32[]{:S(2)}) collective-permute-start(bf16[9,32,320]{2,1,0:T(8,128)(2,1)S(1)} %get-tuple-element.32), channel_id=1, source_target_pairs={{0,2},{1,3},{2,0},{3,1},{4,6},{5,7},{6,4},{7,5},{8,10},{9,11},{10,... | collective-permute-start | bytes 552968 | tf_op jit(solution)/shard_map/ppermute | solution.py:189
  31.4 10.5 %collective-permute-start.4 = (bf16[9,32,320]{2,1,0:T(8,128)(2,1)S(1)}, bf16[9,32,320]{2,1,0:T(8,128)(2,1)S(1)}, u32[]{:S(2)}, u32[]{:S(2)}) collective-permute-start(bf16[9,32,320]{2,1,0:T(8,128)(2,1)S(1)} %get-tuple-element.31), channel_id=1, source_target_pairs={{0,3},{1,0},{2,1},{3,2},{4,7},{5,4},{6,5},{7,6},{8,11},{9,8},{10,9... | collective-permute-start | bytes 552968 | tf_op jit(solution)/shard_map/ppermute | solution.py:189
  33.6 19.5 %collective-permute-start.8 = (bf16[9,32,320]{2,1,0:T(8,128)(2,1)S(1)}, bf16[9,32,320]{2,1,0:T(8,128)(2,1)S(1)}, u32[]{:S(2)}, u32[]{:S(2)}) collective-permute-start(bf16[9,32,320]{2,1,0:T(8,128)(2,1)S(1)} %get-tuple-element.25), channel_id=1, source_target_pairs={{0,1},{1,2},{2,3},{3,0},{4,5},{5,6},{6,7},{7,4},{8,9},{9,10},{10,1... | collective-permute-start | bytes 552968 | tf_op jit(solution)/shard_map/ppermute | solution.py:189
  33.6 19.5 %collective-permute-start.9 = (bf16[9,32,320]{2,1,0:T(8,128)(2,1)}, bf16[9,32,320]{2,1,0:T(8,128)(2,1)S(1)}, u32[]{:S(2)}, u32[]{:S(2)}) collective-permute-start(bf16[9,32,320]{2,1,0:T(8,128)(2,1)} %get-tuple-element.24), channel_id=1, source_target_pairs={{0,2},{1,3},{2,0},{3,1},{4,6},{5,7},{6,4},{7,5},{8,10},{9,11},{10,... | collective-permute-start | bytes 552968 | tf_op jit(solution)/shard_map/ppermute | solution.py:189
  36.9 16.2 %collective-permute-start.10 = (bf16[9,32,320]{2,1,0:T(8,128)(2,1)S(1)}, bf16[9,32,320]{2,1,0:T(8,128)(2,1)S(1)}, u32[]{:S(2)}, u32[]{:S(2)}) collective-permute-start(bf16[9,32,320]{2,1,0:T(8,128)(2,1)S(1)} %get-tuple-element.23), channel_id=1, source_target_pairs={{0,3},{1,0},{2,1},{3,2},{4,7},{5,4},{6,5},{7,6},{8,11},{9,8},{10,9... | collective-permute-start | bytes 552968 | tf_op jit(solution)/shard_map/ppermute | solution.py:189
  50.3 15.2 %collective-permute-start.5 = (bf16[9,32,320]{2,1,0:T(8,128)(2,1)S(1)}, bf16[9,32,320]{2,1,0:T(8,128)(2,1)S(1)}, u32[]{:S(2)}, u32[]{:S(2)}) collective-permute-start(bf16[9,32,320]{2,1,0:T(8,128)(2,1)S(1)} %bitcast.75), channel_id=1, source_target_pairs={{0,3},{1,0},{2,1},{3,2},{4,7},{5,4},{6,5},{7,6},{8,11},{9,8},{10,9... | collective-permute-start | bytes 552968 | tf_op jit(solution)/shard_map/ppermute | solution.py:199
  52.6 13.7 %collective-permute-start.6 = (bf16[9,32,320]{2,1,0:T(8,128)(2,1)S(1)}, bf16[9,32,320]{2,1,0:T(8,128)(2,1)S(1)}, u32[]{:S(2)}, u32[]{:S(2)}) collective-permute-start(bf16[9,32,320]{2,1,0:T(8,128)(2,1)S(1)} %bitcast.71), channel_id=1, source_target_pairs={{0,2},{1,3},{2,0},{3,1},{4,6},{5,7},{6,4},{7,5},{8,10},{9,11},{10,... | collective-permute-start | bytes 552968 | tf_op jit(solution)/shard_map/ppermute | solution.py:199
  53.1 13.2 %collective-permute-start.7 = (bf16[9,32,320]{2,1,0:T(8,128)(2,1)S(1)}, bf16[9,32,320]{2,1,0:T(8,128)(2,1)S(1)}, u32[]{:S(2)}, u32[]{:S(2)}) collective-permute-start(bf16[9,32,320]{2,1,0:T(8,128)(2,1)S(1)} %bitcast.68), channel_id=1, source_target_pairs={{0,1},{1,2},{2,3},{3,0},{4,5},{5,6},{6,7},{7,4},{8,9},{9,10},{10,1... | collective-permute-start | bytes 552968 | tf_op jit(solution)/shard_map/ppermute | solution.py:199
  62.3 7.8 %collective-permute-start.11 = (bf16[9,32,320]{2,1,0:T(8,128)(2,1)}, bf16[9,32,320]{2,1,0:T(8,128)(2,1)S(1)}, u32[]{:S(2)}, u32[]{:S(2)}) collective-permute-start(bf16[9,32,320]{2,1,0:T(8,128)(2,1)} %bitcast.27), channel_id=1, source_target_pairs={{0,3},{1,0},{2,1},{3,2},{4,7},{5,4},{6,5},{7,6},{8,11},{9,8},{10,9... | collective-permute-start | bytes 552968 | tf_op jit(solution)/shard_map/ppermute | solution.py:199
  64.0 12.3 %collective-permute-start.12 = (bf16[9,32,320]{2,1,0:T(8,128)(2,1)}, bf16[9,32,320]{2,1,0:T(8,128)(2,1)}, u32[]{:S(2)}, u32[]{:S(2)}) collective-permute-start(bf16[9,32,320]{2,1,0:T(8,128)(2,1)} %bitcast.29), channel_id=1, source_target_pairs={{0,2},{1,3},{2,0},{3,1},{4,6},{5,7},{6,4},{7,5},{8,10},{9,11},{10,... | collective-permute-start | bytes 552968 | tf_op jit(solution)/shard_map/ppermute | solution.py:199
  65.6 10.8 %collective-permute-start.13 = (bf16[9,32,320]{2,1,0:T(8,128)(2,1)S(1)}, bf16[9,32,320]{2,1,0:T(8,128)(2,1)S(1)}, u32[]{:S(2)}, u32[]{:S(2)}) collective-permute-start(bf16[9,32,320]{2,1,0:T(8,128)(2,1)S(1)} %bitcast.78), channel_id=1, source_target_pairs={{0,1},{1,2},{2,3},{3,0},{4,5},{5,6},{6,7},{7,4},{8,9},{9,10},{10,1... | collective-permute-start | bytes 552968 | tf_op jit(solution)/shard_map/ppermute | solution.py:199
  78.2 0.8 copy-start.7
  78.2 0.8 copy-start.9
  78.3 2.9 %copy-start.6 = (bf16[36,1,320]{2,1,0:T(2,128)(2,1)S(1)}, bf16[36,1,320]{2,1,0:T(2,128)(2,1)}, u32[]{:S(2)}) copy-start(bf16[36,1,320]{2,1,0:T(2,128)(2,1)} %get-tuple-element.11) | copy-start | bytes 69124
  78.3 2.9 %copy-start.8 = (bf16[36,1,320]{2,1,0:T(2,128)(2,1)S(1)}, bf16[36,1,320]{2,1,0:T(2,128)(2,1)}, u32[]{:S(2)}) copy-start(bf16[36,1,320]{2,1,0:T(2,128)(2,1)} %get-tuple-element.15) | copy-start | bytes 69124
  78.5 9.5 %copy-start.3 = (bf16[4,9,32,320]{3,2,1,0:T(8,128)(2,1)}, bf16[4,9,32,320]{3,2,1,0:T(8,128)(2,1)S(1)}, u32[]{:S(2)}) copy-start(bf16[4,9,32,320]{3,2,1,0:T(8,128)(2,1)S(1)} %get-tuple-element.34) | copy-start | bytes 2211844
  78.6 9.5 %copy-start.4 = (bf16[4,9,32,320]{3,2,1,0:T(8,128)(2,1)}, bf16[4,9,32,320]{3,2,1,0:T(8,128)(2,1)S(1)}, u32[]{:S(2)}) copy-start(bf16[4,9,32,320]{3,2,1,0:T(8,128)(2,1)S(1)} %get-tuple-element.35) | copy-start | bytes 2211844
  79.1 4.8 %collective-permute-start.15 = (bf16[72,320]{1,0:T(8,128)(2,1)S(1)}, bf16[72,320]{1,0:T(8,128)(2,1)S(1)}, u32[]{:S(2)}, u32[]{:S(2)}) collective-permute-start(bf16[72,320]{1,0:T(8,128)(2,1)S(1)} %pad_maximum_fusion.5), channel_id=1, source_target_pairs={{4,0},{8,4},{12,8},{0,12},{5,1},{9,5},{13,9},{1,13},{6,2},{10,6},{... | collective-permute-start | bytes 138248 | tf_op jit(solution)/shard_map/ppermute | solution.py:16
  81.2 6.2 %collective-permute-start.14 = (bf16[72,320]{1,0:T(8,128)(2,1)S(1)}, bf16[72,320]{1,0:T(8,128)(2,1)S(1)}, u32[]{:S(2)}, u32[]{:S(2)}) collective-permute-start(bf16[72,320]{1,0:T(8,128)(2,1)S(1)} %pad_maximum_fusion.4), channel_id=1, source_target_pairs={{12,0},{0,4},{4,8},{8,12},{13,1},{1,5},{5,9},{9,13},{14,2},{2,6},{... | collective-permute-start | bytes 138248 | tf_op jit(solution)/shard_map/ppermute | solution.py:16

commit v12 on v11

--- a/solution.py
+++ b/solution.py
@@ -177,14 +177,14 @@
     )(grid, qkv_weight.T, pos_bias.transpose(0, 2, 1)[..., None], out_weight)
 
 
-def rotated_attention(part, qkv_weight, pos_bias, out_weight):
+def rotated_attention(source, lo, rows, qkv_weight, pos_bias, out_weight):
     frames_all = lax.axis_size("frame")
     me = lax.axis_index("frame")
-    rows, col_count, channels = part.shape
+    _, col_count, channels = source.shape
     band = rows // frames_all
     got = []
     for s in range(frames_all):
-        piece = lax.dynamic_slice_in_dim(part, ((me + s) % frames_all) * band, band, axis=0)
+        piece = lax.dynamic_slice_in_dim(source, lo + ((me + s) % frames_all) * band, band, axis=0)
         if s:
             piece = lax.ppermute(piece, "frame", [(i, (i + s) % frames_all) for i in range(frames_all)])
         got.append(piece)
@@ -208,20 +208,25 @@
     tile = latents.reshape(row_count, col_count, channels)
     rims = halo(lambda c: tile[:, c, :])
     half = row_count // 2
-    hidden = []
     returned = []
-    for lo in (0, half):
-        hidden.append(convolve([[tile]], rims, conv1_weight, norm_gelu, lo, lo + half))
+    rotate = frames_all <= 4 and half % frames_all == 0
+    if rotate:
+        whole = convolve([[tile]], rims, conv1_weight, norm_gelu, 0, row_count)
+        for lo in (0, half):
+            returned.append(rotated_attention(whole, lo, half, qkv_weight, pos_bias, out_weight))
+        hidden_rows = [whole]
+        hidden = [whole[:half], whole[half:]]
+    else:
+        hidden = [convolve([[tile]], rims, conv1_weight, norm_gelu, lo, lo + half) for lo in (0, half)]
+        hidden_rows = hidden
     pix_piece = half * col_count // frames_all
     if half % frames_all == 0:
         piece_shape = (frames_all, half // frames_all, col_count, channels)
     else:
         piece_shape = (frames_all, pix_piece, channels)
-    rotate = frames_all <= 4 and half % frames_all == 0
     for part in hidden:
         if rotate:
-            returned.append(rotated_attention(part, qkv_weight, pos_bias, out_weight))
-            continue
+            break
         pieces = lax.all_to_all(part.reshape(piece_shape), "frame", split_axis=0, concat_axis=0, tiled=True)
         attended = attend(pieces.reshape(frames_all, pix_piece, channels), qkv_weight, pos_bias, out_weight)
         back = lax.all_to_all(attended.reshape(piece_shape), "frame", split_axis=0, concat_axis=0, tiled=True)
@@ -231,7 +236,7 @@
         summed = [h[:, c, :].astype(jnp.float32) + r[:, c, :].astype(jnp.float32) for h, r in zip(hidden, returned)]
         return jnp.concatenate(summed, axis=0).astype(jnp.bfloat16)
 
-    second = convolve([hidden, returned], halo(joined_edge), conv2_weight, to_bf16, 0, row_count)
+    second = convolve([hidden_rows, returned], halo(joined_edge), conv2_weight, to_bf16, 0, row_count)
     return second.reshape(frames_dev, row_count, col_count, channels)
 
 

time: 100 us -> 98.4 us (0.984)
  Pallas kernels: 39.6 us -> 36.4 us
  local copies, waits for them, and re-layouts: 13.1 us -> 14.6 us
    pallas_call x3 -> x2, Pallas kernels: 27.7 us -> 24.6 us  [convolve(): pl.pallas_call(functools.partial(conv_kernel, layout=tuple(layout), lo=lo...]
    ppermute x6, waiting for transfers between devices: 9.09 us -> 7.37 us  [rotated_attention(): lax.ppermute(piece, 'frame', [(i, (i - s) % frames_all) for i in range(fr...]
    ppermute x6, waiting for transfers between devices: 7.06 us -> 8.46 us  [rotated_attention(): lax.ppermute(piece, 'frame', [(i, (i + s) % frames_all) for i in range(fr...]
    slice x2 -> x1, local copies, waits for them, and re-layouts: 1.47 us -> 2.14 us  [joined_edge(): h[:, c, :].astype(jnp.float32) + r[:, c, :].astype(jnp.float32)]
    unnamed x22 -> x18, local copies, waits for them, and re-layouts: 3.66 us -> 3.65 us
where the time goes in v12:
time: 98.4 us; the launch traced here: 98 us
  Pallas kernels  36.4 us (37%)
  waiting for transfers between devices  23 us (23%)
  starting transfers between devices  17.1 us (17%)
  local copies, waits for them, and re-layouts  14.6 us (15%)
  other arithmetic  6.69 us (7%)
    pallas_call x2, Pallas kernels, convolve(): pl.pallas_call(functools.partial(conv_kernel, layout=tuple(layout), lo=lo...  24.6 us
    pallas_call x2, Pallas kernels, attend(): pl.pallas_call(attend_kernel, out_shape=jax.ShapeDtypeStruct((frames_all,...  11.9 us
    ppermute x6, waiting for transfers between devices, rotated_attention(): lax.ppermute(piece, 'frame', [(i, (i + s) % frames_all) for i in range(fr...  8.46 us
    ppermute x4, starting transfers between devices, shifted(): moved = lax.ppermute(block, axis, route)  7.46 us
    ppermute x6, waiting for transfers between devices, rotated_attention(): lax.ppermute(piece, 'frame', [(i, (i - s) % frames_all) for i in range(fr...  7.37 us
    ppermute x4, waiting for transfers between devices, shifted(): moved = lax.ppermute(block, axis, route)  7.13 us
    ppermute x6, starting transfers between devices, rotated_attention(): lax.ppermute(piece, 'frame', [(i, (i - s) % frames_all) for i in range(fr...  6.02 us
    ppermute x6, starting transfers between devices, rotated_attention(): lax.ppermute(piece, 'frame', [(i, (i + s) % frames_all) for i in range(fr...  3.66 us
  transfers between devices with their start and end apart: 16, of which 8 were waited for; matrix products, arithmetic and copies ran while one was open for 14% of the time, Pallas kernels for 12%

profile of v12, /device:TPU:0, one launch (start us, length us, event | category | flops | bytes accessed | tf_op | source)
XLA Modules:
  0.0 98.0 jit_solution(8715027603162872141)
XLA Ops:
  0.0 2.2 %copy.64 = bf16[1,72,32,320]{3,1,2,0:T(8,128)(2,1)S(1)} copy(bf16[1,72,32,320]{3,2,1,0:T(8,128)(2,1)} %param.12) | data formatting | bytes 2949120 | tf_op args[0]
  2.2 5.1 %collective-permute-start.1 = (bf16[72,320]{1,0:T(8,128)(2,1)S(1)}, bf16[72,320]{1,0:T(8,128)(2,1)S(1)}, u32[]{:S(2)}, u32[]{:S(2)}) collective-permute-start(bf16[72,320]{1,0:T(8,128)(2,1)S(1)} %get-tuple-element.20), channel_id=1, source_target_pairs={{4,0},{8,4},{12,8},{0,12},{5,1},{9,5},{13,9},{1,13},{6,2},{10,6},{... | collective-permute-start | bytes 138248 | tf_op jit(solution)/shard_map/ppermute | solution.py:16
  8.7 0.8 copy.36.bias_ref
  9.5 1.2 %copy.34 = bf16[320,960]{0,1:T(8,128)(2,1)} copy(bf16[320,960]{1,0:T(8,128)(2,1)S(1)} %copy-done.3) | data formatting | bytes 1228800 | tf_op args[2]
  11.3 2.0 %collective-permute-done = bf16[72,320]{1,0:T(8,128)(2,1)S(1)} collective-permute-done((bf16[72,320]{1,0:T(8,128)(2,1)S(1)}, bf16[72,320]{1,0:T(8,128)(2,1)S(1)}, u32[]{:S(2)}, u32[]{:S(2)}) %collective-permute-start) | collective-permute-done | bytes 46112 | tf_op jit(solution)/shard_map/ppermute | solution.py:16
  13.9 12.6 %shard_map.64.refs_0_ = bf16[72,32,320]{2,1,0:T(8,128)(2,1)} custom-call(bf16[72,32,320]{2,1,0:T(8,128)(2,1)} %bitcast.52, bf16[72,320]{1,0:T(8,128)(2,1)} %broadcast_select_fusion.5.refs_1_, bf16[72,320]{1,0:T(8,128)(2,1)} %broadcast_select_fusion.3.refs_2_, bf16[3,960,320]{2,1,0:T(8,128)(2,1)} %bitcast.59), custom_call_target="tpu_custom_call" | custom-call | tf_op jit(solution)/shard_map/pallas_call | solution.py:100
  26.5 1.7 %constant_dynamic-slice_fusion.3 = (bf16[9,32,320]{2,1,0:T(8,128)(2,1)S(1)}, bf16[9,32,320]{2,1,0:T(8,128)(2,1)S(1)}, bf16[9,32,320]{2,1,0:T(8,128)(2,1)S(1)}, b...) fusion(bf16[72,32,320]{2,1,0:T(8,128)(2,1)} %shard_map.64.refs_, ...), kind=kLoop, calls=%fused_computation.40 | loop fusion | bytes 2949152 | tf_op jit(solution)/shard_map/dynamic_slice | solution.py:187
  28.3 1.6 %collective-permute-start.3 = (bf16[9,32,320]{2,1,0:T(8,128)(2,1)S(1)}, bf16[9,32,320]{2,1,0:T(8,128)(2,1)S(1)}, u32[]{:S(2)}, u32[]{:S(2)}) collective-permute-start(bf16[9,32,320]{2,1,0:T(8,128)(2,1)S(1)} %get-tuple-element.17), channel_id=1, source_target_pairs={{0,2},{1,3},{2,0},{3,1},{4,6},{5,7},{6,4},{7,5},{8,10},{9,11},{10,... | collective-permute-start | bytes 552968 | tf_op jit(solution)/shard_map/ppermute | solution.py:189
  29.9 1.4 %collective-permute-start.4 = (bf16[9,32,320]{2,1,0:T(8,128)(2,1)S(1)}, bf16[9,32,320]{2,1,0:T(8,128)(2,1)S(1)}, u32[]{:S(2)}, u32[]{:S(2)}) collective-permute-start(bf16[9,32,320]{2,1,0:T(8,128)(2,1)S(1)} %get-tuple-element.16), channel_id=1, source_target_pairs={{0,3},{1,0},{2,1},{3,2},{4,7},{5,4},{6,5},{7,6},{8,11},{9,8},{10,9... | collective-permute-start | bytes 552968 | tf_op jit(solution)/shard_map/ppermute | solution.py:189
  31.9 3.5 %collective-permute-done.2 = bf16[9,32,320]{2,1,0:T(8,128)(2,1)S(1)} collective-permute-done((bf16[9,32,320]{2,1,0:T(8,128)(2,1)S(1)}, bf16[9,32,320]{2,1,0:T(8,128)(2,1)S(1)}, u32[]{:S(2)}, u32[]{:S(2)}) %collective-permute-start.2) | collective-permute-done | bytes 184352 | tf_op jit(solution)/shard_map/ppermute | solution.py:189
  35.4 1.2 %collective-permute-done.3 = bf16[9,32,320]{2,1,0:T(8,128)(2,1)S(1)} collective-permute-done((bf16[9,32,320]{2,1,0:T(8,128)(2,1)S(1)}, bf16[9,32,320]{2,1,0:T(8,128)(2,1)S(1)}, u32[]{:S(2)}, u32[]{:S(2)}) %collective-permute-start.3) | collective-permute-done | bytes 184352 | tf_op jit(solution)/shard_map/ppermute | solution.py:189
  36.6 3.8 %collective-permute-done.4 = bf16[9,32,320]{2,1,0:T(8,128)(2,1)S(1)} collective-permute-done((bf16[9,32,320]{2,1,0:T(8,128)(2,1)S(1)}, bf16[9,32,320]{2,1,0:T(8,128)(2,1)S(1)}, u32[]{:S(2)}, u32[]{:S(2)}) %collective-permute-start.4) | collective-permute-done | bytes 184352 | tf_op jit(solution)/shard_map/ppermute | solution.py:189
  40.4 1.1 %pad_maximum_fusion.x_ref = bf16[4,288,320]{2,1,0:T(8,128)(2,1)} fusion(bf16[1,288,320]{2,1,0:T(8,128)(2,1)S(1)} %bitcast.81, bf16[1,288,320]{2,1,0:T(8,128)(2,1)S(1)} %bitcast.80, bf16[1,288,320]{2,1,0:T(8,128)(2,1)S(1)} %bitcast.79, bf16[1,288,320]{2,1,0:T(8,128)(2,1)S(1)} %bitcast.65), kind=kLoop, calls=%fused_computation.5 | loop fusion | flops 1105920 | bytes 1474560 | tf_op jit(solution)/shard_map/stack | solution.py:191
  41.5 5.9 %shard_map.65 = bf16[4,288,320]{2,1,0:T(8,128)(2,1)} custom-call(bf16[4,288,320]{2,1,0:T(8,128)(2,1)} %pad_maximum_fusion.x_ref, bf16[960,320]{1,0:T(8,128)(2,1)} %bitcast.53, f32[5,4,4,1]{3,2,1,0:T(4,128)} %copy.36.bias_ref, bf16[320,320]{1,0:T(8,128)(2,1)} %wout_ref.3), custom_call_target="tpu_custom_call" | custom-call | tf_op jit(solution)/shard_map/pallas_call | solution.py:168
  47.5 1.4 %fusion.10 = (bf16[1,288,320]{2,1,0:T(8,128)(2,1)S(1)}, bf16[1,288,320]{2,1,0:T(8,128)(2,1)S(1)}, bf16[1,288,320]{2,1,0:T(8,128)(2,1)S(1)}, bf16[1,288,320]{2,1,0:T(8,128)(2,1)S(1)}) fusion(bf16[4,288,320]{2,1,0:T(8,128)(2,1)} %shard_map.65), kind=kLoop, calls=%fused_computation.55 | loop fusion | bytes 1474560 | tf_op jit(solution)/shard_map/slice | solution.py:197
  48.8 2.3 %collective-permute-start.5 = (bf16[9,32,320]{2,1,0:T(8,128)(2,1)S(1)}, bf16[9,32,320]{2,1,0:T(8,128)(2,1)S(1)}, u32[]{:S(2)}, u32[]{:S(2)}) collective-permute-start(bf16[9,32,320]{2,1,0:T(8,128)(2,1)S(1)} %bitcast.73), channel_id=1, source_target_pairs={{0,3},{1,0},{2,1},{3,2},{4,7},{5,4},{6,5},{7,6},{8,11},{9,8},{10,9... | collective-permute-start | bytes 552968 | tf_op jit(solution)/shard_map/ppermute | solution.py:199
  51.6 1.1 %pad_maximum_fusion.2.x_ref = bf16[4,288,320]{2,1,0:T(8,128)(2,1)} fusion(bf16[1,288,320]{2,1,0:T(8,128)(2,1)S(1)} %bitcast.74, bf16[1,288,320]{2,1,0:T(8,128)(2,1)S(1)} %bitcast.72, bf16[1,288,320]{2,1,0:T(8,128)(2,1)S(1)} %bitcast.70, bf16[1,288,320]{2,1,0:T(8,128)(2,1)S(1)} %bitcast.64), kind=kLoop, calls=%fused_computation.7 | loop fusion | flops 1105920 | bytes 1474560 | tf_op jit(solution)/shard_map/stack | solution.py:191
  52.7 5.9 %shard_map.66 = bf16[4,288,320]{2,1,0:T(8,128)(2,1)} custom-call(bf16[4,288,320]{2,1,0:T(8,128)(2,1)} %pad_maximum_fusion.2.x_ref, bf16[960,320]{1,0:T(8,128)(2,1)} %bitcast.54, f32[5,4,4,1]{3,2,1,0:T(4,128)} %copy.36.bias_ref, bf16[320,320]{1,0:T(8,128)(2,1)} %wout_ref.3), custom_call_target="tpu_custom_call" | custom-call | tf_op jit(solution)/shard_map/pallas_call | solution.py:168
  58.7 2.0 %fusion.9 = (bf16[1,288,320]{2,1,0:T(8,128)(2,1)S(1)}, bf16[1,288,320]{2,1,0:T(8,128)(2,1)S(1)}, bf16[1,288,320]{2,1,0:T(8,128)(2,1)S(1)}, bf16[1,288,320]{2,1,0:T(8,128)(2,1)}) fusion(bf16[4,288,320]{2,1,0:T(8,128)(2,1)} %shard_map.66), kind=kLoop, calls=%fused_computation.54 | loop fusion | bytes 1474560 | tf_op jit(solution)/shard_map/slice | solution.py:197
  60.7 1.7 %collective-permute-start.11 = (bf16[9,32,320]{2,1,0:T(8,128)(2,1)}, bf16[9,32,320]{2,1,0:T(8,128)(2,1)S(1)}, u32[]{:S(2)}, u32[]{:S(2)}) collective-permute-start(bf16[9,32,320]{2,1,0:T(8,128)(2,1)} %bitcast.27), channel_id=1, source_target_pairs={{0,3},{1,0},{2,1},{3,2},{4,7},{5,4},{6,5},{7,6},{8,11},{9,8},{10,9... | collective-permute-start | bytes 552968 | tf_op jit(solution)/shard_map/ppermute | solution.py:199
  62.4 1.5 %collective-permute-start.12 = (bf16[9,32,320]{2,1,0:T(8,128)(2,1)S(1)}, bf16[9,32,320]{2,1,0:T(8,128)(2,1)S(1)}, u32[]{:S(2)}, u32[]{:S(2)}) collective-permute-start(bf16[9,32,320]{2,1,0:T(8,128)(2,1)S(1)} %bitcast.77), channel_id=1, source_target_pairs={{0,2},{1,3},{2,0},{3,1},{4,6},{5,7},{6,4},{7,5},{8,10},{9,11},{10,... | collective-permute-start | bytes 552968 | tf_op jit(solution)/shard_map/ppermute | solution.py:199
  64.0 2.1 %fusion.6 = (bf16[36,1,320]{2,1,0:T(2,128)(2,1)}, bf16[36,1,320]{2,1,0:T(2,128)(2,1)}, bf16[36,1,320]{2,1,0:T(2,128)(2,1)}, bf16[36,1,320]{2,1,0:T(2,128)(2,1)}) fusion(bf16[72,32,320]{2,1,0:T(8,128)(2,1)} %shard_map.64.refs_0_), kind=kLoop, calls=%fused_computation.51 | loop fusion | bytes 184320 | tf_op jit(solution)/shard_map/slice | solution.py:236
  66.3 0.7 gather_fusion.2
  67.1 1.5 %collective-permute-done.11 = bf16[9,32,320]{2,1,0:T(8,128)(2,1)S(1)} collective-permute-done((bf16[9,32,320]{2,1,0:T(8,128)(2,1)}, bf16[9,32,320]{2,1,0:T(8,128)(2,1)S(1)}, u32[]{:S(2)}, u32[]{:S(2)}) %collective-permute-start.11) | collective-permute-done | bytes 184352 | tf_op jit(solution)/shard_map/ppermute | solution.py:199
  68.5 5.9 %collective-permute-done.12 = bf16[9,32,320]{2,1,0:T(8,128)(2,1)S(1)} collective-permute-done((bf16[9,32,320]{2,1,0:T(8,128)(2,1)S(1)}, bf16[9,32,320]{2,1,0:T(8,128)(2,1)S(1)}, u32[]{:S(2)}, u32[]{:S(2)}) %collective-permute-start.12) | collective-permute-done | bytes 184352 | tf_op jit(solution)/shard_map/ppermute | solution.py:199
  74.4 1.1 %pad_maximum_fusion.3 = bf16[4,9,32,320]{3,2,1,0:T(8,128)(2,1)S(1)} fusion(bf16[1,9,32,320]{3,2,1,0:T(8,128)(2,1)} %bitcast.32, bf16[1,9,32,320]{3,2,1,0:T(8,128)(2,1)S(1)} %bitcast.78, bf16[1,9,32,320]{3,2,1,0:T(8,128)(2,1)S(1)} %bitcast.76, bf16[1,9,32,320]{3,2,1,0:T(8,128)(2,1)S(1)} %bitcast.63), kind=kLoop, calls=%fused_computation.8 | loop fusion | flops 1105920 | bytes 1474560 | tf_op jit(solution)/shard_map/stack | solution.py:202
  75.6 0.7 gather_fusion.3
  77.2 1.9 %collective-permute-start.15 = (bf16[72,320]{1,0:T(8,128)(2,1)S(1)}, bf16[72,320]{1,0:T(8,128)(2,1)S(1)}, u32[]{:S(2)}, u32[]{:S(2)}) collective-permute-start(bf16[72,320]{1,0:T(8,128)(2,1)S(1)} %pad_maximum_fusion.5), channel_id=1, source_target_pairs={{4,0},{8,4},{12,8},{0,12},{5,1},{9,5},{13,9},{1,13},{6,2},{10,6},{... | collective-permute-start | bytes 138248 | tf_op jit(solution)/shard_map/ppermute | solution.py:16
  79.6 2.4 %collective-permute-done.15 = bf16[72,320]{1,0:T(8,128)(2,1)S(1)} collective-permute-done((bf16[72,320]{1,0:T(8,128)(2,1)S(1)}, bf16[72,320]{1,0:T(8,128)(2,1)S(1)}, u32[]{:S(2)}, u32[]{:S(2)}) %collective-permute-start.15) | collective-permute-done | bytes 46112 | tf_op jit(solution)/shard_map/ppermute | solution.py:16
  82.6 2.8 %collective-permute-done.14 = bf16[72,320]{1,0:T(8,128)(2,1)S(1)} collective-permute-done((bf16[72,320]{1,0:T(8,128)(2,1)S(1)}, bf16[72,320]{1,0:T(8,128)(2,1)S(1)}, u32[]{:S(2)}, u32[]{:S(2)}) %collective-permute-start.14) | collective-permute-done | bytes 46112 | tf_op jit(solution)/shard_map/ppermute | solution.py:16
  85.4 0.6 broadcast_select_fusion.4.refs_3_
  86.1 11.9 %shard_map.67 = bf16[72,32,320]{2,1,0:T(8,128)(2,1)} custom-call(bf16[72,32,320]{2,1,0:T(8,128)(2,1)} %shard_map.64.refs_0_, bf16[36,32,320]{2,1,0:T(8,128)(2,1)} %bitcast.58, bf16[36,32,320]{2,1,0:T(8,128)(2,1)} %bitcast.56, bf16[72,320]{1,0:T(8,128)(2,1)} %broadcast_select_fusion.4.refs_3_, bf16[72,320]{1,0:T(8,128)(2,1)} %broadcast_select_fusion.2.refs_4_, ...), custom_call_target="tpu_custom_call" | custom-call | tf_op jit(solution)/shard_map/pallas_call | solution.py:100
  (57 shorter events, 6.0 us)
Async XLA Ops:
  0.0 7.3 %copy-start = (f32[5,4,4]{0,2,1:T(4,128)S(1)}, f32[5,4,4]{0,2,1:T(4,128)}, u32[]{:S(2)}) copy-start(f32[5,4,4]{0,2,1:T(4,128)} %param.16) | copy-start | bytes 964
  0.0 9.5 %copy-start.3 = (bf16[320,960]{1,0:T(8,128)(2,1)S(1)}, bf16[320,960]{1,0:T(8,128)(2,1)}, u32[]{:S(2)}) copy-start(bf16[320,960]{1,0:T(8,128)(2,1)} %param.14) | copy-start | bytes 1843204
  2.2 8.5 %collective-permute-start.1 = (bf16[72,320]{1,0:T(8,128)(2,1)S(1)}, bf16[72,320]{1,0:T(8,128)(2,1)S(1)}, u32[]{:S(2)}, u32[]{:S(2)}) collective-permute-start(bf16[72,320]{1,0:T(8,128)(2,1)S(1)} %get-tuple-element.20), channel_id=1, source_target_pairs={{4,0},{8,4},{12,8},{0,12},{5,1},{9,5},{13,9},{1,13},{6,2},{10,6},{... | collective-permute-start | bytes 138248 | tf_op jit(solution)/shard_map/ppermute | solution.py:16
  7.3 6.0 %collective-permute-start = (bf16[72,320]{1,0:T(8,128)(2,1)S(1)}, bf16[72,320]{1,0:T(8,128)(2,1)S(1)}, u32[]{:S(2)}, u32[]{:S(2)}) collective-permute-start(bf16[72,320]{1,0:T(8,128)(2,1)S(1)} %get-tuple-element.21), channel_id=1, source_target_pairs={{12,0},{0,4},{4,8},{8,12},{13,1},{1,5},{5,9},{9,13},{14,2},{2,6},{... | collective-permute-start | bytes 138248 | tf_op jit(solution)/shard_map/ppermute | solution.py:16
  28.2 7.2 %collective-permute-start.2 = (bf16[9,32,320]{2,1,0:T(8,128)(2,1)S(1)}, bf16[9,32,320]{2,1,0:T(8,128)(2,1)S(1)}, u32[]{:S(2)}, u32[]{:S(2)}) collective-permute-start(bf16[9,32,320]{2,1,0:T(8,128)(2,1)S(1)} %get-tuple-element.18), channel_id=1, source_target_pairs={{0,1},{1,2},{2,3},{3,0},{4,5},{5,6},{6,7},{7,4},{8,9},{9,10},{10,1... | collective-permute-start | bytes 552968 | tf_op jit(solution)/shard_map/ppermute | solution.py:189
  28.3 8.3 %collective-permute-start.3 = (bf16[9,32,320]{2,1,0:T(8,128)(2,1)S(1)}, bf16[9,32,320]{2,1,0:T(8,128)(2,1)S(1)}, u32[]{:S(2)}, u32[]{:S(2)}) collective-permute-start(bf16[9,32,320]{2,1,0:T(8,128)(2,1)S(1)} %get-tuple-element.17), channel_id=1, source_target_pairs={{0,2},{1,3},{2,0},{3,1},{4,6},{5,7},{6,4},{7,5},{8,10},{9,11},{10,... | collective-permute-start | bytes 552968 | tf_op jit(solution)/shard_map/ppermute | solution.py:189
  29.9 10.5 %collective-permute-start.4 = (bf16[9,32,320]{2,1,0:T(8,128)(2,1)S(1)}, bf16[9,32,320]{2,1,0:T(8,128)(2,1)S(1)}, u32[]{:S(2)}, u32[]{:S(2)}) collective-permute-start(bf16[9,32,320]{2,1,0:T(8,128)(2,1)S(1)} %get-tuple-element.16), channel_id=1, source_target_pairs={{0,3},{1,0},{2,1},{3,2},{4,7},{5,4},{6,5},{7,6},{8,11},{9,8},{10,9... | collective-permute-start | bytes 552968 | tf_op jit(solution)/shard_map/ppermute | solution.py:189
  31.3 20.3 %collective-permute-start.8 = (bf16[9,32,320]{2,1,0:T(8,128)(2,1)S(1)}, bf16[9,32,320]{2,1,0:T(8,128)(2,1)S(1)}, u32[]{:S(2)}, u32[]{:S(2)}) collective-permute-start(bf16[9,32,320]{2,1,0:T(8,128)(2,1)S(1)} %get-tuple-element.15), channel_id=1, source_target_pairs={{0,1},{1,2},{2,3},{3,0},{4,5},{5,6},{6,7},{7,4},{8,9},{9,10},{10,1... | collective-permute-start | bytes 552968 | tf_op jit(solution)/shard_map/ppermute | solution.py:189
  31.4 20.2 %collective-permute-start.9 = (bf16[9,32,320]{2,1,0:T(8,128)(2,1)S(1)}, bf16[9,32,320]{2,1,0:T(8,128)(2,1)S(1)}, u32[]{:S(2)}, u32[]{:S(2)}) collective-permute-start(bf16[9,32,320]{2,1,0:T(8,128)(2,1)S(1)} %get-tuple-element.14), channel_id=1, source_target_pairs={{0,2},{1,3},{2,0},{3,1},{4,6},{5,7},{6,4},{7,5},{8,10},{9,11},{10,... | collective-permute-start | bytes 552968 | tf_op jit(solution)/shard_map/ppermute | solution.py:189
  35.4 16.2 %collective-permute-start.10 = (bf16[9,32,320]{2,1,0:T(8,128)(2,1)S(1)}, bf16[9,32,320]{2,1,0:T(8,128)(2,1)S(1)}, u32[]{:S(2)}, u32[]{:S(2)}) collective-permute-start(bf16[9,32,320]{2,1,0:T(8,128)(2,1)S(1)} %get-tuple-element.13), channel_id=1, source_target_pairs={{0,3},{1,0},{2,1},{3,2},{4,7},{5,4},{6,5},{7,6},{8,11},{9,8},{10,9... | collective-permute-start | bytes 552968 | tf_op jit(solution)/shard_map/ppermute | solution.py:189
  48.8 15.1 %collective-permute-start.5 = (bf16[9,32,320]{2,1,0:T(8,128)(2,1)S(1)}, bf16[9,32,320]{2,1,0:T(8,128)(2,1)S(1)}, u32[]{:S(2)}, u32[]{:S(2)}) collective-permute-start(bf16[9,32,320]{2,1,0:T(8,128)(2,1)S(1)} %bitcast.73), channel_id=1, source_target_pairs={{0,3},{1,0},{2,1},{3,2},{4,7},{5,4},{6,5},{7,6},{8,11},{9,8},{10,9... | collective-permute-start | bytes 552968 | tf_op jit(solution)/shard_map/ppermute | solution.py:199
  51.1 15.0 %collective-permute-start.6 = (bf16[9,32,320]{2,1,0:T(8,128)(2,1)S(1)}, bf16[9,32,320]{2,1,0:T(8,128)(2,1)S(1)}, u32[]{:S(2)}, u32[]{:S(2)}) collective-permute-start(bf16[9,32,320]{2,1,0:T(8,128)(2,1)S(1)} %bitcast.68), channel_id=1, source_target_pairs={{0,2},{1,3},{2,0},{3,1},{4,6},{5,7},{6,4},{7,5},{8,10},{9,11},{10,... | collective-permute-start | bytes 552968 | tf_op jit(solution)/shard_map/ppermute | solution.py:199
  51.6 14.5 %collective-permute-start.7 = (bf16[9,32,320]{2,1,0:T(8,128)(2,1)S(1)}, bf16[9,32,320]{2,1,0:T(8,128)(2,1)S(1)}, u32[]{:S(2)}, u32[]{:S(2)}) collective-permute-start(bf16[9,32,320]{2,1,0:T(8,128)(2,1)S(1)} %bitcast.66), channel_id=1, source_target_pairs={{0,1},{1,2},{2,3},{3,0},{4,5},{5,6},{6,7},{7,4},{8,9},{9,10},{10,1... | collective-permute-start | bytes 552968 | tf_op jit(solution)/shard_map/ppermute | solution.py:199
  60.7 7.8 %collective-permute-start.11 = (bf16[9,32,320]{2,1,0:T(8,128)(2,1)}, bf16[9,32,320]{2,1,0:T(8,128)(2,1)S(1)}, u32[]{:S(2)}, u32[]{:S(2)}) collective-permute-start(bf16[9,32,320]{2,1,0:T(8,128)(2,1)} %bitcast.27), channel_id=1, source_target_pairs={{0,3},{1,0},{2,1},{3,2},{4,7},{5,4},{6,5},{7,6},{8,11},{9,8},{10,9... | collective-permute-start | bytes 552968 | tf_op jit(solution)/shard_map/ppermute | solution.py:199
  62.4 12.0 %collective-permute-start.12 = (bf16[9,32,320]{2,1,0:T(8,128)(2,1)S(1)}, bf16[9,32,320]{2,1,0:T(8,128)(2,1)S(1)}, u32[]{:S(2)}, u32[]{:S(2)}) collective-permute-start(bf16[9,32,320]{2,1,0:T(8,128)(2,1)S(1)} %bitcast.77), channel_id=1, source_target_pairs={{0,2},{1,3},{2,0},{3,1},{4,6},{5,7},{6,4},{7,5},{8,10},{9,11},{10,... | collective-permute-start | bytes 552968 | tf_op jit(solution)/shard_map/ppermute | solution.py:199
  64.0 10.5 %collective-permute-start.13 = (bf16[9,32,320]{2,1,0:T(8,128)(2,1)S(1)}, bf16[9,32,320]{2,1,0:T(8,128)(2,1)}, u32[]{:S(2)}, u32[]{:S(2)}) collective-permute-start(bf16[9,32,320]{2,1,0:T(8,128)(2,1)S(1)} %bitcast.75), channel_id=1, source_target_pairs={{0,1},{1,2},{2,3},{3,0},{4,5},{5,6},{6,7},{7,4},{8,9},{9,10},{10,1... | collective-permute-start | bytes 552968 | tf_op jit(solution)/shard_map/ppermute | solution.py:199
  76.3 0.8 copy-start.7
  76.3 0.8 copy-start.6
  76.3 2.8 %copy-start.5 = (bf16[36,1,320]{2,1,0:T(2,128)(2,1)S(1)}, bf16[36,1,320]{2,1,0:T(2,128)(2,1)}, u32[]{:S(2)}) copy-start(bf16[36,1,320]{2,1,0:T(2,128)(2,1)} %get-tuple-element.10) | copy-start | bytes 69124
  76.3 2.8 %copy-start.4 = (bf16[36,1,320]{2,1,0:T(2,128)(2,1)S(1)}, bf16[36,1,320]{2,1,0:T(2,128)(2,1)}, u32[]{:S(2)}) copy-start(bf16[36,1,320]{2,1,0:T(2,128)(2,1)} %get-tuple-element.8) | copy-start | bytes 69124
  76.6 9.4 %copy-start.1 = (bf16[4,9,32,320]{3,2,1,0:T(8,128)(2,1)}, bf16[4,9,32,320]{3,2,1,0:T(8,128)(2,1)S(1)}, u32[]{:S(2)}) copy-start(bf16[4,9,32,320]{3,2,1,0:T(8,128)(2,1)S(1)} %get-tuple-element.34) | copy-start | bytes 2211844
  76.6 9.4 %copy-start.2 = (bf16[4,9,32,320]{3,2,1,0:T(8,128)(2,1)}, bf16[4,9,32,320]{3,2,1,0:T(8,128)(2,1)S(1)}, u32[]{:S(2)}) copy-start(bf16[4,9,32,320]{3,2,1,0:T(8,128)(2,1)S(1)} %get-tuple-element.35) | copy-start | bytes 2211844
  77.2 4.8 %collective-permute-start.15 = (bf16[72,320]{1,0:T(8,128)(2,1)S(1)}, bf16[72,320]{1,0:T(8,128)(2,1)S(1)}, u32[]{:S(2)}, u32[]{:S(2)}) collective-permute-start(bf16[72,320]{1,0:T(8,128)(2,1)S(1)} %pad_maximum_fusion.5), channel_id=1, source_target_pairs={{4,0},{8,4},{12,8},{0,12},{5,1},{9,5},{13,9},{1,13},{6,2},{10,6},{... | collective-permute-start | bytes 138248 | tf_op jit(solution)/shard_map/ppermute | solution.py:16
  79.2 6.2 %collective-permute-start.14 = (bf16[72,320]{1,0:T(8,128)(2,1)S(1)}, bf16[72,320]{1,0:T(8,128)(2,1)S(1)}, u32[]{:S(2)}, u32[]{:S(2)}) collective-permute-start(bf16[72,320]{1,0:T(8,128)(2,1)S(1)} %pad_maximum_fusion.4), channel_id=1, source_target_pairs={{12,0},{0,4},{4,8},{8,12},{13,1},{1,5},{5,9},{9,13},{14,2},{2,6},{... | collective-permute-start | bytes 138248 | tf_op jit(solution)/shard_map/ppermute | solution.py:16

commit v13 on v12

--- a/solution.py
+++ b/solution.py
@@ -109,19 +109,35 @@
     )(*flat, *rims, stacked)
 
 
-def attend_kernel(x_ref, wqkv_ref, bias_ref, wout_ref, o_ref, qkv_s, blend_s):
-    frames_all, count, channels = x_ref.shape
+def attend_kernel(*refs, parts):
+    if parts:
+        x_refs = refs[:parts]
+        wqkv_ref, bias_ref, wout_ref = refs[parts : parts + 3]
+        o_refs = refs[parts + 3 : 2 * parts + 3]
+        qkv_s, blend_s = refs[2 * parts + 3 :]
+        frames_all, _, count = qkv_s.shape
+        channels = wout_ref.shape[0]
+        for f in range(parts):
+            qkv_s[f] = lax.dot_general(
+                wqkv_ref[...],
+                x_refs[f][...].reshape(count, channels),
+                (((1,), (1,)), ((), ())),
+                preferred_element_type=jnp.float32,
+            ).astype(jnp.bfloat16)
+    else:
+        x_ref, wqkv_ref, bias_ref, wout_ref, o_ref, qkv_s, blend_s = refs
+        frames_all, count, channels = x_ref.shape
+
+        def project(f, carry):
+            qkv_s[f] = lax.dot_general(
+                wqkv_ref[...], x_ref[f], (((1,), (1,)), ((), ())), preferred_element_type=jnp.float32
+            ).astype(jnp.bfloat16)
+            return carry
+
+        lax.fori_loop(0, frames_all, project, 0, unroll=frames_all <= 4)
     head_dim = channels // HEADS
     scale = head_dim ** (-0.5)
     block = min(frames_all, 4)
-
-    def project(f, carry):
-        qkv_s[f] = lax.dot_general(
-            wqkv_ref[...], x_ref[f], (((1,), (1,)), ((), ())), preferred_element_type=jnp.float32
-        ).astype(jnp.bfloat16)
-        return carry
-
-    lax.fori_loop(0, frames_all, project, 0, unroll=frames_all <= 4)
 
     def head_block(h, first):
         frames = pl.ds(first, block)
@@ -153,20 +169,45 @@
 
     lax.fori_loop(0, frames_all // block, frame_block, 0, unroll=frames_all <= 4)
 
-    def out_project(f, carry):
-        o_ref[f] = lax.dot_general(
+    def out_product(f):
+        return lax.dot_general(
             blend_s[f], wout_ref[...], (((0,), (0,)), ((), ())), preferred_element_type=jnp.float32
         ).astype(jnp.bfloat16)
+
+    if parts:
+        for f in range(parts):
+            o_refs[f][...] = out_product(f).reshape(o_refs[f].shape)
+        return
+
+    def out_project(f, carry):
+        o_ref[f] = out_product(f)
         return carry
 
     lax.fori_loop(0, frames_all, out_project, 0, unroll=frames_all <= 4)
+
+
+def attend_pieces(pieces, qkv_weight, pos_bias, out_weight):
+    frames_all = len(pieces)
+    band, col_count, channels = pieces[0].shape
+    count = band * col_count
+    vmem = pl.BlockSpec(memory_space=pltpu.VMEM)
+    return pl.pallas_call(
+        functools.partial(attend_kernel, parts=frames_all),
+        out_shape=tuple(jax.ShapeDtypeStruct(pieces[0].shape, jnp.bfloat16) for _ in pieces),
+        in_specs=[vmem] * (frames_all + 3),
+        out_specs=tuple(vmem for _ in pieces),
+        scratch_shapes=[
+            pltpu.VMEM((frames_all, 3 * channels, count), jnp.bfloat16),
+            pltpu.VMEM((frames_all, channels, count), jnp.bfloat16),
+        ],
+    )(*pieces, qkv_weight.T, pos_bias.transpose(0, 2, 1)[..., None], out_weight)
 
 
 def attend(grid, qkv_weight, pos_bias, out_weight):
     frames_all, count, channels = grid.shape
     vmem = pl.BlockSpec(memory_space=pltpu.VMEM)
     return pl.pallas_call(
-        attend_kernel,
+        functools.partial(attend_kernel, parts=0),
         out_shape=jax.ShapeDtypeStruct((frames_all, count, channels), jnp.bfloat16),
         in_specs=[vmem] * 4,
         out_specs=vmem,
@@ -188,10 +229,9 @@
         if s:
             piece = lax.ppermute(piece, "frame", [(i, (i + s) % frames_all) for i in range(frames_all)])
         got.append(piece)
-    grid = jnp.stack(got).reshape(frames_all, band * col_count, channels)
     source = (me - jnp.arange(frames_all)) % frames_all
     bias = jnp.take(jnp.take(pos_bias, source, axis=1), source, axis=2)
-    attended = attend(grid, qkv_weight, bias, out_weight).reshape(frames_all, band, col_count, channels)
+    attended = attend_pieces(got, qkv_weight, bias, out_weight)
     back = []
     for s in range(frames_all):
         piece = attended[s]

time: 98.4 us -> 92.8 us (0.943)
  other arithmetic: 6.69 us -> 3.51 us
  waiting for transfers between devices: 23 us -> 21.1 us
  local copies, waits for them, and re-layouts: 14.6 us -> 13.3 us
    slice x2 -> x0, local copies, waits for them, and re-layouts: 3.39 us -> none  [rotated_attention(): piece = attended[s]]
    ppermute x6, waiting for transfers between devices: 8.46 us -> 5.54 us  [rotated_attention(): lax.ppermute(piece, 'frame', [(i, (i + s) % frames_all) for i in range(fr...]
    another operation x2 -> x0, other arithmetic: 2.25 us -> none  [rotated_attention(): grid = jnp.stack(got).reshape(frames_all, band * col_count, channels)]
    ppermute x6, starting transfers between devices: 3.66 us -> 5.01 us  [rotated_attention(): lax.ppermute(piece, 'frame', [(i, (i + s) % frames_all) for i in range(fr...]
    unnamed x18 -> x34, local copies, waits for them, and re-layouts: 3.65 us -> 4.97 us
  transfers between devices with their start and end apart: 16 -> 16, of which waited for: 8 -> 9; matrix products, arithmetic and copies ran while one was open for 14% -> 8% of each run, Pallas kernels for 12% -> 13%
where the time goes in v13:
time: 92.8 us; the launch traced here: 92.5 us
  Pallas kernels  36.2 us (39%)
  waiting for transfers between devices  21.1 us (23%)
  starting transfers between devices  18 us (19%)
  local copies, waits for them, and re-layouts  13.3 us (14%)
  other arithmetic  3.51 us (4%)
    pallas_call x2, Pallas kernels, convolve(): pl.pallas_call(functools.partial(conv_kernel, layout=tuple(layout), lo=lo...  24.6 us
    pallas_call x2, Pallas kernels, attend_pieces(): pl.pallas_call(functools.partial(attend_kernel, parts=frames_all), out_sh...  11.6 us
    ppermute x4, waiting for transfers between devices, shifted(): moved = lax.ppermute(block, axis, route)  7.98 us
    ppermute x6, waiting for transfers between devices, rotated_attention(): lax.ppermute(piece, 'frame', [(i, (i - s) % frames_all) for i in range(fr...  7.58 us
    ppermute x4, starting transfers between devices, shifted(): moved = lax.ppermute(block, axis, route)  7.46 us
    ppermute x6, starting transfers between devices, rotated_attention(): lax.ppermute(piece, 'frame', [(i, (i - s) % frames_all) for i in range(fr...  5.56 us
    ppermute x6, waiting for transfers between devices, rotated_attention(): lax.ppermute(piece, 'frame', [(i, (i + s) % frames_all) for i in range(fr...  5.54 us
    ppermute x6, starting transfers between devices, rotated_attention(): lax.ppermute(piece, 'frame', [(i, (i + s) % frames_all) for i in range(fr...  5.01 us
  transfers between devices with their start and end apart: 16, of which 9 were waited for; matrix products, arithmetic and copies ran while one was open for 8% of the time, Pallas kernels for 13%

profile of v13, /device:TPU:0, one launch (start us, length us, event | category | flops | bytes accessed | tf_op | source)
XLA Modules:
  0.0 92.5 jit_solution(16724456740197810369)
XLA Ops:
  0.0 2.1 %copy.66 = bf16[1,72,32,320]{3,1,2,0:T(8,128)(2,1)S(1)} copy(bf16[1,72,32,320]{3,2,1,0:T(8,128)(2,1)} %param.12) | data formatting | bytes 2949120 | tf_op args[0]
  2.1 5.1 %collective-permute-start.1 = (bf16[72,320]{1,0:T(8,128)(2,1)S(1)}, bf16[72,320]{1,0:T(8,128)(2,1)S(1)}, u32[]{:S(2)}, u32[]{:S(2)}) collective-permute-start(bf16[72,320]{1,0:T(8,128)(2,1)S(1)} %get-tuple-element.36), channel_id=1, source_target_pairs={{4,0},{8,4},{12,8},{0,12},{5,1},{9,5},{13,9},{1,13},{6,2},{10,6},{... | collective-permute-start | bytes 138248 | tf_op jit(solution)/shard_map/ppermute | solution.py:16
  9.0 0.6 broadcast_select_fusion.3.refs_2_
  9.7 3.5 %collective-permute-done = bf16[72,320]{1,0:T(8,128)(2,1)S(1)} collective-permute-done((bf16[72,320]{1,0:T(8,128)(2,1)S(1)}, bf16[72,320]{1,0:T(8,128)(2,1)S(1)}, u32[]{:S(2)}, u32[]{:S(2)}) %collective-permute-start) | collective-permute-done | bytes 46112 | tf_op jit(solution)/shard_map/ppermute | solution.py:16
  13.2 0.6 broadcast_select_fusion.5.refs_1_
  13.8 12.6 %shard_map.64.refs_0_ = bf16[72,32,320]{2,1,0:T(8,128)(2,1)} custom-call(bf16[72,32,320]{2,1,0:T(8,128)(2,1)} %bitcast.38, bf16[72,320]{1,0:T(8,128)(2,1)} %broadcast_select_fusion.5.refs_1_, bf16[72,320]{1,0:T(8,128)(2,1)} %broadcast_select_fusion.3.refs_2_, bf16[3,960,320]{2,1,0:T(8,128)(2,1)} %bitcast.45), custom_call_target="tpu_custom_call" | custom-call | tf_op jit(solution)/shard_map/pallas_call | solution.py:100
  26.5 2.6 %constant_dynamic-slice_fusion = (bf16[9,32,320]{2,1,0:T(8,128)(2,1)S(1)}, bf16[9,32,320]{2,1,0:T(8,128)(2,1)S(1)}, bf16[9,32,320]{2,1,0:T(8,128)(2,1)S(1)}, bf1...) fusion(bf16[72,32,320]{2,1,0:T(8,128)(2,1)} %shard_map.64.refs_, ...), kind=kLoop, calls=%fused_computation.35 | loop fusion | bytes 2949152 | tf_op jit(solution)/shard_map/dynamic_slice | solution.py:228
  29.1 1.5 %collective-permute-start.3 = (bf16[9,32,320]{2,1,0:T(8,128)(2,1)S(1)}, bf16[9,32,320]{2,1,0:T(8,128)(2,1)S(1)}, u32[]{:S(2)}, u32[]{:S(2)}) collective-permute-start(bf16[9,32,320]{2,1,0:T(8,128)(2,1)S(1)} %get-tuple-element.33), channel_id=1, source_target_pairs={{0,2},{1,3},{2,0},{3,1},{4,6},{5,7},{6,4},{7,5},{8,10},{9,11},{10,... | collective-permute-start | bytes 552968 | tf_op jit(solution)/shard_map/ppermute | solution.py:230
  30.6 1.4 %collective-permute-start.4 = (bf16[9,32,320]{2,1,0:T(8,128)(2,1)S(1)}, bf16[9,32,320]{2,1,0:T(8,128)(2,1)S(1)}, u32[]{:S(2)}, u32[]{:S(2)}) collective-permute-start(bf16[9,32,320]{2,1,0:T(8,128)(2,1)S(1)} %get-tuple-element.32), channel_id=1, source_target_pairs={{0,3},{1,0},{2,1},{3,2},{4,7},{5,4},{6,5},{7,6},{8,11},{9,8},{10,9... | collective-permute-start | bytes 552968 | tf_op jit(solution)/shard_map/ppermute | solution.py:230
  32.1 0.8 copy.38.refs_5_
  32.9 1.2 %copy.36 = bf16[320,960]{0,1:T(8,128)(2,1)} copy(bf16[320,960]{1,0:T(8,128)(2,1)S(1)} %copy-done.3) | data formatting | bytes 1228800 | tf_op args[2]
  34.6 1.6 %collective-permute-done.2.refs_1_ = bf16[9,32,320]{2,1,0:T(8,128)(2,1)S(1)} collective-permute-done((bf16[9,32,320]{2,1,0:T(8,128)(2,1)S(1)}, bf16[9,32,320]{2,1,0:T(8,128)(2,1)S(1)}, u32[]{:S(2)}, u32[]{:S(2)}) %collective-permute-start.2) | collective-permute-done | bytes 184352 | tf_op jit(solution)/shard_map/ppermute | solution.py:230
  36.2 1.5 %collective-permute-start.9 = (bf16[9,32,320]{2,1,0:T(8,128)(2,1)S(1)}, bf16[9,32,320]{2,1,0:T(8,128)(2,1)S(1)}, u32[]{:S(2)}, u32[]{:S(2)}) collective-permute-start(bf16[9,32,320]{2,1,0:T(8,128)(2,1)S(1)} %get-tuple-element.29), channel_id=1, source_target_pairs={{0,2},{1,3},{2,0},{3,1},{4,6},{5,7},{6,4},{7,5},{8,10},{9,11},{10,... | collective-permute-start | bytes 552968 | tf_op jit(solution)/shard_map/ppermute | solution.py:230
  37.8 3.4 %collective-permute-done.4.refs_3_ = bf16[9,32,320]{2,1,0:T(8,128)(2,1)S(1)} collective-permute-done((bf16[9,32,320]{2,1,0:T(8,128)(2,1)S(1)}, bf16[9,32,320]{2,1,0:T(8,128)(2,1)S(1)}, u32[]{:S(2)}, u32[]{:S(2)}) %collective-permute-start.4) | collective-permute-done | bytes 184352 | tf_op jit(solution)/shard_map/ppermute | solution.py:230
  41.1 0.7 copy-done.15
  41.8 5.8 %shard_map.65 = (bf16[9,32,320]{2,1,0:T(8,128)(2,1)}, bf16[9,32,320]{2,1,0:T(8,128)(2,1)}, bf16[9,32,320]{2,1,0:T(8,128)(2,1)}, bf16[9,32,320]{2,1,0:T(8,128)(2,1)}) custom-call(bf16[9,32,320]{2,1,0:T(8,128)(2,1)} %get-tuple-element.35.refs_0_, bf16[9,32,320]{2,1,0:T(8,128)(2,1)} %copy-done.13, bf16[9,32,320]{2,1,0:T(8,128)(2,1)} %copy-done.14, ...), custom_call_target="tpu_custom_call" | custom-call | tf_op jit(solution)/shard_map/pallas_call | solution.py:194
  47.6 2.2 %collective-permute-start.5 = (bf16[9,32,320]{2,1,0:T(8,128)(2,1)}, bf16[9,32,320]{2,1,0:T(8,128)(2,1)S(1)}, u32[]{:S(2)}, u32[]{:S(2)}) collective-permute-start(bf16[9,32,320]{2,1,0:T(8,128)(2,1)} %get-tuple-element.17), channel_id=1, source_target_pairs={{0,3},{1,0},{2,1},{3,2},{4,7},{5,4},{6,5},{7,6},{8,11},{9,8},{10,9... | collective-permute-start | bytes 552968 | tf_op jit(solution)/shard_map/ppermute | solution.py:239
  51.7 5.8 %shard_map.66 = (bf16[9,32,320]{2,1,0:T(8,128)(2,1)}, bf16[9,32,320]{2,1,0:T(8,128)(2,1)}, bf16[9,32,320]{2,1,0:T(8,128)(2,1)}, bf16[9,32,320]{2,1,0:T(8,128)(2,1)}) custom-call(bf16[9,32,320]{2,1,0:T(8,128)(2,1)} %get-tuple-element.31.refs_0_, bf16[9,32,320]{2,1,0:T(8,128)(2,1)} %copy-done.11, bf16[9,32,320]{2,1,0:T(8,128)(2,1)} %copy-done.12, ...), custom_call_target="tpu_custom_call" | custom-call | tf_op jit(solution)/shard_map/pallas_call | solution.py:194
  57.5 1.3 %collective-permute-start.11 = (bf16[9,32,320]{2,1,0:T(8,128)(2,1)}, bf16[9,32,320]{2,1,0:T(8,128)(2,1)S(1)}, u32[]{:S(2)}, u32[]{:S(2)}) collective-permute-start(bf16[9,32,320]{2,1,0:T(8,128)(2,1)} %get-tuple-element.21), channel_id=1, source_target_pairs={{0,3},{1,0},{2,1},{3,2},{4,7},{5,4},{6,5},{7,6},{8,11},{9,8},{10,9... | collective-permute-start | bytes 552968 | tf_op jit(solution)/shard_map/ppermute | solution.py:239
  58.8 1.5 %collective-permute-start.12 = (bf16[9,32,320]{2,1,0:T(8,128)(2,1)}, bf16[9,32,320]{2,1,0:T(8,128)(2,1)S(1)}, u32[]{:S(2)}, u32[]{:S(2)}) collective-permute-start(bf16[9,32,320]{2,1,0:T(8,128)(2,1)} %get-tuple-element.22), channel_id=1, source_target_pairs={{0,2},{1,3},{2,0},{3,1},{4,6},{5,7},{6,4},{7,5},{8,10},{9,11},{10,... | collective-permute-start | bytes 552968 | tf_op jit(solution)/shard_map/ppermute | solution.py:239
  60.3 2.1 %fusion.6 = (bf16[36,1,320]{2,1,0:T(2,128)(2,1)}, bf16[36,1,320]{2,1,0:T(2,128)(2,1)}, bf16[36,1,320]{2,1,0:T(2,128)(2,1)}, bf16[36,1,320]{2,1,0:T(2,128)(2,1)}) fusion(bf16[72,32,320]{2,1,0:T(8,128)(2,1)} %shard_map.64.refs_0_), kind=kLoop, calls=%fused_computation.49 | loop fusion | bytes 184320 | tf_op jit(solution)/shard_map/slice | solution.py:276
  62.7 0.7 gather_fusion.2
  63.4 1.8 %collective-permute-done.11 = bf16[9,32,320]{2,1,0:T(8,128)(2,1)S(1)} collective-permute-done((bf16[9,32,320]{2,1,0:T(8,128)(2,1)}, bf16[9,32,320]{2,1,0:T(8,128)(2,1)S(1)}, u32[]{:S(2)}, u32[]{:S(2)}) %collective-permute-start.11) | collective-permute-done | bytes 184352 | tf_op jit(solution)/shard_map/ppermute | solution.py:239
  65.2 5.8 %collective-permute-done.12 = bf16[9,32,320]{2,1,0:T(8,128)(2,1)S(1)} collective-permute-done((bf16[9,32,320]{2,1,0:T(8,128)(2,1)}, bf16[9,32,320]{2,1,0:T(8,128)(2,1)S(1)}, u32[]{:S(2)}, u32[]{:S(2)}) %collective-permute-start.12) | collective-permute-done | bytes 184352 | tf_op jit(solution)/shard_map/ppermute | solution.py:239
  71.2 0.7 gather_fusion.3
  72.8 0.7 collective-permute-start.15
  73.7 1.6 %collective-permute-start.14 = (bf16[72,320]{1,0:T(8,128)(2,1)S(1)}, bf16[72,320]{1,0:T(8,128)(2,1)S(1)}, u32[]{:S(2)}, u32[]{:S(2)}) collective-permute-start(bf16[72,320]{1,0:T(8,128)(2,1)S(1)} %pad_maximum_fusion.2), channel_id=1, source_target_pairs={{12,0},{0,4},{4,8},{8,12},{13,1},{1,5},{5,9},{9,13},{14,2},{2,6},{... | collective-permute-start | bytes 138248 | tf_op jit(solution)/shard_map/ppermute | solution.py:16
  75.3 2.4 %collective-permute-done.15 = bf16[72,320]{1,0:T(8,128)(2,1)S(1)} collective-permute-done((bf16[72,320]{1,0:T(8,128)(2,1)S(1)}, bf16[72,320]{1,0:T(8,128)(2,1)S(1)}, u32[]{:S(2)}, u32[]{:S(2)}) %collective-permute-start.15) | collective-permute-done | bytes 46112 | tf_op jit(solution)/shard_map/ppermute | solution.py:16
  77.6 0.6 broadcast_select_fusion.2.refs_4_
  78.3 1.6 %collective-permute-done.14 = bf16[72,320]{1,0:T(8,128)(2,1)S(1)} collective-permute-done((bf16[72,320]{1,0:T(8,128)(2,1)S(1)}, bf16[72,320]{1,0:T(8,128)(2,1)S(1)}, u32[]{:S(2)}, u32[]{:S(2)}) %collective-permute-start.14) | collective-permute-done | bytes 46112 | tf_op jit(solution)/shard_map/ppermute | solution.py:16
  79.9 0.6 broadcast_select_fusion.4.refs_3_
  80.5 11.9 %shard_map.67 = bf16[72,32,320]{2,1,0:T(8,128)(2,1)} custom-call(bf16[72,32,320]{2,1,0:T(8,128)(2,1)} %shard_map.64.refs_0_, bf16[36,32,320]{2,1,0:T(8,128)(2,1)} %bitcast.44, bf16[36,32,320]{2,1,0:T(8,128)(2,1)} %bitcast.42, bf16[72,320]{1,0:T(8,128)(2,1)} %broadcast_select_fusion.4.refs_3_, bf16[72,320]{1,0:T(8,128)(2,1)} %broadcast_select_fusion.2.refs_4_, ...), custom_call_target="tpu_custom_call" | custom-call | tf_op jit(solution)/shard_map/pallas_call | solution.py:100
  (69 shorter events, 5.5 us)
Async XLA Ops:
  0.0 7.3 %copy-start = (f32[5,4,4]{0,2,1:T(4,128)S(1)}, f32[5,4,4]{0,2,1:T(4,128)}, u32[]{:S(2)}) copy-start(f32[5,4,4]{0,2,1:T(4,128)} %param.16) | copy-start | bytes 964
  2.1 6.9 %collective-permute-start.1 = (bf16[72,320]{1,0:T(8,128)(2,1)S(1)}, bf16[72,320]{1,0:T(8,128)(2,1)S(1)}, u32[]{:S(2)}, u32[]{:S(2)}) collective-permute-start(bf16[72,320]{1,0:T(8,128)(2,1)S(1)} %get-tuple-element.36), channel_id=1, source_target_pairs={{4,0},{8,4},{12,8},{0,12},{5,1},{9,5},{13,9},{1,13},{6,2},{10,6},{... | collective-permute-start | bytes 138248 | tf_op jit(solution)/shard_map/ppermute | solution.py:16
  7.2 6.0 %collective-permute-start = (bf16[72,320]{1,0:T(8,128)(2,1)S(1)}, bf16[72,320]{1,0:T(8,128)(2,1)S(1)}, u32[]{:S(2)}, u32[]{:S(2)}) collective-permute-start(bf16[72,320]{1,0:T(8,128)(2,1)S(1)} %get-tuple-element.37), channel_id=1, source_target_pairs={{12,0},{0,4},{4,8},{8,12},{13,1},{1,5},{5,9},{9,13},{14,2},{2,6},{... | collective-permute-start | bytes 138248 | tf_op jit(solution)/shard_map/ppermute | solution.py:16
  26.5 6.5 %copy-start.3 = (bf16[320,960]{1,0:T(8,128)(2,1)S(1)}, bf16[320,960]{1,0:T(8,128)(2,1)}, u32[]{:S(2)}) copy-start(bf16[320,960]{1,0:T(8,128)(2,1)} %param.14) | copy-start | bytes 1843204
  29.1 7.2 %collective-permute-start.2 = (bf16[9,32,320]{2,1,0:T(8,128)(2,1)S(1)}, bf16[9,32,320]{2,1,0:T(8,128)(2,1)S(1)}, u32[]{:S(2)}, u32[]{:S(2)}) collective-permute-start(bf16[9,32,320]{2,1,0:T(8,128)(2,1)S(1)} %get-tuple-element.34), channel_id=1, source_target_pairs={{0,1},{1,2},{2,3},{3,0},{4,5},{5,6},{6,7},{7,4},{8,9},{9,10},{10,1... | collective-permute-start | bytes 552968 | tf_op jit(solution)/shard_map/ppermute | solution.py:230
  29.1 8.7 %collective-permute-start.3 = (bf16[9,32,320]{2,1,0:T(8,128)(2,1)S(1)}, bf16[9,32,320]{2,1,0:T(8,128)(2,1)S(1)}, u32[]{:S(2)}, u32[]{:S(2)}) collective-permute-start(bf16[9,32,320]{2,1,0:T(8,128)(2,1)S(1)} %get-tuple-element.33), channel_id=1, source_target_pairs={{0,2},{1,3},{2,0},{3,1},{4,6},{5,7},{6,4},{7,5},{8,10},{9,11},{10,... | collective-permute-start | bytes 552968 | tf_op jit(solution)/shard_map/ppermute | solution.py:230
  30.6 10.5 %collective-permute-start.4 = (bf16[9,32,320]{2,1,0:T(8,128)(2,1)S(1)}, bf16[9,32,320]{2,1,0:T(8,128)(2,1)S(1)}, u32[]{:S(2)}, u32[]{:S(2)}) collective-permute-start(bf16[9,32,320]{2,1,0:T(8,128)(2,1)S(1)} %get-tuple-element.32), channel_id=1, source_target_pairs={{0,3},{1,0},{2,1},{3,2},{4,7},{5,4},{6,5},{7,6},{8,11},{9,8},{10,9... | collective-permute-start | bytes 552968 | tf_op jit(solution)/shard_map/ppermute | solution.py:230
  34.1 16.3 %collective-permute-start.10 = (bf16[9,32,320]{2,1,0:T(8,128)(2,1)S(1)}, bf16[9,32,320]{2,1,0:T(8,128)(2,1)S(1)}, u32[]{:S(2)}, u32[]{:S(2)}) collective-permute-start(bf16[9,32,320]{2,1,0:T(8,128)(2,1)S(1)} %get-tuple-element.28), channel_id=1, source_target_pairs={{0,3},{1,0},{2,1},{3,2},{4,7},{5,4},{6,5},{7,6},{8,11},{9,8},{10,9... | collective-permute-start | bytes 552968 | tf_op jit(solution)/shard_map/ppermute | solution.py:230
  34.1 16.3 %collective-permute-start.8 = (bf16[9,32,320]{2,1,0:T(8,128)(2,1)S(1)}, bf16[9,32,320]{2,1,0:T(8,128)(2,1)S(1)}, u32[]{:S(2)}, u32[]{:S(2)}) collective-permute-start(bf16[9,32,320]{2,1,0:T(8,128)(2,1)S(1)} %get-tuple-element.30), channel_id=1, source_target_pairs={{0,1},{1,2},{2,3},{3,0},{4,5},{5,6},{6,7},{7,4},{8,9},{9,10},{10,1... | collective-permute-start | bytes 552968 | tf_op jit(solution)/shard_map/ppermute | solution.py:230
  36.2 4.9 %copy-start.13 = (bf16[9,32,320]{2,1,0:T(8,128)(2,1)}, bf16[9,32,320]{2,1,0:T(8,128)(2,1)S(1)}, u32[]{:S(2)}) copy-start(bf16[9,32,320]{2,1,0:T(8,128)(2,1)S(1)} %collective-permute-done.2.refs_1_) | copy-start | bytes 552964
  36.2 14.8 %collective-permute-start.9 = (bf16[9,32,320]{2,1,0:T(8,128)(2,1)S(1)}, bf16[9,32,320]{2,1,0:T(8,128)(2,1)S(1)}, u32[]{:S(2)}, u32[]{:S(2)}) collective-permute-start(bf16[9,32,320]{2,1,0:T(8,128)(2,1)S(1)} %get-tuple-element.29), channel_id=1, source_target_pairs={{0,2},{1,3},{2,0},{3,1},{4,6},{5,7},{6,4},{7,5},{8,10},{9,11},{10,... | collective-permute-start | bytes 552968 | tf_op jit(solution)/shard_map/ppermute | solution.py:230
  37.8 3.4 %copy-start.14 = (bf16[9,32,320]{2,1,0:T(8,128)(2,1)}, bf16[9,32,320]{2,1,0:T(8,128)(2,1)S(1)}, u32[]{:S(2)}) copy-start(bf16[9,32,320]{2,1,0:T(8,128)(2,1)S(1)} %collective-permute-done.3.refs_2_) | copy-start | bytes 552964
  41.1 0.7 copy-start.15
  47.6 14.8 %copy-start.4 = (bf16[9,32,320]{2,1,0:T(8,128)(2,1)S(1)}, bf16[9,32,320]{2,1,0:T(8,128)(2,1)}, u32[]{:S(2)}) copy-start(bf16[9,32,320]{2,1,0:T(8,128)(2,1)} %get-tuple-element.16) | copy-start | bytes 552964
  47.6 12.7 %collective-permute-start.5 = (bf16[9,32,320]{2,1,0:T(8,128)(2,1)}, bf16[9,32,320]{2,1,0:T(8,128)(2,1)S(1)}, u32[]{:S(2)}, u32[]{:S(2)}) collective-permute-start(bf16[9,32,320]{2,1,0:T(8,128)(2,1)} %get-tuple-element.17), channel_id=1, source_target_pairs={{0,3},{1,0},{2,1},{3,2},{4,7},{5,4},{6,5},{7,6},{8,11},{9,8},{10,9... | collective-permute-start | bytes 552968 | tf_op jit(solution)/shard_map/ppermute | solution.py:239
  49.8 12.6 %collective-permute-start.6 = (bf16[9,32,320]{2,1,0:T(8,128)(2,1)}, bf16[9,32,320]{2,1,0:T(8,128)(2,1)S(1)}, u32[]{:S(2)}, u32[]{:S(2)}) collective-permute-start(bf16[9,32,320]{2,1,0:T(8,128)(2,1)} %get-tuple-element.18), channel_id=1, source_target_pairs={{0,2},{1,3},{2,0},{3,1},{4,6},{5,7},{6,4},{7,5},{8,10},{9,11},{10,... | collective-permute-start | bytes 552968 | tf_op jit(solution)/shard_map/ppermute | solution.py:239
  50.4 0.7 copy-start.10
  50.4 12.0 %collective-permute-start.7 = (bf16[9,32,320]{2,1,0:T(8,128)(2,1)}, bf16[9,32,320]{2,1,0:T(8,128)(2,1)S(1)}, u32[]{:S(2)}, u32[]{:S(2)}) collective-permute-start(bf16[9,32,320]{2,1,0:T(8,128)(2,1)} %get-tuple-element.19), channel_id=1, source_target_pairs={{0,1},{1,2},{2,3},{3,0},{4,5},{5,6},{6,7},{7,4},{8,9},{9,10},{10,1... | collective-permute-start | bytes 552968 | tf_op jit(solution)/shard_map/ppermute | solution.py:239
  50.4 0.7 copy-start.11
  51.0 0.7 copy-start.12
  57.5 7.7 %collective-permute-start.11 = (bf16[9,32,320]{2,1,0:T(8,128)(2,1)}, bf16[9,32,320]{2,1,0:T(8,128)(2,1)S(1)}, u32[]{:S(2)}, u32[]{:S(2)}) collective-permute-start(bf16[9,32,320]{2,1,0:T(8,128)(2,1)} %get-tuple-element.21), channel_id=1, source_target_pairs={{0,3},{1,0},{2,1},{3,2},{4,7},{5,4},{6,5},{7,6},{8,11},{9,8},{10,9... | collective-permute-start | bytes 552968 | tf_op jit(solution)/shard_map/ppermute | solution.py:239
  58.8 12.2 %collective-permute-start.12 = (bf16[9,32,320]{2,1,0:T(8,128)(2,1)}, bf16[9,32,320]{2,1,0:T(8,128)(2,1)S(1)}, u32[]{:S(2)}, u32[]{:S(2)}) collective-permute-start(bf16[9,32,320]{2,1,0:T(8,128)(2,1)} %get-tuple-element.22), channel_id=1, source_target_pairs={{0,2},{1,3},{2,0},{3,1},{4,6},{5,7},{6,4},{7,5},{8,10},{9,11},{10,... | collective-permute-start | bytes 552968 | tf_op jit(solution)/shard_map/ppermute | solution.py:239
  60.3 10.7 %collective-permute-start.13 = (bf16[9,32,320]{2,1,0:T(8,128)(2,1)}, bf16[9,32,320]{2,1,0:T(8,128)(2,1)S(1)}, u32[]{:S(2)}, u32[]{:S(2)}) collective-permute-start(bf16[9,32,320]{2,1,0:T(8,128)(2,1)} %get-tuple-element.23), channel_id=1, source_target_pairs={{0,1},{1,2},{2,3},{3,0},{4,5},{5,6},{6,7},{7,4},{8,9},{9,10},{10,1... | collective-permute-start | bytes 552968 | tf_op jit(solution)/shard_map/ppermute | solution.py:239
  62.4 8.6 %copy-start.5 = (bf16[9,32,320]{2,1,0:T(8,128)(2,1)S(1)}, bf16[9,32,320]{2,1,0:T(8,128)(2,1)}, u32[]{:S(2)}) copy-start(bf16[9,32,320]{2,1,0:T(8,128)(2,1)} %get-tuple-element.20) | copy-start | bytes 552964
  71.9 0.8 copy-start.9
  72.0 0.8 copy-start.8
  72.0 1.6 %copy-start.7 = (bf16[36,1,320]{2,1,0:T(2,128)(2,1)S(1)}, bf16[36,1,320]{2,1,0:T(2,128)(2,1)}, u32[]{:S(2)}) copy-start(bf16[36,1,320]{2,1,0:T(2,128)(2,1)} %get-tuple-element.26) | copy-start | bytes 69124
  72.0 1.6 %copy-start.6 = (bf16[36,1,320]{2,1,0:T(2,128)(2,1)S(1)}, bf16[36,1,320]{2,1,0:T(2,128)(2,1)}, u32[]{:S(2)}) copy-start(bf16[36,1,320]{2,1,0:T(2,128)(2,1)} %get-tuple-element.25) | copy-start | bytes 69124
  72.3 8.3 %copy-start.1 = (bf16[4,9,32,320]{3,2,1,0:T(8,128)(2,1)}, bf16[4,9,32,320]{3,2,1,0:T(8,128)(2,1)S(1)}, u32[]{:S(2)}) copy-start(bf16[4,9,32,320]{3,2,1,0:T(8,128)(2,1)S(1)} %get-tuple-element.42) | copy-start | bytes 2211844
  72.3 8.3 %copy-start.2 = (bf16[4,9,32,320]{3,2,1,0:T(8,128)(2,1)}, bf16[4,9,32,320]{3,2,1,0:T(8,128)(2,1)S(1)}, u32[]{:S(2)}) copy-start(bf16[4,9,32,320]{3,2,1,0:T(8,128)(2,1)S(1)} %get-tuple-element.43) | copy-start | bytes 2211844
  72.8 4.8 %collective-permute-start.15 = (bf16[72,320]{1,0:T(8,128)(2,1)S(1)}, bf16[72,320]{1,0:T(8,128)(2,1)S(1)}, u32[]{:S(2)}, u32[]{:S(2)}) collective-permute-start(bf16[72,320]{1,0:T(8,128)(2,1)S(1)} %pad_maximum_fusion.3), channel_id=1, source_target_pairs={{4,0},{8,4},{12,8},{0,12},{5,1},{9,5},{13,9},{1,13},{6,2},{10,6},{... | collective-permute-start | bytes 138248 | tf_op jit(solution)/shard_map/ppermute | solution.py:16
  73.7 6.2 %collective-permute-start.14 = (bf16[72,320]{1,0:T(8,128)(2,1)S(1)}, bf16[72,320]{1,0:T(8,128)(2,1)S(1)}, u32[]{:S(2)}, u32[]{:S(2)}) collective-permute-start(bf16[72,320]{1,0:T(8,128)(2,1)S(1)} %pad_maximum_fusion.2), channel_id=1, source_target_pairs={{12,0},{0,4},{4,8},{8,12},{13,1},{1,5},{5,9},{9,13},{14,2},{2,6},{... | collective-permute-start | bytes 138248 | tf_op jit(solution)/shard_map/ppermute | solution.py:16

commit v14 on v13

--- a/solution.py
+++ b/solution.py
@@ -246,7 +246,11 @@
     frames_dev, row_count, col_count, channels = latents.shape
     frames_all = lax.axis_size("frame")
     tile = latents.reshape(row_count, col_count, channels)
-    rims = halo(lambda c: tile[:, c, :])
+    def tile_edge(c):
+        pick = (jnp.arange(col_count) == c % col_count).astype(tile.dtype)
+        return jnp.einsum("rwc,w->rc", tile, pick, preferred_element_type=jnp.float32).astype(tile.dtype)
+
+    rims = halo(tile_edge)
     half = row_count // 2
     returned = []
     rotate = frames_all <= 4 and half % frames_all == 0

time: 92.8 us -> 92.6 us (level)
  matrix products: 0 us -> 2.29 us
  local copies, waits for them, and re-layouts: 13.3 us -> 11.2 us
    dot_general x0 -> x2, matrix products: none -> 2.29 us  [tile_edge(): jnp.einsum('rwc,w->rc', tile, pick, preferred_element_type=jnp.float32)]
    unnamed x34 -> x35, local copies, waits for them, and re-layouts: 4.97 us -> 2.87 us
  transfers between devices with their start and end apart: 16 -> 16, of which waited for: 9 -> 8; matrix products, arithmetic and copies ran while one was open for 8% -> 9% of each run, Pallas kernels for 13% -> 13%
where the time goes in v14:
time: 92.6 us; the launch traced here: 92.3 us
  Pallas kernels  36.2 us (39%)
  waiting for transfers between devices  20.7 us (22%)
  starting transfers between devices  18.1 us (20%)
  local copies, waits for them, and re-layouts  11.2 us (12%)
  other arithmetic  3.51 us (4%)
  matrix products  2.29 us (2%)
    pallas_call x2, Pallas kernels, convolve(): pl.pallas_call(functools.partial(conv_kernel, layout=tuple(layout), lo=lo...  24.6 us
    pallas_call x2, Pallas kernels, attend_pieces(): pl.pallas_call(functools.partial(attend_kernel, parts=frames_all), out_sh...  11.6 us
    ppermute x6, waiting for transfers between devices, rotated_attention(): lax.ppermute(piece, 'frame', [(i, (i - s) % frames_all) for i in range(fr...  7.58 us
    ppermute x4, waiting for transfers between devices, shifted(): moved = lax.ppermute(block, axis, route)  7.55 us
    ppermute x4, starting transfers between devices, shifted(): moved = lax.ppermute(block, axis, route)  7.51 us
    ppermute x6, starting transfers between devices, rotated_attention(): lax.ppermute(piece, 'frame', [(i, (i - s) % frames_all) for i in range(fr...  5.56 us
    ppermute x6, waiting for transfers between devices, rotated_attention(): lax.ppermute(piece, 'frame', [(i, (i + s) % frames_all) for i in range(fr...  5.54 us
    ppermute x6, starting transfers between devices, rotated_attention(): lax.ppermute(piece, 'frame', [(i, (i + s) % frames_all) for i in range(fr...  5.01 us
  transfers between devices with their start and end apart: 16, of which 8 were waited for; matrix products, arithmetic and copies ran while one was open for 9% of the time, Pallas kernels for 13%

profile of v14, /device:TPU:0, one launch (start us, length us, event | category | flops | bytes accessed | tf_op | source)
XLA Modules:
  0.0 92.3 jit_solution(11588589335692255225)
XLA Ops:
  0.0 1.9 %fusion.4 = bf16[1,72,320]{2,0,1:T(2,128)(2,1)S(1)} fusion(bf16[1,72,32,320]{3,2,1,0:T(8,128)(2,1)} %param.12), kind=kOutput, calls=%fused_computation.42 | convolution fusion | flops 1474592 | bytes 1520640 | tf_op jit(solution)/shard_map/rwc,w->rc/dot_general | solution.py:251
  2.0 5.1 %collective-permute-start.1 = (bf16[72,320]{1,0:T(8,128)(2,1)S(1)}, bf16[72,320]{1,0:T(8,128)(2,1)S(1)}, u32[]{:S(2)}, u32[]{:S(2)}) collective-permute-start(bf16[72,320]{1,0:T(8,128)(2,1)S(1)} %bitcast.64), channel_id=1, source_target_pairs={{4,0},{8,4},{12,8},{0,12},{5,1},{9,5},{13,9},{1,13},{6,2},{10,6},{... | collective-permute-start | bytes 138248 | tf_op jit(solution)/shard_map/ppermute | solution.py:16
  8.9 0.6 broadcast_select_fusion.3.refs_2_
  9.5 3.9 %collective-permute-done = bf16[72,320]{1,0:T(8,128)(2,1)S(1)} collective-permute-done((bf16[72,320]{1,0:T(8,128)(2,1)S(1)}, bf16[72,320]{1,0:T(8,128)(2,1)S(1)}, u32[]{:S(2)}, u32[]{:S(2)}) %collective-permute-start) | collective-permute-done | bytes 46112 | tf_op jit(solution)/shard_map/ppermute | solution.py:16
  13.5 0.6 broadcast_select_fusion.5.refs_1_
  14.1 12.6 %shard_map.64.refs_0_ = bf16[72,32,320]{2,1,0:T(8,128)(2,1)} custom-call(bf16[72,32,320]{2,1,0:T(8,128)(2,1)} %bitcast.47, bf16[72,320]{1,0:T(8,128)(2,1)} %broadcast_select_fusion.5.refs_1_, bf16[72,320]{1,0:T(8,128)(2,1)} %broadcast_select_fusion.3.refs_2_, bf16[3,960,320]{2,1,0:T(8,128)(2,1)} %bitcast.54), custom_call_target="tpu_custom_call" | custom-call | tf_op jit(solution)/shard_map/pallas_call | solution.py:100
  26.7 2.6 %constant_dynamic-slice_fusion = (bf16[9,32,320]{2,1,0:T(8,128)(2,1)S(1)}, bf16[9,32,320]{2,1,0:T(8,128)(2,1)S(1)}, bf16[9,32,320]{2,1,0:T(8,128)(2,1)S(1)}, bf1...) fusion(bf16[72,32,320]{2,1,0:T(8,128)(2,1)} %shard_map.64.refs_, ...), kind=kLoop, calls=%fused_computation.34 | loop fusion | bytes 2949152 | tf_op jit(solution)/shard_map/dynamic_slice | solution.py:228
  29.3 1.5 %collective-permute-start.3 = (bf16[9,32,320]{2,1,0:T(8,128)(2,1)S(1)}, bf16[9,32,320]{2,1,0:T(8,128)(2,1)S(1)}, u32[]{:S(2)}, u32[]{:S(2)}) collective-permute-start(bf16[9,32,320]{2,1,0:T(8,128)(2,1)S(1)} %get-tuple-element.33), channel_id=1, source_target_pairs={{0,2},{1,3},{2,0},{3,1},{4,6},{5,7},{6,4},{7,5},{8,10},{9,11},{10,... | collective-permute-start | bytes 552968 | tf_op jit(solution)/shard_map/ppermute | solution.py:230
  30.9 1.4 %collective-permute-start.4 = (bf16[9,32,320]{2,1,0:T(8,128)(2,1)S(1)}, bf16[9,32,320]{2,1,0:T(8,128)(2,1)S(1)}, u32[]{:S(2)}, u32[]{:S(2)}) collective-permute-start(bf16[9,32,320]{2,1,0:T(8,128)(2,1)S(1)} %get-tuple-element.32), channel_id=1, source_target_pairs={{0,3},{1,0},{2,1},{3,2},{4,7},{5,4},{6,5},{7,6},{8,11},{9,8},{10,9... | collective-permute-start | bytes 552968 | tf_op jit(solution)/shard_map/ppermute | solution.py:230
  32.4 0.8 copy.32.refs_5_
  33.2 1.2 %copy.30 = bf16[320,960]{0,1:T(8,128)(2,1)} copy(bf16[320,960]{1,0:T(8,128)(2,1)S(1)} %copy-done.4) | data formatting | bytes 1228800 | tf_op args[2]
  34.9 1.6 %collective-permute-done.2.refs_1_ = bf16[9,32,320]{2,1,0:T(8,128)(2,1)S(1)} collective-permute-done((bf16[9,32,320]{2,1,0:T(8,128)(2,1)S(1)}, bf16[9,32,320]{2,1,0:T(8,128)(2,1)S(1)}, u32[]{:S(2)}, u32[]{:S(2)}) %collective-permute-start.2) | collective-permute-done | bytes 184352 | tf_op jit(solution)/shard_map/ppermute | solution.py:230
  36.5 1.5 %collective-permute-start.9 = (bf16[9,32,320]{2,1,0:T(8,128)(2,1)S(1)}, bf16[9,32,320]{2,1,0:T(8,128)(2,1)S(1)}, u32[]{:S(2)}, u32[]{:S(2)}) collective-permute-start(bf16[9,32,320]{2,1,0:T(8,128)(2,1)S(1)} %get-tuple-element.29), channel_id=1, source_target_pairs={{0,2},{1,3},{2,0},{3,1},{4,6},{5,7},{6,4},{7,5},{8,10},{9,11},{10,... | collective-permute-start | bytes 552968 | tf_op jit(solution)/shard_map/ppermute | solution.py:230
  38.0 3.4 %collective-permute-done.4.refs_3_ = bf16[9,32,320]{2,1,0:T(8,128)(2,1)S(1)} collective-permute-done((bf16[9,32,320]{2,1,0:T(8,128)(2,1)S(1)}, bf16[9,32,320]{2,1,0:T(8,128)(2,1)S(1)}, u32[]{:S(2)}, u32[]{:S(2)}) %collective-permute-start.4) | collective-permute-done | bytes 184352 | tf_op jit(solution)/shard_map/ppermute | solution.py:230
  41.4 0.7 copy-done.16
  42.1 5.8 %shard_map.65 = (bf16[9,32,320]{2,1,0:T(8,128)(2,1)}, bf16[9,32,320]{2,1,0:T(8,128)(2,1)}, bf16[9,32,320]{2,1,0:T(8,128)(2,1)}, bf16[9,32,320]{2,1,0:T(8,128)(2,1)}) custom-call(bf16[9,32,320]{2,1,0:T(8,128)(2,1)} %get-tuple-element.35.refs_0_, bf16[9,32,320]{2,1,0:T(8,128)(2,1)} %copy-done.14, bf16[9,32,320]{2,1,0:T(8,128)(2,1)} %copy-done.15, ...), custom_call_target="tpu_custom_call" | custom-call | tf_op jit(solution)/shard_map/pallas_call | solution.py:194
  47.9 2.2 %collective-permute-start.5 = (bf16[9,32,320]{2,1,0:T(8,128)(2,1)}, bf16[9,32,320]{2,1,0:T(8,128)(2,1)S(1)}, u32[]{:S(2)}, u32[]{:S(2)}) collective-permute-start(bf16[9,32,320]{2,1,0:T(8,128)(2,1)} %get-tuple-element.17), channel_id=1, source_target_pairs={{0,3},{1,0},{2,1},{3,2},{4,7},{5,4},{6,5},{7,6},{8,11},{9,8},{10,9... | collective-permute-start | bytes 552968 | tf_op jit(solution)/shard_map/ppermute | solution.py:239
  50.1 0.6 collective-permute-start.6
  52.0 5.8 %shard_map.66 = (bf16[9,32,320]{2,1,0:T(8,128)(2,1)}, bf16[9,32,320]{2,1,0:T(8,128)(2,1)}, bf16[9,32,320]{2,1,0:T(8,128)(2,1)}, bf16[9,32,320]{2,1,0:T(8,128)(2,1)}) custom-call(bf16[9,32,320]{2,1,0:T(8,128)(2,1)} %get-tuple-element.31.refs_0_, bf16[9,32,320]{2,1,0:T(8,128)(2,1)} %copy-done.12, bf16[9,32,320]{2,1,0:T(8,128)(2,1)} %copy-done.13, ...), custom_call_target="tpu_custom_call" | custom-call | tf_op jit(solution)/shard_map/pallas_call | solution.py:194
  57.8 1.3 %collective-permute-start.11 = (bf16[9,32,320]{2,1,0:T(8,128)(2,1)}, bf16[9,32,320]{2,1,0:T(8,128)(2,1)S(1)}, u32[]{:S(2)}, u32[]{:S(2)}) collective-permute-start(bf16[9,32,320]{2,1,0:T(8,128)(2,1)} %get-tuple-element.21), channel_id=1, source_target_pairs={{0,3},{1,0},{2,1},{3,2},{4,7},{5,4},{6,5},{7,6},{8,11},{9,8},{10,9... | collective-permute-start | bytes 552968 | tf_op jit(solution)/shard_map/ppermute | solution.py:239
  59.0 1.5 %collective-permute-start.12 = (bf16[9,32,320]{2,1,0:T(8,128)(2,1)}, bf16[9,32,320]{2,1,0:T(8,128)(2,1)S(1)}, u32[]{:S(2)}, u32[]{:S(2)}) collective-permute-start(bf16[9,32,320]{2,1,0:T(8,128)(2,1)} %get-tuple-element.22), channel_id=1, source_target_pairs={{0,2},{1,3},{2,0},{3,1},{4,6},{5,7},{6,4},{7,5},{8,10},{9,11},{10,... | collective-permute-start | bytes 552968 | tf_op jit(solution)/shard_map/ppermute | solution.py:239
  60.6 2.1 %fusion.19 = (bf16[36,1,320]{2,1,0:T(2,128)(2,1)}, bf16[36,1,320]{2,1,0:T(2,128)(2,1)}, bf16[36,1,320]{2,1,0:T(2,128)(2,1)}, bf16[36,1,320]{2,1,0:T(2,128)(2,1)}) fusion(bf16[72,32,320]{2,1,0:T(8,128)(2,1)} %shard_map.64.refs_0_), kind=kLoop, calls=%fused_computation.61 | loop fusion | bytes 184320 | tf_op jit(solution)/shard_map/slice | solution.py:280
  62.9 0.7 gather_fusion.2
  63.7 1.8 %collective-permute-done.11 = bf16[9,32,320]{2,1,0:T(8,128)(2,1)S(1)} collective-permute-done((bf16[9,32,320]{2,1,0:T(8,128)(2,1)}, bf16[9,32,320]{2,1,0:T(8,128)(2,1)S(1)}, u32[]{:S(2)}, u32[]{:S(2)}) %collective-permute-start.11) | collective-permute-done | bytes 184352 | tf_op jit(solution)/shard_map/ppermute | solution.py:239
  65.4 5.8 %collective-permute-done.12 = bf16[9,32,320]{2,1,0:T(8,128)(2,1)S(1)} collective-permute-done((bf16[9,32,320]{2,1,0:T(8,128)(2,1)}, bf16[9,32,320]{2,1,0:T(8,128)(2,1)S(1)}, u32[]{:S(2)}, u32[]{:S(2)}) %collective-permute-start.12) | collective-permute-done | bytes 184352 | tf_op jit(solution)/shard_map/ppermute | solution.py:239
  71.5 0.7 gather_fusion.3
  73.5 2.0 %collective-permute-start.14 = (bf16[72,320]{1,0:T(8,128)(2,1)S(1)}, bf16[72,320]{1,0:T(8,128)(2,1)S(1)}, u32[]{:S(2)}, u32[]{:S(2)}) collective-permute-start(bf16[72,320]{1,0:T(8,128)(2,1)S(1)} %pad_maximum_fusion.2), channel_id=1, source_target_pairs={{12,0},{0,4},{4,8},{8,12},{13,1},{1,5},{5,9},{9,13},{14,2},{2,6},{... | collective-permute-start | bytes 138248 | tf_op jit(solution)/shard_map/ppermute | solution.py:16
  75.5 2.2 %collective-permute-done.15 = bf16[72,320]{1,0:T(8,128)(2,1)S(1)} collective-permute-done((bf16[72,320]{1,0:T(8,128)(2,1)S(1)}, bf16[72,320]{1,0:T(8,128)(2,1)S(1)}, u32[]{:S(2)}, u32[]{:S(2)}) %collective-permute-start.15) | collective-permute-done | bytes 46112 | tf_op jit(solution)/shard_map/ppermute | solution.py:16
  77.7 0.6 broadcast_select_fusion.2.refs_4_
  78.4 1.4 %collective-permute-done.14 = bf16[72,320]{1,0:T(8,128)(2,1)S(1)} collective-permute-done((bf16[72,320]{1,0:T(8,128)(2,1)S(1)}, bf16[72,320]{1,0:T(8,128)(2,1)S(1)}, u32[]{:S(2)}, u32[]{:S(2)}) %collective-permute-start.14) | collective-permute-done | bytes 46112 | tf_op jit(solution)/shard_map/ppermute | solution.py:16
  79.7 0.6 broadcast_select_fusion.4.refs_3_
  80.4 11.9 %shard_map.67 = bf16[72,32,320]{2,1,0:T(8,128)(2,1)} custom-call(bf16[72,32,320]{2,1,0:T(8,128)(2,1)} %shard_map.64.refs_0_, bf16[36,32,320]{2,1,0:T(8,128)(2,1)} %bitcast.53, bf16[36,32,320]{2,1,0:T(8,128)(2,1)} %bitcast.51, bf16[72,320]{1,0:T(8,128)(2,1)} %broadcast_select_fusion.4.refs_3_, bf16[72,320]{1,0:T(8,128)(2,1)} %broadcast_select_fusion.2.refs_4_, ...), custom_call_target="tpu_custom_call" | custom-call | tf_op jit(solution)/shard_map/pallas_call | solution.py:100
  (73 shorter events, 5.2 us)
Async XLA Ops:
  0.0 7.6 %copy-start = (f32[5,4,4]{0,2,1:T(4,128)S(1)}, f32[5,4,4]{0,2,1:T(4,128)}, u32[]{:S(2)}) copy-start(f32[5,4,4]{0,2,1:T(4,128)} %param.16) | copy-start | bytes 964
  0.0 7.1 %copy-start.1 = (bf16[1,72,32,320]{3,2,1,0:T(8,128)(2,1)S(1)}, bf16[1,72,32,320]{3,2,1,0:T(8,128)(2,1)}, u32[]{:S(2)}) copy-start(bf16[1,72,32,320]{3,2,1,0:T(8,128)(2,1)} %param.12) | copy-start | bytes 4423684
  2.0 6.9 %collective-permute-start.1 = (bf16[72,320]{1,0:T(8,128)(2,1)S(1)}, bf16[72,320]{1,0:T(8,128)(2,1)S(1)}, u32[]{:S(2)}, u32[]{:S(2)}) collective-permute-start(bf16[72,320]{1,0:T(8,128)(2,1)S(1)} %bitcast.64), channel_id=1, source_target_pairs={{4,0},{8,4},{12,8},{0,12},{5,1},{9,5},{13,9},{1,13},{6,2},{10,6},{... | collective-permute-start | bytes 138248 | tf_op jit(solution)/shard_map/ppermute | solution.py:16
  7.4 6.0 %collective-permute-start = (bf16[72,320]{1,0:T(8,128)(2,1)S(1)}, bf16[72,320]{1,0:T(8,128)(2,1)S(1)}, u32[]{:S(2)}, u32[]{:S(2)}) collective-permute-start(bf16[72,320]{1,0:T(8,128)(2,1)S(1)} %bitcast.65), channel_id=1, source_target_pairs={{12,0},{0,4},{4,8},{8,12},{13,1},{1,5},{5,9},{9,13},{14,2},{2,6},{... | collective-permute-start | bytes 138248 | tf_op jit(solution)/shard_map/ppermute | solution.py:16
  26.7 6.5 %copy-start.4 = (bf16[320,960]{1,0:T(8,128)(2,1)S(1)}, bf16[320,960]{1,0:T(8,128)(2,1)}, u32[]{:S(2)}) copy-start(bf16[320,960]{1,0:T(8,128)(2,1)} %param.14) | copy-start | bytes 1843204
  29.3 7.2 %collective-permute-start.2 = (bf16[9,32,320]{2,1,0:T(8,128)(2,1)S(1)}, bf16[9,32,320]{2,1,0:T(8,128)(2,1)S(1)}, u32[]{:S(2)}, u32[]{:S(2)}) collective-permute-start(bf16[9,32,320]{2,1,0:T(8,128)(2,1)S(1)} %get-tuple-element.34), channel_id=1, source_target_pairs={{0,1},{1,2},{2,3},{3,0},{4,5},{5,6},{6,7},{7,4},{8,9},{9,10},{10,1... | collective-permute-start | bytes 552968 | tf_op jit(solution)/shard_map/ppermute | solution.py:230
  29.3 8.7 %collective-permute-start.3 = (bf16[9,32,320]{2,1,0:T(8,128)(2,1)S(1)}, bf16[9,32,320]{2,1,0:T(8,128)(2,1)S(1)}, u32[]{:S(2)}, u32[]{:S(2)}) collective-permute-start(bf16[9,32,320]{2,1,0:T(8,128)(2,1)S(1)} %get-tuple-element.33), channel_id=1, source_target_pairs={{0,2},{1,3},{2,0},{3,1},{4,6},{5,7},{6,4},{7,5},{8,10},{9,11},{10,... | collective-permute-start | bytes 552968 | tf_op jit(solution)/shard_map/ppermute | solution.py:230
  30.9 10.5 %collective-permute-start.4 = (bf16[9,32,320]{2,1,0:T(8,128)(2,1)S(1)}, bf16[9,32,320]{2,1,0:T(8,128)(2,1)S(1)}, u32[]{:S(2)}, u32[]{:S(2)}) collective-permute-start(bf16[9,32,320]{2,1,0:T(8,128)(2,1)S(1)} %get-tuple-element.32), channel_id=1, source_target_pairs={{0,3},{1,0},{2,1},{3,2},{4,7},{5,4},{6,5},{7,6},{8,11},{9,8},{10,9... | collective-permute-start | bytes 552968 | tf_op jit(solution)/shard_map/ppermute | solution.py:230
  34.4 16.3 %collective-permute-start.10 = (bf16[9,32,320]{2,1,0:T(8,128)(2,1)S(1)}, bf16[9,32,320]{2,1,0:T(8,128)(2,1)S(1)}, u32[]{:S(2)}, u32[]{:S(2)}) collective-permute-start(bf16[9,32,320]{2,1,0:T(8,128)(2,1)S(1)} %get-tuple-element.28), channel_id=1, source_target_pairs={{0,3},{1,0},{2,1},{3,2},{4,7},{5,4},{6,5},{7,6},{8,11},{9,8},{10,9... | collective-permute-start | bytes 552968 | tf_op jit(solution)/shard_map/ppermute | solution.py:230
  34.4 16.3 %collective-permute-start.8 = (bf16[9,32,320]{2,1,0:T(8,128)(2,1)S(1)}, bf16[9,32,320]{2,1,0:T(8,128)(2,1)S(1)}, u32[]{:S(2)}, u32[]{:S(2)}) collective-permute-start(bf16[9,32,320]{2,1,0:T(8,128)(2,1)S(1)} %get-tuple-element.30), channel_id=1, source_target_pairs={{0,1},{1,2},{2,3},{3,0},{4,5},{5,6},{6,7},{7,4},{8,9},{9,10},{10,1... | collective-permute-start | bytes 552968 | tf_op jit(solution)/shard_map/ppermute | solution.py:230
  36.5 4.9 %copy-start.14 = (bf16[9,32,320]{2,1,0:T(8,128)(2,1)}, bf16[9,32,320]{2,1,0:T(8,128)(2,1)S(1)}, u32[]{:S(2)}) copy-start(bf16[9,32,320]{2,1,0:T(8,128)(2,1)S(1)} %collective-permute-done.2.refs_1_) | copy-start | bytes 552964
  36.5 14.8 %collective-permute-start.9 = (bf16[9,32,320]{2,1,0:T(8,128)(2,1)S(1)}, bf16[9,32,320]{2,1,0:T(8,128)(2,1)S(1)}, u32[]{:S(2)}, u32[]{:S(2)}) collective-permute-start(bf16[9,32,320]{2,1,0:T(8,128)(2,1)S(1)} %get-tuple-element.29), channel_id=1, source_target_pairs={{0,2},{1,3},{2,0},{3,1},{4,6},{5,7},{6,4},{7,5},{8,10},{9,11},{10,... | collective-permute-start | bytes 552968 | tf_op jit(solution)/shard_map/ppermute | solution.py:230
  38.0 3.4 %copy-start.15 = (bf16[9,32,320]{2,1,0:T(8,128)(2,1)}, bf16[9,32,320]{2,1,0:T(8,128)(2,1)S(1)}, u32[]{:S(2)}) copy-start(bf16[9,32,320]{2,1,0:T(8,128)(2,1)S(1)} %collective-permute-done.3.refs_2_) | copy-start | bytes 552964
  47.9 14.8 %copy-start.5 = (bf16[9,32,320]{2,1,0:T(8,128)(2,1)S(1)}, bf16[9,32,320]{2,1,0:T(8,128)(2,1)}, u32[]{:S(2)}) copy-start(bf16[9,32,320]{2,1,0:T(8,128)(2,1)} %get-tuple-element.16) | copy-start | bytes 552964
  47.9 12.7 %collective-permute-start.5 = (bf16[9,32,320]{2,1,0:T(8,128)(2,1)}, bf16[9,32,320]{2,1,0:T(8,128)(2,1)S(1)}, u32[]{:S(2)}, u32[]{:S(2)}) collective-permute-start(bf16[9,32,320]{2,1,0:T(8,128)(2,1)} %get-tuple-element.17), channel_id=1, source_target_pairs={{0,3},{1,0},{2,1},{3,2},{4,7},{5,4},{6,5},{7,6},{8,11},{9,8},{10,9... | collective-permute-start | bytes 552968 | tf_op jit(solution)/shard_map/ppermute | solution.py:239
  50.1 12.6 %collective-permute-start.6 = (bf16[9,32,320]{2,1,0:T(8,128)(2,1)}, bf16[9,32,320]{2,1,0:T(8,128)(2,1)S(1)}, u32[]{:S(2)}, u32[]{:S(2)}) collective-permute-start(bf16[9,32,320]{2,1,0:T(8,128)(2,1)} %get-tuple-element.18), channel_id=1, source_target_pairs={{0,2},{1,3},{2,0},{3,1},{4,6},{5,7},{6,4},{7,5},{8,10},{9,11},{10,... | collective-permute-start | bytes 552968 | tf_op jit(solution)/shard_map/ppermute | solution.py:239
  50.7 0.7 copy-start.11
  50.7 12.0 %collective-permute-start.7 = (bf16[9,32,320]{2,1,0:T(8,128)(2,1)}, bf16[9,32,320]{2,1,0:T(8,128)(2,1)S(1)}, u32[]{:S(2)}, u32[]{:S(2)}) collective-permute-start(bf16[9,32,320]{2,1,0:T(8,128)(2,1)} %get-tuple-element.19), channel_id=1, source_target_pairs={{0,1},{1,2},{2,3},{3,0},{4,5},{5,6},{6,7},{7,4},{8,9},{9,10},{10,1... | collective-permute-start | bytes 552968 | tf_op jit(solution)/shard_map/ppermute | solution.py:239
  50.7 0.7 copy-start.12
  51.3 0.7 copy-start.13
  57.8 7.7 %collective-permute-start.11 = (bf16[9,32,320]{2,1,0:T(8,128)(2,1)}, bf16[9,32,320]{2,1,0:T(8,128)(2,1)S(1)}, u32[]{:S(2)}, u32[]{:S(2)}) collective-permute-start(bf16[9,32,320]{2,1,0:T(8,128)(2,1)} %get-tuple-element.21), channel_id=1, source_target_pairs={{0,3},{1,0},{2,1},{3,2},{4,7},{5,4},{6,5},{7,6},{8,11},{9,8},{10,9... | collective-permute-start | bytes 552968 | tf_op jit(solution)/shard_map/ppermute | solution.py:239
  59.0 12.2 %collective-permute-start.12 = (bf16[9,32,320]{2,1,0:T(8,128)(2,1)}, bf16[9,32,320]{2,1,0:T(8,128)(2,1)S(1)}, u32[]{:S(2)}, u32[]{:S(2)}) collective-permute-start(bf16[9,32,320]{2,1,0:T(8,128)(2,1)} %get-tuple-element.22), channel_id=1, source_target_pairs={{0,2},{1,3},{2,0},{3,1},{4,6},{5,7},{6,4},{7,5},{8,10},{9,11},{10,... | collective-permute-start | bytes 552968 | tf_op jit(solution)/shard_map/ppermute | solution.py:239
  60.6 10.7 %collective-permute-start.13 = (bf16[9,32,320]{2,1,0:T(8,128)(2,1)}, bf16[9,32,320]{2,1,0:T(8,128)(2,1)S(1)}, u32[]{:S(2)}, u32[]{:S(2)}) collective-permute-start(bf16[9,32,320]{2,1,0:T(8,128)(2,1)} %get-tuple-element.23), channel_id=1, source_target_pairs={{0,1},{1,2},{2,3},{3,0},{4,5},{5,6},{6,7},{7,4},{8,9},{9,10},{10,1... | collective-permute-start | bytes 552968 | tf_op jit(solution)/shard_map/ppermute | solution.py:239
  62.7 8.6 %copy-start.6 = (bf16[9,32,320]{2,1,0:T(8,128)(2,1)S(1)}, bf16[9,32,320]{2,1,0:T(8,128)(2,1)}, u32[]{:S(2)}) copy-start(bf16[9,32,320]{2,1,0:T(8,128)(2,1)} %get-tuple-element.20) | copy-start | bytes 552964
  72.2 0.8 copy-start.10
  72.2 0.8 copy-start.9
  72.2 1.2 %copy-start.8 = (bf16[36,1,320]{2,1,0:T(2,128)(2,1)S(1)}, bf16[36,1,320]{2,1,0:T(2,128)(2,1)}, u32[]{:S(2)}) copy-start(bf16[36,1,320]{2,1,0:T(2,128)(2,1)} %get-tuple-element.26) | copy-start | bytes 69124
  72.3 1.2 %copy-start.7 = (bf16[36,1,320]{2,1,0:T(2,128)(2,1)S(1)}, bf16[36,1,320]{2,1,0:T(2,128)(2,1)}, u32[]{:S(2)}) copy-start(bf16[36,1,320]{2,1,0:T(2,128)(2,1)} %get-tuple-element.25) | copy-start | bytes 69124
  72.5 7.9 %copy-start.2 = (bf16[4,9,32,320]{3,2,1,0:T(8,128)(2,1)}, bf16[4,9,32,320]{3,2,1,0:T(8,128)(2,1)S(1)}, u32[]{:S(2)}) copy-start(bf16[4,9,32,320]{3,2,1,0:T(8,128)(2,1)S(1)} %get-tuple-element.40) | copy-start | bytes 2211844
  72.5 7.8 %copy-start.3 = (bf16[4,9,32,320]{3,2,1,0:T(8,128)(2,1)}, bf16[4,9,32,320]{3,2,1,0:T(8,128)(2,1)S(1)}, u32[]{:S(2)}) copy-start(bf16[4,9,32,320]{3,2,1,0:T(8,128)(2,1)S(1)} %get-tuple-element.41) | copy-start | bytes 2211844
  73.1 4.6 %collective-permute-start.15 = (bf16[72,320]{1,0:T(8,128)(2,1)S(1)}, bf16[72,320]{1,0:T(8,128)(2,1)S(1)}, u32[]{:S(2)}, u32[]{:S(2)}) collective-permute-start(bf16[72,320]{1,0:T(8,128)(2,1)S(1)} %pad_maximum_fusion.3), channel_id=1, source_target_pairs={{4,0},{8,4},{12,8},{0,12},{5,1},{9,5},{13,9},{1,13},{6,2},{10,6},{... | collective-permute-start | bytes 138248 | tf_op jit(solution)/shard_map/ppermute | solution.py:16
  73.5 6.2 %collective-permute-start.14 = (bf16[72,320]{1,0:T(8,128)(2,1)S(1)}, bf16[72,320]{1,0:T(8,128)(2,1)S(1)}, u32[]{:S(2)}, u32[]{:S(2)}) collective-permute-start(bf16[72,320]{1,0:T(8,128)(2,1)S(1)} %pad_maximum_fusion.2), channel_id=1, source_target_pairs={{12,0},{0,4},{4,8},{8,12},{13,1},{1,5},{5,9},{9,13},{14,2},{2,6},{... | collective-permute-start | bytes 138248 | tf_op jit(solution)/shard_map/ppermute | solution.py:16
  (1 other events, 0.7 us)

commit v15 on v14

--- a/solution.py
+++ b/solution.py
@@ -256,10 +256,9 @@
     rotate = frames_all <= 4 and half % frames_all == 0
     if rotate:
         whole = convolve([[tile]], rims, conv1_weight, norm_gelu, 0, row_count)
-        for lo in (0, half):
-            returned.append(rotated_attention(whole, lo, half, qkv_weight, pos_bias, out_weight))
+        returned.append(rotated_attention(whole, 0, row_count, qkv_weight, pos_bias, out_weight))
         hidden_rows = [whole]
-        hidden = [whole[:half], whole[half:]]
+        hidden = [whole]
     else:
         hidden = [convolve([[tile]], rims, conv1_weight, norm_gelu, lo, lo + half) for lo in (0, half)]
         hidden_rows = hidden

time: 92.6 us -> 105 us (1.13)
  waiting for transfers between devices: 20.7 us -> 41.4 us
  starting transfers between devices: 18.1 us -> 12.6 us
  Pallas kernels: 36.2 us -> 32.6 us
  other arithmetic: 3.51 us -> 4.84 us
    ppermute x6 -> x3, waiting for transfers between devices: 7.58 us -> 18 us  [rotated_attention(): lax.ppermute(piece, 'frame', [(i, (i - s) % frames_all) for i in range(fr...]
    ppermute x6 -> x3, waiting for transfers between devices: 5.54 us -> 15.3 us  [rotated_attention(): lax.ppermute(piece, 'frame', [(i, (i + s) % frames_all) for i in range(fr...]
    pallas_call x2 -> x1, Pallas kernels: 11.6 us -> 8.01 us  [attend_pieces(): pl.pallas_call(functools.partial(attend_kernel, parts=frames_all), out_sh...]
    ppermute x6 -> x3, starting transfers between devices: 5.56 us -> 2.42 us  [rotated_attention(): lax.ppermute(piece, 'frame', [(i, (i - s) % frames_all) for i in range(fr...]
    ppermute x6 -> x3, starting transfers between devices: 5.01 us -> 2.98 us  [rotated_attention(): lax.ppermute(piece, 'frame', [(i, (i + s) % frames_all) for i in range(fr...]
    select_n x0 -> x1, local copies, waits for them, and re-layouts: none -> 1.47 us  [rotated_attention(): jnp.take(jnp.stack(back), order, axis=0).reshape(rows, col_count, channels)]
    unnamed x35 -> x17, local copies, waits for them, and re-layouts: 2.87 us -> 2.21 us
  transfers between devices with their start and end apart: 16 -> 10, of which waited for: 8 -> 9; matrix products, arithmetic and copies ran while one was open for 9% -> 8% of each run, Pallas kernels for 13% -> 0%
where the time goes in v15:
time: 105 us
  waiting for transfers between devices  41.4 us (39%)
  Pallas kernels  32.6 us (31%)
  starting transfers between devices  12.6 us (12%)
  local copies, waits for them, and re-layouts  11.2 us (11%)
  other arithmetic  4.84 us (5%)
  matrix products  2.29 us (2%)
    pallas_call x2, Pallas kernels, convolve(): pl.pallas_call(functools.partial(conv_kernel, layout=tuple(layout), lo=lo...  24.6 us
    ppermute x3, waiting for transfers between devices, rotated_attention(): lax.ppermute(piece, 'frame', [(i, (i - s) % frames_all) for i in range(fr...  18 us
    ppermute x3, waiting for transfers between devices, rotated_attention(): lax.ppermute(piece, 'frame', [(i, (i + s) % frames_all) for i in range(fr...  15.3 us
    ppermute x4, waiting for transfers between devices, shifted(): moved = lax.ppermute(block, axis, route)  8.17 us
    pallas_call x1, Pallas kernels, attend_pieces(): pl.pallas_call(functools.partial(attend_kernel, parts=frames_all), out_sh...  8.01 us
    ppermute x4, starting transfers between devices, shifted(): moved = lax.ppermute(block, axis, route)  7.24 us
    ppermute x3, starting transfers between devices, rotated_attention(): lax.ppermute(piece, 'frame', [(i, (i + s) % frames_all) for i in range(fr...  2.98 us
    select_n x4, other arithmetic, shifted(): return jnp.where(inside, moved, jnp.zeros_like(moved))  2.52 us
  transfers between devices with their start and end apart: 10, of which 9 were waited for; matrix products, arithmetic and copies ran while one was open for 8% of the time, Pallas kernels for 0%

profile of v15, /device:TPU:0, one launch (start us, length us, event | category | flops | bytes accessed | tf_op | source)
XLA Modules:
  0.0 105.2 jit_solution(9291132234731270027)
XLA Ops:
  0.0 1.9 %fusion.2 = bf16[1,72,320]{2,0,1:T(2,128)(2,1)S(1)} fusion(bf16[1,72,32,320]{3,2,1,0:T(8,128)(2,1)} %param.6), kind=kOutput, calls=%fused_computation.31 | convolution fusion | flops 1474592 | bytes 1520640 | tf_op jit(solution)/shard_map/rwc,w->rc/dot_general | solution.py:251
  2.0 5.1 %collective-permute-start.1 = (bf16[72,320]{1,0:T(8,128)(2,1)S(1)}, bf16[72,320]{1,0:T(8,128)(2,1)S(1)}, u32[]{:S(2)}, u32[]{:S(2)}) collective-permute-start(bf16[72,320]{1,0:T(8,128)(2,1)S(1)} %bitcast.49), channel_id=1, source_target_pairs={{4,0},{8,4},{12,8},{0,12},{5,1},{9,5},{13,9},{1,13},{6,2},{10,6},{... | collective-permute-start | bytes 138248 | tf_op jit(solution)/shard_map/ppermute | solution.py:16
  7.6 0.6 gather_fusion
  8.2 0.7 collective-permute-done.1
  8.9 0.6 broadcast_select_fusion.1.refs_2_
  9.5 3.9 %collective-permute-done = bf16[72,320]{1,0:T(8,128)(2,1)S(1)} collective-permute-done((bf16[72,320]{1,0:T(8,128)(2,1)S(1)}, bf16[72,320]{1,0:T(8,128)(2,1)S(1)}, u32[]{:S(2)}, u32[]{:S(2)}) %collective-permute-start) | collective-permute-done | bytes 46112 | tf_op jit(solution)/shard_map/ppermute | solution.py:16
  13.5 0.6 broadcast_select_fusion.3.refs_1_
  14.1 12.6 %shard_map.64.refs_0_ = bf16[72,32,320]{2,1,0:T(8,128)(2,1)} custom-call(bf16[72,32,320]{2,1,0:T(8,128)(2,1)} %bitcast.40, bf16[72,320]{1,0:T(8,128)(2,1)} %broadcast_select_fusion.3.refs_1_, bf16[72,320]{1,0:T(8,128)(2,1)} %broadcast_select_fusion.1.refs_2_, bf16[3,960,320]{2,1,0:T(8,128)(2,1)} %bitcast.43), custom_call_target="tpu_custom_call" | custom-call | tf_op jit(solution)/shard_map/pallas_call | solution.py:100
  26.7 2.4 %constant_dynamic-slice_fusion = (bf16[18,32,320]{2,1,0:T(8,128)(2,1)S(1)}, bf16[18,32,320]{2,1,0:T(8,128)(2,1)S(1)}, bf16[18,32,320]{2,1,0:T(8,128)(2,1)S(1)}, bf16[18,32,320]{2,1,0:T(8,128)(2,1)}) fusion(bf16[72,32,320]{2,1,0:T(8,128)(2,1)} %shard_map.64.refs_0_, s32[]{:T(128)S(6)} %select_n.148, s32[]{:T(128)S(6)} %select_n.146, s32[]{:T(128)S(6)} %select_n.144, ...), kind=kLoop, calls=%fused_computation.43 | loop fusion | bytes 2949136 | tf_op jit(solution)/shard_map/dynamic_slice | solution.py:228
  29.2 1.5 %collective-permute-start.3 = (bf16[18,32,320]{2,1,0:T(8,128)(2,1)S(1)}, bf16[18,32,320]{2,1,0:T(8,128)(2,1)S(1)}, u32[]{:S(2)}, u32[]{:S(2)}) collective-permute-start(bf16[18,32,320]{2,1,0:T(8,128)(2,1)S(1)} %get-tuple-element.18), channel_id=1, source_target_pairs={{0,2},{1,3},{2,0},{3,1},{4,6},{5,7},{6,4},{7,5},{8,10},{9,11},{10,... | collective-permute-start | bytes 1105928 | tf_op jit(solution)/shard_map/ppermute | solution.py:230
  30.7 1.4 %collective-permute-start.4 = (bf16[18,32,320]{2,1,0:T(8,128)(2,1)S(1)}, bf16[18,32,320]{2,1,0:T(8,128)(2,1)S(1)}, u32[]{:S(2)}, u32[]{:S(2)}) collective-permute-start(bf16[18,32,320]{2,1,0:T(8,128)(2,1)S(1)} %get-tuple-element.17), channel_id=1, source_target_pairs={{0,3},{1,0},{2,1},{3,2},{4,7},{5,4},{6,5},{7,6},{8,11},{9,8},{10,9... | collective-permute-start | bytes 1105928 | tf_op jit(solution)/shard_map/ppermute | solution.py:230
  32.9 0.8 copy.18.refs_5_
  33.7 1.2 %copy.16 = bf16[320,960]{0,1:T(8,128)(2,1)} copy(bf16[320,960]{1,0:T(8,128)(2,1)S(1)} %copy-done.2) | data formatting | bytes 1228800 | tf_op args[2]
  34.9 6.2 %collective-permute-done.2.refs_1_ = bf16[18,32,320]{2,1,0:T(8,128)(2,1)S(1)} collective-permute-done((bf16[18,32,320]{2,1,0:T(8,128)(2,1)S(1)}, bf16[18,32,320]{2,1,0:T(8,128)(2,1)S(1)}, u32[]{:S(2)}, u32[]{:S(2)}) %collective-permute-start.2) | collective-permute-done | bytes 368672 | tf_op jit(solution)/shard_map/ppermute | solution.py:230
  41.1 1.1 %collective-permute-done.3.refs_2_ = bf16[18,32,320]{2,1,0:T(8,128)(2,1)S(1)} collective-permute-done((bf16[18,32,320]{2,1,0:T(8,128)(2,1)S(1)}, bf16[18,32,320]{2,1,0:T(8,128)(2,1)S(1)}, u32[]{:S(2)}, u32[]{:S(2)}) %collective-permute-start.3) | collective-permute-done | bytes 368672 | tf_op jit(solution)/shard_map/ppermute | solution.py:230
  42.2 8.0 %collective-permute-done.4.refs_3_ = bf16[18,32,320]{2,1,0:T(8,128)(2,1)S(1)} collective-permute-done((bf16[18,32,320]{2,1,0:T(8,128)(2,1)S(1)}, bf16[18,32,320]{2,1,0:T(8,128)(2,1)S(1)}, u32[]{:S(2)}, u32[]{:S(2)}) %collective-permute-start.4) | collective-permute-done | bytes 368672 | tf_op jit(solution)/shard_map/ppermute | solution.py:230
  50.2 0.8 copy-done.7
  50.9 8.0 %shard_map.65 = (bf16[18,32,320]{2,1,0:T(8,128)(2,1)}, bf16[18,32,320]{2,1,0:T(8,128)(2,1)}, bf16[18,32,320]{2,1,0:T(8,128)(2,1)}, bf16[18,32,320]{2,1,0:T(8,128)(2,1)}) custom-call(bf16[18,32,320]{2,1,0:T(8,128)(2,1)} %get-tuple-element.20.refs_0_, bf16[18,32,320]{2,1,0:T(8,128)(2,1)} %copy-done.5, bf16[18,32,320]{2,1,0:T(8,128)(2,1)} %copy-done.6, ...), custom_call_target="tpu_custom_call" | custom-call | tf_op jit(solution)/shard_map/pallas_call | solution.py:194
  58.9 1.9 %collective-permute-start.5 = (bf16[18,32,320]{2,1,0:T(8,128)(2,1)}, bf16[18,32,320]{2,1,0:T(8,128)(2,1)S(1)}, u32[]{:S(2)}, u32[]{:S(2)}) collective-permute-start(bf16[18,32,320]{2,1,0:T(8,128)(2,1)} %get-tuple-element.10), channel_id=1, source_target_pairs={{0,3},{1,0},{2,1},{3,2},{4,7},{5,4},{6,5},{7,6},{8,11},{9,8},{10,9... | collective-permute-start | bytes 1105928 | tf_op jit(solution)/shard_map/ppermute | solution.py:239
  61.5 2.0 %fusion.21 = (bf16[72,1,320]{2,1,0:T(2,128)(2,1)}, bf16[72,1,320]{2,1,0:T(2,128)(2,1)}) fusion(bf16[72,32,320]{2,1,0:T(8,128)(2,1)} %shard_map.64.refs_0_), kind=kLoop, calls=%fused_computation.60 | loop fusion | bytes 184320 | tf_op jit(solution)/shard_map/slice | solution.py:279
  63.6 8.1 %collective-permute-done.5 = bf16[18,32,320]{2,1,0:T(8,128)(2,1)S(1)} collective-permute-done((bf16[18,32,320]{2,1,0:T(8,128)(2,1)}, bf16[18,32,320]{2,1,0:T(8,128)(2,1)S(1)}, u32[]{:S(2)}, u32[]{:S(2)}) %collective-permute-start.5) | collective-permute-done | bytes 368672 | tf_op jit(solution)/shard_map/ppermute | solution.py:239
  71.7 9.9 %collective-permute-done.6 = bf16[18,32,320]{2,1,0:T(8,128)(2,1)S(1)} collective-permute-done((bf16[18,32,320]{2,1,0:T(8,128)(2,1)}, bf16[18,32,320]{2,1,0:T(8,128)(2,1)S(1)}, u32[]{:S(2)}, u32[]{:S(2)}) %collective-permute-start.6) | collective-permute-done | bytes 368672 | tf_op jit(solution)/shard_map/ppermute | solution.py:239
  81.5 1.4 %pad_maximum_fusion = bf16[4,18,32,320]{3,2,1,0:T(8,128)(2,1)S(1)} fusion(bf16[1,18,32,320]{3,2,1,0:T(8,128)(2,1)S(1)} %bitcast.48, bf16[1,18,32,320]{3,2,1,0:T(8,128)(2,1)S(1)} %bitcast.47, bf16[1,18,32,320]{3,2,1,0:T(8,128)(2,1)S(1)} %bitcast.46, bf16[1,18,32,320]{3,2,1,0:T(8,128)(2,1)} %bitcast.45), kind=kLoop, calls=%fused_computation.3 | loop fusion | flops 2211840 | bytes 2949120 | tf_op jit(solution)/shard_map/stack | solution.py:242
  83.0 0.9 gather_fusion.2
  83.9 0.7 copy_select_fusion
  85.2 1.5 %copy.22.refs_1_ = bf16[72,32,320]{2,1,0:T(8,128)(2,1)} copy(bf16[72,32,320]{2,0,1:T(8,128)(2,1)S(1)} %copy_select_fusion) | data formatting | bytes 2949120 | tf_op jit(solution)/shard_map/jit(_take)/select_n | solution.py:242
  86.7 1.8 %collective-permute-start.8 = (bf16[72,320]{1,0:T(8,128)(2,1)S(1)}, bf16[72,320]{1,0:T(8,128)(2,1)S(1)}, u32[]{:S(2)}, u32[]{:S(2)}) collective-permute-start(bf16[72,320]{1,0:T(8,128)(2,1)S(1)} %get-tuple-element.14), channel_id=1, source_target_pairs={{12,0},{0,4},{4,8},{8,12},{13,1},{1,5},{5,9},{9,13},{14,2},{2,6},{... | collective-permute-start | bytes 138248 | tf_op jit(solution)/shard_map/ppermute | solution.py:16
  88.5 0.7 collective-permute-done.9
  89.1 0.6 broadcast_select_fusion.refs_3_
  89.7 2.9 %collective-permute-done.8 = bf16[72,320]{1,0:T(8,128)(2,1)S(1)} collective-permute-done((bf16[72,320]{1,0:T(8,128)(2,1)S(1)}, bf16[72,320]{1,0:T(8,128)(2,1)S(1)}, u32[]{:S(2)}, u32[]{:S(2)}) %collective-permute-start.8) | collective-permute-done | bytes 46112 | tf_op jit(solution)/shard_map/ppermute | solution.py:16
  92.7 0.6 broadcast_select_fusion.2.refs_2_
  93.3 11.9 %shard_map.66 = bf16[72,32,320]{2,1,0:T(8,128)(2,1)} custom-call(bf16[72,32,320]{2,1,0:T(8,128)(2,1)} %shard_map.64.refs_0_, bf16[72,32,320]{2,1,0:T(8,128)(2,1)} %copy.22.refs_1_, bf16[72,320]{1,0:T(8,128)(2,1)} %broadcast_select_fusion.2.refs_2_, bf16[72,320]{1,0:T(8,128)(2,1)} %broadcast_select_fusion.refs_3_, bf16[3,960,320]{2,1,0:T(8,128)(2,1)} %bitcast.44), custom_call_target="tpu_custom_call" | custom-call | tf_op jit(solution)/shard_map/pallas_call | solution.py:100
  (36 shorter events, 2.5 us)
Async XLA Ops:
  0.0 7.6 %copy-start = (f32[5,4,4]{0,2,1:T(4,128)S(1)}, f32[5,4,4]{0,2,1:T(4,128)}, u32[]{:S(2)}) copy-start(f32[5,4,4]{0,2,1:T(4,128)} %param.10) | copy-start | bytes 964
  0.0 7.1 %copy-start.1 = (bf16[1,72,32,320]{3,2,1,0:T(8,128)(2,1)S(1)}, bf16[1,72,32,320]{3,2,1,0:T(8,128)(2,1)}, u32[]{:S(2)}) copy-start(bf16[1,72,32,320]{3,2,1,0:T(8,128)(2,1)} %param.6) | copy-start | bytes 4423684
  2.0 6.9 %collective-permute-start.1 = (bf16[72,320]{1,0:T(8,128)(2,1)S(1)}, bf16[72,320]{1,0:T(8,128)(2,1)S(1)}, u32[]{:S(2)}, u32[]{:S(2)}) collective-permute-start(bf16[72,320]{1,0:T(8,128)(2,1)S(1)} %bitcast.49), channel_id=1, source_target_pairs={{4,0},{8,4},{12,8},{0,12},{5,1},{9,5},{13,9},{1,13},{6,2},{10,6},{... | collective-permute-start | bytes 138248 | tf_op jit(solution)/shard_map/ppermute | solution.py:16
  7.4 6.0 %collective-permute-start = (bf16[72,320]{1,0:T(8,128)(2,1)S(1)}, bf16[72,320]{1,0:T(8,128)(2,1)S(1)}, u32[]{:S(2)}, u32[]{:S(2)}) collective-permute-start(bf16[72,320]{1,0:T(8,128)(2,1)S(1)} %bitcast.50), channel_id=1, source_target_pairs={{12,0},{0,4},{4,8},{8,12},{13,1},{1,5},{5,9},{9,13},{14,2},{2,6},{... | collective-permute-start | bytes 138248 | tf_op jit(solution)/shard_map/ppermute | solution.py:16
  26.7 7.0 %copy-start.2 = (bf16[320,960]{1,0:T(8,128)(2,1)S(1)}, bf16[320,960]{1,0:T(8,128)(2,1)}, u32[]{:S(2)}) copy-start(bf16[320,960]{1,0:T(8,128)(2,1)} %param.8) | copy-start | bytes 1843204
  29.2 11.9 %collective-permute-start.2 = (bf16[18,32,320]{2,1,0:T(8,128)(2,1)S(1)}, bf16[18,32,320]{2,1,0:T(8,128)(2,1)S(1)}, u32[]{:S(2)}, u32[]{:S(2)}) collective-permute-start(bf16[18,32,320]{2,1,0:T(8,128)(2,1)S(1)} %get-tuple-element.19), channel_id=1, source_target_pairs={{0,1},{1,2},{2,3},{3,0},{4,5},{5,6},{6,7},{7,4},{8,9},{9,10},{10,1... | collective-permute-start | bytes 1105928 | tf_op jit(solution)/shard_map/ppermute | solution.py:230
  29.2 13.0 %collective-permute-start.3 = (bf16[18,32,320]{2,1,0:T(8,128)(2,1)S(1)}, bf16[18,32,320]{2,1,0:T(8,128)(2,1)S(1)}, u32[]{:S(2)}, u32[]{:S(2)}) collective-permute-start(bf16[18,32,320]{2,1,0:T(8,128)(2,1)S(1)} %get-tuple-element.18), channel_id=1, source_target_pairs={{0,2},{1,3},{2,0},{3,1},{4,6},{5,7},{6,4},{7,5},{8,10},{9,11},{10,... | collective-permute-start | bytes 1105928 | tf_op jit(solution)/shard_map/ppermute | solution.py:230
  30.7 19.4 %collective-permute-start.4 = (bf16[18,32,320]{2,1,0:T(8,128)(2,1)S(1)}, bf16[18,32,320]{2,1,0:T(8,128)(2,1)S(1)}, u32[]{:S(2)}, u32[]{:S(2)}) collective-permute-start(bf16[18,32,320]{2,1,0:T(8,128)(2,1)S(1)} %get-tuple-element.17), channel_id=1, source_target_pairs={{0,3},{1,0},{2,1},{3,2},{4,7},{5,4},{6,5},{7,6},{8,11},{9,8},{10,9... | collective-permute-start | bytes 1105928 | tf_op jit(solution)/shard_map/ppermute | solution.py:230
  41.1 9.1 %copy-start.5 = (bf16[18,32,320]{2,1,0:T(8,128)(2,1)}, bf16[18,32,320]{2,1,0:T(8,128)(2,1)S(1)}, u32[]{:S(2)}) copy-start(bf16[18,32,320]{2,1,0:T(8,128)(2,1)S(1)} %collective-permute-done.2.refs_1_) | copy-start | bytes 1105924
  42.2 8.0 %copy-start.6 = (bf16[18,32,320]{2,1,0:T(8,128)(2,1)}, bf16[18,32,320]{2,1,0:T(8,128)(2,1)S(1)}, u32[]{:S(2)}) copy-start(bf16[18,32,320]{2,1,0:T(8,128)(2,1)S(1)} %collective-permute-done.3.refs_2_) | copy-start | bytes 1105924
  50.2 0.8 copy-start.7
  58.9 12.7 %collective-permute-start.5 = (bf16[18,32,320]{2,1,0:T(8,128)(2,1)}, bf16[18,32,320]{2,1,0:T(8,128)(2,1)S(1)}, u32[]{:S(2)}, u32[]{:S(2)}) collective-permute-start(bf16[18,32,320]{2,1,0:T(8,128)(2,1)} %get-tuple-element.10), channel_id=1, source_target_pairs={{0,3},{1,0},{2,1},{3,2},{4,7},{5,4},{6,5},{7,6},{8,11},{9,8},{10,9... | collective-permute-start | bytes 1105928 | tf_op jit(solution)/shard_map/ppermute | solution.py:239
  60.9 20.7 %collective-permute-start.6 = (bf16[18,32,320]{2,1,0:T(8,128)(2,1)}, bf16[18,32,320]{2,1,0:T(8,128)(2,1)S(1)}, u32[]{:S(2)}, u32[]{:S(2)}) collective-permute-start(bf16[18,32,320]{2,1,0:T(8,128)(2,1)} %get-tuple-element.11), channel_id=1, source_target_pairs={{0,2},{1,3},{2,0},{3,1},{4,6},{5,7},{6,4},{7,5},{8,10},{9,11},{10,... | collective-permute-start | bytes 1105928 | tf_op jit(solution)/shard_map/ppermute | solution.py:239
  61.4 20.2 %collective-permute-start.7 = (bf16[18,32,320]{2,1,0:T(8,128)(2,1)}, bf16[18,32,320]{2,1,0:T(8,128)(2,1)S(1)}, u32[]{:S(2)}, u32[]{:S(2)}) collective-permute-start(bf16[18,32,320]{2,1,0:T(8,128)(2,1)} %get-tuple-element.12), channel_id=1, source_target_pairs={{0,1},{1,2},{2,3},{3,0},{4,5},{5,6},{6,7},{7,4},{8,9},{9,10},{10,1... | collective-permute-start | bytes 1105928 | tf_op jit(solution)/shard_map/ppermute | solution.py:239
  83.9 0.9 copy-start.3
  83.9 0.9 copy-start.4
  84.9 4.2 %collective-permute-start.9 = (bf16[72,320]{1,0:T(8,128)(2,1)S(1)}, bf16[72,320]{1,0:T(8,128)(2,1)S(1)}, u32[]{:S(2)}, u32[]{:S(2)}) collective-permute-start(bf16[72,320]{1,0:T(8,128)(2,1)S(1)} %get-tuple-element.13), channel_id=1, source_target_pairs={{4,0},{8,4},{12,8},{0,12},{5,1},{9,5},{13,9},{1,13},{6,2},{10,6},{... | collective-permute-start | bytes 138248 | tf_op jit(solution)/shard_map/ppermute | solution.py:16
  86.7 6.0 %collective-permute-start.8 = (bf16[72,320]{1,0:T(8,128)(2,1)S(1)}, bf16[72,320]{1,0:T(8,128)(2,1)S(1)}, u32[]{:S(2)}, u32[]{:S(2)}) collective-permute-start(bf16[72,320]{1,0:T(8,128)(2,1)S(1)} %get-tuple-element.14), channel_id=1, source_target_pairs={{12,0},{0,4},{4,8},{8,12},{13,1},{1,5},{5,9},{9,13},{14,2},{2,6},{... | collective-permute-start | bytes 138248 | tf_op jit(solution)/shard_map/ppermute | solution.py:16

commit v16 on v15

--- a/solution.py
+++ b/solution.py
@@ -256,9 +256,12 @@
     rotate = frames_all <= 4 and half % frames_all == 0
     if rotate:
         whole = convolve([[tile]], rims, conv1_weight, norm_gelu, 0, row_count)
-        returned.append(rotated_attention(whole, 0, row_count, qkv_weight, pos_bias, out_weight))
+        chunks = 3 if row_count % 3 == 0 and (row_count // 3) % (12 * frames_all // 4) == 0 else 2
+        rows = row_count // chunks
+        for lo in range(0, row_count, rows):
+            returned.append(rotated_attention(whole, lo, rows, qkv_weight, pos_bias, out_weight))
         hidden_rows = [whole]
-        hidden = [whole]
+        hidden = [whole[lo : lo + rows] for lo in range(0, row_count, rows)]
     else:
         hidden = [convolve([[tile]], rims, conv1_weight, norm_gelu, lo, lo + half) for lo in (0, half)]
         hidden_rows = hidden

time: 105 us -> 92.7 us (0.88)
  waiting for transfers between devices: 41.4 us -> 12.1 us
  starting transfers between devices: 12.6 us -> 24.7 us
  Pallas kernels: 32.6 us -> 38.5 us
  other arithmetic: 4.84 us -> 3.48 us
    ppermute x3 -> x9, waiting for transfers between devices: 15.3 us -> 3.06 us  [rotated_attention(): lax.ppermute(piece, 'frame', [(i, (i + s) % frames_all) for i in range(fr...]
    ppermute x3 -> x9, waiting for transfers between devices: 18 us -> 6.2 us  [rotated_attention(): lax.ppermute(piece, 'frame', [(i, (i - s) % frames_all) for i in range(fr...]
    pallas_call x1 -> x3, Pallas kernels: 8.01 us -> 13.9 us  [attend_pieces(): pl.pallas_call(functools.partial(attend_kernel, parts=frames_all), out_sh...]
    ppermute x3 -> x9, starting transfers between devices: 2.42 us -> 8.26 us  [rotated_attention(): lax.ppermute(piece, 'frame', [(i, (i - s) % frames_all) for i in range(fr...]
    ppermute x4, waiting for transfers between devices: 8.17 us -> 2.79 us  [shifted(): moved = lax.ppermute(block, axis, route)]
    ppermute x3 -> x9, starting transfers between devices: 2.98 us -> 7.12 us  [rotated_attention(): lax.ppermute(piece, 'frame', [(i, (i + s) % frames_all) for i in range(fr...]
    ppermute x4, starting transfers between devices: 7.24 us -> 9.32 us  [shifted(): moved = lax.ppermute(block, axis, route)]
    select_n x1 -> x0, local copies, waits for them, and re-layouts: 1.47 us -> none  [rotated_attention(): jnp.take(jnp.stack(back), order, axis=0).reshape(rows, col_count, channels)]
  transfers between devices with their start and end apart: 10 -> 22, of which waited for: 9 -> 7; matrix products, arithmetic and copies ran while one was open for 8% -> 10% of each run, Pallas kernels for 0% -> 15%
where the time goes in v16:
time: 92.7 us; the launch traced here: 92.3 us
  Pallas kernels  38.5 us (42%)
  starting transfers between devices  24.7 us (27%)
  waiting for transfers between devices  12.1 us (13%)
  local copies, waits for them, and re-layouts  10.9 us (12%)
  other arithmetic  3.48 us (4%)
  matrix products  2.29 us (2%)
    pallas_call x2, Pallas kernels, convolve(): pl.pallas_call(functools.partial(conv_kernel, layout=tuple(layout), lo=lo...  24.6 us
    pallas_call x3, Pallas kernels, attend_pieces(): pl.pallas_call(functools.partial(attend_kernel, parts=frames_all), out_sh...  13.9 us
    ppermute x4, starting transfers between devices, shifted(): moved = lax.ppermute(block, axis, route)  9.32 us
    ppermute x9, starting transfers between devices, rotated_attention(): lax.ppermute(piece, 'frame', [(i, (i - s) % frames_all) for i in range(fr...  8.26 us
    ppermute x9, starting transfers between devices, rotated_attention(): lax.ppermute(piece, 'frame', [(i, (i + s) % frames_all) for i in range(fr...  7.12 us
    ppermute x9, waiting for transfers between devices, rotated_attention(): lax.ppermute(piece, 'frame', [(i, (i - s) % frames_all) for i in range(fr...  6.2 us
    ppermute x9, waiting for transfers between devices, rotated_attention(): lax.ppermute(piece, 'frame', [(i, (i + s) % frames_all) for i in range(fr...  3.06 us
    ppermute x4, waiting for transfers between devices, shifted(): moved = lax.ppermute(block, axis, route)  2.79 us
  transfers between devices with their start and end apart: 22, of which 7 were waited for; matrix products, arithmetic and copies ran while one was open for 10% of the time, Pallas kernels for 15%

profile of v16, /device:TPU:0, one launch (start us, length us, event | category | flops | bytes accessed | tf_op | source)
XLA Modules:
  0.0 92.3 jit_solution(10848233509153209378)
XLA Ops:
  0.0 1.9 %fusion.8 = bf16[1,72,320]{2,0,1:T(2,128)(2,1)S(1)} fusion(bf16[1,72,32,320]{3,2,1,0:T(8,128)(2,1)} %param.12), kind=kOutput, calls=%fused_computation.55 | convolution fusion | flops 1474592 | bytes 1520640 | tf_op jit(solution)/shard_map/rwc,w->rc/dot_general | solution.py:251
  2.0 3.1 %collective-permute-start = (bf16[72,320]{1,0:T(8,128)(2,1)S(1)}, bf16[72,320]{1,0:T(8,128)(2,1)S(1)}, u32[]{:S(2)}, u32[]{:S(2)}) collective-permute-start(bf16[72,320]{1,0:T(8,128)(2,1)S(1)} %bitcast.80), channel_id=1, source_target_pairs={{12,0},{0,4},{4,8},{8,12},{13,1},{1,5},{5,9},{9,13},{14,2},{2,6},{... | collective-permute-start | bytes 138248 | tf_op jit(solution)/shard_map/ppermute | solution.py:16
  5.4 2.1 %collective-permute-start.1 = (bf16[72,320]{1,0:T(8,128)(2,1)S(1)}, bf16[72,320]{1,0:T(8,128)(2,1)S(1)}, u32[]{:S(2)}, u32[]{:S(2)}) collective-permute-start(bf16[72,320]{1,0:T(8,128)(2,1)S(1)} %bitcast.81), channel_id=1, source_target_pairs={{4,0},{8,4},{12,8},{0,12},{5,1},{9,5},{13,9},{1,13},{6,2},{10,6},{... | collective-permute-start | bytes 138248 | tf_op jit(solution)/shard_map/ppermute | solution.py:16
  10.0 0.6 broadcast_select_fusion.4.refs_2_
  10.6 12.7 %shard_map.64.refs_0_ = bf16[72,32,320]{2,1,0:T(8,128)(2,1)} custom-call(bf16[72,32,320]{2,1,0:T(8,128)(2,1)} %bitcast.56, bf16[72,320]{1,0:T(8,128)(2,1)} %broadcast_select_fusion.6.refs_1_, bf16[72,320]{1,0:T(8,128)(2,1)} %broadcast_select_fusion.4.refs_2_, bf16[3,960,320]{2,1,0:T(8,128)(2,1)} %bitcast.66), custom_call_target="tpu_custom_call" | custom-call | tf_op jit(solution)/shard_map/pallas_call | solution.py:100
  23.3 2.5 %constant_dynamic-slice_fusion = (bf16[6,32,320]{2,1,0:T(8,128)(2,1)S(1)}, bf16[6,32,320]{2,1,0:T(8,128)(2,1)S(1)}, bf16[6,32,320]{2,1,0:T(8,128)(2,1)S(1)}, bf1...) fusion(bf16[72,32,320]{2,1,0:T(8,128)(2,1)} %shard_map.64.refs_, ...), kind=kLoop, calls=%fused_computation.35 | loop fusion | bytes 2949168 | tf_op jit(solution)/shard_map/dynamic_slice | solution.py:228
  25.9 1.6 %collective-permute-start.15 = (bf16[6,32,320]{2,1,0:T(8,128)(2,1)S(1)}, bf16[6,32,320]{2,1,0:T(8,128)(2,1)S(1)}, u32[]{:S(2)}, u32[]{:S(2)}) collective-permute-start(bf16[6,32,320]{2,1,0:T(8,128)(2,1)S(1)} %get-tuple-element.39), channel_id=1, source_target_pairs={{0,2},{1,3},{2,0},{3,1},{4,6},{5,7},{6,4},{7,5},{8,10},{9,11},{10,... | collective-permute-start | bytes 368648 | tf_op jit(solution)/shard_map/ppermute | solution.py:230
  27.8 1.6 %collective-permute-start.10 = (bf16[6,32,320]{2,1,0:T(8,128)(2,1)S(1)}, bf16[6,32,320]{2,1,0:T(8,128)(2,1)S(1)}, u32[]{:S(2)}, u32[]{:S(2)}) collective-permute-start(bf16[6,32,320]{2,1,0:T(8,128)(2,1)S(1)} %get-tuple-element.42), channel_id=1, source_target_pairs={{0,3},{1,0},{2,1},{3,2},{4,7},{5,4},{6,5},{7,6},{8,11},{9,8},{10,9... | collective-permute-start | bytes 368648 | tf_op jit(solution)/shard_map/ppermute | solution.py:230
  29.8 2.5 %collective-permute-start.8 = (bf16[6,32,320]{2,1,0:T(8,128)(2,1)S(1)}, bf16[6,32,320]{2,1,0:T(8,128)(2,1)S(1)}, u32[]{:S(2)}, u32[]{:S(2)}) collective-permute-start(bf16[6,32,320]{2,1,0:T(8,128)(2,1)S(1)} %get-tuple-element.44), channel_id=1, source_target_pairs={{0,1},{1,2},{2,3},{3,0},{4,5},{5,6},{6,7},{7,4},{8,9},{9,10},{10,1... | collective-permute-start | bytes 368648 | tf_op jit(solution)/shard_map/ppermute | solution.py:230
  32.3 3.0 %collective-permute-done.15.refs_2_ = bf16[6,32,320]{2,1,0:T(8,128)(2,1)S(1)} collective-permute-done((bf16[6,32,320]{2,1,0:T(8,128)(2,1)S(1)}, bf16[6,32,320]{2,1,0:T(8,128)(2,1)S(1)}, u32[]{:S(2)}, u32[]{:S(2)}) %collective-permute-start.15) | collective-permute-done | bytes 122912 | tf_op jit(solution)/shard_map/ppermute | solution.py:230
  35.4 0.8 copy.42.refs_5_
  36.2 1.2 %copy.40 = bf16[320,960]{0,1:T(8,128)(2,1)} copy(bf16[320,960]{1,0:T(8,128)(2,1)S(1)} %copy-done.5) | data formatting | bytes 1228800 | tf_op args[2]
  38.1 4.6 %shard_map.67 = (bf16[6,32,320]{2,1,0:T(8,128)(2,1)}, bf16[6,32,320]{2,1,0:T(8,128)(2,1)}, bf16[6,32,320]{2,1,0:T(8,128)(2,1)}, bf16[6,32,320]{2,1,0:T(8,128)(2,1)}) custom-call(bf16[6,32,320]{2,1,0:T(8,128)(2,1)} %get-tuple-element.41.refs_0_, bf16[6,32,320]{2,1,0:T(8,128)(2,1)} %copy-done.17, bf16[6,32,320]{2,1,0:T(8,128)(2,1)} %copy-done.16, ...), custom_call_target="tpu_custom_call" | custom-call | tf_op jit(solution)/shard_map/pallas_call | solution.py:194
  43.2 1.2 %collective-permute-start.17 = (bf16[6,32,320]{2,1,0:T(8,128)(2,1)}, bf16[6,32,320]{2,1,0:T(8,128)(2,1)S(1)}, u32[]{:S(2)}, u32[]{:S(2)}) collective-permute-start(bf16[6,32,320]{2,1,0:T(8,128)(2,1)} %get-tuple-element.29), channel_id=1, source_target_pairs={{0,3},{1,0},{2,1},{3,2},{4,7},{5,4},{6,5},{7,6},{8,11},{9,8},{10,9... | collective-permute-start | bytes 368648 | tf_op jit(solution)/shard_map/ppermute | solution.py:239
  44.5 1.4 %collective-permute-start.18 = (bf16[6,32,320]{2,1,0:T(8,128)(2,1)}, bf16[6,32,320]{2,1,0:T(8,128)(2,1)S(1)}, u32[]{:S(2)}, u32[]{:S(2)}) collective-permute-start(bf16[6,32,320]{2,1,0:T(8,128)(2,1)} %get-tuple-element.30), channel_id=1, source_target_pairs={{0,2},{1,3},{2,0},{3,1},{4,6},{5,7},{6,4},{7,5},{8,10},{9,11},{10,... | collective-permute-start | bytes 368648 | tf_op jit(solution)/shard_map/ppermute | solution.py:239
  46.0 2.2 %fusion.21 = (bf16[24,1,320]{2,1,0:T(2,128)(2,1)}, bf16[24,1,320]{2,1,0:T(2,128)(2,1)}, bf16[24,1,320]{2,1,0:T(2,128)(2,1)}, bf16[24,1,320]{2,1,0:T(2,128)(2,1)}...) fusion(bf16[72,32,320]{2,1,0:T(8,128)(2,1)} %shard_map.64.refs_0_), kind=kLoop, calls=%fused_computation.72 | loop fusion | bytes 184320 | tf_op jit(solution)/shard_map/slice | solution.py:282
  48.1 4.6 %shard_map.66 = (bf16[6,32,320]{2,1,0:T(8,128)(2,1)}, bf16[6,32,320]{2,1,0:T(8,128)(2,1)}, bf16[6,32,320]{2,1,0:T(8,128)(2,1)}, bf16[6,32,320]{2,1,0:T(8,128)(2,1)}) custom-call(bf16[6,32,320]{2,1,0:T(8,128)(2,1)} %get-tuple-element.45.refs_0_, bf16[6,32,320]{2,1,0:T(8,128)(2,1)} %copy-done.12, bf16[6,32,320]{2,1,0:T(8,128)(2,1)} %copy-done.9, ...), custom_call_target="tpu_custom_call" | custom-call | tf_op jit(solution)/shard_map/pallas_call | solution.py:194
  52.8 1.7 %collective-permute-start.11 = (bf16[6,32,320]{2,1,0:T(8,128)(2,1)}, bf16[6,32,320]{2,1,0:T(8,128)(2,1)S(1)}, u32[]{:S(2)}, u32[]{:S(2)}) collective-permute-start(bf16[6,32,320]{2,1,0:T(8,128)(2,1)} %get-tuple-element.25), channel_id=1, source_target_pairs={{0,3},{1,0},{2,1},{3,2},{4,7},{5,4},{6,5},{7,6},{8,11},{9,8},{10,9... | collective-permute-start | bytes 368648 | tf_op jit(solution)/shard_map/ppermute | solution.py:239
  54.5 0.6 collective-permute-start.12
  55.1 4.6 %shard_map.65 = (bf16[6,32,320]{2,1,0:T(8,128)(2,1)}, bf16[6,32,320]{2,1,0:T(8,128)(2,1)}, bf16[6,32,320]{2,1,0:T(8,128)(2,1)}, bf16[6,32,320]{2,1,0:T(8,128)(2,1)}) custom-call(bf16[6,32,320]{2,1,0:T(8,128)(2,1)} %get-tuple-element.49.refs_0_, bf16[6,32,320]{2,1,0:T(8,128)(2,1)} %copy-done.14, bf16[6,32,320]{2,1,0:T(8,128)(2,1)} %copy-done.10, ...), custom_call_target="tpu_custom_call" | custom-call | tf_op jit(solution)/shard_map/pallas_call | solution.py:194
  59.9 1.7 %collective-permute-start.5 = (bf16[6,32,320]{2,1,0:T(8,128)(2,1)}, bf16[6,32,320]{2,1,0:T(8,128)(2,1)S(1)}, u32[]{:S(2)}, u32[]{:S(2)}) collective-permute-start(bf16[6,32,320]{2,1,0:T(8,128)(2,1)} %get-tuple-element.21), channel_id=1, source_target_pairs={{0,3},{1,0},{2,1},{3,2},{4,7},{5,4},{6,5},{7,6},{8,11},{9,8},{10,9... | collective-permute-start | bytes 368648 | tf_op jit(solution)/shard_map/ppermute | solution.py:239
  61.6 1.4 %collective-permute-start.6 = (bf16[6,32,320]{2,1,0:T(8,128)(2,1)}, bf16[6,32,320]{2,1,0:T(8,128)(2,1)S(1)}, u32[]{:S(2)}, u32[]{:S(2)}) collective-permute-start(bf16[6,32,320]{2,1,0:T(8,128)(2,1)} %get-tuple-element.22), channel_id=1, source_target_pairs={{0,2},{1,3},{2,0},{3,1},{4,6},{5,7},{6,4},{7,5},{8,10},{9,11},{10,... | collective-permute-start | bytes 368648 | tf_op jit(solution)/shard_map/ppermute | solution.py:239
  63.1 0.7 gather_fusion.4
  63.9 0.7 collective-permute-done.13
  64.8 0.7 gather_fusion.3
  65.4 0.7 collective-permute-done.5
  66.1 4.8 %collective-permute-done.6 = bf16[6,32,320]{2,1,0:T(8,128)(2,1)S(1)} collective-permute-done((bf16[6,32,320]{2,1,0:T(8,128)(2,1)}, bf16[6,32,320]{2,1,0:T(8,128)(2,1)S(1)}, u32[]{:S(2)}, u32[]{:S(2)}) %collective-permute-start.6) | collective-permute-done | bytes 122912 | tf_op jit(solution)/shard_map/ppermute | solution.py:239
  71.1 0.7 gather_fusion.2
  72.6 1.0 %collective-permute-start.20 = (bf16[72,320]{1,0:T(8,128)(2,1)S(1)}, bf16[72,320]{1,0:T(8,128)(2,1)S(1)}, u32[]{:S(2)}, u32[]{:S(2)}) collective-permute-start(bf16[72,320]{1,0:T(8,128)(2,1)S(1)} %pad_maximum_fusion.3), channel_id=1, source_target_pairs={{12,0},{0,4},{4,8},{8,12},{13,1},{1,5},{5,9},{9,13},{14,2},{2,6},{... | collective-permute-start | bytes 138248 | tf_op jit(solution)/shard_map/ppermute | solution.py:16
  73.7 3.2 %collective-permute-start.21 = (bf16[72,320]{1,0:T(8,128)(2,1)S(1)}, bf16[72,320]{1,0:T(8,128)(2,1)S(1)}, u32[]{:S(2)}, u32[]{:S(2)}) collective-permute-start(bf16[72,320]{1,0:T(8,128)(2,1)S(1)} %pad_maximum_fusion.4), channel_id=1, source_target_pairs={{4,0},{8,4},{12,8},{0,12},{5,1},{9,5},{13,9},{1,13},{6,2},{10,6},{... | collective-permute-start | bytes 138248 | tf_op jit(solution)/shard_map/ppermute | solution.py:16
  76.9 2.3 %collective-permute-done.20 = bf16[72,320]{1,0:T(8,128)(2,1)S(1)} collective-permute-done((bf16[72,320]{1,0:T(8,128)(2,1)S(1)}, bf16[72,320]{1,0:T(8,128)(2,1)S(1)}, u32[]{:S(2)}, u32[]{:S(2)}) %collective-permute-start.20) | collective-permute-done | bytes 46112 | tf_op jit(solution)/shard_map/ppermute | solution.py:16
  80.4 11.9 %shard_map.68 = bf16[72,32,320]{2,1,0:T(8,128)(2,1)} custom-call(bf16[72,32,320]{2,1,0:T(8,128)(2,1)} %shard_map.64.refs_0_, bf16[24,32,320]{2,1,0:T(8,128)(2,1)} %bitcast.65, bf16[24,32,320]{2,1,0:T(8,128)(2,1)} %bitcast.63, bf16[24,32,320]{2,1,0:T(8,128)(2,1)} %bitcast.61, bf16[72,320]{1,0:T(8,128)(2,1)} %broadcast_select_fusion.5.refs_4_, ...), custom_call_target="tpu_custom_call" | custom-call | tf_op jit(solution)/shard_map/pallas_call | solution.py:100
  (107 shorter events, 7.5 us)
Async XLA Ops:
  0.0 7.6 %copy-start = (f32[5,4,4]{0,2,1:T(4,128)S(1)}, f32[5,4,4]{0,2,1:T(4,128)}, u32[]{:S(2)}) copy-start(f32[5,4,4]{0,2,1:T(4,128)} %param.16) | copy-start | bytes 964
  2.0 7.3 %collective-permute-start = (bf16[72,320]{1,0:T(8,128)(2,1)S(1)}, bf16[72,320]{1,0:T(8,128)(2,1)S(1)}, u32[]{:S(2)}, u32[]{:S(2)}) collective-permute-start(bf16[72,320]{1,0:T(8,128)(2,1)S(1)} %bitcast.80), channel_id=1, source_target_pairs={{12,0},{0,4},{4,8},{8,12},{13,1},{1,5},{5,9},{9,13},{14,2},{2,6},{... | collective-permute-start | bytes 138248 | tf_op jit(solution)/shard_map/ppermute | solution.py:16
  5.4 4.6 %collective-permute-start.1 = (bf16[72,320]{1,0:T(8,128)(2,1)S(1)}, bf16[72,320]{1,0:T(8,128)(2,1)S(1)}, u32[]{:S(2)}, u32[]{:S(2)}) collective-permute-start(bf16[72,320]{1,0:T(8,128)(2,1)S(1)} %bitcast.81), channel_id=1, source_target_pairs={{4,0},{8,4},{12,8},{0,12},{5,1},{9,5},{13,9},{1,13},{6,2},{10,6},{... | collective-permute-start | bytes 138248 | tf_op jit(solution)/shard_map/ppermute | solution.py:16
  23.3 12.9 %copy-start.5 = (bf16[320,960]{1,0:T(8,128)(2,1)S(1)}, bf16[320,960]{1,0:T(8,128)(2,1)}, u32[]{:S(2)}) copy-start(bf16[320,960]{1,0:T(8,128)(2,1)} %param.14) | copy-start | bytes 1843204
  25.8 4.0 %collective-permute-start.16 = (bf16[6,32,320]{2,1,0:T(8,128)(2,1)S(1)}, bf16[6,32,320]{2,1,0:T(8,128)(2,1)S(1)}, u32[]{:S(2)}, u32[]{:S(2)}) collective-permute-start(bf16[6,32,320]{2,1,0:T(8,128)(2,1)S(1)} %get-tuple-element.38), channel_id=1, source_target_pairs={{0,3},{1,0},{2,1},{3,2},{4,7},{5,4},{6,5},{7,6},{8,11},{9,8},{10,9... | collective-permute-start | bytes 368648 | tf_op jit(solution)/shard_map/ppermute | solution.py:230
  25.9 9.4 %collective-permute-start.15 = (bf16[6,32,320]{2,1,0:T(8,128)(2,1)S(1)}, bf16[6,32,320]{2,1,0:T(8,128)(2,1)S(1)}, u32[]{:S(2)}, u32[]{:S(2)}) collective-permute-start(bf16[6,32,320]{2,1,0:T(8,128)(2,1)S(1)} %get-tuple-element.39), channel_id=1, source_target_pairs={{0,2},{1,3},{2,0},{3,1},{4,6},{5,7},{6,4},{7,5},{8,10},{9,11},{10,... | collective-permute-start | bytes 368648 | tf_op jit(solution)/shard_map/ppermute | solution.py:230
  27.6 9.7 %collective-permute-start.14 = (bf16[6,32,320]{2,1,0:T(8,128)(2,1)S(1)}, bf16[6,32,320]{2,1,0:T(8,128)(2,1)S(1)}, u32[]{:S(2)}, u32[]{:S(2)}) collective-permute-start(bf16[6,32,320]{2,1,0:T(8,128)(2,1)S(1)} %get-tuple-element.40), channel_id=1, source_target_pairs={{0,1},{1,2},{2,3},{3,0},{4,5},{5,6},{6,7},{7,4},{8,9},{9,10},{10,1... | collective-permute-start | bytes 368648 | tf_op jit(solution)/shard_map/ppermute | solution.py:230
  27.8 14.8 %collective-permute-start.10 = (bf16[6,32,320]{2,1,0:T(8,128)(2,1)S(1)}, bf16[6,32,320]{2,1,0:T(8,128)(2,1)S(1)}, u32[]{:S(2)}, u32[]{:S(2)}) collective-permute-start(bf16[6,32,320]{2,1,0:T(8,128)(2,1)S(1)} %get-tuple-element.42), channel_id=1, source_target_pairs={{0,3},{1,0},{2,1},{3,2},{4,7},{5,4},{6,5},{7,6},{8,11},{9,8},{10,9... | collective-permute-start | bytes 368648 | tf_op jit(solution)/shard_map/ppermute | solution.py:230
  29.4 13.9 %collective-permute-start.9 = (bf16[6,32,320]{2,1,0:T(8,128)(2,1)S(1)}, bf16[6,32,320]{2,1,0:T(8,128)(2,1)S(1)}, u32[]{:S(2)}, u32[]{:S(2)}) collective-permute-start(bf16[6,32,320]{2,1,0:T(8,128)(2,1)S(1)} %get-tuple-element.43), channel_id=1, source_target_pairs={{0,2},{1,3},{2,0},{3,1},{4,6},{5,7},{6,4},{7,5},{8,10},{9,11},{10,... | collective-permute-start | bytes 368648 | tf_op jit(solution)/shard_map/ppermute | solution.py:230
  29.8 7.7 %copy-start.15 = (bf16[6,32,320]{2,1,0:T(8,128)(2,1)}, bf16[6,32,320]{2,1,0:T(8,128)(2,1)S(1)}, u32[]{:S(2)}) copy-start(bf16[6,32,320]{2,1,0:T(8,128)(2,1)S(1)} %collective-permute-done.16.refs_3_) | copy-start | bytes 368644
  29.8 14.7 %collective-permute-start.8 = (bf16[6,32,320]{2,1,0:T(8,128)(2,1)S(1)}, bf16[6,32,320]{2,1,0:T(8,128)(2,1)S(1)}, u32[]{:S(2)}, u32[]{:S(2)}) collective-permute-start(bf16[6,32,320]{2,1,0:T(8,128)(2,1)S(1)} %get-tuple-element.44), channel_id=1, source_target_pairs={{0,1},{1,2},{2,3},{3,0},{4,5},{5,6},{6,7},{7,4},{8,9},{9,10},{10,1... | collective-permute-start | bytes 368648 | tf_op jit(solution)/shard_map/ppermute | solution.py:230
  35.4 10.6 %collective-permute-start.4 = (bf16[6,32,320]{2,1,0:T(8,128)(2,1)S(1)}, bf16[6,32,320]{2,1,0:T(8,128)(2,1)S(1)}, u32[]{:S(2)}, u32[]{:S(2)}) collective-permute-start(bf16[6,32,320]{2,1,0:T(8,128)(2,1)S(1)} %get-tuple-element.46), channel_id=1, source_target_pairs={{0,3},{1,0},{2,1},{3,2},{4,7},{5,4},{6,5},{7,6},{8,11},{9,8},{10,9... | collective-permute-start | bytes 368648 | tf_op jit(solution)/shard_map/ppermute | solution.py:230
  37.4 15.4 %collective-permute-start.3 = (bf16[6,32,320]{2,1,0:T(8,128)(2,1)S(1)}, bf16[6,32,320]{2,1,0:T(8,128)(2,1)S(1)}, u32[]{:S(2)}, u32[]{:S(2)}) collective-permute-start(bf16[6,32,320]{2,1,0:T(8,128)(2,1)S(1)} %get-tuple-element.47), channel_id=1, source_target_pairs={{0,2},{1,3},{2,0},{3,1},{4,6},{5,7},{6,4},{7,5},{8,10},{9,11},{10,... | collective-permute-start | bytes 368648 | tf_op jit(solution)/shard_map/ppermute | solution.py:230
  42.7 11.8 %collective-permute-start.2 = (bf16[6,32,320]{2,1,0:T(8,128)(2,1)S(1)}, bf16[6,32,320]{2,1,0:T(8,128)(2,1)S(1)}, u32[]{:S(2)}, u32[]{:S(2)}) collective-permute-start(bf16[6,32,320]{2,1,0:T(8,128)(2,1)S(1)} %get-tuple-element.48), channel_id=1, source_target_pairs={{0,1},{1,2},{2,3},{3,0},{4,5},{5,6},{6,7},{7,4},{8,9},{9,10},{10,1... | collective-permute-start | bytes 368648 | tf_op jit(solution)/shard_map/ppermute | solution.py:230
  43.2 16.5 %collective-permute-start.17 = (bf16[6,32,320]{2,1,0:T(8,128)(2,1)}, bf16[6,32,320]{2,1,0:T(8,128)(2,1)S(1)}, u32[]{:S(2)}, u32[]{:S(2)}) collective-permute-start(bf16[6,32,320]{2,1,0:T(8,128)(2,1)} %get-tuple-element.29), channel_id=1, source_target_pairs={{0,3},{1,0},{2,1},{3,2},{4,7},{5,4},{6,5},{7,6},{8,11},{9,8},{10,9... | collective-permute-start | bytes 368648 | tf_op jit(solution)/shard_map/ppermute | solution.py:239
  44.5 15.4 %collective-permute-start.18 = (bf16[6,32,320]{2,1,0:T(8,128)(2,1)}, bf16[6,32,320]{2,1,0:T(8,128)(2,1)S(1)}, u32[]{:S(2)}, u32[]{:S(2)}) collective-permute-start(bf16[6,32,320]{2,1,0:T(8,128)(2,1)} %get-tuple-element.30), channel_id=1, source_target_pairs={{0,2},{1,3},{2,0},{3,1},{4,6},{5,7},{6,4},{7,5},{8,10},{9,11},{10,... | collective-permute-start | bytes 368648 | tf_op jit(solution)/shard_map/ppermute | solution.py:239
  45.9 9.2 %copy-start.7 = (bf16[6,32,320]{2,1,0:T(8,128)(2,1)}, bf16[6,32,320]{2,1,0:T(8,128)(2,1)S(1)}, u32[]{:S(2)}) copy-start(bf16[6,32,320]{2,1,0:T(8,128)(2,1)S(1)} %collective-permute-done.4.refs_3_) | copy-start | bytes 368644
  45.9 17.0 %copy-start.6 = (bf16[6,32,320]{2,1,0:T(8,128)(2,1)S(1)}, bf16[6,32,320]{2,1,0:T(8,128)(2,1)}, u32[]{:S(2)}) copy-start(bf16[6,32,320]{2,1,0:T(8,128)(2,1)} %get-tuple-element.28) | copy-start | bytes 368644
  45.9 15.6 %collective-permute-start.19 = (bf16[6,32,320]{2,1,0:T(8,128)(2,1)}, bf16[6,32,320]{2,1,0:T(8,128)(2,1)S(1)}, u32[]{:S(2)}, u32[]{:S(2)}) collective-permute-start(bf16[6,32,320]{2,1,0:T(8,128)(2,1)} %get-tuple-element.31), channel_id=1, source_target_pairs={{0,1},{1,2},{2,3},{3,0},{4,5},{5,6},{6,7},{7,4},{8,9},{9,10},{10,1... | collective-permute-start | bytes 368648 | tf_op jit(solution)/shard_map/ppermute | solution.py:239
  52.8 11.1 %collective-permute-start.11 = (bf16[6,32,320]{2,1,0:T(8,128)(2,1)}, bf16[6,32,320]{2,1,0:T(8,128)(2,1)S(1)}, u32[]{:S(2)}, u32[]{:S(2)}) collective-permute-start(bf16[6,32,320]{2,1,0:T(8,128)(2,1)} %get-tuple-element.25), channel_id=1, source_target_pairs={{0,3},{1,0},{2,1},{3,2},{4,7},{5,4},{6,5},{7,6},{8,11},{9,8},{10,9... | collective-permute-start | bytes 368648 | tf_op jit(solution)/shard_map/ppermute | solution.py:239
  54.5 9.4 %collective-permute-start.12 = (bf16[6,32,320]{2,1,0:T(8,128)(2,1)}, bf16[6,32,320]{2,1,0:T(8,128)(2,1)S(1)}, u32[]{:S(2)}, u32[]{:S(2)}) collective-permute-start(bf16[6,32,320]{2,1,0:T(8,128)(2,1)} %get-tuple-element.26), channel_id=1, source_target_pairs={{0,2},{1,3},{2,0},{3,1},{4,6},{5,7},{6,4},{7,5},{8,10},{9,11},{10,... | collective-permute-start | bytes 368648 | tf_op jit(solution)/shard_map/ppermute | solution.py:239
  55.1 9.5 %copy-start.11 = (bf16[6,32,320]{2,1,0:T(8,128)(2,1)S(1)}, bf16[6,32,320]{2,1,0:T(8,128)(2,1)}, u32[]{:S(2)}) copy-start(bf16[6,32,320]{2,1,0:T(8,128)(2,1)} %get-tuple-element.24) | copy-start | bytes 368644
  59.8 4.8 %collective-permute-start.13 = (bf16[6,32,320]{2,1,0:T(8,128)(2,1)}, bf16[6,32,320]{2,1,0:T(8,128)(2,1)S(1)}, u32[]{:S(2)}, u32[]{:S(2)}) collective-permute-start(bf16[6,32,320]{2,1,0:T(8,128)(2,1)} %get-tuple-element.27), channel_id=1, source_target_pairs={{0,1},{1,2},{2,3},{3,0},{4,5},{5,6},{6,7},{7,4},{8,9},{9,10},{10,1... | collective-permute-start | bytes 368648 | tf_op jit(solution)/shard_map/ppermute | solution.py:239
  59.9 6.3 %collective-permute-start.5 = (bf16[6,32,320]{2,1,0:T(8,128)(2,1)}, bf16[6,32,320]{2,1,0:T(8,128)(2,1)S(1)}, u32[]{:S(2)}, u32[]{:S(2)}) collective-permute-start(bf16[6,32,320]{2,1,0:T(8,128)(2,1)} %get-tuple-element.21), channel_id=1, source_target_pairs={{0,3},{1,0},{2,1},{3,2},{4,7},{5,4},{6,5},{7,6},{8,11},{9,8},{10,9... | collective-permute-start | bytes 368648 | tf_op jit(solution)/shard_map/ppermute | solution.py:239
  61.6 9.3 %collective-permute-start.6 = (bf16[6,32,320]{2,1,0:T(8,128)(2,1)}, bf16[6,32,320]{2,1,0:T(8,128)(2,1)S(1)}, u32[]{:S(2)}, u32[]{:S(2)}) collective-permute-start(bf16[6,32,320]{2,1,0:T(8,128)(2,1)} %get-tuple-element.22), channel_id=1, source_target_pairs={{0,2},{1,3},{2,0},{3,1},{4,6},{5,7},{6,4},{7,5},{8,10},{9,11},{10,... | collective-permute-start | bytes 368648 | tf_op jit(solution)/shard_map/ppermute | solution.py:239
  63.1 7.8 %copy-start.13 = (bf16[6,32,320]{2,1,0:T(8,128)(2,1)S(1)}, bf16[6,32,320]{2,1,0:T(8,128)(2,1)}, u32[]{:S(2)}) copy-start(bf16[6,32,320]{2,1,0:T(8,128)(2,1)} %get-tuple-element.20) | copy-start | bytes 368644
  63.8 7.1 %collective-permute-start.7 = (bf16[6,32,320]{2,1,0:T(8,128)(2,1)S(1)}, bf16[6,32,320]{2,1,0:T(8,128)(2,1)S(1)}, u32[]{:S(2)}, u32[]{:S(2)}) collective-permute-start(bf16[6,32,320]{2,1,0:T(8,128)(2,1)S(1)} %copy-done.24), channel_id=1, source_target_pairs={{0,1},{1,2},{2,3},{3,0},{4,5},{5,6},{6,7},{7,4},{8,9},{9,10},{10,1... | collective-permute-start | bytes 368648 | tf_op jit(solution)/shard_map/ppermute | solution.py:239
  72.1 8.3 %copy-start.2 = (bf16[4,6,32,320]{3,2,1,0:T(8,128)(2,1)}, bf16[4,6,32,320]{3,2,1,0:T(8,128)(2,1)S(1)}, u32[]{:S(2)}) copy-start(bf16[4,6,32,320]{3,2,1,0:T(8,128)(2,1)S(1)} %get-tuple-element.56) | copy-start | bytes 1474564
  72.1 8.3 %copy-start.3 = (bf16[4,6,32,320]{3,2,1,0:T(8,128)(2,1)}, bf16[4,6,32,320]{3,2,1,0:T(8,128)(2,1)S(1)}, u32[]{:S(2)}) copy-start(bf16[4,6,32,320]{3,2,1,0:T(8,128)(2,1)S(1)} %get-tuple-element.57) | copy-start | bytes 1474564
  72.1 8.3 %copy-start.4 = (bf16[4,6,32,320]{3,2,1,0:T(8,128)(2,1)}, bf16[4,6,32,320]{3,2,1,0:T(8,128)(2,1)S(1)}, u32[]{:S(2)}) copy-start(bf16[4,6,32,320]{3,2,1,0:T(8,128)(2,1)S(1)} %get-tuple-element.58) | copy-start | bytes 1474564
  72.6 6.5 %collective-permute-start.20 = (bf16[72,320]{1,0:T(8,128)(2,1)S(1)}, bf16[72,320]{1,0:T(8,128)(2,1)S(1)}, u32[]{:S(2)}, u32[]{:S(2)}) collective-permute-start(bf16[72,320]{1,0:T(8,128)(2,1)S(1)} %pad_maximum_fusion.3), channel_id=1, source_target_pairs={{12,0},{0,4},{4,8},{8,12},{13,1},{1,5},{5,9},{9,13},{14,2},{2,6},{... | collective-permute-start | bytes 138248 | tf_op jit(solution)/shard_map/ppermute | solution.py:16
  73.7 6.1 %collective-permute-start.21 = (bf16[72,320]{1,0:T(8,128)(2,1)S(1)}, bf16[72,320]{1,0:T(8,128)(2,1)S(1)}, u32[]{:S(2)}, u32[]{:S(2)}) collective-permute-start(bf16[72,320]{1,0:T(8,128)(2,1)S(1)} %pad_maximum_fusion.4), channel_id=1, source_target_pairs={{4,0},{8,4},{12,8},{0,12},{5,1},{9,5},{13,9},{1,13},{6,2},{10,6},{... | collective-permute-start | bytes 138248 | tf_op jit(solution)/shard_map/ppermute | solution.py:16
  (15 other events, 36.7 us)

commit v17 on v14

--- a/solution.py
+++ b/solution.py
@@ -19,14 +19,13 @@
     return jnp.where(inside, moved, jnp.zeros_like(moved))
 
 
-def conv_kernel(*refs, layout, lo, hi, finish):
+def conv_kernel(*refs, layout, lo, hi, band, finish):
     count = sum(len(segments) for segments in layout)
     flat = refs[:count]
     left_ref, right_ref, w_ref, o_ref, slab, shift_s = refs[count:]
     row_count = left_ref.shape[0]
     _, col_count, channels = o_ref.shape
     lanes = slab.shape[1] // 3
-    band = 12
     span = band * col_count
     padded_rows = slab.shape[0]
     slab[pl.ds(0, col_count)] = jnp.zeros((col_count, slab.shape[1]), jnp.bfloat16)
@@ -82,7 +81,7 @@
     return shifted(edge_of(-1), "quarter", 1), shifted(edge_of(0), "quarter", -1)
 
 
-def convolve(groups, rims, weight, finish, lo, hi):
+def convolve(groups, rims, weight, finish, lo, hi, band=12):
     row_count, channels = rims[0].shape
     col_count = groups[0][0].shape[1]
     layout = []
@@ -98,13 +97,13 @@
     padded = (row_count + 2) * col_count
     stacked = weight.reshape(3, 3 * channels, channels)
     return pl.pallas_call(
-        functools.partial(conv_kernel, layout=tuple(layout), lo=lo, hi=hi, finish=finish),
+        functools.partial(conv_kernel, layout=tuple(layout), lo=lo, hi=hi, band=band, finish=finish),
         out_shape=jax.ShapeDtypeStruct((hi - lo, col_count, channels), jnp.bfloat16),
         in_specs=[vmem] * (len(flat) + 3),
         out_specs=vmem,
         scratch_shapes=[
             pltpu.VMEM((padded, 3 * channels), jnp.bfloat16),
-            pltpu.VMEM((12 * col_count + 16, channels), jnp.float32),
+            pltpu.VMEM((band * col_count + 16, channels), jnp.float32),
         ],
     )(*flat, *rims, stacked)
 
@@ -280,7 +279,7 @@
         summed = [h[:, c, :].astype(jnp.float32) + r[:, c, :].astype(jnp.float32) for h, r in zip(hidden, returned)]
         return jnp.concatenate(summed, axis=0).astype(jnp.bfloat16)
 
-    second = convolve([hidden_rows, returned], halo(joined_edge), conv2_weight, to_bf16, 0, row_count)
+    second = convolve([hidden_rows, returned], halo(joined_edge), conv2_weight, to_bf16, 0, row_count, 6)
     return second.reshape(frames_dev, row_count, col_count, channels)
 
 

time: 92.6 us -> 92.3 us (level)
  no operation moved by 1% of the time
where the time goes in v17:
time: 92.3 us; the launch traced here: 92 us
  Pallas kernels  35.9 us (39%)
  waiting for transfers between devices  20.7 us (22%)
  starting transfers between devices  18.1 us (20%)
  local copies, waits for them, and re-layouts  11.2 us (12%)
  other arithmetic  3.51 us (4%)
  matrix products  2.29 us (2%)
    pallas_call x2, Pallas kernels, convolve(): pl.pallas_call(functools.partial(conv_kernel, layout=tuple(layout), lo=lo...  24.2 us
    pallas_call x2, Pallas kernels, attend_pieces(): pl.pallas_call(functools.partial(attend_kernel, parts=frames_all), out_sh...  11.6 us
    ppermute x6, waiting for transfers between devices, rotated_attention(): lax.ppermute(piece, 'frame', [(i, (i - s) % frames_all) for i in range(fr...  7.58 us
    ppermute x4, waiting for transfers between devices, shifted(): moved = lax.ppermute(block, axis, route)  7.55 us
    ppermute x4, starting transfers between devices, shifted(): moved = lax.ppermute(block, axis, route)  7.51 us
    ppermute x6, starting transfers between devices, rotated_attention(): lax.ppermute(piece, 'frame', [(i, (i - s) % frames_all) for i in range(fr...  5.56 us
    ppermute x6, waiting for transfers between devices, rotated_attention(): lax.ppermute(piece, 'frame', [(i, (i + s) % frames_all) for i in range(fr...  5.54 us
    ppermute x6, starting transfers between devices, rotated_attention(): lax.ppermute(piece, 'frame', [(i, (i + s) % frames_all) for i in range(fr...  5.01 us
  transfers between devices with their start and end apart: 16, of which 8 were waited for; matrix products, arithmetic and copies ran while one was open for 9% of the time, Pallas kernels for 13%

profile of v17, /device:TPU:0, one launch (start us, length us, event | category | flops | bytes accessed | tf_op | source)
XLA Modules:
  0.0 92.0 jit_solution(11740897699439704859)
XLA Ops:
  0.0 1.9 %fusion.4 = bf16[1,72,320]{2,0,1:T(2,128)(2,1)S(1)} fusion(bf16[1,72,32,320]{3,2,1,0:T(8,128)(2,1)} %param.12), kind=kOutput, calls=%fused_computation.42 | convolution fusion | flops 1474592 | bytes 1520640 | tf_op jit(solution)/shard_map/rwc,w->rc/dot_general | solution.py:250
  2.0 5.1 %collective-permute-start.1 = (bf16[72,320]{1,0:T(8,128)(2,1)S(1)}, bf16[72,320]{1,0:T(8,128)(2,1)S(1)}, u32[]{:S(2)}, u32[]{:S(2)}) collective-permute-start(bf16[72,320]{1,0:T(8,128)(2,1)S(1)} %bitcast.64), channel_id=1, source_target_pairs={{4,0},{8,4},{12,8},{0,12},{5,1},{9,5},{13,9},{1,13},{6,2},{10,6},{... | collective-permute-start | bytes 138248 | tf_op jit(solution)/shard_map/ppermute | solution.py:16
  8.9 0.6 broadcast_select_fusion.3.refs_2_
  9.5 3.9 %collective-permute-done = bf16[72,320]{1,0:T(8,128)(2,1)S(1)} collective-permute-done((bf16[72,320]{1,0:T(8,128)(2,1)S(1)}, bf16[72,320]{1,0:T(8,128)(2,1)S(1)}, u32[]{:S(2)}, u32[]{:S(2)}) %collective-permute-start) | collective-permute-done | bytes 46112 | tf_op jit(solution)/shard_map/ppermute | solution.py:16
  13.5 0.6 broadcast_select_fusion.5.refs_1_
  14.1 12.6 %shard_map.64.refs_0_ = bf16[72,32,320]{2,1,0:T(8,128)(2,1)} custom-call(bf16[72,32,320]{2,1,0:T(8,128)(2,1)} %bitcast.47, bf16[72,320]{1,0:T(8,128)(2,1)} %broadcast_select_fusion.5.refs_1_, bf16[72,320]{1,0:T(8,128)(2,1)} %broadcast_select_fusion.3.refs_2_, bf16[3,960,320]{2,1,0:T(8,128)(2,1)} %bitcast.54), custom_call_target="tpu_custom_call" | custom-call | tf_op jit(solution)/shard_map/pallas_call | solution.py:99
  26.7 2.6 %constant_dynamic-slice_fusion = (bf16[9,32,320]{2,1,0:T(8,128)(2,1)S(1)}, bf16[9,32,320]{2,1,0:T(8,128)(2,1)S(1)}, bf16[9,32,320]{2,1,0:T(8,128)(2,1)S(1)}, bf1...) fusion(bf16[72,32,320]{2,1,0:T(8,128)(2,1)} %shard_map.64.refs_, ...), kind=kLoop, calls=%fused_computation.34 | loop fusion | bytes 2949152 | tf_op jit(solution)/shard_map/dynamic_slice | solution.py:227
  29.3 1.5 %collective-permute-start.3 = (bf16[9,32,320]{2,1,0:T(8,128)(2,1)S(1)}, bf16[9,32,320]{2,1,0:T(8,128)(2,1)S(1)}, u32[]{:S(2)}, u32[]{:S(2)}) collective-permute-start(bf16[9,32,320]{2,1,0:T(8,128)(2,1)S(1)} %get-tuple-element.33), channel_id=1, source_target_pairs={{0,2},{1,3},{2,0},{3,1},{4,6},{5,7},{6,4},{7,5},{8,10},{9,11},{10,... | collective-permute-start | bytes 552968 | tf_op jit(solution)/shard_map/ppermute | solution.py:229
  30.9 1.4 %collective-permute-start.4 = (bf16[9,32,320]{2,1,0:T(8,128)(2,1)S(1)}, bf16[9,32,320]{2,1,0:T(8,128)(2,1)S(1)}, u32[]{:S(2)}, u32[]{:S(2)}) collective-permute-start(bf16[9,32,320]{2,1,0:T(8,128)(2,1)S(1)} %get-tuple-element.32), channel_id=1, source_target_pairs={{0,3},{1,0},{2,1},{3,2},{4,7},{5,4},{6,5},{7,6},{8,11},{9,8},{10,9... | collective-permute-start | bytes 552968 | tf_op jit(solution)/shard_map/ppermute | solution.py:229
  32.4 0.8 copy.32.refs_5_
  33.2 1.2 %copy.30 = bf16[320,960]{0,1:T(8,128)(2,1)} copy(bf16[320,960]{1,0:T(8,128)(2,1)S(1)} %copy-done.4) | data formatting | bytes 1228800 | tf_op args[2]
  34.9 1.6 %collective-permute-done.2.refs_1_ = bf16[9,32,320]{2,1,0:T(8,128)(2,1)S(1)} collective-permute-done((bf16[9,32,320]{2,1,0:T(8,128)(2,1)S(1)}, bf16[9,32,320]{2,1,0:T(8,128)(2,1)S(1)}, u32[]{:S(2)}, u32[]{:S(2)}) %collective-permute-start.2) | collective-permute-done | bytes 184352 | tf_op jit(solution)/shard_map/ppermute | solution.py:229
  36.5 1.5 %collective-permute-start.9 = (bf16[9,32,320]{2,1,0:T(8,128)(2,1)S(1)}, bf16[9,32,320]{2,1,0:T(8,128)(2,1)S(1)}, u32[]{:S(2)}, u32[]{:S(2)}) collective-permute-start(bf16[9,32,320]{2,1,0:T(8,128)(2,1)S(1)} %get-tuple-element.29), channel_id=1, source_target_pairs={{0,2},{1,3},{2,0},{3,1},{4,6},{5,7},{6,4},{7,5},{8,10},{9,11},{10,... | collective-permute-start | bytes 552968 | tf_op jit(solution)/shard_map/ppermute | solution.py:229
  38.0 3.4 %collective-permute-done.4.refs_3_ = bf16[9,32,320]{2,1,0:T(8,128)(2,1)S(1)} collective-permute-done((bf16[9,32,320]{2,1,0:T(8,128)(2,1)S(1)}, bf16[9,32,320]{2,1,0:T(8,128)(2,1)S(1)}, u32[]{:S(2)}, u32[]{:S(2)}) %collective-permute-start.4) | collective-permute-done | bytes 184352 | tf_op jit(solution)/shard_map/ppermute | solution.py:229
  41.4 0.7 copy-done.16
  42.1 5.8 %shard_map.65 = (bf16[9,32,320]{2,1,0:T(8,128)(2,1)}, bf16[9,32,320]{2,1,0:T(8,128)(2,1)}, bf16[9,32,320]{2,1,0:T(8,128)(2,1)}, bf16[9,32,320]{2,1,0:T(8,128)(2,1)}) custom-call(bf16[9,32,320]{2,1,0:T(8,128)(2,1)} %get-tuple-element.35.refs_0_, bf16[9,32,320]{2,1,0:T(8,128)(2,1)} %copy-done.14, bf16[9,32,320]{2,1,0:T(8,128)(2,1)} %copy-done.15, ...), custom_call_target="tpu_custom_call" | custom-call | tf_op jit(solution)/shard_map/pallas_call | solution.py:193
  47.9 2.2 %collective-permute-start.5 = (bf16[9,32,320]{2,1,0:T(8,128)(2,1)}, bf16[9,32,320]{2,1,0:T(8,128)(2,1)S(1)}, u32[]{:S(2)}, u32[]{:S(2)}) collective-permute-start(bf16[9,32,320]{2,1,0:T(8,128)(2,1)} %get-tuple-element.17), channel_id=1, source_target_pairs={{0,3},{1,0},{2,1},{3,2},{4,7},{5,4},{6,5},{7,6},{8,11},{9,8},{10,9... | collective-permute-start | bytes 552968 | tf_op jit(solution)/shard_map/ppermute | solution.py:238
  50.1 0.6 collective-permute-start.6
  52.0 5.8 %shard_map.66 = (bf16[9,32,320]{2,1,0:T(8,128)(2,1)}, bf16[9,32,320]{2,1,0:T(8,128)(2,1)}, bf16[9,32,320]{2,1,0:T(8,128)(2,1)}, bf16[9,32,320]{2,1,0:T(8,128)(2,1)}) custom-call(bf16[9,32,320]{2,1,0:T(8,128)(2,1)} %get-tuple-element.31.refs_0_, bf16[9,32,320]{2,1,0:T(8,128)(2,1)} %copy-done.12, bf16[9,32,320]{2,1,0:T(8,128)(2,1)} %copy-done.13, ...), custom_call_target="tpu_custom_call" | custom-call | tf_op jit(solution)/shard_map/pallas_call | solution.py:193
  57.8 1.3 %collective-permute-start.11 = (bf16[9,32,320]{2,1,0:T(8,128)(2,1)}, bf16[9,32,320]{2,1,0:T(8,128)(2,1)S(1)}, u32[]{:S(2)}, u32[]{:S(2)}) collective-permute-start(bf16[9,32,320]{2,1,0:T(8,128)(2,1)} %get-tuple-element.21), channel_id=1, source_target_pairs={{0,3},{1,0},{2,1},{3,2},{4,7},{5,4},{6,5},{7,6},{8,11},{9,8},{10,9... | collective-permute-start | bytes 552968 | tf_op jit(solution)/shard_map/ppermute | solution.py:238
  59.0 1.5 %collective-permute-start.12 = (bf16[9,32,320]{2,1,0:T(8,128)(2,1)}, bf16[9,32,320]{2,1,0:T(8,128)(2,1)S(1)}, u32[]{:S(2)}, u32[]{:S(2)}) collective-permute-start(bf16[9,32,320]{2,1,0:T(8,128)(2,1)} %get-tuple-element.22), channel_id=1, source_target_pairs={{0,2},{1,3},{2,0},{3,1},{4,6},{5,7},{6,4},{7,5},{8,10},{9,11},{10,... | collective-permute-start | bytes 552968 | tf_op jit(solution)/shard_map/ppermute | solution.py:238
  60.6 2.1 %fusion.19 = (bf16[36,1,320]{2,1,0:T(2,128)(2,1)}, bf16[36,1,320]{2,1,0:T(2,128)(2,1)}, bf16[36,1,320]{2,1,0:T(2,128)(2,1)}, bf16[36,1,320]{2,1,0:T(2,128)(2,1)}) fusion(bf16[72,32,320]{2,1,0:T(8,128)(2,1)} %shard_map.64.refs_0_), kind=kLoop, calls=%fused_computation.61 | loop fusion | bytes 184320 | tf_op jit(solution)/shard_map/slice | solution.py:279
  62.9 0.7 gather_fusion.2
  63.7 1.8 %collective-permute-done.11 = bf16[9,32,320]{2,1,0:T(8,128)(2,1)S(1)} collective-permute-done((bf16[9,32,320]{2,1,0:T(8,128)(2,1)}, bf16[9,32,320]{2,1,0:T(8,128)(2,1)S(1)}, u32[]{:S(2)}, u32[]{:S(2)}) %collective-permute-start.11) | collective-permute-done | bytes 184352 | tf_op jit(solution)/shard_map/ppermute | solution.py:238
  65.4 5.8 %collective-permute-done.12 = bf16[9,32,320]{2,1,0:T(8,128)(2,1)S(1)} collective-permute-done((bf16[9,32,320]{2,1,0:T(8,128)(2,1)}, bf16[9,32,320]{2,1,0:T(8,128)(2,1)S(1)}, u32[]{:S(2)}, u32[]{:S(2)}) %collective-permute-start.12) | collective-permute-done | bytes 184352 | tf_op jit(solution)/shard_map/ppermute | solution.py:238
  71.5 0.7 gather_fusion.3
  73.5 2.0 %collective-permute-start.14 = (bf16[72,320]{1,0:T(8,128)(2,1)S(1)}, bf16[72,320]{1,0:T(8,128)(2,1)S(1)}, u32[]{:S(2)}, u32[]{:S(2)}) collective-permute-start(bf16[72,320]{1,0:T(8,128)(2,1)S(1)} %pad_maximum_fusion.2), channel_id=1, source_target_pairs={{12,0},{0,4},{4,8},{8,12},{13,1},{1,5},{5,9},{9,13},{14,2},{2,6},{... | collective-permute-start | bytes 138248 | tf_op jit(solution)/shard_map/ppermute | solution.py:16
  75.5 2.2 %collective-permute-done.15 = bf16[72,320]{1,0:T(8,128)(2,1)S(1)} collective-permute-done((bf16[72,320]{1,0:T(8,128)(2,1)S(1)}, bf16[72,320]{1,0:T(8,128)(2,1)S(1)}, u32[]{:S(2)}, u32[]{:S(2)}) %collective-permute-start.15) | collective-permute-done | bytes 46112 | tf_op jit(solution)/shard_map/ppermute | solution.py:16
  77.7 0.6 broadcast_select_fusion.2.refs_4_
  78.4 1.4 %collective-permute-done.14 = bf16[72,320]{1,0:T(8,128)(2,1)S(1)} collective-permute-done((bf16[72,320]{1,0:T(8,128)(2,1)S(1)}, bf16[72,320]{1,0:T(8,128)(2,1)S(1)}, u32[]{:S(2)}, u32[]{:S(2)}) %collective-permute-start.14) | collective-permute-done | bytes 46112 | tf_op jit(solution)/shard_map/ppermute | solution.py:16
  79.7 0.6 broadcast_select_fusion.4.refs_3_
  80.4 11.6 %shard_map.67 = bf16[72,32,320]{2,1,0:T(8,128)(2,1)} custom-call(bf16[72,32,320]{2,1,0:T(8,128)(2,1)} %shard_map.64.refs_0_, bf16[36,32,320]{2,1,0:T(8,128)(2,1)} %bitcast.53, bf16[36,32,320]{2,1,0:T(8,128)(2,1)} %bitcast.51, bf16[72,320]{1,0:T(8,128)(2,1)} %broadcast_select_fusion.4.refs_3_, bf16[72,320]{1,0:T(8,128)(2,1)} %broadcast_select_fusion.2.refs_4_, ...), custom_call_target="tpu_custom_call" | custom-call | tf_op jit(solution)/shard_map/pallas_call | solution.py:99
  (73 shorter events, 5.2 us)
Async XLA Ops:
  0.0 7.6 %copy-start = (f32[5,4,4]{0,2,1:T(4,128)S(1)}, f32[5,4,4]{0,2,1:T(4,128)}, u32[]{:S(2)}) copy-start(f32[5,4,4]{0,2,1:T(4,128)} %param.16) | copy-start | bytes 964
  0.0 7.1 %copy-start.1 = (bf16[1,72,32,320]{3,2,1,0:T(8,128)(2,1)S(1)}, bf16[1,72,32,320]{3,2,1,0:T(8,128)(2,1)}, u32[]{:S(2)}) copy-start(bf16[1,72,32,320]{3,2,1,0:T(8,128)(2,1)} %param.12) | copy-start | bytes 4423684
  2.0 6.9 %collective-permute-start.1 = (bf16[72,320]{1,0:T(8,128)(2,1)S(1)}, bf16[72,320]{1,0:T(8,128)(2,1)S(1)}, u32[]{:S(2)}, u32[]{:S(2)}) collective-permute-start(bf16[72,320]{1,0:T(8,128)(2,1)S(1)} %bitcast.64), channel_id=1, source_target_pairs={{4,0},{8,4},{12,8},{0,12},{5,1},{9,5},{13,9},{1,13},{6,2},{10,6},{... | collective-permute-start | bytes 138248 | tf_op jit(solution)/shard_map/ppermute | solution.py:16
  7.4 6.0 %collective-permute-start = (bf16[72,320]{1,0:T(8,128)(2,1)S(1)}, bf16[72,320]{1,0:T(8,128)(2,1)S(1)}, u32[]{:S(2)}, u32[]{:S(2)}) collective-permute-start(bf16[72,320]{1,0:T(8,128)(2,1)S(1)} %bitcast.65), channel_id=1, source_target_pairs={{12,0},{0,4},{4,8},{8,12},{13,1},{1,5},{5,9},{9,13},{14,2},{2,6},{... | collective-permute-start | bytes 138248 | tf_op jit(solution)/shard_map/ppermute | solution.py:16
  26.7 6.5 %copy-start.4 = (bf16[320,960]{1,0:T(8,128)(2,1)S(1)}, bf16[320,960]{1,0:T(8,128)(2,1)}, u32[]{:S(2)}) copy-start(bf16[320,960]{1,0:T(8,128)(2,1)} %param.14) | copy-start | bytes 1843204
  29.3 7.2 %collective-permute-start.2 = (bf16[9,32,320]{2,1,0:T(8,128)(2,1)S(1)}, bf16[9,32,320]{2,1,0:T(8,128)(2,1)S(1)}, u32[]{:S(2)}, u32[]{:S(2)}) collective-permute-start(bf16[9,32,320]{2,1,0:T(8,128)(2,1)S(1)} %get-tuple-element.34), channel_id=1, source_target_pairs={{0,1},{1,2},{2,3},{3,0},{4,5},{5,6},{6,7},{7,4},{8,9},{9,10},{10,1... | collective-permute-start | bytes 552968 | tf_op jit(solution)/shard_map/ppermute | solution.py:229
  29.3 8.7 %collective-permute-start.3 = (bf16[9,32,320]{2,1,0:T(8,128)(2,1)S(1)}, bf16[9,32,320]{2,1,0:T(8,128)(2,1)S(1)}, u32[]{:S(2)}, u32[]{:S(2)}) collective-permute-start(bf16[9,32,320]{2,1,0:T(8,128)(2,1)S(1)} %get-tuple-element.33), channel_id=1, source_target_pairs={{0,2},{1,3},{2,0},{3,1},{4,6},{5,7},{6,4},{7,5},{8,10},{9,11},{10,... | collective-permute-start | bytes 552968 | tf_op jit(solution)/shard_map/ppermute | solution.py:229
  30.9 10.5 %collective-permute-start.4 = (bf16[9,32,320]{2,1,0:T(8,128)(2,1)S(1)}, bf16[9,32,320]{2,1,0:T(8,128)(2,1)S(1)}, u32[]{:S(2)}, u32[]{:S(2)}) collective-permute-start(bf16[9,32,320]{2,1,0:T(8,128)(2,1)S(1)} %get-tuple-element.32), channel_id=1, source_target_pairs={{0,3},{1,0},{2,1},{3,2},{4,7},{5,4},{6,5},{7,6},{8,11},{9,8},{10,9... | collective-permute-start | bytes 552968 | tf_op jit(solution)/shard_map/ppermute | solution.py:229
  34.4 16.3 %collective-permute-start.10 = (bf16[9,32,320]{2,1,0:T(8,128)(2,1)S(1)}, bf16[9,32,320]{2,1,0:T(8,128)(2,1)S(1)}, u32[]{:S(2)}, u32[]{:S(2)}) collective-permute-start(bf16[9,32,320]{2,1,0:T(8,128)(2,1)S(1)} %get-tuple-element.28), channel_id=1, source_target_pairs={{0,3},{1,0},{2,1},{3,2},{4,7},{5,4},{6,5},{7,6},{8,11},{9,8},{10,9... | collective-permute-start | bytes 552968 | tf_op jit(solution)/shard_map/ppermute | solution.py:229
  34.4 16.3 %collective-permute-start.8 = (bf16[9,32,320]{2,1,0:T(8,128)(2,1)S(1)}, bf16[9,32,320]{2,1,0:T(8,128)(2,1)S(1)}, u32[]{:S(2)}, u32[]{:S(2)}) collective-permute-start(bf16[9,32,320]{2,1,0:T(8,128)(2,1)S(1)} %get-tuple-element.30), channel_id=1, source_target_pairs={{0,1},{1,2},{2,3},{3,0},{4,5},{5,6},{6,7},{7,4},{8,9},{9,10},{10,1... | collective-permute-start | bytes 552968 | tf_op jit(solution)/shard_map/ppermute | solution.py:229
  36.5 4.9 %copy-start.14 = (bf16[9,32,320]{2,1,0:T(8,128)(2,1)}, bf16[9,32,320]{2,1,0:T(8,128)(2,1)S(1)}, u32[]{:S(2)}) copy-start(bf16[9,32,320]{2,1,0:T(8,128)(2,1)S(1)} %collective-permute-done.2.refs_1_) | copy-start | bytes 552964
  36.5 14.8 %collective-permute-start.9 = (bf16[9,32,320]{2,1,0:T(8,128)(2,1)S(1)}, bf16[9,32,320]{2,1,0:T(8,128)(2,1)S(1)}, u32[]{:S(2)}, u32[]{:S(2)}) collective-permute-start(bf16[9,32,320]{2,1,0:T(8,128)(2,1)S(1)} %get-tuple-element.29), channel_id=1, source_target_pairs={{0,2},{1,3},{2,0},{3,1},{4,6},{5,7},{6,4},{7,5},{8,10},{9,11},{10,... | collective-permute-start | bytes 552968 | tf_op jit(solution)/shard_map/ppermute | solution.py:229
  38.0 3.4 %copy-start.15 = (bf16[9,32,320]{2,1,0:T(8,128)(2,1)}, bf16[9,32,320]{2,1,0:T(8,128)(2,1)S(1)}, u32[]{:S(2)}) copy-start(bf16[9,32,320]{2,1,0:T(8,128)(2,1)S(1)} %collective-permute-done.3.refs_2_) | copy-start | bytes 552964
  47.9 14.8 %copy-start.5 = (bf16[9,32,320]{2,1,0:T(8,128)(2,1)S(1)}, bf16[9,32,320]{2,1,0:T(8,128)(2,1)}, u32[]{:S(2)}) copy-start(bf16[9,32,320]{2,1,0:T(8,128)(2,1)} %get-tuple-element.16) | copy-start | bytes 552964
  47.9 12.7 %collective-permute-start.5 = (bf16[9,32,320]{2,1,0:T(8,128)(2,1)}, bf16[9,32,320]{2,1,0:T(8,128)(2,1)S(1)}, u32[]{:S(2)}, u32[]{:S(2)}) collective-permute-start(bf16[9,32,320]{2,1,0:T(8,128)(2,1)} %get-tuple-element.17), channel_id=1, source_target_pairs={{0,3},{1,0},{2,1},{3,2},{4,7},{5,4},{6,5},{7,6},{8,11},{9,8},{10,9... | collective-permute-start | bytes 552968 | tf_op jit(solution)/shard_map/ppermute | solution.py:238
  50.1 12.6 %collective-permute-start.6 = (bf16[9,32,320]{2,1,0:T(8,128)(2,1)}, bf16[9,32,320]{2,1,0:T(8,128)(2,1)S(1)}, u32[]{:S(2)}, u32[]{:S(2)}) collective-permute-start(bf16[9,32,320]{2,1,0:T(8,128)(2,1)} %get-tuple-element.18), channel_id=1, source_target_pairs={{0,2},{1,3},{2,0},{3,1},{4,6},{5,7},{6,4},{7,5},{8,10},{9,11},{10,... | collective-permute-start | bytes 552968 | tf_op jit(solution)/shard_map/ppermute | solution.py:238
  50.7 0.7 copy-start.11
  50.7 12.0 %collective-permute-start.7 = (bf16[9,32,320]{2,1,0:T(8,128)(2,1)}, bf16[9,32,320]{2,1,0:T(8,128)(2,1)S(1)}, u32[]{:S(2)}, u32[]{:S(2)}) collective-permute-start(bf16[9,32,320]{2,1,0:T(8,128)(2,1)} %get-tuple-element.19), channel_id=1, source_target_pairs={{0,1},{1,2},{2,3},{3,0},{4,5},{5,6},{6,7},{7,4},{8,9},{9,10},{10,1... | collective-permute-start | bytes 552968 | tf_op jit(solution)/shard_map/ppermute | solution.py:238
  50.7 0.7 copy-start.12
  51.3 0.7 copy-start.13
  57.8 7.7 %collective-permute-start.11 = (bf16[9,32,320]{2,1,0:T(8,128)(2,1)}, bf16[9,32,320]{2,1,0:T(8,128)(2,1)S(1)}, u32[]{:S(2)}, u32[]{:S(2)}) collective-permute-start(bf16[9,32,320]{2,1,0:T(8,128)(2,1)} %get-tuple-element.21), channel_id=1, source_target_pairs={{0,3},{1,0},{2,1},{3,2},{4,7},{5,4},{6,5},{7,6},{8,11},{9,8},{10,9... | collective-permute-start | bytes 552968 | tf_op jit(solution)/shard_map/ppermute | solution.py:238
  59.0 12.2 %collective-permute-start.12 = (bf16[9,32,320]{2,1,0:T(8,128)(2,1)}, bf16[9,32,320]{2,1,0:T(8,128)(2,1)S(1)}, u32[]{:S(2)}, u32[]{:S(2)}) collective-permute-start(bf16[9,32,320]{2,1,0:T(8,128)(2,1)} %get-tuple-element.22), channel_id=1, source_target_pairs={{0,2},{1,3},{2,0},{3,1},{4,6},{5,7},{6,4},{7,5},{8,10},{9,11},{10,... | collective-permute-start | bytes 552968 | tf_op jit(solution)/shard_map/ppermute | solution.py:238
  60.6 10.7 %collective-permute-start.13 = (bf16[9,32,320]{2,1,0:T(8,128)(2,1)}, bf16[9,32,320]{2,1,0:T(8,128)(2,1)S(1)}, u32[]{:S(2)}, u32[]{:S(2)}) collective-permute-start(bf16[9,32,320]{2,1,0:T(8,128)(2,1)} %get-tuple-element.23), channel_id=1, source_target_pairs={{0,1},{1,2},{2,3},{3,0},{4,5},{5,6},{6,7},{7,4},{8,9},{9,10},{10,1... | collective-permute-start | bytes 552968 | tf_op jit(solution)/shard_map/ppermute | solution.py:238
  62.7 8.6 %copy-start.6 = (bf16[9,32,320]{2,1,0:T(8,128)(2,1)S(1)}, bf16[9,32,320]{2,1,0:T(8,128)(2,1)}, u32[]{:S(2)}) copy-start(bf16[9,32,320]{2,1,0:T(8,128)(2,1)} %get-tuple-element.20) | copy-start | bytes 552964
  72.2 0.8 copy-start.10
  72.2 0.8 copy-start.9
  72.2 1.2 %copy-start.8 = (bf16[36,1,320]{2,1,0:T(2,128)(2,1)S(1)}, bf16[36,1,320]{2,1,0:T(2,128)(2,1)}, u32[]{:S(2)}) copy-start(bf16[36,1,320]{2,1,0:T(2,128)(2,1)} %get-tuple-element.26) | copy-start | bytes 69124
  72.3 1.2 %copy-start.7 = (bf16[36,1,320]{2,1,0:T(2,128)(2,1)S(1)}, bf16[36,1,320]{2,1,0:T(2,128)(2,1)}, u32[]{:S(2)}) copy-start(bf16[36,1,320]{2,1,0:T(2,128)(2,1)} %get-tuple-element.25) | copy-start | bytes 69124
  72.5 7.9 %copy-start.2 = (bf16[4,9,32,320]{3,2,1,0:T(8,128)(2,1)}, bf16[4,9,32,320]{3,2,1,0:T(8,128)(2,1)S(1)}, u32[]{:S(2)}) copy-start(bf16[4,9,32,320]{3,2,1,0:T(8,128)(2,1)S(1)} %get-tuple-element.40) | copy-start | bytes 2211844
  72.5 7.8 %copy-start.3 = (bf16[4,9,32,320]{3,2,1,0:T(8,128)(2,1)}, bf16[4,9,32,320]{3,2,1,0:T(8,128)(2,1)S(1)}, u32[]{:S(2)}) copy-start(bf16[4,9,32,320]{3,2,1,0:T(8,128)(2,1)S(1)} %get-tuple-element.41) | copy-start | bytes 2211844
  73.1 4.6 %collective-permute-start.15 = (bf16[72,320]{1,0:T(8,128)(2,1)S(1)}, bf16[72,320]{1,0:T(8,128)(2,1)S(1)}, u32[]{:S(2)}, u32[]{:S(2)}) collective-permute-start(bf16[72,320]{1,0:T(8,128)(2,1)S(1)} %pad_maximum_fusion.3), channel_id=1, source_target_pairs={{4,0},{8,4},{12,8},{0,12},{5,1},{9,5},{13,9},{1,13},{6,2},{10,6},{... | collective-permute-start | bytes 138248 | tf_op jit(solution)/shard_map/ppermute | solution.py:16
  73.5 6.2 %collective-permute-start.14 = (bf16[72,320]{1,0:T(8,128)(2,1)S(1)}, bf16[72,320]{1,0:T(8,128)(2,1)S(1)}, u32[]{:S(2)}, u32[]{:S(2)}) collective-permute-start(bf16[72,320]{1,0:T(8,128)(2,1)S(1)} %pad_maximum_fusion.2), channel_id=1, source_target_pairs={{12,0},{0,4},{4,8},{8,12},{13,1},{1,5},{5,9},{9,13},{14,2},{2,6},{... | collective-permute-start | bytes 138248 | tf_op jit(solution)/shard_map/ppermute | solution.py:16
  (1 other events, 0.7 us)

commit v18 on v17

--- a/solution.py
+++ b/solution.py
@@ -254,7 +254,7 @@
     returned = []
     rotate = frames_all <= 4 and half % frames_all == 0
     if rotate:
-        whole = convolve([[tile]], rims, conv1_weight, norm_gelu, 0, row_count)
+        whole = convolve([[tile]], rims, conv1_weight, norm_gelu, 0, row_count, 6)
         for lo in (0, half):
             returned.append(rotated_attention(whole, lo, half, qkv_weight, pos_bias, out_weight))
         hidden_rows = [whole]

time: 92.3 us -> 92.6 us (level)
  no operation moved by 1% of the time
where the time goes in v18:
time: 92.6 us; the launch traced here: 92.3 us
  Pallas kernels  36.2 us (39%)
  waiting for transfers between devices  20.7 us (22%)
  starting transfers between devices  18.1 us (20%)
  local copies, waits for them, and re-layouts  11.2 us (12%)
  other arithmetic  3.51 us (4%)
  matrix products  2.29 us (2%)
    pallas_call x2, Pallas kernels, convolve(): pl.pallas_call(functools.partial(conv_kernel, layout=tuple(layout), lo=lo...  24.5 us
    pallas_call x2, Pallas kernels, attend_pieces(): pl.pallas_call(functools.partial(attend_kernel, parts=frames_all), out_sh...  11.6 us
    ppermute x6, waiting for transfers between devices, rotated_attention(): lax.ppermute(piece, 'frame', [(i, (i - s) % frames_all) for i in range(fr...  7.58 us
    ppermute x4, waiting for transfers between devices, shifted(): moved = lax.ppermute(block, axis, route)  7.55 us
    ppermute x4, starting transfers between devices, shifted(): moved = lax.ppermute(block, axis, route)  7.51 us
    ppermute x6, starting transfers between devices, rotated_attention(): lax.ppermute(piece, 'frame', [(i, (i - s) % frames_all) for i in range(fr...  5.56 us
    ppermute x6, waiting for transfers between devices, rotated_attention(): lax.ppermute(piece, 'frame', [(i, (i + s) % frames_all) for i in range(fr...  5.54 us
    ppermute x6, starting transfers between devices, rotated_attention(): lax.ppermute(piece, 'frame', [(i, (i + s) % frames_all) for i in range(fr...  5.01 us
  transfers between devices with their start and end apart: 16, of which 8 were waited for; matrix products, arithmetic and copies ran while one was open for 9% of the time, Pallas kernels for 13%

profile of v18, /device:TPU:0, one launch (start us, length us, event | category | flops | bytes accessed | tf_op | source)
XLA Modules:
  0.0 92.3 jit_solution(6511828239704695268)
XLA Ops:
  0.0 1.9 %fusion.4 = bf16[1,72,320]{2,0,1:T(2,128)(2,1)S(1)} fusion(bf16[1,72,32,320]{3,2,1,0:T(8,128)(2,1)} %param.12), kind=kOutput, calls=%fused_computation.42 | convolution fusion | flops 1474592 | bytes 1520640 | tf_op jit(solution)/shard_map/rwc,w->rc/dot_general | solution.py:250
  2.0 5.1 %collective-permute-start.1 = (bf16[72,320]{1,0:T(8,128)(2,1)S(1)}, bf16[72,320]{1,0:T(8,128)(2,1)S(1)}, u32[]{:S(2)}, u32[]{:S(2)}) collective-permute-start(bf16[72,320]{1,0:T(8,128)(2,1)S(1)} %bitcast.64), channel_id=1, source_target_pairs={{4,0},{8,4},{12,8},{0,12},{5,1},{9,5},{13,9},{1,13},{6,2},{10,6},{... | collective-permute-start | bytes 138248 | tf_op jit(solution)/shard_map/ppermute | solution.py:16
  8.9 0.6 broadcast_select_fusion.3.refs_2_
  9.5 3.9 %collective-permute-done = bf16[72,320]{1,0:T(8,128)(2,1)S(1)} collective-permute-done((bf16[72,320]{1,0:T(8,128)(2,1)S(1)}, bf16[72,320]{1,0:T(8,128)(2,1)S(1)}, u32[]{:S(2)}, u32[]{:S(2)}) %collective-permute-start) | collective-permute-done | bytes 46112 | tf_op jit(solution)/shard_map/ppermute | solution.py:16
  13.5 0.6 broadcast_select_fusion.5.refs_1_
  14.1 12.9 %shard_map.64.refs_0_ = bf16[72,32,320]{2,1,0:T(8,128)(2,1)} custom-call(bf16[72,32,320]{2,1,0:T(8,128)(2,1)} %bitcast.47, bf16[72,320]{1,0:T(8,128)(2,1)} %broadcast_select_fusion.5.refs_1_, bf16[72,320]{1,0:T(8,128)(2,1)} %broadcast_select_fusion.3.refs_2_, bf16[3,960,320]{2,1,0:T(8,128)(2,1)} %bitcast.54), custom_call_target="tpu_custom_call" | custom-call | tf_op jit(solution)/shard_map/pallas_call | solution.py:99
  27.0 2.6 %constant_dynamic-slice_fusion = (bf16[9,32,320]{2,1,0:T(8,128)(2,1)S(1)}, bf16[9,32,320]{2,1,0:T(8,128)(2,1)S(1)}, bf16[9,32,320]{2,1,0:T(8,128)(2,1)S(1)}, bf1...) fusion(bf16[72,32,320]{2,1,0:T(8,128)(2,1)} %shard_map.64.refs_, ...), kind=kLoop, calls=%fused_computation.34 | loop fusion | bytes 2949152 | tf_op jit(solution)/shard_map/dynamic_slice | solution.py:227
  29.6 1.5 %collective-permute-start.3 = (bf16[9,32,320]{2,1,0:T(8,128)(2,1)S(1)}, bf16[9,32,320]{2,1,0:T(8,128)(2,1)S(1)}, u32[]{:S(2)}, u32[]{:S(2)}) collective-permute-start(bf16[9,32,320]{2,1,0:T(8,128)(2,1)S(1)} %get-tuple-element.33), channel_id=1, source_target_pairs={{0,2},{1,3},{2,0},{3,1},{4,6},{5,7},{6,4},{7,5},{8,10},{9,11},{10,... | collective-permute-start | bytes 552968 | tf_op jit(solution)/shard_map/ppermute | solution.py:229
  31.2 1.4 %collective-permute-start.4 = (bf16[9,32,320]{2,1,0:T(8,128)(2,1)S(1)}, bf16[9,32,320]{2,1,0:T(8,128)(2,1)S(1)}, u32[]{:S(2)}, u32[]{:S(2)}) collective-permute-start(bf16[9,32,320]{2,1,0:T(8,128)(2,1)S(1)} %get-tuple-element.32), channel_id=1, source_target_pairs={{0,3},{1,0},{2,1},{3,2},{4,7},{5,4},{6,5},{7,6},{8,11},{9,8},{10,9... | collective-permute-start | bytes 552968 | tf_op jit(solution)/shard_map/ppermute | solution.py:229
  32.7 0.8 copy.32.refs_5_
  33.5 1.2 %copy.30 = bf16[320,960]{0,1:T(8,128)(2,1)} copy(bf16[320,960]{1,0:T(8,128)(2,1)S(1)} %copy-done.4) | data formatting | bytes 1228800 | tf_op args[2]
  35.2 1.6 %collective-permute-done.2.refs_1_ = bf16[9,32,320]{2,1,0:T(8,128)(2,1)S(1)} collective-permute-done((bf16[9,32,320]{2,1,0:T(8,128)(2,1)S(1)}, bf16[9,32,320]{2,1,0:T(8,128)(2,1)S(1)}, u32[]{:S(2)}, u32[]{:S(2)}) %collective-permute-start.2) | collective-permute-done | bytes 184352 | tf_op jit(solution)/shard_map/ppermute | solution.py:229
  36.8 1.5 %collective-permute-start.9 = (bf16[9,32,320]{2,1,0:T(8,128)(2,1)S(1)}, bf16[9,32,320]{2,1,0:T(8,128)(2,1)S(1)}, u32[]{:S(2)}, u32[]{:S(2)}) collective-permute-start(bf16[9,32,320]{2,1,0:T(8,128)(2,1)S(1)} %get-tuple-element.29), channel_id=1, source_target_pairs={{0,2},{1,3},{2,0},{3,1},{4,6},{5,7},{6,4},{7,5},{8,10},{9,11},{10,... | collective-permute-start | bytes 552968 | tf_op jit(solution)/shard_map/ppermute | solution.py:229
  38.3 3.4 %collective-permute-done.4.refs_3_ = bf16[9,32,320]{2,1,0:T(8,128)(2,1)S(1)} collective-permute-done((bf16[9,32,320]{2,1,0:T(8,128)(2,1)S(1)}, bf16[9,32,320]{2,1,0:T(8,128)(2,1)S(1)}, u32[]{:S(2)}, u32[]{:S(2)}) %collective-permute-start.4) | collective-permute-done | bytes 184352 | tf_op jit(solution)/shard_map/ppermute | solution.py:229
  41.7 0.7 copy-done.16
  42.4 5.8 %shard_map.65 = (bf16[9,32,320]{2,1,0:T(8,128)(2,1)}, bf16[9,32,320]{2,1,0:T(8,128)(2,1)}, bf16[9,32,320]{2,1,0:T(8,128)(2,1)}, bf16[9,32,320]{2,1,0:T(8,128)(2,1)}) custom-call(bf16[9,32,320]{2,1,0:T(8,128)(2,1)} %get-tuple-element.35.refs_0_, bf16[9,32,320]{2,1,0:T(8,128)(2,1)} %copy-done.14, bf16[9,32,320]{2,1,0:T(8,128)(2,1)} %copy-done.15, ...), custom_call_target="tpu_custom_call" | custom-call | tf_op jit(solution)/shard_map/pallas_call | solution.py:193
  48.2 2.2 %collective-permute-start.5 = (bf16[9,32,320]{2,1,0:T(8,128)(2,1)}, bf16[9,32,320]{2,1,0:T(8,128)(2,1)S(1)}, u32[]{:S(2)}, u32[]{:S(2)}) collective-permute-start(bf16[9,32,320]{2,1,0:T(8,128)(2,1)} %get-tuple-element.17), channel_id=1, source_target_pairs={{0,3},{1,0},{2,1},{3,2},{4,7},{5,4},{6,5},{7,6},{8,11},{9,8},{10,9... | collective-permute-start | bytes 552968 | tf_op jit(solution)/shard_map/ppermute | solution.py:238
  50.4 0.6 collective-permute-start.6
  52.3 5.8 %shard_map.66 = (bf16[9,32,320]{2,1,0:T(8,128)(2,1)}, bf16[9,32,320]{2,1,0:T(8,128)(2,1)}, bf16[9,32,320]{2,1,0:T(8,128)(2,1)}, bf16[9,32,320]{2,1,0:T(8,128)(2,1)}) custom-call(bf16[9,32,320]{2,1,0:T(8,128)(2,1)} %get-tuple-element.31.refs_0_, bf16[9,32,320]{2,1,0:T(8,128)(2,1)} %copy-done.12, bf16[9,32,320]{2,1,0:T(8,128)(2,1)} %copy-done.13, ...), custom_call_target="tpu_custom_call" | custom-call | tf_op jit(solution)/shard_map/pallas_call | solution.py:193
  58.1 1.3 %collective-permute-start.11 = (bf16[9,32,320]{2,1,0:T(8,128)(2,1)}, bf16[9,32,320]{2,1,0:T(8,128)(2,1)S(1)}, u32[]{:S(2)}, u32[]{:S(2)}) collective-permute-start(bf16[9,32,320]{2,1,0:T(8,128)(2,1)} %get-tuple-element.21), channel_id=1, source_target_pairs={{0,3},{1,0},{2,1},{3,2},{4,7},{5,4},{6,5},{7,6},{8,11},{9,8},{10,9... | collective-permute-start | bytes 552968 | tf_op jit(solution)/shard_map/ppermute | solution.py:238
  59.4 1.5 %collective-permute-start.12 = (bf16[9,32,320]{2,1,0:T(8,128)(2,1)}, bf16[9,32,320]{2,1,0:T(8,128)(2,1)S(1)}, u32[]{:S(2)}, u32[]{:S(2)}) collective-permute-start(bf16[9,32,320]{2,1,0:T(8,128)(2,1)} %get-tuple-element.22), channel_id=1, source_target_pairs={{0,2},{1,3},{2,0},{3,1},{4,6},{5,7},{6,4},{7,5},{8,10},{9,11},{10,... | collective-permute-start | bytes 552968 | tf_op jit(solution)/shard_map/ppermute | solution.py:238
  60.9 2.1 %fusion.19 = (bf16[36,1,320]{2,1,0:T(2,128)(2,1)}, bf16[36,1,320]{2,1,0:T(2,128)(2,1)}, bf16[36,1,320]{2,1,0:T(2,128)(2,1)}, bf16[36,1,320]{2,1,0:T(2,128)(2,1)}) fusion(bf16[72,32,320]{2,1,0:T(8,128)(2,1)} %shard_map.64.refs_0_), kind=kLoop, calls=%fused_computation.61 | loop fusion | bytes 184320 | tf_op jit(solution)/shard_map/slice | solution.py:279
  63.2 0.7 gather_fusion.2
  64.0 1.8 %collective-permute-done.11 = bf16[9,32,320]{2,1,0:T(8,128)(2,1)S(1)} collective-permute-done((bf16[9,32,320]{2,1,0:T(8,128)(2,1)}, bf16[9,32,320]{2,1,0:T(8,128)(2,1)S(1)}, u32[]{:S(2)}, u32[]{:S(2)}) %collective-permute-start.11) | collective-permute-done | bytes 184352 | tf_op jit(solution)/shard_map/ppermute | solution.py:238
  65.7 5.8 %collective-permute-done.12 = bf16[9,32,320]{2,1,0:T(8,128)(2,1)S(1)} collective-permute-done((bf16[9,32,320]{2,1,0:T(8,128)(2,1)}, bf16[9,32,320]{2,1,0:T(8,128)(2,1)S(1)}, u32[]{:S(2)}, u32[]{:S(2)}) %collective-permute-start.12) | collective-permute-done | bytes 184352 | tf_op jit(solution)/shard_map/ppermute | solution.py:238
  71.8 0.7 gather_fusion.3
  73.8 2.0 %collective-permute-start.14 = (bf16[72,320]{1,0:T(8,128)(2,1)S(1)}, bf16[72,320]{1,0:T(8,128)(2,1)S(1)}, u32[]{:S(2)}, u32[]{:S(2)}) collective-permute-start(bf16[72,320]{1,0:T(8,128)(2,1)S(1)} %pad_maximum_fusion.2), channel_id=1, source_target_pairs={{12,0},{0,4},{4,8},{8,12},{13,1},{1,5},{5,9},{9,13},{14,2},{2,6},{... | collective-permute-start | bytes 138248 | tf_op jit(solution)/shard_map/ppermute | solution.py:16
  75.8 2.2 %collective-permute-done.15 = bf16[72,320]{1,0:T(8,128)(2,1)S(1)} collective-permute-done((bf16[72,320]{1,0:T(8,128)(2,1)S(1)}, bf16[72,320]{1,0:T(8,128)(2,1)S(1)}, u32[]{:S(2)}, u32[]{:S(2)}) %collective-permute-start.15) | collective-permute-done | bytes 46112 | tf_op jit(solution)/shard_map/ppermute | solution.py:16
  78.1 0.6 broadcast_select_fusion.2.refs_4_
  78.7 1.4 %collective-permute-done.14 = bf16[72,320]{1,0:T(8,128)(2,1)S(1)} collective-permute-done((bf16[72,320]{1,0:T(8,128)(2,1)S(1)}, bf16[72,320]{1,0:T(8,128)(2,1)S(1)}, u32[]{:S(2)}, u32[]{:S(2)}) %collective-permute-start.14) | collective-permute-done | bytes 46112 | tf_op jit(solution)/shard_map/ppermute | solution.py:16
  80.0 0.6 broadcast_select_fusion.4.refs_3_
  80.7 11.6 %shard_map.67 = bf16[72,32,320]{2,1,0:T(8,128)(2,1)} custom-call(bf16[72,32,320]{2,1,0:T(8,128)(2,1)} %shard_map.64.refs_0_, bf16[36,32,320]{2,1,0:T(8,128)(2,1)} %bitcast.53, bf16[36,32,320]{2,1,0:T(8,128)(2,1)} %bitcast.51, bf16[72,320]{1,0:T(8,128)(2,1)} %broadcast_select_fusion.4.refs_3_, bf16[72,320]{1,0:T(8,128)(2,1)} %broadcast_select_fusion.2.refs_4_, ...), custom_call_target="tpu_custom_call" | custom-call | tf_op jit(solution)/shard_map/pallas_call | solution.py:99
  (73 shorter events, 5.2 us)
Async XLA Ops:
  0.0 7.6 %copy-start = (f32[5,4,4]{0,2,1:T(4,128)S(1)}, f32[5,4,4]{0,2,1:T(4,128)}, u32[]{:S(2)}) copy-start(f32[5,4,4]{0,2,1:T(4,128)} %param.16) | copy-start | bytes 964
  0.0 7.1 %copy-start.1 = (bf16[1,72,32,320]{3,2,1,0:T(8,128)(2,1)S(1)}, bf16[1,72,32,320]{3,2,1,0:T(8,128)(2,1)}, u32[]{:S(2)}) copy-start(bf16[1,72,32,320]{3,2,1,0:T(8,128)(2,1)} %param.12) | copy-start | bytes 4423684
  2.0 6.9 %collective-permute-start.1 = (bf16[72,320]{1,0:T(8,128)(2,1)S(1)}, bf16[72,320]{1,0:T(8,128)(2,1)S(1)}, u32[]{:S(2)}, u32[]{:S(2)}) collective-permute-start(bf16[72,320]{1,0:T(8,128)(2,1)S(1)} %bitcast.64), channel_id=1, source_target_pairs={{4,0},{8,4},{12,8},{0,12},{5,1},{9,5},{13,9},{1,13},{6,2},{10,6},{... | collective-permute-start | bytes 138248 | tf_op jit(solution)/shard_map/ppermute | solution.py:16
  7.4 6.0 %collective-permute-start = (bf16[72,320]{1,0:T(8,128)(2,1)S(1)}, bf16[72,320]{1,0:T(8,128)(2,1)S(1)}, u32[]{:S(2)}, u32[]{:S(2)}) collective-permute-start(bf16[72,320]{1,0:T(8,128)(2,1)S(1)} %bitcast.65), channel_id=1, source_target_pairs={{12,0},{0,4},{4,8},{8,12},{13,1},{1,5},{5,9},{9,13},{14,2},{2,6},{... | collective-permute-start | bytes 138248 | tf_op jit(solution)/shard_map/ppermute | solution.py:16
  27.0 6.5 %copy-start.4 = (bf16[320,960]{1,0:T(8,128)(2,1)S(1)}, bf16[320,960]{1,0:T(8,128)(2,1)}, u32[]{:S(2)}) copy-start(bf16[320,960]{1,0:T(8,128)(2,1)} %param.14) | copy-start | bytes 1843204
  29.6 7.2 %collective-permute-start.2 = (bf16[9,32,320]{2,1,0:T(8,128)(2,1)S(1)}, bf16[9,32,320]{2,1,0:T(8,128)(2,1)S(1)}, u32[]{:S(2)}, u32[]{:S(2)}) collective-permute-start(bf16[9,32,320]{2,1,0:T(8,128)(2,1)S(1)} %get-tuple-element.34), channel_id=1, source_target_pairs={{0,1},{1,2},{2,3},{3,0},{4,5},{5,6},{6,7},{7,4},{8,9},{9,10},{10,1... | collective-permute-start | bytes 552968 | tf_op jit(solution)/shard_map/ppermute | solution.py:229
  29.6 8.7 %collective-permute-start.3 = (bf16[9,32,320]{2,1,0:T(8,128)(2,1)S(1)}, bf16[9,32,320]{2,1,0:T(8,128)(2,1)S(1)}, u32[]{:S(2)}, u32[]{:S(2)}) collective-permute-start(bf16[9,32,320]{2,1,0:T(8,128)(2,1)S(1)} %get-tuple-element.33), channel_id=1, source_target_pairs={{0,2},{1,3},{2,0},{3,1},{4,6},{5,7},{6,4},{7,5},{8,10},{9,11},{10,... | collective-permute-start | bytes 552968 | tf_op jit(solution)/shard_map/ppermute | solution.py:229
  31.2 10.5 %collective-permute-start.4 = (bf16[9,32,320]{2,1,0:T(8,128)(2,1)S(1)}, bf16[9,32,320]{2,1,0:T(8,128)(2,1)S(1)}, u32[]{:S(2)}, u32[]{:S(2)}) collective-permute-start(bf16[9,32,320]{2,1,0:T(8,128)(2,1)S(1)} %get-tuple-element.32), channel_id=1, source_target_pairs={{0,3},{1,0},{2,1},{3,2},{4,7},{5,4},{6,5},{7,6},{8,11},{9,8},{10,9... | collective-permute-start | bytes 552968 | tf_op jit(solution)/shard_map/ppermute | solution.py:229
  34.7 16.3 %collective-permute-start.10 = (bf16[9,32,320]{2,1,0:T(8,128)(2,1)S(1)}, bf16[9,32,320]{2,1,0:T(8,128)(2,1)S(1)}, u32[]{:S(2)}, u32[]{:S(2)}) collective-permute-start(bf16[9,32,320]{2,1,0:T(8,128)(2,1)S(1)} %get-tuple-element.28), channel_id=1, source_target_pairs={{0,3},{1,0},{2,1},{3,2},{4,7},{5,4},{6,5},{7,6},{8,11},{9,8},{10,9... | collective-permute-start | bytes 552968 | tf_op jit(solution)/shard_map/ppermute | solution.py:229
  34.7 16.3 %collective-permute-start.8 = (bf16[9,32,320]{2,1,0:T(8,128)(2,1)S(1)}, bf16[9,32,320]{2,1,0:T(8,128)(2,1)S(1)}, u32[]{:S(2)}, u32[]{:S(2)}) collective-permute-start(bf16[9,32,320]{2,1,0:T(8,128)(2,1)S(1)} %get-tuple-element.30), channel_id=1, source_target_pairs={{0,1},{1,2},{2,3},{3,0},{4,5},{5,6},{6,7},{7,4},{8,9},{9,10},{10,1... | collective-permute-start | bytes 552968 | tf_op jit(solution)/shard_map/ppermute | solution.py:229
  36.8 4.9 %copy-start.14 = (bf16[9,32,320]{2,1,0:T(8,128)(2,1)}, bf16[9,32,320]{2,1,0:T(8,128)(2,1)S(1)}, u32[]{:S(2)}) copy-start(bf16[9,32,320]{2,1,0:T(8,128)(2,1)S(1)} %collective-permute-done.2.refs_1_) | copy-start | bytes 552964
  36.8 14.8 %collective-permute-start.9 = (bf16[9,32,320]{2,1,0:T(8,128)(2,1)S(1)}, bf16[9,32,320]{2,1,0:T(8,128)(2,1)S(1)}, u32[]{:S(2)}, u32[]{:S(2)}) collective-permute-start(bf16[9,32,320]{2,1,0:T(8,128)(2,1)S(1)} %get-tuple-element.29), channel_id=1, source_target_pairs={{0,2},{1,3},{2,0},{3,1},{4,6},{5,7},{6,4},{7,5},{8,10},{9,11},{10,... | collective-permute-start | bytes 552968 | tf_op jit(solution)/shard_map/ppermute | solution.py:229
  38.3 3.4 %copy-start.15 = (bf16[9,32,320]{2,1,0:T(8,128)(2,1)}, bf16[9,32,320]{2,1,0:T(8,128)(2,1)S(1)}, u32[]{:S(2)}) copy-start(bf16[9,32,320]{2,1,0:T(8,128)(2,1)S(1)} %collective-permute-done.3.refs_2_) | copy-start | bytes 552964
  48.2 14.8 %copy-start.5 = (bf16[9,32,320]{2,1,0:T(8,128)(2,1)S(1)}, bf16[9,32,320]{2,1,0:T(8,128)(2,1)}, u32[]{:S(2)}) copy-start(bf16[9,32,320]{2,1,0:T(8,128)(2,1)} %get-tuple-element.16) | copy-start | bytes 552964
  48.2 12.7 %collective-permute-start.5 = (bf16[9,32,320]{2,1,0:T(8,128)(2,1)}, bf16[9,32,320]{2,1,0:T(8,128)(2,1)S(1)}, u32[]{:S(2)}, u32[]{:S(2)}) collective-permute-start(bf16[9,32,320]{2,1,0:T(8,128)(2,1)} %get-tuple-element.17), channel_id=1, source_target_pairs={{0,3},{1,0},{2,1},{3,2},{4,7},{5,4},{6,5},{7,6},{8,11},{9,8},{10,9... | collective-permute-start | bytes 552968 | tf_op jit(solution)/shard_map/ppermute | solution.py:238
  50.4 12.6 %collective-permute-start.6 = (bf16[9,32,320]{2,1,0:T(8,128)(2,1)}, bf16[9,32,320]{2,1,0:T(8,128)(2,1)S(1)}, u32[]{:S(2)}, u32[]{:S(2)}) collective-permute-start(bf16[9,32,320]{2,1,0:T(8,128)(2,1)} %get-tuple-element.18), channel_id=1, source_target_pairs={{0,2},{1,3},{2,0},{3,1},{4,6},{5,7},{6,4},{7,5},{8,10},{9,11},{10,... | collective-permute-start | bytes 552968 | tf_op jit(solution)/shard_map/ppermute | solution.py:238
  51.0 0.7 copy-start.11
  51.0 12.0 %collective-permute-start.7 = (bf16[9,32,320]{2,1,0:T(8,128)(2,1)}, bf16[9,32,320]{2,1,0:T(8,128)(2,1)S(1)}, u32[]{:S(2)}, u32[]{:S(2)}) collective-permute-start(bf16[9,32,320]{2,1,0:T(8,128)(2,1)} %get-tuple-element.19), channel_id=1, source_target_pairs={{0,1},{1,2},{2,3},{3,0},{4,5},{5,6},{6,7},{7,4},{8,9},{9,10},{10,1... | collective-permute-start | bytes 552968 | tf_op jit(solution)/shard_map/ppermute | solution.py:238
  51.0 0.7 copy-start.12
  51.6 0.7 copy-start.13
  58.1 7.7 %collective-permute-start.11 = (bf16[9,32,320]{2,1,0:T(8,128)(2,1)}, bf16[9,32,320]{2,1,0:T(8,128)(2,1)S(1)}, u32[]{:S(2)}, u32[]{:S(2)}) collective-permute-start(bf16[9,32,320]{2,1,0:T(8,128)(2,1)} %get-tuple-element.21), channel_id=1, source_target_pairs={{0,3},{1,0},{2,1},{3,2},{4,7},{5,4},{6,5},{7,6},{8,11},{9,8},{10,9... | collective-permute-start | bytes 552968 | tf_op jit(solution)/shard_map/ppermute | solution.py:238
  59.4 12.2 %collective-permute-start.12 = (bf16[9,32,320]{2,1,0:T(8,128)(2,1)}, bf16[9,32,320]{2,1,0:T(8,128)(2,1)S(1)}, u32[]{:S(2)}, u32[]{:S(2)}) collective-permute-start(bf16[9,32,320]{2,1,0:T(8,128)(2,1)} %get-tuple-element.22), channel_id=1, source_target_pairs={{0,2},{1,3},{2,0},{3,1},{4,6},{5,7},{6,4},{7,5},{8,10},{9,11},{10,... | collective-permute-start | bytes 552968 | tf_op jit(solution)/shard_map/ppermute | solution.py:238
  60.9 10.7 %collective-permute-start.13 = (bf16[9,32,320]{2,1,0:T(8,128)(2,1)}, bf16[9,32,320]{2,1,0:T(8,128)(2,1)S(1)}, u32[]{:S(2)}, u32[]{:S(2)}) collective-permute-start(bf16[9,32,320]{2,1,0:T(8,128)(2,1)} %get-tuple-element.23), channel_id=1, source_target_pairs={{0,1},{1,2},{2,3},{3,0},{4,5},{5,6},{6,7},{7,4},{8,9},{9,10},{10,1... | collective-permute-start | bytes 552968 | tf_op jit(solution)/shard_map/ppermute | solution.py:238
  63.0 8.6 %copy-start.6 = (bf16[9,32,320]{2,1,0:T(8,128)(2,1)S(1)}, bf16[9,32,320]{2,1,0:T(8,128)(2,1)}, u32[]{:S(2)}) copy-start(bf16[9,32,320]{2,1,0:T(8,128)(2,1)} %get-tuple-element.20) | copy-start | bytes 552964
  72.5 0.8 copy-start.10
  72.5 0.8 copy-start.9
  72.6 1.2 %copy-start.8 = (bf16[36,1,320]{2,1,0:T(2,128)(2,1)S(1)}, bf16[36,1,320]{2,1,0:T(2,128)(2,1)}, u32[]{:S(2)}) copy-start(bf16[36,1,320]{2,1,0:T(2,128)(2,1)} %get-tuple-element.26) | copy-start | bytes 69124
  72.6 1.2 %copy-start.7 = (bf16[36,1,320]{2,1,0:T(2,128)(2,1)S(1)}, bf16[36,1,320]{2,1,0:T(2,128)(2,1)}, u32[]{:S(2)}) copy-start(bf16[36,1,320]{2,1,0:T(2,128)(2,1)} %get-tuple-element.25) | copy-start | bytes 69124
  72.8 7.9 %copy-start.2 = (bf16[4,9,32,320]{3,2,1,0:T(8,128)(2,1)}, bf16[4,9,32,320]{3,2,1,0:T(8,128)(2,1)S(1)}, u32[]{:S(2)}) copy-start(bf16[4,9,32,320]{3,2,1,0:T(8,128)(2,1)S(1)} %get-tuple-element.40) | copy-start | bytes 2211844
  72.9 7.8 %copy-start.3 = (bf16[4,9,32,320]{3,2,1,0:T(8,128)(2,1)}, bf16[4,9,32,320]{3,2,1,0:T(8,128)(2,1)S(1)}, u32[]{:S(2)}) copy-start(bf16[4,9,32,320]{3,2,1,0:T(8,128)(2,1)S(1)} %get-tuple-element.41) | copy-start | bytes 2211844
  73.4 4.6 %collective-permute-start.15 = (bf16[72,320]{1,0:T(8,128)(2,1)S(1)}, bf16[72,320]{1,0:T(8,128)(2,1)S(1)}, u32[]{:S(2)}, u32[]{:S(2)}) collective-permute-start(bf16[72,320]{1,0:T(8,128)(2,1)S(1)} %pad_maximum_fusion.3), channel_id=1, source_target_pairs={{4,0},{8,4},{12,8},{0,12},{5,1},{9,5},{13,9},{1,13},{6,2},{10,6},{... | collective-permute-start | bytes 138248 | tf_op jit(solution)/shard_map/ppermute | solution.py:16
  73.8 6.2 %collective-permute-start.14 = (bf16[72,320]{1,0:T(8,128)(2,1)S(1)}, bf16[72,320]{1,0:T(8,128)(2,1)S(1)}, u32[]{:S(2)}, u32[]{:S(2)}) collective-permute-start(bf16[72,320]{1,0:T(8,128)(2,1)S(1)} %pad_maximum_fusion.2), channel_id=1, source_target_pairs={{12,0},{0,4},{4,8},{8,12},{13,1},{1,5},{5,9},{9,13},{14,2},{2,6},{... | collective-permute-start | bytes 138248 | tf_op jit(solution)/shard_map/ppermute | solution.py:16
  (1 other events, 0.7 us)

commit v19 on v17

--- a/solution.py
+++ b/solution.py
@@ -279,7 +279,7 @@
         summed = [h[:, c, :].astype(jnp.float32) + r[:, c, :].astype(jnp.float32) for h, r in zip(hidden, returned)]
         return jnp.concatenate(summed, axis=0).astype(jnp.bfloat16)
 
-    second = convolve([hidden_rows, returned], halo(joined_edge), conv2_weight, to_bf16, 0, row_count, 6)
+    second = convolve([hidden_rows, returned], halo(joined_edge), conv2_weight, to_bf16, 0, row_count, 4)
     return second.reshape(frames_dev, row_count, col_count, channels)
 
 

time: 92.3 us -> 92.3 us (level)
  no operation moved by 1% of the time
where the time goes in v19:
time: 92.3 us; the launch traced here: 92 us
  Pallas kernels  35.9 us (39%)
  waiting for transfers between devices  20.7 us (22%)
  starting transfers between devices  18.1 us (20%)
  local copies, waits for them, and re-layouts  11.2 us (12%)
  other arithmetic  3.51 us (4%)
  matrix products  2.29 us (2%)
    pallas_call x2, Pallas kernels, convolve(): pl.pallas_call(functools.partial(conv_kernel, layout=tuple(layout), lo=lo...  24.2 us
    pallas_call x2, Pallas kernels, attend_pieces(): pl.pallas_call(functools.partial(attend_kernel, parts=frames_all), out_sh...  11.6 us
    ppermute x6, waiting for transfers between devices, rotated_attention(): lax.ppermute(piece, 'frame', [(i, (i - s) % frames_all) for i in range(fr...  7.58 us
    ppermute x4, waiting for transfers between devices, shifted(): moved = lax.ppermute(block, axis, route)  7.55 us
    ppermute x4, starting transfers between devices, shifted(): moved = lax.ppermute(block, axis, route)  7.51 us
    ppermute x6, starting transfers between devices, rotated_attention(): lax.ppermute(piece, 'frame', [(i, (i - s) % frames_all) for i in range(fr...  5.56 us
    ppermute x6, waiting for transfers between devices, rotated_attention(): lax.ppermute(piece, 'frame', [(i, (i + s) % frames_all) for i in range(fr...  5.54 us
    ppermute x6, starting transfers between devices, rotated_attention(): lax.ppermute(piece, 'frame', [(i, (i + s) % frames_all) for i in range(fr...  5.01 us
  transfers between devices with their start and end apart: 16, of which 8 were waited for; matrix products, arithmetic and copies ran while one was open for 9% of the time, Pallas kernels for 13%

profile of v19, /device:TPU:0, one launch (start us, length us, event | category | flops | bytes accessed | tf_op | source)
XLA Modules:
  0.0 92.0 jit_solution(4003951777796815937)
XLA Ops:
  0.0 1.9 %fusion.4 = bf16[1,72,320]{2,0,1:T(2,128)(2,1)S(1)} fusion(bf16[1,72,32,320]{3,2,1,0:T(8,128)(2,1)} %param.12), kind=kOutput, calls=%fused_computation.42 | convolution fusion | flops 1474592 | bytes 1520640 | tf_op jit(solution)/shard_map/rwc,w->rc/dot_general | solution.py:250
  2.0 5.1 %collective-permute-start.1 = (bf16[72,320]{1,0:T(8,128)(2,1)S(1)}, bf16[72,320]{1,0:T(8,128)(2,1)S(1)}, u32[]{:S(2)}, u32[]{:S(2)}) collective-permute-start(bf16[72,320]{1,0:T(8,128)(2,1)S(1)} %bitcast.64), channel_id=1, source_target_pairs={{4,0},{8,4},{12,8},{0,12},{5,1},{9,5},{13,9},{1,13},{6,2},{10,6},{... | collective-permute-start | bytes 138248 | tf_op jit(solution)/shard_map/ppermute | solution.py:16
  8.9 0.6 broadcast_select_fusion.3.refs_2_
  9.5 3.9 %collective-permute-done = bf16[72,320]{1,0:T(8,128)(2,1)S(1)} collective-permute-done((bf16[72,320]{1,0:T(8,128)(2,1)S(1)}, bf16[72,320]{1,0:T(8,128)(2,1)S(1)}, u32[]{:S(2)}, u32[]{:S(2)}) %collective-permute-start) | collective-permute-done | bytes 46112 | tf_op jit(solution)/shard_map/ppermute | solution.py:16
  13.5 0.6 broadcast_select_fusion.5.refs_1_
  14.1 12.6 %shard_map.64.refs_0_ = bf16[72,32,320]{2,1,0:T(8,128)(2,1)} custom-call(bf16[72,32,320]{2,1,0:T(8,128)(2,1)} %bitcast.47, bf16[72,320]{1,0:T(8,128)(2,1)} %broadcast_select_fusion.5.refs_1_, bf16[72,320]{1,0:T(8,128)(2,1)} %broadcast_select_fusion.3.refs_2_, bf16[3,960,320]{2,1,0:T(8,128)(2,1)} %bitcast.54), custom_call_target="tpu_custom_call" | custom-call | tf_op jit(solution)/shard_map/pallas_call | solution.py:99
  26.7 2.6 %constant_dynamic-slice_fusion = (bf16[9,32,320]{2,1,0:T(8,128)(2,1)S(1)}, bf16[9,32,320]{2,1,0:T(8,128)(2,1)S(1)}, bf16[9,32,320]{2,1,0:T(8,128)(2,1)S(1)}, bf1...) fusion(bf16[72,32,320]{2,1,0:T(8,128)(2,1)} %shard_map.64.refs_, ...), kind=kLoop, calls=%fused_computation.34 | loop fusion | bytes 2949152 | tf_op jit(solution)/shard_map/dynamic_slice | solution.py:227
  29.3 1.5 %collective-permute-start.3 = (bf16[9,32,320]{2,1,0:T(8,128)(2,1)S(1)}, bf16[9,32,320]{2,1,0:T(8,128)(2,1)S(1)}, u32[]{:S(2)}, u32[]{:S(2)}) collective-permute-start(bf16[9,32,320]{2,1,0:T(8,128)(2,1)S(1)} %get-tuple-element.33), channel_id=1, source_target_pairs={{0,2},{1,3},{2,0},{3,1},{4,6},{5,7},{6,4},{7,5},{8,10},{9,11},{10,... | collective-permute-start | bytes 552968 | tf_op jit(solution)/shard_map/ppermute | solution.py:229
  30.9 1.4 %collective-permute-start.4 = (bf16[9,32,320]{2,1,0:T(8,128)(2,1)S(1)}, bf16[9,32,320]{2,1,0:T(8,128)(2,1)S(1)}, u32[]{:S(2)}, u32[]{:S(2)}) collective-permute-start(bf16[9,32,320]{2,1,0:T(8,128)(2,1)S(1)} %get-tuple-element.32), channel_id=1, source_target_pairs={{0,3},{1,0},{2,1},{3,2},{4,7},{5,4},{6,5},{7,6},{8,11},{9,8},{10,9... | collective-permute-start | bytes 552968 | tf_op jit(solution)/shard_map/ppermute | solution.py:229
  32.4 0.8 copy.32.refs_5_
  33.2 1.2 %copy.30 = bf16[320,960]{0,1:T(8,128)(2,1)} copy(bf16[320,960]{1,0:T(8,128)(2,1)S(1)} %copy-done.4) | data formatting | bytes 1228800 | tf_op args[2]
  34.9 1.6 %collective-permute-done.2.refs_1_ = bf16[9,32,320]{2,1,0:T(8,128)(2,1)S(1)} collective-permute-done((bf16[9,32,320]{2,1,0:T(8,128)(2,1)S(1)}, bf16[9,32,320]{2,1,0:T(8,128)(2,1)S(1)}, u32[]{:S(2)}, u32[]{:S(2)}) %collective-permute-start.2) | collective-permute-done | bytes 184352 | tf_op jit(solution)/shard_map/ppermute | solution.py:229
  36.5 1.5 %collective-permute-start.9 = (bf16[9,32,320]{2,1,0:T(8,128)(2,1)S(1)}, bf16[9,32,320]{2,1,0:T(8,128)(2,1)S(1)}, u32[]{:S(2)}, u32[]{:S(2)}) collective-permute-start(bf16[9,32,320]{2,1,0:T(8,128)(2,1)S(1)} %get-tuple-element.29), channel_id=1, source_target_pairs={{0,2},{1,3},{2,0},{3,1},{4,6},{5,7},{6,4},{7,5},{8,10},{9,11},{10,... | collective-permute-start | bytes 552968 | tf_op jit(solution)/shard_map/ppermute | solution.py:229
  38.0 3.4 %collective-permute-done.4.refs_3_ = bf16[9,32,320]{2,1,0:T(8,128)(2,1)S(1)} collective-permute-done((bf16[9,32,320]{2,1,0:T(8,128)(2,1)S(1)}, bf16[9,32,320]{2,1,0:T(8,128)(2,1)S(1)}, u32[]{:S(2)}, u32[]{:S(2)}) %collective-permute-start.4) | collective-permute-done | bytes 184352 | tf_op jit(solution)/shard_map/ppermute | solution.py:229
  41.4 0.7 copy-done.16
  42.1 5.8 %shard_map.65 = (bf16[9,32,320]{2,1,0:T(8,128)(2,1)}, bf16[9,32,320]{2,1,0:T(8,128)(2,1)}, bf16[9,32,320]{2,1,0:T(8,128)(2,1)}, bf16[9,32,320]{2,1,0:T(8,128)(2,1)}) custom-call(bf16[9,32,320]{2,1,0:T(8,128)(2,1)} %get-tuple-element.35.refs_0_, bf16[9,32,320]{2,1,0:T(8,128)(2,1)} %copy-done.14, bf16[9,32,320]{2,1,0:T(8,128)(2,1)} %copy-done.15, ...), custom_call_target="tpu_custom_call" | custom-call | tf_op jit(solution)/shard_map/pallas_call | solution.py:193
  47.9 2.2 %collective-permute-start.5 = (bf16[9,32,320]{2,1,0:T(8,128)(2,1)}, bf16[9,32,320]{2,1,0:T(8,128)(2,1)S(1)}, u32[]{:S(2)}, u32[]{:S(2)}) collective-permute-start(bf16[9,32,320]{2,1,0:T(8,128)(2,1)} %get-tuple-element.17), channel_id=1, source_target_pairs={{0,3},{1,0},{2,1},{3,2},{4,7},{5,4},{6,5},{7,6},{8,11},{9,8},{10,9... | collective-permute-start | bytes 552968 | tf_op jit(solution)/shard_map/ppermute | solution.py:238
  50.1 0.6 collective-permute-start.6
  52.0 5.8 %shard_map.66 = (bf16[9,32,320]{2,1,0:T(8,128)(2,1)}, bf16[9,32,320]{2,1,0:T(8,128)(2,1)}, bf16[9,32,320]{2,1,0:T(8,128)(2,1)}, bf16[9,32,320]{2,1,0:T(8,128)(2,1)}) custom-call(bf16[9,32,320]{2,1,0:T(8,128)(2,1)} %get-tuple-element.31.refs_0_, bf16[9,32,320]{2,1,0:T(8,128)(2,1)} %copy-done.12, bf16[9,32,320]{2,1,0:T(8,128)(2,1)} %copy-done.13, ...), custom_call_target="tpu_custom_call" | custom-call | tf_op jit(solution)/shard_map/pallas_call | solution.py:193
  57.8 1.3 %collective-permute-start.11 = (bf16[9,32,320]{2,1,0:T(8,128)(2,1)}, bf16[9,32,320]{2,1,0:T(8,128)(2,1)S(1)}, u32[]{:S(2)}, u32[]{:S(2)}) collective-permute-start(bf16[9,32,320]{2,1,0:T(8,128)(2,1)} %get-tuple-element.21), channel_id=1, source_target_pairs={{0,3},{1,0},{2,1},{3,2},{4,7},{5,4},{6,5},{7,6},{8,11},{9,8},{10,9... | collective-permute-start | bytes 552968 | tf_op jit(solution)/shard_map/ppermute | solution.py:238
  59.0 1.5 %collective-permute-start.12 = (bf16[9,32,320]{2,1,0:T(8,128)(2,1)}, bf16[9,32,320]{2,1,0:T(8,128)(2,1)S(1)}, u32[]{:S(2)}, u32[]{:S(2)}) collective-permute-start(bf16[9,32,320]{2,1,0:T(8,128)(2,1)} %get-tuple-element.22), channel_id=1, source_target_pairs={{0,2},{1,3},{2,0},{3,1},{4,6},{5,7},{6,4},{7,5},{8,10},{9,11},{10,... | collective-permute-start | bytes 552968 | tf_op jit(solution)/shard_map/ppermute | solution.py:238
  60.6 2.1 %fusion.19 = (bf16[36,1,320]{2,1,0:T(2,128)(2,1)}, bf16[36,1,320]{2,1,0:T(2,128)(2,1)}, bf16[36,1,320]{2,1,0:T(2,128)(2,1)}, bf16[36,1,320]{2,1,0:T(2,128)(2,1)}) fusion(bf16[72,32,320]{2,1,0:T(8,128)(2,1)} %shard_map.64.refs_0_), kind=kLoop, calls=%fused_computation.61 | loop fusion | bytes 184320 | tf_op jit(solution)/shard_map/slice | solution.py:279
  62.9 0.7 gather_fusion.2
  63.7 1.8 %collective-permute-done.11 = bf16[9,32,320]{2,1,0:T(8,128)(2,1)S(1)} collective-permute-done((bf16[9,32,320]{2,1,0:T(8,128)(2,1)}, bf16[9,32,320]{2,1,0:T(8,128)(2,1)S(1)}, u32[]{:S(2)}, u32[]{:S(2)}) %collective-permute-start.11) | collective-permute-done | bytes 184352 | tf_op jit(solution)/shard_map/ppermute | solution.py:238
  65.4 5.8 %collective-permute-done.12 = bf16[9,32,320]{2,1,0:T(8,128)(2,1)S(1)} collective-permute-done((bf16[9,32,320]{2,1,0:T(8,128)(2,1)}, bf16[9,32,320]{2,1,0:T(8,128)(2,1)S(1)}, u32[]{:S(2)}, u32[]{:S(2)}) %collective-permute-start.12) | collective-permute-done | bytes 184352 | tf_op jit(solution)/shard_map/ppermute | solution.py:238
  71.5 0.7 gather_fusion.3
  73.5 2.0 %collective-permute-start.14 = (bf16[72,320]{1,0:T(8,128)(2,1)S(1)}, bf16[72,320]{1,0:T(8,128)(2,1)S(1)}, u32[]{:S(2)}, u32[]{:S(2)}) collective-permute-start(bf16[72,320]{1,0:T(8,128)(2,1)S(1)} %pad_maximum_fusion.2), channel_id=1, source_target_pairs={{12,0},{0,4},{4,8},{8,12},{13,1},{1,5},{5,9},{9,13},{14,2},{2,6},{... | collective-permute-start | bytes 138248 | tf_op jit(solution)/shard_map/ppermute | solution.py:16
  75.5 2.2 %collective-permute-done.15 = bf16[72,320]{1,0:T(8,128)(2,1)S(1)} collective-permute-done((bf16[72,320]{1,0:T(8,128)(2,1)S(1)}, bf16[72,320]{1,0:T(8,128)(2,1)S(1)}, u32[]{:S(2)}, u32[]{:S(2)}) %collective-permute-start.15) | collective-permute-done | bytes 46112 | tf_op jit(solution)/shard_map/ppermute | solution.py:16
  77.7 0.6 broadcast_select_fusion.2.refs_4_
  78.4 1.4 %collective-permute-done.14 = bf16[72,320]{1,0:T(8,128)(2,1)S(1)} collective-permute-done((bf16[72,320]{1,0:T(8,128)(2,1)S(1)}, bf16[72,320]{1,0:T(8,128)(2,1)S(1)}, u32[]{:S(2)}, u32[]{:S(2)}) %collective-permute-start.14) | collective-permute-done | bytes 46112 | tf_op jit(solution)/shard_map/ppermute | solution.py:16
  79.7 0.6 broadcast_select_fusion.4.refs_3_
  80.4 11.6 %shard_map.67 = bf16[72,32,320]{2,1,0:T(8,128)(2,1)} custom-call(bf16[72,32,320]{2,1,0:T(8,128)(2,1)} %shard_map.64.refs_0_, bf16[36,32,320]{2,1,0:T(8,128)(2,1)} %bitcast.53, bf16[36,32,320]{2,1,0:T(8,128)(2,1)} %bitcast.51, bf16[72,320]{1,0:T(8,128)(2,1)} %broadcast_select_fusion.4.refs_3_, bf16[72,320]{1,0:T(8,128)(2,1)} %broadcast_select_fusion.2.refs_4_, ...), custom_call_target="tpu_custom_call" | custom-call | tf_op jit(solution)/shard_map/pallas_call | solution.py:99
  (73 shorter events, 5.2 us)
Async XLA Ops:
  0.0 7.6 %copy-start = (f32[5,4,4]{0,2,1:T(4,128)S(1)}, f32[5,4,4]{0,2,1:T(4,128)}, u32[]{:S(2)}) copy-start(f32[5,4,4]{0,2,1:T(4,128)} %param.16) | copy-start | bytes 964
  0.0 7.1 %copy-start.1 = (bf16[1,72,32,320]{3,2,1,0:T(8,128)(2,1)S(1)}, bf16[1,72,32,320]{3,2,1,0:T(8,128)(2,1)}, u32[]{:S(2)}) copy-start(bf16[1,72,32,320]{3,2,1,0:T(8,128)(2,1)} %param.12) | copy-start | bytes 4423684
  2.0 6.9 %collective-permute-start.1 = (bf16[72,320]{1,0:T(8,128)(2,1)S(1)}, bf16[72,320]{1,0:T(8,128)(2,1)S(1)}, u32[]{:S(2)}, u32[]{:S(2)}) collective-permute-start(bf16[72,320]{1,0:T(8,128)(2,1)S(1)} %bitcast.64), channel_id=1, source_target_pairs={{4,0},{8,4},{12,8},{0,12},{5,1},{9,5},{13,9},{1,13},{6,2},{10,6},{... | collective-permute-start | bytes 138248 | tf_op jit(solution)/shard_map/ppermute | solution.py:16
  7.4 6.0 %collective-permute-start = (bf16[72,320]{1,0:T(8,128)(2,1)S(1)}, bf16[72,320]{1,0:T(8,128)(2,1)S(1)}, u32[]{:S(2)}, u32[]{:S(2)}) collective-permute-start(bf16[72,320]{1,0:T(8,128)(2,1)S(1)} %bitcast.65), channel_id=1, source_target_pairs={{12,0},{0,4},{4,8},{8,12},{13,1},{1,5},{5,9},{9,13},{14,2},{2,6},{... | collective-permute-start | bytes 138248 | tf_op jit(solution)/shard_map/ppermute | solution.py:16
  26.7 6.5 %copy-start.4 = (bf16[320,960]{1,0:T(8,128)(2,1)S(1)}, bf16[320,960]{1,0:T(8,128)(2,1)}, u32[]{:S(2)}) copy-start(bf16[320,960]{1,0:T(8,128)(2,1)} %param.14) | copy-start | bytes 1843204
  29.3 7.2 %collective-permute-start.2 = (bf16[9,32,320]{2,1,0:T(8,128)(2,1)S(1)}, bf16[9,32,320]{2,1,0:T(8,128)(2,1)S(1)}, u32[]{:S(2)}, u32[]{:S(2)}) collective-permute-start(bf16[9,32,320]{2,1,0:T(8,128)(2,1)S(1)} %get-tuple-element.34), channel_id=1, source_target_pairs={{0,1},{1,2},{2,3},{3,0},{4,5},{5,6},{6,7},{7,4},{8,9},{9,10},{10,1... | collective-permute-start | bytes 552968 | tf_op jit(solution)/shard_map/ppermute | solution.py:229
  29.3 8.7 %collective-permute-start.3 = (bf16[9,32,320]{2,1,0:T(8,128)(2,1)S(1)}, bf16[9,32,320]{2,1,0:T(8,128)(2,1)S(1)}, u32[]{:S(2)}, u32[]{:S(2)}) collective-permute-start(bf16[9,32,320]{2,1,0:T(8,128)(2,1)S(1)} %get-tuple-element.33), channel_id=1, source_target_pairs={{0,2},{1,3},{2,0},{3,1},{4,6},{5,7},{6,4},{7,5},{8,10},{9,11},{10,... | collective-permute-start | bytes 552968 | tf_op jit(solution)/shard_map/ppermute | solution.py:229
  30.9 10.5 %collective-permute-start.4 = (bf16[9,32,320]{2,1,0:T(8,128)(2,1)S(1)}, bf16[9,32,320]{2,1,0:T(8,128)(2,1)S(1)}, u32[]{:S(2)}, u32[]{:S(2)}) collective-permute-start(bf16[9,32,320]{2,1,0:T(8,128)(2,1)S(1)} %get-tuple-element.32), channel_id=1, source_target_pairs={{0,3},{1,0},{2,1},{3,2},{4,7},{5,4},{6,5},{7,6},{8,11},{9,8},{10,9... | collective-permute-start | bytes 552968 | tf_op jit(solution)/shard_map/ppermute | solution.py:229
  34.4 16.3 %collective-permute-start.10 = (bf16[9,32,320]{2,1,0:T(8,128)(2,1)S(1)}, bf16[9,32,320]{2,1,0:T(8,128)(2,1)S(1)}, u32[]{:S(2)}, u32[]{:S(2)}) collective-permute-start(bf16[9,32,320]{2,1,0:T(8,128)(2,1)S(1)} %get-tuple-element.28), channel_id=1, source_target_pairs={{0,3},{1,0},{2,1},{3,2},{4,7},{5,4},{6,5},{7,6},{8,11},{9,8},{10,9... | collective-permute-start | bytes 552968 | tf_op jit(solution)/shard_map/ppermute | solution.py:229
  34.4 16.3 %collective-permute-start.8 = (bf16[9,32,320]{2,1,0:T(8,128)(2,1)S(1)}, bf16[9,32,320]{2,1,0:T(8,128)(2,1)S(1)}, u32[]{:S(2)}, u32[]{:S(2)}) collective-permute-start(bf16[9,32,320]{2,1,0:T(8,128)(2,1)S(1)} %get-tuple-element.30), channel_id=1, source_target_pairs={{0,1},{1,2},{2,3},{3,0},{4,5},{5,6},{6,7},{7,4},{8,9},{9,10},{10,1... | collective-permute-start | bytes 552968 | tf_op jit(solution)/shard_map/ppermute | solution.py:229
  36.5 4.9 %copy-start.14 = (bf16[9,32,320]{2,1,0:T(8,128)(2,1)}, bf16[9,32,320]{2,1,0:T(8,128)(2,1)S(1)}, u32[]{:S(2)}) copy-start(bf16[9,32,320]{2,1,0:T(8,128)(2,1)S(1)} %collective-permute-done.2.refs_1_) | copy-start | bytes 552964
  36.5 14.8 %collective-permute-start.9 = (bf16[9,32,320]{2,1,0:T(8,128)(2,1)S(1)}, bf16[9,32,320]{2,1,0:T(8,128)(2,1)S(1)}, u32[]{:S(2)}, u32[]{:S(2)}) collective-permute-start(bf16[9,32,320]{2,1,0:T(8,128)(2,1)S(1)} %get-tuple-element.29), channel_id=1, source_target_pairs={{0,2},{1,3},{2,0},{3,1},{4,6},{5,7},{6,4},{7,5},{8,10},{9,11},{10,... | collective-permute-start | bytes 552968 | tf_op jit(solution)/shard_map/ppermute | solution.py:229
  38.0 3.4 %copy-start.15 = (bf16[9,32,320]{2,1,0:T(8,128)(2,1)}, bf16[9,32,320]{2,1,0:T(8,128)(2,1)S(1)}, u32[]{:S(2)}) copy-start(bf16[9,32,320]{2,1,0:T(8,128)(2,1)S(1)} %collective-permute-done.3.refs_2_) | copy-start | bytes 552964
  47.9 14.8 %copy-start.5 = (bf16[9,32,320]{2,1,0:T(8,128)(2,1)S(1)}, bf16[9,32,320]{2,1,0:T(8,128)(2,1)}, u32[]{:S(2)}) copy-start(bf16[9,32,320]{2,1,0:T(8,128)(2,1)} %get-tuple-element.16) | copy-start | bytes 552964
  47.9 12.7 %collective-permute-start.5 = (bf16[9,32,320]{2,1,0:T(8,128)(2,1)}, bf16[9,32,320]{2,1,0:T(8,128)(2,1)S(1)}, u32[]{:S(2)}, u32[]{:S(2)}) collective-permute-start(bf16[9,32,320]{2,1,0:T(8,128)(2,1)} %get-tuple-element.17), channel_id=1, source_target_pairs={{0,3},{1,0},{2,1},{3,2},{4,7},{5,4},{6,5},{7,6},{8,11},{9,8},{10,9... | collective-permute-start | bytes 552968 | tf_op jit(solution)/shard_map/ppermute | solution.py:238
  50.1 12.6 %collective-permute-start.6 = (bf16[9,32,320]{2,1,0:T(8,128)(2,1)}, bf16[9,32,320]{2,1,0:T(8,128)(2,1)S(1)}, u32[]{:S(2)}, u32[]{:S(2)}) collective-permute-start(bf16[9,32,320]{2,1,0:T(8,128)(2,1)} %get-tuple-element.18), channel_id=1, source_target_pairs={{0,2},{1,3},{2,0},{3,1},{4,6},{5,7},{6,4},{7,5},{8,10},{9,11},{10,... | collective-permute-start | bytes 552968 | tf_op jit(solution)/shard_map/ppermute | solution.py:238
  50.7 0.7 copy-start.11
  50.7 12.0 %collective-permute-start.7 = (bf16[9,32,320]{2,1,0:T(8,128)(2,1)}, bf16[9,32,320]{2,1,0:T(8,128)(2,1)S(1)}, u32[]{:S(2)}, u32[]{:S(2)}) collective-permute-start(bf16[9,32,320]{2,1,0:T(8,128)(2,1)} %get-tuple-element.19), channel_id=1, source_target_pairs={{0,1},{1,2},{2,3},{3,0},{4,5},{5,6},{6,7},{7,4},{8,9},{9,10},{10,1... | collective-permute-start | bytes 552968 | tf_op jit(solution)/shard_map/ppermute | solution.py:238
  50.7 0.7 copy-start.12
  51.3 0.7 copy-start.13
  57.8 7.7 %collective-permute-start.11 = (bf16[9,32,320]{2,1,0:T(8,128)(2,1)}, bf16[9,32,320]{2,1,0:T(8,128)(2,1)S(1)}, u32[]{:S(2)}, u32[]{:S(2)}) collective-permute-start(bf16[9,32,320]{2,1,0:T(8,128)(2,1)} %get-tuple-element.21), channel_id=1, source_target_pairs={{0,3},{1,0},{2,1},{3,2},{4,7},{5,4},{6,5},{7,6},{8,11},{9,8},{10,9... | collective-permute-start | bytes 552968 | tf_op jit(solution)/shard_map/ppermute | solution.py:238
  59.0 12.2 %collective-permute-start.12 = (bf16[9,32,320]{2,1,0:T(8,128)(2,1)}, bf16[9,32,320]{2,1,0:T(8,128)(2,1)S(1)}, u32[]{:S(2)}, u32[]{:S(2)}) collective-permute-start(bf16[9,32,320]{2,1,0:T(8,128)(2,1)} %get-tuple-element.22), channel_id=1, source_target_pairs={{0,2},{1,3},{2,0},{3,1},{4,6},{5,7},{6,4},{7,5},{8,10},{9,11},{10,... | collective-permute-start | bytes 552968 | tf_op jit(solution)/shard_map/ppermute | solution.py:238
  60.6 10.7 %collective-permute-start.13 = (bf16[9,32,320]{2,1,0:T(8,128)(2,1)}, bf16[9,32,320]{2,1,0:T(8,128)(2,1)S(1)}, u32[]{:S(2)}, u32[]{:S(2)}) collective-permute-start(bf16[9,32,320]{2,1,0:T(8,128)(2,1)} %get-tuple-element.23), channel_id=1, source_target_pairs={{0,1},{1,2},{2,3},{3,0},{4,5},{5,6},{6,7},{7,4},{8,9},{9,10},{10,1... | collective-permute-start | bytes 552968 | tf_op jit(solution)/shard_map/ppermute | solution.py:238
  62.7 8.6 %copy-start.6 = (bf16[9,32,320]{2,1,0:T(8,128)(2,1)S(1)}, bf16[9,32,320]{2,1,0:T(8,128)(2,1)}, u32[]{:S(2)}) copy-start(bf16[9,32,320]{2,1,0:T(8,128)(2,1)} %get-tuple-element.20) | copy-start | bytes 552964
  72.2 0.8 copy-start.10
  72.2 0.8 copy-start.9
  72.2 1.2 %copy-start.8 = (bf16[36,1,320]{2,1,0:T(2,128)(2,1)S(1)}, bf16[36,1,320]{2,1,0:T(2,128)(2,1)}, u32[]{:S(2)}) copy-start(bf16[36,1,320]{2,1,0:T(2,128)(2,1)} %get-tuple-element.26) | copy-start | bytes 69124
  72.3 1.2 %copy-start.7 = (bf16[36,1,320]{2,1,0:T(2,128)(2,1)S(1)}, bf16[36,1,320]{2,1,0:T(2,128)(2,1)}, u32[]{:S(2)}) copy-start(bf16[36,1,320]{2,1,0:T(2,128)(2,1)} %get-tuple-element.25) | copy-start | bytes 69124
  72.5 7.9 %copy-start.2 = (bf16[4,9,32,320]{3,2,1,0:T(8,128)(2,1)}, bf16[4,9,32,320]{3,2,1,0:T(8,128)(2,1)S(1)}, u32[]{:S(2)}) copy-start(bf16[4,9,32,320]{3,2,1,0:T(8,128)(2,1)S(1)} %get-tuple-element.40) | copy-start | bytes 2211844
  72.5 7.8 %copy-start.3 = (bf16[4,9,32,320]{3,2,1,0:T(8,128)(2,1)}, bf16[4,9,32,320]{3,2,1,0:T(8,128)(2,1)S(1)}, u32[]{:S(2)}) copy-start(bf16[4,9,32,320]{3,2,1,0:T(8,128)(2,1)S(1)} %get-tuple-element.41) | copy-start | bytes 2211844
  73.1 4.6 %collective-permute-start.15 = (bf16[72,320]{1,0:T(8,128)(2,1)S(1)}, bf16[72,320]{1,0:T(8,128)(2,1)S(1)}, u32[]{:S(2)}, u32[]{:S(2)}) collective-permute-start(bf16[72,320]{1,0:T(8,128)(2,1)S(1)} %pad_maximum_fusion.3), channel_id=1, source_target_pairs={{4,0},{8,4},{12,8},{0,12},{5,1},{9,5},{13,9},{1,13},{6,2},{10,6},{... | collective-permute-start | bytes 138248 | tf_op jit(solution)/shard_map/ppermute | solution.py:16
  73.5 6.2 %collective-permute-start.14 = (bf16[72,320]{1,0:T(8,128)(2,1)S(1)}, bf16[72,320]{1,0:T(8,128)(2,1)S(1)}, u32[]{:S(2)}, u32[]{:S(2)}) collective-permute-start(bf16[72,320]{1,0:T(8,128)(2,1)S(1)} %pad_maximum_fusion.2), channel_id=1, source_target_pairs={{12,0},{0,4},{4,8},{8,12},{13,1},{1,5},{5,9},{9,13},{14,2},{2,6},{... | collective-permute-start | bytes 138248 | tf_op jit(solution)/shard_map/ppermute | solution.py:16
  (1 other events, 0.7 us)

commit v20 on v18

--- a/solution.py
+++ b/solution.py
@@ -254,7 +254,7 @@
     returned = []
     rotate = frames_all <= 4 and half % frames_all == 0
     if rotate:
-        whole = convolve([[tile]], rims, conv1_weight, norm_gelu, 0, row_count, 6)
+        whole = convolve([[tile]], rims, conv1_weight, norm_gelu, 0, row_count, 18)
         for lo in (0, half):
             returned.append(rotated_attention(whole, lo, half, qkv_weight, pos_bias, out_weight))
         hidden_rows = [whole]

time: 92.6 us -> 92.3 us (level)
  no operation moved by 1% of the time
where the time goes in v20:
time: 92.3 us; the launch traced here: 92 us
  Pallas kernels  35.9 us (39%)
  waiting for transfers between devices  20.7 us (22%)
  starting transfers between devices  18.1 us (20%)
  local copies, waits for them, and re-layouts  11.2 us (12%)
  other arithmetic  3.51 us (4%)
  matrix products  2.29 us (2%)
    pallas_call x2, Pallas kernels, convolve(): pl.pallas_call(functools.partial(conv_kernel, layout=tuple(layout), lo=lo...  24.2 us
    pallas_call x2, Pallas kernels, attend_pieces(): pl.pallas_call(functools.partial(attend_kernel, parts=frames_all), out_sh...  11.6 us
    ppermute x6, waiting for transfers between devices, rotated_attention(): lax.ppermute(piece, 'frame', [(i, (i - s) % frames_all) for i in range(fr...  7.58 us
    ppermute x4, waiting for transfers between devices, shifted(): moved = lax.ppermute(block, axis, route)  7.55 us
    ppermute x4, starting transfers between devices, shifted(): moved = lax.ppermute(block, axis, route)  7.51 us
    ppermute x6, starting transfers between devices, rotated_attention(): lax.ppermute(piece, 'frame', [(i, (i - s) % frames_all) for i in range(fr...  5.57 us
    ppermute x6, waiting for transfers between devices, rotated_attention(): lax.ppermute(piece, 'frame', [(i, (i + s) % frames_all) for i in range(fr...  5.53 us
    ppermute x6, starting transfers between devices, rotated_attention(): lax.ppermute(piece, 'frame', [(i, (i + s) % frames_all) for i in range(fr...  5.02 us
  transfers between devices with their start and end apart: 16, of which 8 were waited for; matrix products, arithmetic and copies ran while one was open for 9% of the time, Pallas kernels for 13%

profile of v20, /device:TPU:0, one launch (start us, length us, event | category | flops | bytes accessed | tf_op | source)
XLA Modules:
  0.0 92.0 jit_solution(15329341528019021565)
XLA Ops:
  0.0 1.9 %fusion.4 = bf16[1,72,320]{2,0,1:T(2,128)(2,1)S(1)} fusion(bf16[1,72,32,320]{3,2,1,0:T(8,128)(2,1)} %param.12), kind=kOutput, calls=%fused_computation.42 | convolution fusion | flops 1474592 | bytes 1520640 | tf_op jit(solution)/shard_map/rwc,w->rc/dot_general | solution.py:250
  2.0 5.1 %collective-permute-start.1 = (bf16[72,320]{1,0:T(8,128)(2,1)S(1)}, bf16[72,320]{1,0:T(8,128)(2,1)S(1)}, u32[]{:S(2)}, u32[]{:S(2)}) collective-permute-start(bf16[72,320]{1,0:T(8,128)(2,1)S(1)} %bitcast.64), channel_id=1, source_target_pairs={{4,0},{8,4},{12,8},{0,12},{5,1},{9,5},{13,9},{1,13},{6,2},{10,6},{... | collective-permute-start | bytes 138248 | tf_op jit(solution)/shard_map/ppermute | solution.py:16
  7.6 0.6 gather_fusion
  8.9 0.6 broadcast_select_fusion.3.refs_2_
  9.5 3.9 %collective-permute-done = bf16[72,320]{1,0:T(8,128)(2,1)S(1)} collective-permute-done((bf16[72,320]{1,0:T(8,128)(2,1)S(1)}, bf16[72,320]{1,0:T(8,128)(2,1)S(1)}, u32[]{:S(2)}, u32[]{:S(2)}) %collective-permute-start) | collective-permute-done | bytes 46112 | tf_op jit(solution)/shard_map/ppermute | solution.py:16
  13.5 0.6 broadcast_select_fusion.5.refs_1_
  14.1 12.7 %shard_map.64.refs_0_ = bf16[72,32,320]{2,1,0:T(8,128)(2,1)} custom-call(bf16[72,32,320]{2,1,0:T(8,128)(2,1)} %bitcast.47, bf16[72,320]{1,0:T(8,128)(2,1)} %broadcast_select_fusion.5.refs_1_, bf16[72,320]{1,0:T(8,128)(2,1)} %broadcast_select_fusion.3.refs_2_, bf16[3,960,320]{2,1,0:T(8,128)(2,1)} %bitcast.54), custom_call_target="tpu_custom_call" | custom-call | tf_op jit(solution)/shard_map/pallas_call | solution.py:99
  26.7 2.6 %constant_dynamic-slice_fusion = (bf16[9,32,320]{2,1,0:T(8,128)(2,1)S(1)}, bf16[9,32,320]{2,1,0:T(8,128)(2,1)S(1)}, bf16[9,32,320]{2,1,0:T(8,128)(2,1)S(1)}, bf1...) fusion(bf16[72,32,320]{2,1,0:T(8,128)(2,1)} %shard_map.64.refs_, ...), kind=kLoop, calls=%fused_computation.34 | loop fusion | bytes 2949152 | tf_op jit(solution)/shard_map/dynamic_slice | solution.py:227
  29.4 1.6 %collective-permute-start.3 = (bf16[9,32,320]{2,1,0:T(8,128)(2,1)S(1)}, bf16[9,32,320]{2,1,0:T(8,128)(2,1)S(1)}, u32[]{:S(2)}, u32[]{:S(2)}) collective-permute-start(bf16[9,32,320]{2,1,0:T(8,128)(2,1)S(1)} %get-tuple-element.33), channel_id=1, source_target_pairs={{0,2},{1,3},{2,0},{3,1},{4,6},{5,7},{6,4},{7,5},{8,10},{9,11},{10,... | collective-permute-start | bytes 552968 | tf_op jit(solution)/shard_map/ppermute | solution.py:229
  30.9 1.4 %collective-permute-start.4 = (bf16[9,32,320]{2,1,0:T(8,128)(2,1)S(1)}, bf16[9,32,320]{2,1,0:T(8,128)(2,1)S(1)}, u32[]{:S(2)}, u32[]{:S(2)}) collective-permute-start(bf16[9,32,320]{2,1,0:T(8,128)(2,1)S(1)} %get-tuple-element.32), channel_id=1, source_target_pairs={{0,3},{1,0},{2,1},{3,2},{4,7},{5,4},{6,5},{7,6},{8,11},{9,8},{10,9... | collective-permute-start | bytes 552968 | tf_op jit(solution)/shard_map/ppermute | solution.py:229
  32.4 0.8 copy.32.refs_5_
  33.2 1.2 %copy.30 = bf16[320,960]{0,1:T(8,128)(2,1)} copy(bf16[320,960]{1,0:T(8,128)(2,1)S(1)} %copy-done.4) | data formatting | bytes 1228800 | tf_op args[2]
  34.9 1.6 %collective-permute-done.2.refs_1_ = bf16[9,32,320]{2,1,0:T(8,128)(2,1)S(1)} collective-permute-done((bf16[9,32,320]{2,1,0:T(8,128)(2,1)S(1)}, bf16[9,32,320]{2,1,0:T(8,128)(2,1)S(1)}, u32[]{:S(2)}, u32[]{:S(2)}) %collective-permute-start.2) | collective-permute-done | bytes 184352 | tf_op jit(solution)/shard_map/ppermute | solution.py:229
  36.5 1.5 %collective-permute-start.9 = (bf16[9,32,320]{2,1,0:T(8,128)(2,1)S(1)}, bf16[9,32,320]{2,1,0:T(8,128)(2,1)S(1)}, u32[]{:S(2)}, u32[]{:S(2)}) collective-permute-start(bf16[9,32,320]{2,1,0:T(8,128)(2,1)S(1)} %get-tuple-element.29), channel_id=1, source_target_pairs={{0,2},{1,3},{2,0},{3,1},{4,6},{5,7},{6,4},{7,5},{8,10},{9,11},{10,... | collective-permute-start | bytes 552968 | tf_op jit(solution)/shard_map/ppermute | solution.py:229
  38.1 3.4 %collective-permute-done.4.refs_3_ = bf16[9,32,320]{2,1,0:T(8,128)(2,1)S(1)} collective-permute-done((bf16[9,32,320]{2,1,0:T(8,128)(2,1)S(1)}, bf16[9,32,320]{2,1,0:T(8,128)(2,1)S(1)}, u32[]{:S(2)}, u32[]{:S(2)}) %collective-permute-start.4) | collective-permute-done | bytes 184352 | tf_op jit(solution)/shard_map/ppermute | solution.py:229
  41.4 0.7 copy-done.16
  42.1 5.8 %shard_map.65 = (bf16[9,32,320]{2,1,0:T(8,128)(2,1)}, bf16[9,32,320]{2,1,0:T(8,128)(2,1)}, bf16[9,32,320]{2,1,0:T(8,128)(2,1)}, bf16[9,32,320]{2,1,0:T(8,128)(2,1)}) custom-call(bf16[9,32,320]{2,1,0:T(8,128)(2,1)} %get-tuple-element.35.refs_0_, bf16[9,32,320]{2,1,0:T(8,128)(2,1)} %copy-done.14, bf16[9,32,320]{2,1,0:T(8,128)(2,1)} %copy-done.15, ...), custom_call_target="tpu_custom_call" | custom-call | tf_op jit(solution)/shard_map/pallas_call | solution.py:193
  47.9 2.2 %collective-permute-start.5 = (bf16[9,32,320]{2,1,0:T(8,128)(2,1)}, bf16[9,32,320]{2,1,0:T(8,128)(2,1)S(1)}, u32[]{:S(2)}, u32[]{:S(2)}) collective-permute-start(bf16[9,32,320]{2,1,0:T(8,128)(2,1)} %get-tuple-element.17), channel_id=1, source_target_pairs={{0,3},{1,0},{2,1},{3,2},{4,7},{5,4},{6,5},{7,6},{8,11},{9,8},{10,9... | collective-permute-start | bytes 552968 | tf_op jit(solution)/shard_map/ppermute | solution.py:238
  52.0 5.8 %shard_map.66 = (bf16[9,32,320]{2,1,0:T(8,128)(2,1)}, bf16[9,32,320]{2,1,0:T(8,128)(2,1)}, bf16[9,32,320]{2,1,0:T(8,128)(2,1)}, bf16[9,32,320]{2,1,0:T(8,128)(2,1)}) custom-call(bf16[9,32,320]{2,1,0:T(8,128)(2,1)} %get-tuple-element.31.refs_0_, bf16[9,32,320]{2,1,0:T(8,128)(2,1)} %copy-done.12, bf16[9,32,320]{2,1,0:T(8,128)(2,1)} %copy-done.13, ...), custom_call_target="tpu_custom_call" | custom-call | tf_op jit(solution)/shard_map/pallas_call | solution.py:193
  57.8 1.3 %collective-permute-start.11 = (bf16[9,32,320]{2,1,0:T(8,128)(2,1)}, bf16[9,32,320]{2,1,0:T(8,128)(2,1)S(1)}, u32[]{:S(2)}, u32[]{:S(2)}) collective-permute-start(bf16[9,32,320]{2,1,0:T(8,128)(2,1)} %get-tuple-element.21), channel_id=1, source_target_pairs={{0,3},{1,0},{2,1},{3,2},{4,7},{5,4},{6,5},{7,6},{8,11},{9,8},{10,9... | collective-permute-start | bytes 552968 | tf_op jit(solution)/shard_map/ppermute | solution.py:238
  59.1 1.5 %collective-permute-start.12 = (bf16[9,32,320]{2,1,0:T(8,128)(2,1)}, bf16[9,32,320]{2,1,0:T(8,128)(2,1)S(1)}, u32[]{:S(2)}, u32[]{:S(2)}) collective-permute-start(bf16[9,32,320]{2,1,0:T(8,128)(2,1)} %get-tuple-element.22), channel_id=1, source_target_pairs={{0,2},{1,3},{2,0},{3,1},{4,6},{5,7},{6,4},{7,5},{8,10},{9,11},{10,... | collective-permute-start | bytes 552968 | tf_op jit(solution)/shard_map/ppermute | solution.py:238
  60.6 2.1 %fusion.19 = (bf16[36,1,320]{2,1,0:T(2,128)(2,1)}, bf16[36,1,320]{2,1,0:T(2,128)(2,1)}, bf16[36,1,320]{2,1,0:T(2,128)(2,1)}, bf16[36,1,320]{2,1,0:T(2,128)(2,1)}) fusion(bf16[72,32,320]{2,1,0:T(8,128)(2,1)} %shard_map.64.refs_0_), kind=kLoop, calls=%fused_computation.61 | loop fusion | bytes 184320 | tf_op jit(solution)/shard_map/slice | solution.py:279
  63.0 0.7 gather_fusion.2
  63.7 1.8 %collective-permute-done.11 = bf16[9,32,320]{2,1,0:T(8,128)(2,1)S(1)} collective-permute-done((bf16[9,32,320]{2,1,0:T(8,128)(2,1)}, bf16[9,32,320]{2,1,0:T(8,128)(2,1)S(1)}, u32[]{:S(2)}, u32[]{:S(2)}) %collective-permute-start.11) | collective-permute-done | bytes 184352 | tf_op jit(solution)/shard_map/ppermute | solution.py:238
  65.5 5.8 %collective-permute-done.12 = bf16[9,32,320]{2,1,0:T(8,128)(2,1)S(1)} collective-permute-done((bf16[9,32,320]{2,1,0:T(8,128)(2,1)}, bf16[9,32,320]{2,1,0:T(8,128)(2,1)S(1)}, u32[]{:S(2)}, u32[]{:S(2)}) %collective-permute-start.12) | collective-permute-done | bytes 184352 | tf_op jit(solution)/shard_map/ppermute | solution.py:238
  71.5 0.7 gather_fusion.3
  73.5 2.0 %collective-permute-start.14 = (bf16[72,320]{1,0:T(8,128)(2,1)S(1)}, bf16[72,320]{1,0:T(8,128)(2,1)S(1)}, u32[]{:S(2)}, u32[]{:S(2)}) collective-permute-start(bf16[72,320]{1,0:T(8,128)(2,1)S(1)} %pad_maximum_fusion.2), channel_id=1, source_target_pairs={{12,0},{0,4},{4,8},{8,12},{13,1},{1,5},{5,9},{9,13},{14,2},{2,6},{... | collective-permute-start | bytes 138248 | tf_op jit(solution)/shard_map/ppermute | solution.py:16
  75.6 2.2 %collective-permute-done.15 = bf16[72,320]{1,0:T(8,128)(2,1)S(1)} collective-permute-done((bf16[72,320]{1,0:T(8,128)(2,1)S(1)}, bf16[72,320]{1,0:T(8,128)(2,1)S(1)}, u32[]{:S(2)}, u32[]{:S(2)}) %collective-permute-start.15) | collective-permute-done | bytes 46112 | tf_op jit(solution)/shard_map/ppermute | solution.py:16
  77.8 0.6 broadcast_select_fusion.2.refs_4_
  78.4 1.4 %collective-permute-done.14 = bf16[72,320]{1,0:T(8,128)(2,1)S(1)} collective-permute-done((bf16[72,320]{1,0:T(8,128)(2,1)S(1)}, bf16[72,320]{1,0:T(8,128)(2,1)S(1)}, u32[]{:S(2)}, u32[]{:S(2)}) %collective-permute-start.14) | collective-permute-done | bytes 46112 | tf_op jit(solution)/shard_map/ppermute | solution.py:16
  79.8 0.6 broadcast_select_fusion.4.refs_3_
  80.4 11.6 %shard_map.67 = bf16[72,32,320]{2,1,0:T(8,128)(2,1)} custom-call(bf16[72,32,320]{2,1,0:T(8,128)(2,1)} %shard_map.64.refs_0_, bf16[36,32,320]{2,1,0:T(8,128)(2,1)} %bitcast.53, bf16[36,32,320]{2,1,0:T(8,128)(2,1)} %bitcast.51, bf16[72,320]{1,0:T(8,128)(2,1)} %broadcast_select_fusion.4.refs_3_, bf16[72,320]{1,0:T(8,128)(2,1)} %broadcast_select_fusion.2.refs_4_, ...), custom_call_target="tpu_custom_call" | custom-call | tf_op jit(solution)/shard_map/pallas_call | solution.py:99
  (73 shorter events, 5.2 us)
Async XLA Ops:
  0.0 7.6 %copy-start = (f32[5,4,4]{0,2,1:T(4,128)S(1)}, f32[5,4,4]{0,2,1:T(4,128)}, u32[]{:S(2)}) copy-start(f32[5,4,4]{0,2,1:T(4,128)} %param.16) | copy-start | bytes 964
  0.0 7.1 %copy-start.1 = (bf16[1,72,32,320]{3,2,1,0:T(8,128)(2,1)S(1)}, bf16[1,72,32,320]{3,2,1,0:T(8,128)(2,1)}, u32[]{:S(2)}) copy-start(bf16[1,72,32,320]{3,2,1,0:T(8,128)(2,1)} %param.12) | copy-start | bytes 4423684
  2.0 6.9 %collective-permute-start.1 = (bf16[72,320]{1,0:T(8,128)(2,1)S(1)}, bf16[72,320]{1,0:T(8,128)(2,1)S(1)}, u32[]{:S(2)}, u32[]{:S(2)}) collective-permute-start(bf16[72,320]{1,0:T(8,128)(2,1)S(1)} %bitcast.64), channel_id=1, source_target_pairs={{4,0},{8,4},{12,8},{0,12},{5,1},{9,5},{13,9},{1,13},{6,2},{10,6},{... | collective-permute-start | bytes 138248 | tf_op jit(solution)/shard_map/ppermute | solution.py:16
  7.4 6.0 %collective-permute-start = (bf16[72,320]{1,0:T(8,128)(2,1)S(1)}, bf16[72,320]{1,0:T(8,128)(2,1)S(1)}, u32[]{:S(2)}, u32[]{:S(2)}) collective-permute-start(bf16[72,320]{1,0:T(8,128)(2,1)S(1)} %bitcast.65), channel_id=1, source_target_pairs={{12,0},{0,4},{4,8},{8,12},{13,1},{1,5},{5,9},{9,13},{14,2},{2,6},{... | collective-permute-start | bytes 138248 | tf_op jit(solution)/shard_map/ppermute | solution.py:16
  26.7 6.5 %copy-start.4 = (bf16[320,960]{1,0:T(8,128)(2,1)S(1)}, bf16[320,960]{1,0:T(8,128)(2,1)}, u32[]{:S(2)}) copy-start(bf16[320,960]{1,0:T(8,128)(2,1)} %param.14) | copy-start | bytes 1843204
  29.3 7.2 %collective-permute-start.2 = (bf16[9,32,320]{2,1,0:T(8,128)(2,1)S(1)}, bf16[9,32,320]{2,1,0:T(8,128)(2,1)S(1)}, u32[]{:S(2)}, u32[]{:S(2)}) collective-permute-start(bf16[9,32,320]{2,1,0:T(8,128)(2,1)S(1)} %get-tuple-element.34), channel_id=1, source_target_pairs={{0,1},{1,2},{2,3},{3,0},{4,5},{5,6},{6,7},{7,4},{8,9},{9,10},{10,1... | collective-permute-start | bytes 552968 | tf_op jit(solution)/shard_map/ppermute | solution.py:229
  29.4 8.7 %collective-permute-start.3 = (bf16[9,32,320]{2,1,0:T(8,128)(2,1)S(1)}, bf16[9,32,320]{2,1,0:T(8,128)(2,1)S(1)}, u32[]{:S(2)}, u32[]{:S(2)}) collective-permute-start(bf16[9,32,320]{2,1,0:T(8,128)(2,1)S(1)} %get-tuple-element.33), channel_id=1, source_target_pairs={{0,2},{1,3},{2,0},{3,1},{4,6},{5,7},{6,4},{7,5},{8,10},{9,11},{10,... | collective-permute-start | bytes 552968 | tf_op jit(solution)/shard_map/ppermute | solution.py:229
  30.9 10.5 %collective-permute-start.4 = (bf16[9,32,320]{2,1,0:T(8,128)(2,1)S(1)}, bf16[9,32,320]{2,1,0:T(8,128)(2,1)S(1)}, u32[]{:S(2)}, u32[]{:S(2)}) collective-permute-start(bf16[9,32,320]{2,1,0:T(8,128)(2,1)S(1)} %get-tuple-element.32), channel_id=1, source_target_pairs={{0,3},{1,0},{2,1},{3,2},{4,7},{5,4},{6,5},{7,6},{8,11},{9,8},{10,9... | collective-permute-start | bytes 552968 | tf_op jit(solution)/shard_map/ppermute | solution.py:229
  34.4 16.3 %collective-permute-start.10 = (bf16[9,32,320]{2,1,0:T(8,128)(2,1)S(1)}, bf16[9,32,320]{2,1,0:T(8,128)(2,1)S(1)}, u32[]{:S(2)}, u32[]{:S(2)}) collective-permute-start(bf16[9,32,320]{2,1,0:T(8,128)(2,1)S(1)} %get-tuple-element.28), channel_id=1, source_target_pairs={{0,3},{1,0},{2,1},{3,2},{4,7},{5,4},{6,5},{7,6},{8,11},{9,8},{10,9... | collective-permute-start | bytes 552968 | tf_op jit(solution)/shard_map/ppermute | solution.py:229
  34.4 16.3 %collective-permute-start.8 = (bf16[9,32,320]{2,1,0:T(8,128)(2,1)S(1)}, bf16[9,32,320]{2,1,0:T(8,128)(2,1)S(1)}, u32[]{:S(2)}, u32[]{:S(2)}) collective-permute-start(bf16[9,32,320]{2,1,0:T(8,128)(2,1)S(1)} %get-tuple-element.30), channel_id=1, source_target_pairs={{0,1},{1,2},{2,3},{3,0},{4,5},{5,6},{6,7},{7,4},{8,9},{9,10},{10,1... | collective-permute-start | bytes 552968 | tf_op jit(solution)/shard_map/ppermute | solution.py:229
  36.5 4.9 %copy-start.14 = (bf16[9,32,320]{2,1,0:T(8,128)(2,1)}, bf16[9,32,320]{2,1,0:T(8,128)(2,1)S(1)}, u32[]{:S(2)}) copy-start(bf16[9,32,320]{2,1,0:T(8,128)(2,1)S(1)} %collective-permute-done.2.refs_1_) | copy-start | bytes 552964
  36.5 14.8 %collective-permute-start.9 = (bf16[9,32,320]{2,1,0:T(8,128)(2,1)S(1)}, bf16[9,32,320]{2,1,0:T(8,128)(2,1)S(1)}, u32[]{:S(2)}, u32[]{:S(2)}) collective-permute-start(bf16[9,32,320]{2,1,0:T(8,128)(2,1)S(1)} %get-tuple-element.29), channel_id=1, source_target_pairs={{0,2},{1,3},{2,0},{3,1},{4,6},{5,7},{6,4},{7,5},{8,10},{9,11},{10,... | collective-permute-start | bytes 552968 | tf_op jit(solution)/shard_map/ppermute | solution.py:229
  38.1 3.4 %copy-start.15 = (bf16[9,32,320]{2,1,0:T(8,128)(2,1)}, bf16[9,32,320]{2,1,0:T(8,128)(2,1)S(1)}, u32[]{:S(2)}) copy-start(bf16[9,32,320]{2,1,0:T(8,128)(2,1)S(1)} %collective-permute-done.3.refs_2_) | copy-start | bytes 552964
  47.9 14.8 %copy-start.5 = (bf16[9,32,320]{2,1,0:T(8,128)(2,1)S(1)}, bf16[9,32,320]{2,1,0:T(8,128)(2,1)}, u32[]{:S(2)}) copy-start(bf16[9,32,320]{2,1,0:T(8,128)(2,1)} %get-tuple-element.16) | copy-start | bytes 552964
  47.9 12.7 %collective-permute-start.5 = (bf16[9,32,320]{2,1,0:T(8,128)(2,1)}, bf16[9,32,320]{2,1,0:T(8,128)(2,1)S(1)}, u32[]{:S(2)}, u32[]{:S(2)}) collective-permute-start(bf16[9,32,320]{2,1,0:T(8,128)(2,1)} %get-tuple-element.17), channel_id=1, source_target_pairs={{0,3},{1,0},{2,1},{3,2},{4,7},{5,4},{6,5},{7,6},{8,11},{9,8},{10,9... | collective-permute-start | bytes 552968 | tf_op jit(solution)/shard_map/ppermute | solution.py:238
  50.1 12.6 %collective-permute-start.6 = (bf16[9,32,320]{2,1,0:T(8,128)(2,1)}, bf16[9,32,320]{2,1,0:T(8,128)(2,1)S(1)}, u32[]{:S(2)}, u32[]{:S(2)}) collective-permute-start(bf16[9,32,320]{2,1,0:T(8,128)(2,1)} %get-tuple-element.18), channel_id=1, source_target_pairs={{0,2},{1,3},{2,0},{3,1},{4,6},{5,7},{6,4},{7,5},{8,10},{9,11},{10,... | collective-permute-start | bytes 552968 | tf_op jit(solution)/shard_map/ppermute | solution.py:238
  50.7 0.7 copy-start.11
  50.7 12.0 %collective-permute-start.7 = (bf16[9,32,320]{2,1,0:T(8,128)(2,1)}, bf16[9,32,320]{2,1,0:T(8,128)(2,1)S(1)}, u32[]{:S(2)}, u32[]{:S(2)}) collective-permute-start(bf16[9,32,320]{2,1,0:T(8,128)(2,1)} %get-tuple-element.19), channel_id=1, source_target_pairs={{0,1},{1,2},{2,3},{3,0},{4,5},{5,6},{6,7},{7,4},{8,9},{9,10},{10,1... | collective-permute-start | bytes 552968 | tf_op jit(solution)/shard_map/ppermute | solution.py:238
  50.7 0.7 copy-start.12
  51.3 0.7 copy-start.13
  57.8 7.7 %collective-permute-start.11 = (bf16[9,32,320]{2,1,0:T(8,128)(2,1)}, bf16[9,32,320]{2,1,0:T(8,128)(2,1)S(1)}, u32[]{:S(2)}, u32[]{:S(2)}) collective-permute-start(bf16[9,32,320]{2,1,0:T(8,128)(2,1)} %get-tuple-element.21), channel_id=1, source_target_pairs={{0,3},{1,0},{2,1},{3,2},{4,7},{5,4},{6,5},{7,6},{8,11},{9,8},{10,9... | collective-permute-start | bytes 552968 | tf_op jit(solution)/shard_map/ppermute | solution.py:238
  59.1 12.2 %collective-permute-start.12 = (bf16[9,32,320]{2,1,0:T(8,128)(2,1)}, bf16[9,32,320]{2,1,0:T(8,128)(2,1)S(1)}, u32[]{:S(2)}, u32[]{:S(2)}) collective-permute-start(bf16[9,32,320]{2,1,0:T(8,128)(2,1)} %get-tuple-element.22), channel_id=1, source_target_pairs={{0,2},{1,3},{2,0},{3,1},{4,6},{5,7},{6,4},{7,5},{8,10},{9,11},{10,... | collective-permute-start | bytes 552968 | tf_op jit(solution)/shard_map/ppermute | solution.py:238
  60.6 10.7 %collective-permute-start.13 = (bf16[9,32,320]{2,1,0:T(8,128)(2,1)}, bf16[9,32,320]{2,1,0:T(8,128)(2,1)S(1)}, u32[]{:S(2)}, u32[]{:S(2)}) collective-permute-start(bf16[9,32,320]{2,1,0:T(8,128)(2,1)} %get-tuple-element.23), channel_id=1, source_target_pairs={{0,1},{1,2},{2,3},{3,0},{4,5},{5,6},{6,7},{7,4},{8,9},{9,10},{10,1... | collective-permute-start | bytes 552968 | tf_op jit(solution)/shard_map/ppermute | solution.py:238
  62.7 8.6 %copy-start.6 = (bf16[9,32,320]{2,1,0:T(8,128)(2,1)S(1)}, bf16[9,32,320]{2,1,0:T(8,128)(2,1)}, u32[]{:S(2)}) copy-start(bf16[9,32,320]{2,1,0:T(8,128)(2,1)} %get-tuple-element.20) | copy-start | bytes 552964
  72.2 0.8 copy-start.10
  72.3 0.8 copy-start.9
  72.3 1.2 %copy-start.8 = (bf16[36,1,320]{2,1,0:T(2,128)(2,1)S(1)}, bf16[36,1,320]{2,1,0:T(2,128)(2,1)}, u32[]{:S(2)}) copy-start(bf16[36,1,320]{2,1,0:T(2,128)(2,1)} %get-tuple-element.26) | copy-start | bytes 69124
  72.3 1.2 %copy-start.7 = (bf16[36,1,320]{2,1,0:T(2,128)(2,1)S(1)}, bf16[36,1,320]{2,1,0:T(2,128)(2,1)}, u32[]{:S(2)}) copy-start(bf16[36,1,320]{2,1,0:T(2,128)(2,1)} %get-tuple-element.25) | copy-start | bytes 69124
  72.6 7.9 %copy-start.2 = (bf16[4,9,32,320]{3,2,1,0:T(8,128)(2,1)}, bf16[4,9,32,320]{3,2,1,0:T(8,128)(2,1)S(1)}, u32[]{:S(2)}) copy-start(bf16[4,9,32,320]{3,2,1,0:T(8,128)(2,1)S(1)} %get-tuple-element.40) | copy-start | bytes 2211844
  72.6 7.8 %copy-start.3 = (bf16[4,9,32,320]{3,2,1,0:T(8,128)(2,1)}, bf16[4,9,32,320]{3,2,1,0:T(8,128)(2,1)S(1)}, u32[]{:S(2)}) copy-start(bf16[4,9,32,320]{3,2,1,0:T(8,128)(2,1)S(1)} %get-tuple-element.41) | copy-start | bytes 2211844
  73.1 4.6 %collective-permute-start.15 = (bf16[72,320]{1,0:T(8,128)(2,1)S(1)}, bf16[72,320]{1,0:T(8,128)(2,1)S(1)}, u32[]{:S(2)}, u32[]{:S(2)}) collective-permute-start(bf16[72,320]{1,0:T(8,128)(2,1)S(1)} %pad_maximum_fusion.3), channel_id=1, source_target_pairs={{4,0},{8,4},{12,8},{0,12},{5,1},{9,5},{13,9},{1,13},{6,2},{10,6},{... | collective-permute-start | bytes 138248 | tf_op jit(solution)/shard_map/ppermute | solution.py:16
  73.5 6.2 %collective-permute-start.14 = (bf16[72,320]{1,0:T(8,128)(2,1)S(1)}, bf16[72,320]{1,0:T(8,128)(2,1)S(1)}, u32[]{:S(2)}, u32[]{:S(2)}) collective-permute-start(bf16[72,320]{1,0:T(8,128)(2,1)S(1)} %pad_maximum_fusion.2), channel_id=1, source_target_pairs={{12,0},{0,4},{4,8},{8,12},{13,1},{1,5},{5,9},{9,13},{14,2},{2,6},{... | collective-permute-start | bytes 138248 | tf_op jit(solution)/shard_map/ppermute | solution.py:16
  (1 other events, 0.7 us)
